TPU v7x, 128 devices: a whole 4x4x4 slice. The times are simulated.
128 devices in a mesh: img: 8 (over z_hi, y), cap: 16 (over x, z_lo, core).
Axes of the slice: x: 4, y: 4, z: 4 (z_hi: 2, z_lo: 2; z = z_hi * 2 + z_lo), core: 2. Of those that a mesh axis runs over, the one named last changes fastest.
Arguments:
- images: float32 [16384, 768], P('img'), may hold values from -100 to 100
- captions: float32 [16384, 768], P('cap', 'img'), may hold values from -8 to 8
- bank: float32 [16384, 768], P('img'), may hold values from -100 to 100
Outputs:
- expected: float32 [16384, 768], P('img')
All inputs are finite; a program needn't handle non-finite values.
Results may differ from a plain program's by a relative error of at most 0.0003.
Values sent between devices are 32-bit elements; how exact they have to be, the bound alone decides.
No kernel may reach another device: no remote copies, remote signals or barrier semaphores. Data moves between devices by JAX's collectives and lax.ppermute only.
A program may use at most 448 MiB of HBM per device.

v0:
```python
import jax
import jax.numpy as jnp
from jax import lax
from jax.sharding import Mesh
from jax.sharding import PartitionSpec as P

exponent_divisor = 0.03

IMG = ("zh", "y")
CAP = ("x", "zl", "core")


def similar(query_factor, target_factor):
    return exponent_divisor * lax.dot_general(
        query_factor,
        target_factor,
        (((1,), (1,)), ((), ())),
        precision=lax.Precision.HIGHEST,
        preferred_element_type=jnp.float32,
    )


def rescaled_affinity(weights, features):
    return jnp.dot(
        weights, features, precision=lax.Precision.HIGHEST, preferred_element_type=jnp.float32
    )


def merge_peaks(rounds, peak, total):
    pair = jnp.stack([peak, total])
    for axis, size, dist in rounds:
        other = lax.ppermute(pair, axis, [(j, j ^ dist) for j in range(size)])
        top = jnp.maximum(pair[0], other[0])
        both = pair[1] * jnp.exp(pair[0] - top) + other[1] * jnp.exp(other[0] - top)
        pair = jnp.stack([top, both])
    return pair[0], pair[1]


def ring(axis, size, step):
    return [(j, (j + step) % size) for j in range(size)]


def pick(stack, index):
    return lax.dynamic_index_in_dim(stack, index, axis=0, keepdims=False)


def reduce_rows(summed, row_total, offset, sizes):
    x_size = sizes["x"]
    c, p, z = lax.axis_index("core"), lax.axis_index("x"), lax.axis_index("zl")
    rows, width = summed.shape
    half = rows // 2
    piece = half // (2 * x_size)
    halves = summed.reshape(2, half, width)
    swap = [(0, 1), (1, 0)]
    held = pick(halves, c) + lax.ppermute(pick(halves, 1 - c), "core", swap)
    own = held.reshape(x_size, 2, piece, width)
    right, left = pick(own[:, 0], (p - 1) % x_size), pick(own[:, 1], (p + 1) % x_size)
    for s in range(x_size - 1):
        right = lax.ppermute(right, "x", ring("x", x_size, 1)) + pick(own[:, 0], (p - s - 2) % x_size)
        left = lax.ppermute(left, "x", ring("x", x_size, -1)) + pick(own[:, 1], (p + s + 2) % x_size)
    block = jnp.stack([right, left])
    mine = pick(block, z) + lax.ppermute(pick(block, 1 - z), "zl", swap)
    start = offset + c * half + p * (2 * piece) + z * piece
    mine = mine / lax.dynamic_slice_in_dim(row_total, start, piece)[:, None]
    other = lax.ppermute(mine, "zl", swap)
    block = jnp.where(z == 0, jnp.stack([mine, other]), jnp.stack([other, mine]))
    gathered = jnp.zeros((x_size, 2, piece, width), summed.dtype).at[p].set(block)
    right, left = block[0], block[1]
    for s in range(x_size - 1):
        right = lax.ppermute(right, "x", ring("x", x_size, 1))
        left = lax.ppermute(left, "x", ring("x", x_size, -1))
        gathered = gathered.at[(p - s - 1) % x_size, 0].set(right)
        gathered = gathered.at[(p + s + 1) % x_size, 1].set(left)
    held = gathered.reshape(half, width)
    other = lax.ppermute(held, "core", swap)
    return jnp.where(c == 0, jnp.stack([held, other]), jnp.stack([other, held])).reshape(rows, width)


def local(images, captions, bank, sizes):
    img_rounds = [("zh", sizes["zh"], 1)] + [("y", sizes["y"], d) for d in (1, 2)]
    cap_rounds = [("core", sizes["core"], 1), ("zl", sizes["zl"], 1)] + [
        ("x", sizes["x"], d) for d in (1, 2)
    ]
    features = lax.all_gather(captions, IMG, axis=1, tiled=True)
    querybank_similarity = similar(bank, features)
    local_peak = jnp.max(querybank_similarity, axis=0)
    local_total = jnp.sum(jnp.exp(querybank_similarity - local_peak[None, :]), axis=0)
    raw = lax.optimization_barrier(similar(images, features))
    peak, total = merge_peaks(img_rounds, local_peak, local_total)
    col_log = peak + jnp.log(total)
    logits = raw - col_log[None, :]
    row_peak = jnp.max(logits, axis=1)
    weights = jnp.exp(logits - row_peak[:, None])
    row_sum = jnp.sum(weights, axis=1)
    top, row_total = merge_peaks(cap_rounds, row_peak, row_sum)
    scale = jnp.exp(row_peak - top)
    rows = weights.shape[0]
    chunk = rows // 2
    parts = []
    for k in range(2):
        part = slice(k * chunk, (k + 1) * chunk)
        summed = rescaled_affinity(weights[part], features) * scale[part, None]
        parts.append(reduce_rows(summed, row_total, k * chunk, sizes))
    return jnp.concatenate(parts, axis=0)


def solution(mesh):
    zh, y = 2, mesh.shape["img"] // 2
    zl, core = 2, 2
    x = mesh.shape["cap"] // (zl * core)
    sizes = dict(zh=zh, y=y, x=x, zl=zl, core=core)
    fine = Mesh(mesh.devices.reshape(zh, y, x, zl, core), ("zh", "y", "x", "zl", "core"))

    def run(images, captions, bank):
        return local(images, captions, bank, sizes)

    return jax.shard_map(
        run,
        mesh=fine,
        in_specs=(P(IMG, None), P(CAP, IMG), P(IMG, None)),
        out_specs=P(IMG, None),
        check_vma=False,
    )
```

profile of v0, /device:TPU:1, one launch (start us, length us, event | category | flops | bytes accessed | tf_op | source)
XLA Modules:
  0.0 292.1 jit_solution(12426825481357225335)
XLA Ops:
  6.5 0.7 all-gather.2.cloned.1.call-update
  7.3 68.4 %all-gather.2.cloned.1.call-done = f32[1024,768]{0,1:T(8,128)} async-done(((f32[1024,96]{0,1:T(8,128)}), f32[1024,768]{0,1:T(8,128)}) %all-gather.2.cloned.1.call-update) | async-done | bytes 3145744 | tf_op jit(solution)/shard_map/all_gather | solution.py:84
  75.7 23.4 %multiply_reduce_fusion = (f32[1024]{0:T(1024)S(1)}, f32[2048,1024]{1,0:T(8,128)S(1)}) fusion(f32[2048,768]{1,0:T(8,128)} %param.33, f32[1024,768]{0,1:T(8,128)} %all-gather.2.cloned.1.call-done), kind=kOutput, calls=%fused_computation.3 | convolution fusion | flops 19331547136 | bytes 17829888 | tf_op jit(solution)/shard_map/dot_general | solution.py:14
  99.1 1.4 exponential_reduce_fusion
  100.8 3.9 %collective-permute-done = f32[2,1024]{1,0:T(2,128)S(1)} collective-permute-done((f32[2,1024]{1,0:T(2,128)S(1)}, f32[2,1024]{1,0:T(2,128)S(1)}, u32[]{:S(2)}, u32[]{:S(2)}) %collective-permute-start) | collective-permute-done | bytes 8224 | tf_op jit(solution)/shard_map/ppermute | solution.py:32
  104.8 2.5 collective-permute-done.1
  107.3 1.6 collective-permute-start.2
  108.9 34.0 %convolution_multiply_fusion = f32[2048,1024]{1,0:T(8,128)S(1)} fusion(f32[2048,768]{1,0:T(8,128)S(1)} %copy-done.6, f32[1024,768]{0,1:T(8,128)S(1)} %copy-done.2), kind=kOutput, calls=%fused_computation.5 | convolution fusion | flops 19329449984 | bytes 17825792 | tf_op jit(solution)/shard_map/dot_general | solution.py:14
  143.6 4.2 %fusion.50 = (f32[2048]{0:T(1024)S(1)}, f32[2048,1024]{1,0:T(8,128)}) fusion(f32[2048]{0:T(1024)S(1)} %subtract_reduce_fusion, f32[2048,1024]{1,0:T(8,128)S(1)} %convolution_multiply_fusion, f32[1024]{0:T(1024)S(1)} %bitcast.203), kind=kLoop, calls=%fused_computation.153 | loop fusion | flops 6289408 | bytes 16797696 | tf_op jit(solution)/shard_map/reduce_sum | solution.py:94
  147.8 3.7 %collective-permute-start.3 = (f32[2,2048]{1,0:T(2,128)S(1)}, f32[2,2048]{1,0:T(2,128)S(1)}, u32[]{:S(2)}, u32[]{:S(2)}) collective-permute-start(f32[2,2048]{1,0:T(2,128)S(1)} %pad_maximum_fusion.1), channel_id=1, source_target_pairs={{0,1},{1,0},{2,3},{3,2},{4,5},{5,4},{6,7},{7,6},{8,9},{9,8},{10,11... | collective-permute-start | bytes 49160 | tf_op jit(solution)/shard_map/ppermute | solution.py:32
  151.5 0.8 collective-permute-done.3
  152.9 2.2 collective-permute-done.4
  155.2 1.3 collective-permute-start.5
  156.4 1.4 collective-permute-done.5
  157.9 2.8 collective-permute-start.6
  160.7 1.4 collective-permute-done.6
  162.2 12.5 %fusion.4 = f32[1024,768]{1,0:T(8,128)S(1)} fusion(f32[1024,768]{0,1:T(8,128)S(1)} %copy-done.2, f32[2048,1024]{1,0:T(8,128)} %get-tuple-element.184, f32[1024]{0:T(1024)S(1)} %get-tuple-element.211), kind=kOutput, calls=%fused_computation.12 | convolution fusion | flops 9664462848 | bytes 10489856 | tf_op jit(solution)/shard_map/dot_general | solution.py:24
  174.7 1.3 dynamic-slice_bitcast_fusion.1
  176.0 4.2 %collective-permute-start.7 = (f32[512,768]{1,0:T(8,128)}, f32[512,768]{1,0:T(8,128)}, u32[]{:S(2)}, u32[]{:S(2)}) collective-permute-start(f32[512,768]{1,0:T(8,128)} %dynamic-slice_bitcast_fusion.1), channel_id=1, source_target_pairs={{0,1},{1,0},{2,3},{3,2},{4,5},{5,4},{6,7},{7,6},{8,9},{9,8},{10,11... | collective-permute-start | bytes 4718600 | tf_op jit(solution)/shard_map/ppermute | solution.py:55
  180.1 10.2 %fusion.7 = f32[1024,768]{1,0:T(8,128)S(1)} fusion(f32[1024,768]{0,1:T(8,128)S(1)} %copy-done.3, f32[2048,1024]{1,0:T(8,128)S(1)} %copy-done, f32[1024]{0:T(1024)S(1)} %get-tuple-element.212), kind=kOutput, calls=%fused_computation.13 | convolution fusion | flops 9664462848 | bytes 10489856 | tf_op jit(solution)/shard_map/dot_general | solution.py:24
  190.4 1.3 dynamic-slice_bitcast_fusion
  191.7 1.9 collective-permute-start.23
  193.5 0.7 and_reduce_fusion.6
  194.3 0.8 and_reduce_fusion.4
  195.1 0.7 and_reduce_fusion.2
  195.8 0.8 and_reduce_fusion
  196.7 2.1 bitcast_add_fusion.1
  198.9 2.7 collective-permute-start.11
  201.7 1.6 bitcast_add_fusion
  203.4 2.7 collective-permute-start.27
  206.3 3.1 %collective-permute-start.12 = (f32[64,768]{1,0:T(8,128)S(1)}, f32[64,768]{1,0:T(8,128)S(1)}, u32[]{:S(2)}, u32[]{:S(2)}) collective-permute-start(f32[64,768]{1,0:T(8,128)S(1)} %bitcast_add_fusion.10), channel_id=1, source_target_pairs={{0,12},{4,0},{8,4},{12,8},{1,13},{5,1},{9,5},{13,9},{2,14},{6,2},{... | collective-permute-start | bytes 589832 | tf_op jit(solution)/shard_map/ppermute | solution.py:60
  209.9 3.5 %collective-permute-start.28 = (f32[64,768]{1,0:T(8,128)S(1)}, f32[64,768]{1,0:T(8,128)S(1)}, u32[]{:S(2)}, u32[]{:S(2)}) collective-permute-start(f32[64,768]{1,0:T(8,128)S(1)} %bitcast_add_fusion.4), channel_id=1, source_target_pairs={{0,12},{4,0},{8,4},{12,8},{1,13},{5,1},{9,5},{13,9},{2,14},{6,2},{... | collective-permute-start | bytes 589832 | tf_op jit(solution)/shard_map/ppermute | solution.py:60
  213.5 0.7 collective-permute-done.12
  214.2 3.5 %collective-permute-start.13 = (f32[64,768]{1,0:T(8,128)S(1)}, f32[64,768]{1,0:T(8,128)S(1)}, u32[]{:S(2)}, u32[]{:S(2)}) collective-permute-start(f32[64,768]{1,0:T(8,128)S(1)} %bitcast_add_fusion.9), channel_id=1, source_target_pairs={{0,12},{4,0},{8,4},{12,8},{1,13},{5,1},{9,5},{13,9},{2,14},{6,2},{... | collective-permute-start | bytes 589832 | tf_op jit(solution)/shard_map/ppermute | solution.py:60
  218.0 3.2 %collective-permute-start.29 = (f32[64,768]{1,0:T(8,128)S(1)}, f32[64,768]{1,0:T(8,128)S(1)}, u32[]{:S(2)}, u32[]{:S(2)}) collective-permute-start(f32[64,768]{1,0:T(8,128)S(1)} %bitcast_add_fusion.3), channel_id=1, source_target_pairs={{0,12},{4,0},{8,4},{12,8},{1,13},{5,1},{9,5},{13,9},{2,14},{6,2},{... | collective-permute-start | bytes 589832 | tf_op jit(solution)/shard_map/ppermute | solution.py:60
  221.3 0.9 collective-permute-done.13
  222.2 2.9 collective-permute-done.10
  225.6 0.7 collective-permute-done.29
  226.3 2.9 collective-permute-done.26
  230.2 0.8 collective-permute-start.15
  231.0 4.9 %collective-permute-done.30 = f32[64,768]{1,0:T(8,128)S(1)} collective-permute-done((f32[64,768]{1,0:T(8,128)S(1)}, f32[64,768]{1,0:T(8,128)S(1)}, u32[]{:S(2)}, u32[]{:S(2)}) %collective-permute-start.30) | collective-permute-done | bytes 196640 | tf_op jit(solution)/shard_map/ppermute | solution.py:62
  236.4 3.7 %collective-permute-done.15 = f32[64,768]{1,0:T(8,128)S(1)} collective-permute-done((f32[64,768]{1,0:T(8,128)S(1)}, f32[64,768]{1,0:T(8,128)S(1)}, u32[]{:S(2)}, u32[]{:S(2)}) %collective-permute-start.15) | collective-permute-done | bytes 196640 | tf_op jit(solution)/shard_map/ppermute | solution.py:65
  240.2 2.7 collective-permute-start.17
  242.9 1.4 collective-permute-done.31
  244.4 2.7 collective-permute-start.33
  247.2 0.7 fusion.11
  248.0 0.7 fusion.13
  248.8 2.7 collective-permute-start.19
  251.5 0.7 fusion.39
  252.2 0.7 fusion.31
  252.9 2.7 collective-permute-start.35
  255.7 0.7 fusion.38
  256.3 0.7 fusion.30
  257.1 2.7 collective-permute-start.21
  261.3 2.7 collective-permute-start.37
  264.0 0.7 fusion.36
  264.7 0.7 fusion.28
  265.4 0.7 fusion.35
  266.8 7.5 %collective-permute-start.22 = (f32[512,768]{1,0:T(8,128)S(1)}, f32[512,768]{1,0:T(8,128)}, u32[]{:S(2)}, u32[]{:S(2)}) collective-permute-start(f32[512,768]{1,0:T(8,128)S(1)} %bitcast.182), channel_id=1, source_target_pairs={{0,1},{1,0},{2,3},{3,2},{4,5},{5,4},{6,7},{7,6},{8,9},{9,8},{10,11... | collective-permute-start | bytes 4718600 | tf_op jit(solution)/shard_map/ppermute | solution.py:75
  274.3 0.7 fusion.27
  275.8 1.7 collective-permute-done.22
  277.5 2.2 maximum_select_fusion
  279.7 2.2 maximum_select_fusion.1
  281.9 3.1 %pad_maximum_fusion = f32[2048,768]{1,0:T(8,128)} fusion(f32[1024,768]{1,0:T(8,128)S(1)} %bitcast.179, f32[1024,768]{1,0:T(8,128)S(1)} %bitcast.178), kind=kLoop, calls=%fused_computation.4 | loop fusion | flops 1572864 | bytes 12582912 | tf_op jit(solution)/shard_map/concatenate | solution.py:104
  (108 shorter events, 9.0 us)
Async XLA Ops:
  6.5 69.1 %all-gather.2.cloned.1.call-start = ((), (), s32[]{:S(2)}) async-start(), calls=%async_computation | async-start | bytes 3538944 | tf_op jit(solution)/shard_map/all_gather | solution.py:84
  75.7 33.2 %copy-start.6 = (f32[2048,768]{1,0:T(8,128)S(1)}, f32[2048,768]{1,0:T(8,128)}, u32[]{:S(2)}) copy-start(f32[2048,768]{1,0:T(8,128)} %param.31) | copy-start | bytes 18874372
  99.1 9.8 %copy-start.2 = (f32[1024,768]{0,1:T(8,128)S(1)}, f32[1024,768]{0,1:T(8,128)}, u32[]{:S(2)}) copy-start(f32[1024,768]{0,1:T(8,128)} %all-gather.2.cloned.1.call-done) | copy-start | bytes 9437188
  100.6 4.1 %collective-permute-start = (f32[2,1024]{1,0:T(2,128)S(1)}, f32[2,1024]{1,0:T(2,128)S(1)}, u32[]{:S(2)}, u32[]{:S(2)}) collective-permute-start(f32[2,1024]{1,0:T(2,128)S(1)} %pad_maximum_fusion.5), channel_id=1, source_target_pairs={{0,64},{64,0},{1,65},{65,1},{2,66},{66,2},{3,67},{67,3},{4,68},{68... | collective-permute-start | bytes 24584 | tf_op jit(solution)/shard_map/ppermute | solution.py:32
  104.7 2.6 collective-permute-start.1
  107.3 35.6 %collective-permute-start.2 = (f32[2,1024]{1,0:T(2,128)S(1)}, f32[2,1024]{1,0:T(2,128)S(1)}, u32[]{:S(2)}, u32[]{:S(2)}) collective-permute-start(f32[2,1024]{1,0:T(2,128)S(1)} %pad_maximum_fusion.7), channel_id=1, source_target_pairs={{0,32},{16,48},{32,0},{48,16},{1,33},{17,49},{33,1},{49,17},{2,34}... | collective-permute-start | bytes 24584 | tf_op jit(solution)/shard_map/ppermute | solution.py:32
  147.8 4.6 %collective-permute-start.3 = (f32[2,2048]{1,0:T(2,128)S(1)}, f32[2,2048]{1,0:T(2,128)S(1)}, u32[]{:S(2)}, u32[]{:S(2)}) collective-permute-start(f32[2,2048]{1,0:T(2,128)S(1)} %pad_maximum_fusion.1), channel_id=1, source_target_pairs={{0,1},{1,0},{2,3},{3,2},{4,5},{5,4},{6,7},{7,6},{8,9},{9,8},{10,11... | collective-permute-start | bytes 49160 | tf_op jit(solution)/shard_map/ppermute | solution.py:32
  152.4 2.7 collective-permute-start.4
  155.2 2.7 collective-permute-start.5
  157.9 4.2 %collective-permute-start.6 = (f32[2,2048]{1,0:T(2,128)S(1)}, f32[2,2048]{1,0:T(2,128)S(1)}, u32[]{:S(2)}, u32[]{:S(2)}) collective-permute-start(f32[2,2048]{1,0:T(2,128)S(1)} %pad_maximum_fusion.4), channel_id=1, source_target_pairs={{0,8},{4,12},{8,0},{12,4},{1,9},{5,13},{9,1},{13,5},{2,10},{6,14},... | collective-permute-start | bytes 49160 | tf_op jit(solution)/shard_map/ppermute | solution.py:32
  162.2 18.0 %copy-start = (f32[2048,1024]{1,0:T(8,128)S(1)}, f32[2048,1024]{1,0:T(8,128)}, u32[]{:S(2)}) copy-start(f32[2048,1024]{1,0:T(8,128)} %get-tuple-element.184) | copy-start | bytes 25165828
  174.6 15.7 %copy-start.1 = (f32[1024,768]{1,0:T(8,128)}, f32[1024,768]{1,0:T(8,128)S(1)}, u32[]{:S(2)}) copy-start(f32[1024,768]{1,0:T(8,128)S(1)} %fusion.4) | copy-start | bytes 9437188
  174.6 5.5 %copy-start.3 = (f32[1024,768]{0,1:T(8,128)S(1)}, f32[1024,768]{0,1:T(8,128)}, u32[]{:S(2)}) copy-start(f32[1024,768]{0,1:T(8,128)} %all-gather.2.cloned.1.call-done) | copy-start | bytes 9437188
  176.0 20.7 %collective-permute-start.7 = (f32[512,768]{1,0:T(8,128)}, f32[512,768]{1,0:T(8,128)}, u32[]{:S(2)}, u32[]{:S(2)}) collective-permute-start(f32[512,768]{1,0:T(8,128)} %dynamic-slice_bitcast_fusion.1), channel_id=1, source_target_pairs={{0,1},{1,0},{2,3},{3,2},{4,5},{5,4},{6,7},{7,6},{8,9},{9,8},{10,11... | collective-permute-start | bytes 4718600 | tf_op jit(solution)/shard_map/ppermute | solution.py:55
  190.4 3.2 %copy-start.5 = (s32[4]{0:T(128)S(1)}, s32[4]{0:T(128)}, u32[]{:S(2)}) copy-start(s32[4]{0:T(128)} %constant.493.clone.1) | copy-start | bytes 52
  190.4 3.9 %copy-start.4 = (s32[4]{0:T(128)S(1)}, s32[4]{0:T(128)}, u32[]{:S(2)}) copy-start(s32[4]{0:T(128)} %constant.508.clone.1) | copy-start | bytes 52
  191.7 10.0 %collective-permute-start.23 = (f32[512,768]{1,0:T(8,128)}, f32[512,768]{1,0:T(8,128)}, u32[]{:S(2)}, u32[]{:S(2)}) collective-permute-start(f32[512,768]{1,0:T(8,128)} %dynamic-slice_bitcast_fusion), channel_id=1, source_target_pairs={{0,1},{1,0},{2,3},{3,2},{4,5},{5,4},{6,7},{7,6},{8,9},{9,8},{10,11... | collective-permute-start | bytes 4718600 | tf_op jit(solution)/shard_map/ppermute | solution.py:55
  198.9 7.4 %collective-permute-start.11 = (f32[64,768]{1,0:T(8,128)S(1)}, f32[64,768]{1,0:T(8,128)S(1)}, u32[]{:S(2)}, u32[]{:S(2)}) collective-permute-start(f32[64,768]{1,0:T(8,128)S(1)} %dynamic-slice_bitcast_fusion.4), channel_id=1, source_target_pairs={{0,12},{4,0},{8,4},{12,8},{1,13},{5,1},{9,5},{13,9},{2,14},{6,2},{... | collective-permute-start | bytes 589832 | tf_op jit(solution)/shard_map/ppermute | solution.py:60
  201.6 7.8 %collective-permute-start.8 = (f32[64,768]{1,0:T(8,128)S(1)}, f32[64,768]{1,0:T(8,128)S(1)}, u32[]{:S(2)}, u32[]{:S(2)}) collective-permute-start(f32[64,768]{1,0:T(8,128)S(1)} %dynamic-slice_bitcast_fusion.5), channel_id=1, source_target_pairs={{0,4},{4,8},{8,12},{12,0},{1,5},{5,9},{9,13},{13,1},{2,6},{6,10},{... | collective-permute-start | bytes 589832 | tf_op jit(solution)/shard_map/ppermute | solution.py:59
  203.4 6.4 %collective-permute-start.27 = (f32[64,768]{1,0:T(8,128)S(1)}, f32[64,768]{1,0:T(8,128)S(1)}, u32[]{:S(2)}, u32[]{:S(2)}) collective-permute-start(f32[64,768]{1,0:T(8,128)S(1)} %dynamic-slice_bitcast_fusion.2), channel_id=1, source_target_pairs={{0,12},{4,0},{8,4},{12,8},{1,13},{5,1},{9,5},{13,9},{2,14},{6,2},{... | collective-permute-start | bytes 589832 | tf_op jit(solution)/shard_map/ppermute | solution.py:60
  206.2 7.2 %collective-permute-start.24 = (f32[64,768]{1,0:T(8,128)S(1)}, f32[64,768]{1,0:T(8,128)S(1)}, u32[]{:S(2)}, u32[]{:S(2)}) collective-permute-start(f32[64,768]{1,0:T(8,128)S(1)} %dynamic-slice_bitcast_fusion.3), channel_id=1, source_target_pairs={{0,4},{4,8},{8,12},{12,0},{1,5},{5,9},{9,13},{13,1},{2,6},{6,10},{... | collective-permute-start | bytes 589832 | tf_op jit(solution)/shard_map/ppermute | solution.py:59
  206.3 7.9 %collective-permute-start.12 = (f32[64,768]{1,0:T(8,128)S(1)}, f32[64,768]{1,0:T(8,128)S(1)}, u32[]{:S(2)}, u32[]{:S(2)}) collective-permute-start(f32[64,768]{1,0:T(8,128)S(1)} %bitcast_add_fusion.10), channel_id=1, source_target_pairs={{0,12},{4,0},{8,4},{12,8},{1,13},{5,1},{9,5},{13,9},{2,14},{6,2},{... | collective-permute-start | bytes 589832 | tf_op jit(solution)/shard_map/ppermute | solution.py:60
  209.4 8.3 %collective-permute-start.9 = (f32[64,768]{1,0:T(8,128)S(1)}, f32[64,768]{1,0:T(8,128)S(1)}, u32[]{:S(2)}, u32[]{:S(2)}) collective-permute-start(f32[64,768]{1,0:T(8,128)S(1)} %bitcast_add_fusion.13), channel_id=1, source_target_pairs={{0,4},{4,8},{8,12},{12,0},{1,5},{5,9},{9,13},{13,1},{2,6},{6,10},{... | collective-permute-start | bytes 589832 | tf_op jit(solution)/shard_map/ppermute | solution.py:59
  209.9 8.1 %collective-permute-start.28 = (f32[64,768]{1,0:T(8,128)S(1)}, f32[64,768]{1,0:T(8,128)S(1)}, u32[]{:S(2)}, u32[]{:S(2)}) collective-permute-start(f32[64,768]{1,0:T(8,128)S(1)} %bitcast_add_fusion.4), channel_id=1, source_target_pairs={{0,12},{4,0},{8,4},{12,8},{1,13},{5,1},{9,5},{13,9},{2,14},{6,2},{... | collective-permute-start | bytes 589832 | tf_op jit(solution)/shard_map/ppermute | solution.py:60
  213.4 7.8 %collective-permute-start.25 = (f32[64,768]{1,0:T(8,128)S(1)}, f32[64,768]{1,0:T(8,128)S(1)}, u32[]{:S(2)}, u32[]{:S(2)}) collective-permute-start(f32[64,768]{1,0:T(8,128)S(1)} %bitcast_add_fusion.7), channel_id=1, source_target_pairs={{0,4},{4,8},{8,12},{12,0},{1,5},{5,9},{9,13},{13,1},{2,6},{6,10},{... | collective-permute-start | bytes 589832 | tf_op jit(solution)/shard_map/ppermute | solution.py:59
  214.2 8.0 %collective-permute-start.13 = (f32[64,768]{1,0:T(8,128)S(1)}, f32[64,768]{1,0:T(8,128)S(1)}, u32[]{:S(2)}, u32[]{:S(2)}) collective-permute-start(f32[64,768]{1,0:T(8,128)S(1)} %bitcast_add_fusion.9), channel_id=1, source_target_pairs={{0,12},{4,0},{8,4},{12,8},{1,13},{5,1},{9,5},{13,9},{2,14},{6,2},{... | collective-permute-start | bytes 589832 | tf_op jit(solution)/shard_map/ppermute | solution.py:60
  217.7 7.4 %collective-permute-start.10 = (f32[64,768]{1,0:T(8,128)S(1)}, f32[64,768]{1,0:T(8,128)S(1)}, u32[]{:S(2)}, u32[]{:S(2)}) collective-permute-start(f32[64,768]{1,0:T(8,128)S(1)} %bitcast_add_fusion.12), channel_id=1, source_target_pairs={{0,4},{4,8},{8,12},{12,0},{1,5},{5,9},{9,13},{13,1},{2,6},{6,10},{... | collective-permute-start | bytes 589832 | tf_op jit(solution)/shard_map/ppermute | solution.py:59
  218.0 8.3 %collective-permute-start.29 = (f32[64,768]{1,0:T(8,128)S(1)}, f32[64,768]{1,0:T(8,128)S(1)}, u32[]{:S(2)}, u32[]{:S(2)}) collective-permute-start(f32[64,768]{1,0:T(8,128)S(1)} %bitcast_add_fusion.3), channel_id=1, source_target_pairs={{0,12},{4,0},{8,4},{12,8},{1,13},{5,1},{9,5},{13,9},{2,14},{6,2},{... | collective-permute-start | bytes 589832 | tf_op jit(solution)/shard_map/ppermute | solution.py:60
  221.2 8.0 %collective-permute-start.26 = (f32[64,768]{1,0:T(8,128)S(1)}, f32[64,768]{1,0:T(8,128)S(1)}, u32[]{:S(2)}, u32[]{:S(2)}) collective-permute-start(f32[64,768]{1,0:T(8,128)S(1)} %bitcast_add_fusion.6), channel_id=1, source_target_pairs={{0,4},{4,8},{8,12},{12,0},{1,5},{5,9},{9,13},{13,1},{2,6},{6,10},{... | collective-permute-start | bytes 589832 | tf_op jit(solution)/shard_map/ppermute | solution.py:59
  225.2 4.9 %collective-permute-start.14 = (f32[64,768]{1,0:T(8,128)S(1)}, f32[64,768]{1,0:T(8,128)S(1)}, u32[]{:S(2)}, u32[]{:S(2)}) collective-permute-start(f32[64,768]{1,0:T(8,128)S(1)} %fusion.21), channel_id=1, source_target_pairs={{0,2},{2,0},{1,3},{3,1},{4,6},{6,4},{5,7},{7,5},{8,10},{10,8},{9,1... | collective-permute-start | bytes 589832 | tf_op jit(solution)/shard_map/ppermute | solution.py:62
  229.3 6.6 %collective-permute-start.30 = (f32[64,768]{1,0:T(8,128)S(1)}, f32[64,768]{1,0:T(8,128)S(1)}, u32[]{:S(2)}, u32[]{:S(2)}) collective-permute-start(f32[64,768]{1,0:T(8,128)S(1)} %fusion.15), channel_id=1, source_target_pairs={{0,2},{2,0},{1,3},{3,1},{4,6},{6,4},{5,7},{7,5},{8,10},{10,8},{9,1... | collective-permute-start | bytes 589832 | tf_op jit(solution)/shard_map/ppermute | solution.py:62
  230.2 9.9 %collective-permute-start.15 = (f32[64,768]{1,0:T(8,128)S(1)}, f32[64,768]{1,0:T(8,128)S(1)}, u32[]{:S(2)}, u32[]{:S(2)}) collective-permute-start(f32[64,768]{1,0:T(8,128)S(1)} %fusion.25), channel_id=1, source_target_pairs={{0,2},{2,0},{1,3},{3,1},{4,6},{6,4},{5,7},{7,5},{8,10},{10,8},{9,1... | collective-permute-start | bytes 589832 | tf_op jit(solution)/shard_map/ppermute | solution.py:65
  236.0 8.3 %collective-permute-start.31 = (f32[64,768]{1,0:T(8,128)S(1)}, f32[64,768]{1,0:T(8,128)S(1)}, u32[]{:S(2)}, u32[]{:S(2)}) collective-permute-start(f32[64,768]{1,0:T(8,128)S(1)} %fusion.19), channel_id=1, source_target_pairs={{0,2},{2,0},{1,3},{3,1},{4,6},{6,4},{5,7},{7,5},{8,10},{10,8},{9,1... | collective-permute-start | bytes 589832 | tf_op jit(solution)/shard_map/ppermute | solution.py:65
  240.2 8.6 %collective-permute-start.16 = (f32[64,768]{1,0:T(8,128)S(1)}, f32[64,768]{1,0:T(8,128)S(1)}, u32[]{:S(2)}, u32[]{:S(2)}) collective-permute-start(f32[64,768]{1,0:T(8,128)S(1)} %get-tuple-element.194), channel_id=1, source_target_pairs={{0,4},{4,8},{8,12},{12,0},{1,5},{5,9},{9,13},{13,1},{2,6},{6,10},{... | collective-permute-start | bytes 589832 | tf_op jit(solution)/shard_map/ppermute | solution.py:70
  240.2 8.6 %collective-permute-start.17 = (f32[64,768]{1,0:T(8,128)S(1)}, f32[64,768]{1,0:T(8,128)S(1)}, u32[]{:S(2)}, u32[]{:S(2)}) collective-permute-start(f32[64,768]{1,0:T(8,128)S(1)} %get-tuple-element.193), channel_id=1, source_target_pairs={{0,12},{4,0},{8,4},{12,8},{1,13},{5,1},{9,5},{13,9},{2,14},{6,2},{... | collective-permute-start | bytes 589832 | tf_op jit(solution)/shard_map/ppermute | solution.py:71
  244.4 7.1 %collective-permute-start.32 = (f32[64,768]{1,0:T(8,128)S(1)}, f32[64,768]{1,0:T(8,128)S(1)}, u32[]{:S(2)}, u32[]{:S(2)}) collective-permute-start(f32[64,768]{1,0:T(8,128)S(1)} %get-tuple-element.196), channel_id=1, source_target_pairs={{0,4},{4,8},{8,12},{12,0},{1,5},{5,9},{9,13},{13,1},{2,6},{6,10},{... | collective-permute-start | bytes 589832 | tf_op jit(solution)/shard_map/ppermute | solution.py:70
  244.4 8.5 %collective-permute-start.33 = (f32[64,768]{1,0:T(8,128)S(1)}, f32[64,768]{1,0:T(8,128)S(1)}, u32[]{:S(2)}, u32[]{:S(2)}) collective-permute-start(f32[64,768]{1,0:T(8,128)S(1)} %get-tuple-element.195), channel_id=1, source_target_pairs={{0,12},{4,0},{8,4},{12,8},{1,13},{5,1},{9,5},{13,9},{2,14},{6,2},{... | collective-permute-start | bytes 589832 | tf_op jit(solution)/shard_map/ppermute | solution.py:71
  248.7 8.3 %collective-permute-start.18 = (f32[64,768]{1,0:T(8,128)S(1)}, f32[64,768]{1,0:T(8,128)S(1)}, u32[]{:S(2)}, u32[]{:S(2)}) collective-permute-start(f32[64,768]{1,0:T(8,128)S(1)} %collective-permute-done.16), channel_id=1, source_target_pairs={{0,4},{4,8},{8,12},{12,0},{1,5},{5,9},{9,13},{13,1},{2,6},{6,10},{... | collective-permute-start | bytes 589832 | tf_op jit(solution)/shard_map/ppermute | solution.py:70
  248.8 8.3 %collective-permute-start.19 = (f32[64,768]{1,0:T(8,128)S(1)}, f32[64,768]{1,0:T(8,128)S(1)}, u32[]{:S(2)}, u32[]{:S(2)}) collective-permute-start(f32[64,768]{1,0:T(8,128)S(1)} %collective-permute-done.17), channel_id=1, source_target_pairs={{0,12},{4,0},{8,4},{12,8},{1,13},{5,1},{9,5},{13,9},{2,14},{6,2},{... | collective-permute-start | bytes 589832 | tf_op jit(solution)/shard_map/ppermute | solution.py:71
  251.5 8.6 %collective-permute-start.34 = (f32[64,768]{1,0:T(8,128)S(1)}, f32[64,768]{1,0:T(8,128)S(1)}, u32[]{:S(2)}, u32[]{:S(2)}) collective-permute-start(f32[64,768]{1,0:T(8,128)S(1)} %collective-permute-done.32), channel_id=1, source_target_pairs={{0,4},{4,8},{8,12},{12,0},{1,5},{5,9},{9,13},{13,1},{2,6},{6,10},{... | collective-permute-start | bytes 589832 | tf_op jit(solution)/shard_map/ppermute | solution.py:70
  252.9 8.3 %collective-permute-start.35 = (f32[64,768]{1,0:T(8,128)S(1)}, f32[64,768]{1,0:T(8,128)S(1)}, u32[]{:S(2)}, u32[]{:S(2)}) collective-permute-start(f32[64,768]{1,0:T(8,128)S(1)} %collective-permute-done.33), channel_id=1, source_target_pairs={{0,12},{4,0},{8,4},{12,8},{1,13},{5,1},{9,5},{13,9},{2,14},{6,2},{... | collective-permute-start | bytes 589832 | tf_op jit(solution)/shard_map/ppermute | solution.py:71
  257.0 8.3 %collective-permute-start.20 = (f32[64,768]{1,0:T(8,128)S(1)}, f32[64,768]{1,0:T(8,128)S(1)}, u32[]{:S(2)}, u32[]{:S(2)}) collective-permute-start(f32[64,768]{1,0:T(8,128)S(1)} %collective-permute-done.18), channel_id=1, source_target_pairs={{0,4},{4,8},{8,12},{12,0},{1,5},{5,9},{9,13},{13,1},{2,6},{6,10},{... | collective-permute-start | bytes 589832 | tf_op jit(solution)/shard_map/ppermute | solution.py:70
  257.1 9.0 %collective-permute-start.21 = (f32[64,768]{1,0:T(8,128)S(1)}, f32[64,768]{1,0:T(8,128)S(1)}, u32[]{:S(2)}, u32[]{:S(2)}) collective-permute-start(f32[64,768]{1,0:T(8,128)S(1)} %collective-permute-done.19), channel_id=1, source_target_pairs={{0,12},{4,0},{8,4},{12,8},{1,13},{5,1},{9,5},{13,9},{2,14},{6,2},{... | collective-permute-start | bytes 589832 | tf_op jit(solution)/shard_map/ppermute | solution.py:71
  260.1 14.2 %collective-permute-start.36 = (f32[64,768]{1,0:T(8,128)S(1)}, f32[64,768]{1,0:T(8,128)S(1)}, u32[]{:S(2)}, u32[]{:S(2)}) collective-permute-start(f32[64,768]{1,0:T(8,128)S(1)} %collective-permute-done.34), channel_id=1, source_target_pairs={{0,4},{4,8},{8,12},{12,0},{1,5},{5,9},{9,13},{13,1},{2,6},{6,10},{... | collective-permute-start | bytes 589832 | tf_op jit(solution)/shard_map/ppermute | solution.py:70
  261.3 13.8 %collective-permute-start.37 = (f32[64,768]{1,0:T(8,128)S(1)}, f32[64,768]{1,0:T(8,128)S(1)}, u32[]{:S(2)}, u32[]{:S(2)}) collective-permute-start(f32[64,768]{1,0:T(8,128)S(1)} %collective-permute-done.35), channel_id=1, source_target_pairs={{0,12},{4,0},{8,4},{12,8},{1,13},{5,1},{9,5},{13,9},{2,14},{6,2},{... | collective-permute-start | bytes 589832 | tf_op jit(solution)/shard_map/ppermute | solution.py:71
  266.8 10.7 %collective-permute-start.22 = (f32[512,768]{1,0:T(8,128)S(1)}, f32[512,768]{1,0:T(8,128)}, u32[]{:S(2)}, u32[]{:S(2)}) collective-permute-start(f32[512,768]{1,0:T(8,128)S(1)} %bitcast.182), channel_id=1, source_target_pairs={{0,1},{1,0},{2,3},{3,2},{4,5},{5,4},{6,7},{7,6},{8,9},{9,8},{10,11... | collective-permute-start | bytes 4718600 | tf_op jit(solution)/shard_map/ppermute | solution.py:75
  275.7 4.0 %collective-permute-start.38 = (f32[512,768]{1,0:T(8,128)S(1)}, f32[512,768]{1,0:T(8,128)}, u32[]{:S(2)}, u32[]{:S(2)}) collective-permute-start(f32[512,768]{1,0:T(8,128)S(1)} %bitcast.180), channel_id=1, source_target_pairs={{0,1},{1,0},{2,3},{3,2},{4,5},{5,4},{6,7},{7,6},{8,9},{9,8},{10,11... | collective-permute-start | bytes 4718600 | tf_op jit(solution)/shard_map/ppermute | solution.py:75
Sparse Core Ops, SparseCore 0:
  9.7 65.9 all-gather.1
where the time goes:
time: 295 us; the launch traced here: 292 us
  waiting for transfers between devices  102 us (35%)
  matrix products  80.1 us (27%)
  starting transfers between devices  61.4 us (21%)
  other arithmetic  30.6 us (10%)
  between operations  14.2 us (5%)
  local copies, waits for them, and re-layouts  3.36 us (1%)
    all_gather x1, waiting for transfers between devices, local(): features = lax.all_gather(captions, IMG, axis=1, tiled=True)  68.4 us
    dot_general x2, matrix products, similar(): lax.dot_general(query_factor, target_factor, (((1,), (1,)), ((), ())), pr...  57.4 us
    dot_general x2, matrix products, rescaled_affinity(): jnp.dot(weights, features, precision=lax.Precision.HIGHEST, preferred_ele...  22.6 us
    ppermute x6, starting transfers between devices, reduce_rows(): lax.ppermute(left, 'x', ring('x', x_size, -1))  18.6 us
    ppermute x6, starting transfers between devices, reduce_rows(): left = lax.ppermute(left, 'x', ring('x', x_size, -1))  16.1 us
    ppermute x7, waiting for transfers between devices, merge_peaks(): other = lax.ppermute(pair, axis, [(j, j ^ dist) for j in range(size)])  12.3 us
    ppermute x7, starting transfers between devices, merge_peaks(): other = lax.ppermute(pair, axis, [(j, j ^ dist) for j in range(size)])  10.1 us
    ppermute x2, starting transfers between devices, reduce_rows(): other = lax.ppermute(held, 'core', swap)  7.65 us
  transfers between devices with their start and end apart: 40, of which 21 were waited for; matrix products, arithmetic and copies ran while one was open for 22% of the time, Pallas kernels for 0%

commit v1 on v0

--- a/solution.py
+++ b/solution.py
@@ -76,12 +76,32 @@
     return jnp.where(c == 0, jnp.stack([held, other]), jnp.stack([other, held])).reshape(rows, width)
 
 
+def gather_features(captions, sizes):
+    y_size = sizes["y"]
+    rows, width = captions.shape
+    half = rows // 2
+    offloaded = lax.all_gather(captions[:half], IMG, axis=1, tiled=True)
+    mine = captions[half:]
+    h, y = lax.axis_index("zh"), lax.axis_index("y")
+    other = lax.ppermute(mine, "zh", [(0, 1), (1, 0)])
+    pair = jnp.where(h == 0, jnp.stack([mine, other]), jnp.stack([other, mine]))
+    got = jnp.zeros((y_size, 2, half, width), captions.dtype).at[y].set(pair)
+    right, left = pair[0], pair[1]
+    for s in range(y_size - 1):
+        right = lax.ppermute(right, "y", ring("y", y_size, 1))
+        left = lax.ppermute(left, "y", ring("y", y_size, -1))
+        got = got.at[(y - s - 1) % y_size, 0].set(right)
+        got = got.at[(y + s + 1) % y_size, 1].set(left)
+    ringed = got.transpose(2, 1, 0, 3).reshape(half, 2 * y_size * width)
+    return jnp.concatenate([offloaded, ringed], axis=0)
+
+
 def local(images, captions, bank, sizes):
     img_rounds = [("zh", sizes["zh"], 1)] + [("y", sizes["y"], d) for d in (1, 2)]
     cap_rounds = [("core", sizes["core"], 1), ("zl", sizes["zl"], 1)] + [
         ("x", sizes["x"], d) for d in (1, 2)
     ]
-    features = lax.all_gather(captions, IMG, axis=1, tiled=True)
+    features = gather_features(captions, sizes)
     querybank_similarity = similar(bank, features)
     local_peak = jnp.max(querybank_similarity, axis=0)
     local_total = jnp.sum(jnp.exp(querybank_similarity - local_peak[None, :]), axis=0)

time: 295 us -> 348 us (1.18)
  matrix products: 80.1 us -> 144 us
  waiting for transfers between devices: 102 us -> 65.3 us
  starting transfers between devices: 61.4 us -> 74.8 us
  other arithmetic: 30.6 us -> 38.4 us
  local copies, waits for them, and re-layouts: 3.36 us -> 7.18 us
    all_gather x1, waiting for transfers between devices: 68.4 us -> 24.4 us  [gather_features(): offloaded = lax.all_gather(captions[:half], IMG, axis=1, tiled=True)]
    dot_general x2, matrix products: 57.4 us -> 100 us  [similar(): lax.dot_general(query_factor, target_factor, (((1,), (1,)), ((), ())), pr...]
    dot_general x2, matrix products: 22.6 us -> 43.8 us  [rescaled_affinity(): jnp.dot(weights, features, precision=lax.Precision.HIGHEST, preferred_ele...]
    ppermute x0 -> x7, starting transfers between devices: none -> 13.2 us  [the longest x3 7.35 us: gather_features(): left = lax.ppermute(left, 'y', ring('y', y_size, -1))]
    ppermute x0 -> x7, waiting for transfers between devices: none -> 9.11 us  [the longest x3 6.72 us: gather_features(): right = lax.ppermute(right, 'y', ring('y', y_size, 1))]
    scatter x0 -> x7, other arithmetic: none -> 4.57 us  [the longest x3 2.03 us: gather_features(): got = got.at[(y - s - 1) % y_size, 0].set(right)]
  transfers between devices with their start and end apart: 40 -> 47, of which waited for: 21 -> 22; matrix products, arithmetic and copies ran while one was open for 22% -> 31% of each run, Pallas kernels for 0% -> 0%
where the time goes in v1:
time: 348 us; the launch traced here: 344 us
  matrix products  144 us (41%)
  starting transfers between devices  74.8 us (21%)
  waiting for transfers between devices  65.3 us (19%)
  other arithmetic  38.4 us (11%)
  between operations  14.4 us (4%)
  local copies, waits for them, and re-layouts  7.18 us (2%)
    dot_general x2, matrix products, similar(): lax.dot_general(query_factor, target_factor, (((1,), (1,)), ((), ())), pr...  100 us
    dot_general x2, matrix products, rescaled_affinity(): jnp.dot(weights, features, precision=lax.Precision.HIGHEST, preferred_ele...  43.8 us
    all_gather x1, waiting for transfers between devices, gather_features(): offloaded = lax.all_gather(captions[:half], IMG, axis=1, tiled=True)  24.4 us
    ppermute x6, starting transfers between devices, reduce_rows(): lax.ppermute(left, 'x', ring('x', x_size, -1))  18.3 us
    ppermute x6, starting transfers between devices, reduce_rows(): left = lax.ppermute(left, 'x', ring('x', x_size, -1))  16.1 us
    ppermute x7, waiting for transfers between devices, merge_peaks(): other = lax.ppermute(pair, axis, [(j, j ^ dist) for j in range(size)])  11.8 us
    ppermute x7, starting transfers between devices, merge_peaks(): other = lax.ppermute(pair, axis, [(j, j ^ dist) for j in range(size)])  11.8 us
    ppermute x2, starting transfers between devices, reduce_rows(): other = lax.ppermute(held, 'core', swap)  8.35 us
  transfers between devices with their start and end apart: 47, of which 22 were waited for; matrix products, arithmetic and copies ran while one was open for 31% of the time, Pallas kernels for 0%

profile of v1, /device:TPU:1, one launch (start us, length us, event | category | flops | bytes accessed | tf_op | source)
XLA Modules:
  0.0 344.2 jit_solution(904693625575606734)
XLA Ops:
  6.5 1.8 fusion.66
  8.3 4.5 %collective-permute-start = (f32[512,96]{0,1:T(8,128)S(1)}, f32[512,96]{0,1:T(8,128)S(1)}, u32[]{:S(2)}, u32[]{:S(2)}) collective-permute-start(f32[512,96]{0,1:T(8,128)S(1)} %get-tuple-element.292), channel_id=1, source_target_pairs={{0,64},{64,0},{1,65},{65,1},{2,66},{66,2},{3,67},{67,3},{4,68},{68... | collective-permute-start | bytes 589832 | tf_op jit(solution)/shard_map/ppermute | solution.py:86
  12.8 0.8 and_reduce_fusion.10
  15.1 2.4 collective-permute-done
  17.5 1.4 collective-permute-start.1
  18.9 1.5 collective-permute-start.2
  20.4 0.8 and_reduce_fusion.13
  22.1 2.0 collective-permute-done.1
  24.1 2.7 collective-permute-start.4
  28.1 2.4 collective-permute-done.3
  30.6 3.2 collective-permute-start.6
  35.0 2.3 collective-permute-done.5
  38.6 24.4 %all-gather.2.cloned.1.call-done = f32[512,768]{0,1:T(8,128)} async-done(((f32[512,96]{0,1:T(8,128)}), f32[512,768]{0,1:T(8,128)}) %all-gather.2.cloned.1.call-update) | async-done | bytes 1572880 | tf_op jit(solution)/shard_map/all_gather | solution.py:83
  63.0 43.5 %multiply_reduce_fusion = (f32[1024]{0:T(1024)S(1)}, f32[1024,2048]{1,0:T(8,128)S(1)}) fusion(f32[2048,768]{1,0:T(8,128)} %param.47, f32[512,768]{0,1:T(8,128)S(1)} %bitcast.236, f32[512,768]{0,1:T(8,128)} %all-gather.2.cloned.1.call-done), kind=kOutput, calls=%fused_computation.4 | convolution fusion | flops 19332333568 | bytes 17829888 | tf_op jit(solution)/shard_map/dot_general | solution.py:14
  106.5 1.9 exponential_reduce_fusion
  108.7 3.9 %collective-permute-done.7 = f32[2,1024]{1,0:T(2,128)S(1)} collective-permute-done((f32[2,1024]{1,0:T(2,128)S(1)}, f32[2,1024]{1,0:T(2,128)S(1)}, u32[]{:S(2)}, u32[]{:S(2)}) %collective-permute-start.7) | collective-permute-done | bytes 8224 | tf_op jit(solution)/shard_map/ppermute | solution.py:32
  112.6 0.8 collective-permute-start.8
  113.4 2.0 collective-permute-done.8
  115.5 1.5 collective-permute-start.9
  117.0 56.8 %multiply_bitcast_fusion = f32[2048,1024]{0,1:T(8,128)S(1)} fusion(f32[2048,768]{1,0:T(8,128)} %param.45, f32[512,768]{0,1:T(8,128)S(1)} %bitcast.237, f32[512,768]{0,1:T(8,128)S(1)} %copy-done.6), kind=kOutput, calls=%fused_computation.2 | convolution fusion | flops 19330236416 | bytes 17825792 | tf_op jit(solution)/shard_map/dot_general | solution.py:14
  174.5 4.3 %fusion.63 = (f32[2048]{0:T(1024)S(1)}, f32[2048,1024]{0,1:T(8,128)}) fusion(f32[2048]{0:T(1024)S(1)} %subtract_reduce_fusion, f32[2048,1024]{0,1:T(8,128)S(1)} %multiply_bitcast_fusion, f32[1024]{0:T(1024)S(1)} %bitcast.263), kind=kLoop, calls=%fused_computation.207 | loop fusion | flops 6289408 | bytes 16797696 | tf_op jit(solution)/shard_map/reduce_sum | solution.py:114
  178.8 4.8 %collective-permute-start.10 = (f32[2,2048]{1,0:T(2,128)S(1)}, f32[2,2048]{1,0:T(2,128)S(1)}, u32[]{:S(2)}, u32[]{:S(2)}) collective-permute-start(f32[2,2048]{1,0:T(2,128)S(1)} %pad_maximum_fusion.6), channel_id=1, source_target_pairs={{0,1},{1,0},{2,3},{3,2},{4,5},{5,4},{6,7},{7,6},{8,9},{9,8},{10,11... | collective-permute-start | bytes 49160 | tf_op jit(solution)/shard_map/ppermute | solution.py:32
  183.6 0.8 collective-permute-done.10
  185.0 2.2 collective-permute-done.11
  187.2 1.3 collective-permute-start.12
  188.5 1.4 collective-permute-done.12
  190.0 2.8 collective-permute-start.13
  192.8 1.4 collective-permute-done.13
  194.2 21.8 %fusion.4 = f32[1024,768]{1,0:T(8,128)S(1)} fusion(f32[2048,1024]{0,1:T(8,128)} %get-tuple-element.276, f32[1024]{0:T(1024)S(1)} %get-tuple-element.309, f32[512,768]{0,1:T(8,128)S(1)} %bitcast.238, f32[512,768]{0,1:T(8,128)S(1)} %copy-done.6), kind=kOutput, calls=%fused_computation.13 | convolution fusion | flops 9665249280 | bytes 10489856 | tf_op jit(solution)/shard_map/dot_general | solution.py:24
  216.1 1.3 dynamic-slice_bitcast_fusion.1
  218.2 3.8 %collective-permute-start.14 = (f32[512,768]{1,0:T(8,128)}, f32[512,768]{1,0:T(8,128)}, u32[]{:S(2)}, u32[]{:S(2)}) collective-permute-start(f32[512,768]{1,0:T(8,128)} %dynamic-slice_bitcast_fusion.1), channel_id=1, source_target_pairs={{0,1},{1,0},{2,3},{3,2},{4,5},{5,4},{6,7},{7,6},{8,9},{9,8},{10,11... | collective-permute-start | bytes 4718600 | tf_op jit(solution)/shard_map/ppermute | solution.py:55
  222.0 22.0 %fusion.7 = f32[1024,768]{1,0:T(8,128)S(1)} fusion(f32[2048,1024]{0,1:T(8,128)} %get-tuple-element.276, f32[1024]{0:T(1024)S(1)} %get-tuple-element.310, f32[512,768]{0,1:T(8,128)S(1)} %bitcast.239, f32[512,768]{0,1:T(8,128)S(1)} %copy-done.6), kind=kOutput, calls=%fused_computation.14 | convolution fusion | flops 9665249280 | bytes 10489856 | tf_op jit(solution)/shard_map/dot_general | solution.py:24
  244.0 1.3 dynamic-slice_bitcast_fusion
  245.3 1.1 copy-done
  246.4 0.8 and_reduce_fusion.4
  247.2 0.8 and_reduce_fusion.2
  248.0 0.8 and_reduce_fusion
  248.8 1.7 bitcast_add_fusion.1
  250.7 2.5 collective-permute-start.18
  253.3 1.7 bitcast_add_fusion
  255.1 2.9 collective-permute-start.34
  258.2 2.7 collective-permute-start.19
  261.2 3.5 %collective-permute-start.35 = (f32[64,768]{1,0:T(8,128)S(1)}, f32[64,768]{1,0:T(8,128)S(1)}, u32[]{:S(2)}, u32[]{:S(2)}) collective-permute-start(f32[64,768]{1,0:T(8,128)S(1)} %bitcast_add_fusion.4), channel_id=1, source_target_pairs={{0,12},{4,0},{8,4},{12,8},{1,13},{5,1},{9,5},{13,9},{2,14},{6,2},{... | collective-permute-start | bytes 589832 | tf_op jit(solution)/shard_map/ppermute | solution.py:60
  264.8 0.9 collective-permute-done.19
  265.7 3.5 %collective-permute-start.20 = (f32[64,768]{1,0:T(8,128)S(1)}, f32[64,768]{1,0:T(8,128)S(1)}, u32[]{:S(2)}, u32[]{:S(2)}) collective-permute-start(f32[64,768]{1,0:T(8,128)S(1)} %bitcast_add_fusion.9), channel_id=1, source_target_pairs={{0,12},{4,0},{8,4},{12,8},{1,13},{5,1},{9,5},{13,9},{2,14},{6,2},{... | collective-permute-start | bytes 589832 | tf_op jit(solution)/shard_map/ppermute | solution.py:60
  269.5 3.2 collective-permute-start.36
  272.8 0.9 collective-permute-done.20
  273.7 2.9 collective-permute-done.17
  277.7 3.4 collective-permute-done.33
  281.7 1.2 collective-permute-start.22
  282.9 4.4 %collective-permute-done.37 = f32[64,768]{1,0:T(8,128)S(1)} collective-permute-done((f32[64,768]{1,0:T(8,128)S(1)}, f32[64,768]{1,0:T(8,128)S(1)}, u32[]{:S(2)}, u32[]{:S(2)}) %collective-permute-start.37) | collective-permute-done | bytes 196640 | tf_op jit(solution)/shard_map/ppermute | solution.py:62
  287.8 3.7 %collective-permute-done.22 = f32[64,768]{1,0:T(8,128)S(1)} collective-permute-done((f32[64,768]{1,0:T(8,128)S(1)}, f32[64,768]{1,0:T(8,128)S(1)}, u32[]{:S(2)}, u32[]{:S(2)}) %collective-permute-start.22) | collective-permute-done | bytes 196640 | tf_op jit(solution)/shard_map/ppermute | solution.py:65
  291.6 2.7 collective-permute-start.24
  294.3 1.4 collective-permute-done.38
  295.8 2.7 collective-permute-start.40
  300.3 2.7 collective-permute-start.26
  304.2 2.7 collective-permute-start.42
  308.4 2.7 collective-permute-start.28
  312.4 2.7 collective-permute-start.44
  318.0 8.2 %collective-permute-start.29 = (f32[512,768]{1,0:T(8,128)S(1)}, f32[512,768]{1,0:T(8,128)}, u32[]{:S(2)}, u32[]{:S(2)}) collective-permute-start(f32[512,768]{1,0:T(8,128)S(1)} %bitcast.232), channel_id=1, source_target_pairs={{0,1},{1,0},{2,3},{3,2},{4,5},{5,4},{6,7},{7,6},{8,9},{9,8},{10,11... | collective-permute-start | bytes 4718600 | tf_op jit(solution)/shard_map/ppermute | solution.py:75
  327.8 1.6 collective-permute-done.29
  329.4 2.3 maximum_select_fusion
  331.8 2.2 maximum_select_fusion.1
  334.0 3.1 pad_maximum_fusion
  (136 shorter events, 22.6 us)
Async XLA Ops:
  6.5 6.3 %copy-start.4 = (s32[4]{0:T(128)S(1)}, s32[4]{0:T(128)}, u32[]{:S(2)}) copy-start(s32[4]{0:T(128)} %constant.689.clone.1) | copy-start | bytes 52
  6.5 13.9 %copy-start.5 = (s32[4]{0:T(128)S(1)}, s32[4]{0:T(128)}, u32[]{:S(2)}) copy-start(s32[4]{0:T(128)} %constant.683.clone.1) | copy-start | bytes 52
  6.5 56.4 %all-gather.2.cloned.1.call-start = ((), (), s32[]{:S(2)}) async-start(), calls=%async_computation | async-start | bytes 1769472 | tf_op jit(solution)/shard_map/all_gather | solution.py:83
  8.3 9.1 %collective-permute-start = (f32[512,96]{0,1:T(8,128)S(1)}, f32[512,96]{0,1:T(8,128)S(1)}, u32[]{:S(2)}, u32[]{:S(2)}) collective-permute-start(f32[512,96]{0,1:T(8,128)S(1)} %get-tuple-element.292), channel_id=1, source_target_pairs={{0,64},{64,0},{1,65},{65,1},{2,66},{66,2},{3,67},{67,3},{4,68},{68... | collective-permute-start | bytes 589832 | tf_op jit(solution)/shard_map/ppermute | solution.py:86
  17.5 6.6 %collective-permute-start.1 = (f32[512,96]{0,1:T(8,128)S(1)}, f32[512,96]{0,1:T(8,128)S(1)}, u32[]{:S(2)}, u32[]{:S(2)}) collective-permute-start(f32[512,96]{0,1:T(8,128)S(1)} %get-tuple-element.294), channel_id=1, source_target_pairs={{0,16},{16,32},{32,48},{48,0},{1,17},{17,33},{33,49},{49,1},{2,18}... | collective-permute-start | bytes 589832 | tf_op jit(solution)/shard_map/ppermute | solution.py:91
  18.9 5.2 %collective-permute-start.2 = (f32[512,96]{0,1:T(8,128)S(1)}, f32[512,96]{0,1:T(8,128)S(1)}, u32[]{:S(2)}, u32[]{:S(2)}) collective-permute-start(f32[512,96]{0,1:T(8,128)S(1)} %get-tuple-element.293), channel_id=1, source_target_pairs={{0,48},{16,0},{32,16},{48,32},{1,49},{17,1},{33,17},{49,33},{2,50}... | collective-permute-start | bytes 589832 | tf_op jit(solution)/shard_map/ppermute | solution.py:92
  24.1 6.4 %collective-permute-start.3 = (f32[512,96]{0,1:T(8,128)S(1)}, f32[512,96]{0,1:T(8,128)S(1)}, u32[]{:S(2)}, u32[]{:S(2)}) collective-permute-start(f32[512,96]{0,1:T(8,128)S(1)} %collective-permute-done.1), channel_id=1, source_target_pairs={{0,16},{16,32},{32,48},{48,0},{1,17},{17,33},{33,49},{49,1},{2,18}... | collective-permute-start | bytes 589832 | tf_op jit(solution)/shard_map/ppermute | solution.py:91
  24.1 6.4 %collective-permute-start.4 = (f32[512,96]{0,1:T(8,128)S(1)}, f32[512,96]{0,1:T(8,128)S(1)}, u32[]{:S(2)}, u32[]{:S(2)}) collective-permute-start(f32[512,96]{0,1:T(8,128)S(1)} %collective-permute-done.2), channel_id=1, source_target_pairs={{0,48},{16,0},{32,16},{48,32},{1,49},{17,1},{33,17},{49,33},{2,50}... | collective-permute-start | bytes 589832 | tf_op jit(solution)/shard_map/ppermute | solution.py:92
  30.5 6.7 %collective-permute-start.5 = (f32[512,96]{0,1:T(8,128)S(1)}, f32[512,96]{0,1:T(8,128)S(1)}, u32[]{:S(2)}, u32[]{:S(2)}) collective-permute-start(f32[512,96]{0,1:T(8,128)S(1)} %collective-permute-done.3), channel_id=1, source_target_pairs={{0,16},{16,32},{32,48},{48,0},{1,17},{17,33},{33,49},{49,1},{2,18}... | collective-permute-start | bytes 589832 | tf_op jit(solution)/shard_map/ppermute | solution.py:91
  30.6 7.4 %collective-permute-start.6 = (f32[512,96]{0,1:T(8,128)S(1)}, f32[512,96]{0,1:T(8,128)S(1)}, u32[]{:S(2)}, u32[]{:S(2)}) collective-permute-start(f32[512,96]{0,1:T(8,128)S(1)} %collective-permute-done.4), channel_id=1, source_target_pairs={{0,48},{16,0},{32,16},{48,32},{1,49},{17,1},{33,17},{49,33},{2,50}... | collective-permute-start | bytes 589832 | tf_op jit(solution)/shard_map/ppermute | solution.py:92
  106.5 10.5 %copy-start.6 = (f32[512,768]{0,1:T(8,128)S(1)}, f32[512,768]{0,1:T(8,128)}, u32[]{:S(2)}) copy-start(f32[512,768]{0,1:T(8,128)} %all-gather.2.cloned.1.call-done) | copy-start | bytes 4718596
  108.5 4.1 %collective-permute-start.7 = (f32[2,1024]{1,0:T(2,128)S(1)}, f32[2,1024]{1,0:T(2,128)S(1)}, u32[]{:S(2)}, u32[]{:S(2)}) collective-permute-start(f32[2,1024]{1,0:T(2,128)S(1)} %pad_maximum_fusion.10), channel_id=1, source_target_pairs={{0,64},{64,0},{1,65},{65,1},{2,66},{66,2},{3,67},{67,3},{4,68},{68... | collective-permute-start | bytes 24584 | tf_op jit(solution)/shard_map/ppermute | solution.py:32
  112.6 2.9 collective-permute-start.8
  115.5 58.3 %collective-permute-start.9 = (f32[2,1024]{1,0:T(2,128)S(1)}, f32[2,1024]{1,0:T(2,128)S(1)}, u32[]{:S(2)}, u32[]{:S(2)}) collective-permute-start(f32[2,1024]{1,0:T(2,128)S(1)} %pad_maximum_fusion.12), channel_id=1, source_target_pairs={{0,32},{16,48},{32,0},{48,16},{1,33},{17,49},{33,1},{49,17},{2,34}... | collective-permute-start | bytes 24584 | tf_op jit(solution)/shard_map/ppermute | solution.py:32
  178.8 5.6 %collective-permute-start.10 = (f32[2,2048]{1,0:T(2,128)S(1)}, f32[2,2048]{1,0:T(2,128)S(1)}, u32[]{:S(2)}, u32[]{:S(2)}) collective-permute-start(f32[2,2048]{1,0:T(2,128)S(1)} %pad_maximum_fusion.6), channel_id=1, source_target_pairs={{0,1},{1,0},{2,3},{3,2},{4,5},{5,4},{6,7},{7,6},{8,9},{9,8},{10,11... | collective-permute-start | bytes 49160 | tf_op jit(solution)/shard_map/ppermute | solution.py:32
  184.5 2.7 collective-permute-start.11
  187.2 2.7 collective-permute-start.12
  190.0 4.2 %collective-permute-start.13 = (f32[2,2048]{1,0:T(2,128)S(1)}, f32[2,2048]{1,0:T(2,128)S(1)}, u32[]{:S(2)}, u32[]{:S(2)}) collective-permute-start(f32[2,2048]{1,0:T(2,128)S(1)} %pad_maximum_fusion.9), channel_id=1, source_target_pairs={{0,8},{4,12},{8,0},{12,4},{1,9},{5,13},{9,1},{13,5},{2,10},{6,14},... | collective-permute-start | bytes 49160 | tf_op jit(solution)/shard_map/ppermute | solution.py:32
  216.1 2.1 copy-start.2
  218.2 30.6 %collective-permute-start.14 = (f32[512,768]{1,0:T(8,128)}, f32[512,768]{1,0:T(8,128)}, u32[]{:S(2)}, u32[]{:S(2)}) collective-permute-start(f32[512,768]{1,0:T(8,128)} %dynamic-slice_bitcast_fusion.1), channel_id=1, source_target_pairs={{0,1},{1,0},{2,3},{3,2},{4,5},{5,4},{6,7},{7,6},{8,9},{9,8},{10,11... | collective-permute-start | bytes 4718600 | tf_op jit(solution)/shard_map/ppermute | solution.py:55
  244.0 2.4 copy-start
  244.0 4.8 %copy-start.3 = (f32[1024,768]{1,0:T(8,128)S(1)}, f32[1024,768]{1,0:T(8,128)}, u32[]{:S(2)}) copy-start(f32[1024,768]{1,0:T(8,128)} %copy-done.2) | copy-start | bytes 9437188
  246.4 6.9 %collective-permute-start.30 = (f32[512,768]{1,0:T(8,128)}, f32[512,768]{1,0:T(8,128)}, u32[]{:S(2)}, u32[]{:S(2)}) collective-permute-start(f32[512,768]{1,0:T(8,128)} %dynamic-slice_bitcast_fusion), channel_id=1, source_target_pairs={{0,1},{1,0},{2,3},{3,2},{4,5},{5,4},{6,7},{7,6},{8,9},{9,8},{10,11... | collective-permute-start | bytes 4718600 | tf_op jit(solution)/shard_map/ppermute | solution.py:55
  250.5 2.8 copy-start.1
  250.7 7.5 %collective-permute-start.18 = (f32[64,768]{1,0:T(8,128)S(1)}, f32[64,768]{1,0:T(8,128)S(1)}, u32[]{:S(2)}, u32[]{:S(2)}) collective-permute-start(f32[64,768]{1,0:T(8,128)S(1)} %dynamic-slice_bitcast_fusion.4), channel_id=1, source_target_pairs={{0,12},{4,0},{8,4},{12,8},{1,13},{5,1},{9,5},{13,9},{2,14},{6,2},{... | collective-permute-start | bytes 589832 | tf_op jit(solution)/shard_map/ppermute | solution.py:60
  253.2 7.7 %collective-permute-start.15 = (f32[64,768]{1,0:T(8,128)S(1)}, f32[64,768]{1,0:T(8,128)S(1)}, u32[]{:S(2)}, u32[]{:S(2)}) collective-permute-start(f32[64,768]{1,0:T(8,128)S(1)} %dynamic-slice_bitcast_fusion.5), channel_id=1, source_target_pairs={{0,4},{4,8},{8,12},{12,0},{1,5},{5,9},{9,13},{13,1},{2,6},{6,10},{... | collective-permute-start | bytes 589832 | tf_op jit(solution)/shard_map/ppermute | solution.py:59
  255.1 6.0 %collective-permute-start.34 = (f32[64,768]{1,0:T(8,128)S(1)}, f32[64,768]{1,0:T(8,128)S(1)}, u32[]{:S(2)}, u32[]{:S(2)}) collective-permute-start(f32[64,768]{1,0:T(8,128)S(1)} %dynamic-slice_bitcast_fusion.2), channel_id=1, source_target_pairs={{0,12},{4,0},{8,4},{12,8},{1,13},{5,1},{9,5},{13,9},{2,14},{6,2},{... | collective-permute-start | bytes 589832 | tf_op jit(solution)/shard_map/ppermute | solution.py:60
  258.1 6.6 %collective-permute-start.31 = (f32[64,768]{1,0:T(8,128)S(1)}, f32[64,768]{1,0:T(8,128)S(1)}, u32[]{:S(2)}, u32[]{:S(2)}) collective-permute-start(f32[64,768]{1,0:T(8,128)S(1)} %dynamic-slice_bitcast_fusion.3), channel_id=1, source_target_pairs={{0,4},{4,8},{8,12},{12,0},{1,5},{5,9},{9,13},{13,1},{2,6},{6,10},{... | collective-permute-start | bytes 589832 | tf_op jit(solution)/shard_map/ppermute | solution.py:59
  258.2 7.5 %collective-permute-start.19 = (f32[64,768]{1,0:T(8,128)S(1)}, f32[64,768]{1,0:T(8,128)S(1)}, u32[]{:S(2)}, u32[]{:S(2)}) collective-permute-start(f32[64,768]{1,0:T(8,128)S(1)} %bitcast_add_fusion.10), channel_id=1, source_target_pairs={{0,12},{4,0},{8,4},{12,8},{1,13},{5,1},{9,5},{13,9},{2,14},{6,2},{... | collective-permute-start | bytes 589832 | tf_op jit(solution)/shard_map/ppermute | solution.py:60
  260.9 8.2 %collective-permute-start.16 = (f32[64,768]{1,0:T(8,128)S(1)}, f32[64,768]{1,0:T(8,128)S(1)}, u32[]{:S(2)}, u32[]{:S(2)}) collective-permute-start(f32[64,768]{1,0:T(8,128)S(1)} %bitcast_add_fusion.13), channel_id=1, source_target_pairs={{0,4},{4,8},{8,12},{12,0},{1,5},{5,9},{9,13},{13,1},{2,6},{6,10},{... | collective-permute-start | bytes 589832 | tf_op jit(solution)/shard_map/ppermute | solution.py:59
  261.2 8.3 %collective-permute-start.35 = (f32[64,768]{1,0:T(8,128)S(1)}, f32[64,768]{1,0:T(8,128)S(1)}, u32[]{:S(2)}, u32[]{:S(2)}) collective-permute-start(f32[64,768]{1,0:T(8,128)S(1)} %bitcast_add_fusion.4), channel_id=1, source_target_pairs={{0,12},{4,0},{8,4},{12,8},{1,13},{5,1},{9,5},{13,9},{2,14},{6,2},{... | collective-permute-start | bytes 589832 | tf_op jit(solution)/shard_map/ppermute | solution.py:60
  264.7 8.0 %collective-permute-start.32 = (f32[64,768]{1,0:T(8,128)S(1)}, f32[64,768]{1,0:T(8,128)S(1)}, u32[]{:S(2)}, u32[]{:S(2)}) collective-permute-start(f32[64,768]{1,0:T(8,128)S(1)} %bitcast_add_fusion.7), channel_id=1, source_target_pairs={{0,4},{4,8},{8,12},{12,0},{1,5},{5,9},{9,13},{13,1},{2,6},{6,10},{... | collective-permute-start | bytes 589832 | tf_op jit(solution)/shard_map/ppermute | solution.py:59
  265.7 8.0 %collective-permute-start.20 = (f32[64,768]{1,0:T(8,128)S(1)}, f32[64,768]{1,0:T(8,128)S(1)}, u32[]{:S(2)}, u32[]{:S(2)}) collective-permute-start(f32[64,768]{1,0:T(8,128)S(1)} %bitcast_add_fusion.9), channel_id=1, source_target_pairs={{0,12},{4,0},{8,4},{12,8},{1,13},{5,1},{9,5},{13,9},{2,14},{6,2},{... | collective-permute-start | bytes 589832 | tf_op jit(solution)/shard_map/ppermute | solution.py:60
  269.2 7.4 %collective-permute-start.17 = (f32[64,768]{1,0:T(8,128)S(1)}, f32[64,768]{1,0:T(8,128)S(1)}, u32[]{:S(2)}, u32[]{:S(2)}) collective-permute-start(f32[64,768]{1,0:T(8,128)S(1)} %bitcast_add_fusion.12), channel_id=1, source_target_pairs={{0,4},{4,8},{8,12},{12,0},{1,5},{5,9},{9,13},{13,1},{2,6},{6,10},{... | collective-permute-start | bytes 589832 | tf_op jit(solution)/shard_map/ppermute | solution.py:59
  269.5 8.2 %collective-permute-start.36 = (f32[64,768]{1,0:T(8,128)S(1)}, f32[64,768]{1,0:T(8,128)S(1)}, u32[]{:S(2)}, u32[]{:S(2)}) collective-permute-start(f32[64,768]{1,0:T(8,128)S(1)} %bitcast_add_fusion.3), channel_id=1, source_target_pairs={{0,12},{4,0},{8,4},{12,8},{1,13},{5,1},{9,5},{13,9},{2,14},{6,2},{... | collective-permute-start | bytes 589832 | tf_op jit(solution)/shard_map/ppermute | solution.py:60
  272.7 8.4 %collective-permute-start.33 = (f32[64,768]{1,0:T(8,128)S(1)}, f32[64,768]{1,0:T(8,128)S(1)}, u32[]{:S(2)}, u32[]{:S(2)}) collective-permute-start(f32[64,768]{1,0:T(8,128)S(1)} %bitcast_add_fusion.6), channel_id=1, source_target_pairs={{0,4},{4,8},{8,12},{12,0},{1,5},{5,9},{9,13},{13,1},{2,6},{6,10},{... | collective-permute-start | bytes 589832 | tf_op jit(solution)/shard_map/ppermute | solution.py:59
  276.7 4.9 %collective-permute-start.21 = (f32[64,768]{1,0:T(8,128)S(1)}, f32[64,768]{1,0:T(8,128)S(1)}, u32[]{:S(2)}, u32[]{:S(2)}) collective-permute-start(f32[64,768]{1,0:T(8,128)S(1)} %fusion.24), channel_id=1, source_target_pairs={{0,2},{2,0},{1,3},{3,1},{4,6},{6,4},{5,7},{7,5},{8,10},{10,8},{9,1... | collective-permute-start | bytes 589832 | tf_op jit(solution)/shard_map/ppermute | solution.py:62
  281.2 6.1 %collective-permute-start.37 = (f32[64,768]{1,0:T(8,128)S(1)}, f32[64,768]{1,0:T(8,128)S(1)}, u32[]{:S(2)}, u32[]{:S(2)}) collective-permute-start(f32[64,768]{1,0:T(8,128)S(1)} %fusion.18), channel_id=1, source_target_pairs={{0,2},{2,0},{1,3},{3,1},{4,6},{6,4},{5,7},{7,5},{8,10},{10,8},{9,1... | collective-permute-start | bytes 589832 | tf_op jit(solution)/shard_map/ppermute | solution.py:62
  281.7 9.7 %collective-permute-start.22 = (f32[64,768]{1,0:T(8,128)S(1)}, f32[64,768]{1,0:T(8,128)S(1)}, u32[]{:S(2)}, u32[]{:S(2)}) collective-permute-start(f32[64,768]{1,0:T(8,128)S(1)} %fusion.28), channel_id=1, source_target_pairs={{0,2},{2,0},{1,3},{3,1},{4,6},{6,4},{5,7},{7,5},{8,10},{10,8},{9,1... | collective-permute-start | bytes 589832 | tf_op jit(solution)/shard_map/ppermute | solution.py:65
  287.4 8.3 %collective-permute-start.38 = (f32[64,768]{1,0:T(8,128)S(1)}, f32[64,768]{1,0:T(8,128)S(1)}, u32[]{:S(2)}, u32[]{:S(2)}) collective-permute-start(f32[64,768]{1,0:T(8,128)S(1)} %fusion.22), channel_id=1, source_target_pairs={{0,2},{2,0},{1,3},{3,1},{4,6},{6,4},{5,7},{7,5},{8,10},{10,8},{9,1... | collective-permute-start | bytes 589832 | tf_op jit(solution)/shard_map/ppermute | solution.py:65
  291.5 8.7 %collective-permute-start.23 = (f32[64,768]{1,0:T(8,128)S(1)}, f32[64,768]{1,0:T(8,128)S(1)}, u32[]{:S(2)}, u32[]{:S(2)}) collective-permute-start(f32[64,768]{1,0:T(8,128)S(1)} %get-tuple-element.286), channel_id=1, source_target_pairs={{0,4},{4,8},{8,12},{12,0},{1,5},{5,9},{9,13},{13,1},{2,6},{6,10},{... | collective-permute-start | bytes 589832 | tf_op jit(solution)/shard_map/ppermute | solution.py:70
  291.6 8.7 %collective-permute-start.24 = (f32[64,768]{1,0:T(8,128)S(1)}, f32[64,768]{1,0:T(8,128)S(1)}, u32[]{:S(2)}, u32[]{:S(2)}) collective-permute-start(f32[64,768]{1,0:T(8,128)S(1)} %get-tuple-element.285), channel_id=1, source_target_pairs={{0,12},{4,0},{8,4},{12,8},{1,13},{5,1},{9,5},{13,9},{2,14},{6,2},{... | collective-permute-start | bytes 589832 | tf_op jit(solution)/shard_map/ppermute | solution.py:71
  295.8 7.2 %collective-permute-start.39 = (f32[64,768]{1,0:T(8,128)S(1)}, f32[64,768]{1,0:T(8,128)S(1)}, u32[]{:S(2)}, u32[]{:S(2)}) collective-permute-start(f32[64,768]{1,0:T(8,128)S(1)} %get-tuple-element.288), channel_id=1, source_target_pairs={{0,4},{4,8},{8,12},{12,0},{1,5},{5,9},{9,13},{13,1},{2,6},{6,10},{... | collective-permute-start | bytes 589832 | tf_op jit(solution)/shard_map/ppermute | solution.py:70
  295.8 8.3 %collective-permute-start.40 = (f32[64,768]{1,0:T(8,128)S(1)}, f32[64,768]{1,0:T(8,128)S(1)}, u32[]{:S(2)}, u32[]{:S(2)}) collective-permute-start(f32[64,768]{1,0:T(8,128)S(1)} %get-tuple-element.287), channel_id=1, source_target_pairs={{0,12},{4,0},{8,4},{12,8},{1,13},{5,1},{9,5},{13,9},{2,14},{6,2},{... | collective-permute-start | bytes 589832 | tf_op jit(solution)/shard_map/ppermute | solution.py:71
  300.2 8.1 %collective-permute-start.25 = (f32[64,768]{1,0:T(8,128)S(1)}, f32[64,768]{1,0:T(8,128)S(1)}, u32[]{:S(2)}, u32[]{:S(2)}) collective-permute-start(f32[64,768]{1,0:T(8,128)S(1)} %collective-permute-done.23), channel_id=1, source_target_pairs={{0,4},{4,8},{8,12},{12,0},{1,5},{5,9},{9,13},{13,1},{2,6},{6,10},{... | collective-permute-start | bytes 589832 | tf_op jit(solution)/shard_map/ppermute | solution.py:70
  300.3 8.1 %collective-permute-start.26 = (f32[64,768]{1,0:T(8,128)S(1)}, f32[64,768]{1,0:T(8,128)S(1)}, u32[]{:S(2)}, u32[]{:S(2)}) collective-permute-start(f32[64,768]{1,0:T(8,128)S(1)} %collective-permute-done.24), channel_id=1, source_target_pairs={{0,12},{4,0},{8,4},{12,8},{1,13},{5,1},{9,5},{13,9},{2,14},{6,2},{... | collective-permute-start | bytes 589832 | tf_op jit(solution)/shard_map/ppermute | solution.py:71
  303.0 8.1 %collective-permute-start.41 = (f32[64,768]{1,0:T(8,128)S(1)}, f32[64,768]{1,0:T(8,128)S(1)}, u32[]{:S(2)}, u32[]{:S(2)}) collective-permute-start(f32[64,768]{1,0:T(8,128)S(1)} %collective-permute-done.39), channel_id=1, source_target_pairs={{0,4},{4,8},{8,12},{12,0},{1,5},{5,9},{9,13},{13,1},{2,6},{6,10},{... | collective-permute-start | bytes 589832 | tf_op jit(solution)/shard_map/ppermute | solution.py:70
  304.2 8.3 %collective-permute-start.42 = (f32[64,768]{1,0:T(8,128)S(1)}, f32[64,768]{1,0:T(8,128)S(1)}, u32[]{:S(2)}, u32[]{:S(2)}) collective-permute-start(f32[64,768]{1,0:T(8,128)S(1)} %collective-permute-done.40), channel_id=1, source_target_pairs={{0,12},{4,0},{8,4},{12,8},{1,13},{5,1},{9,5},{13,9},{2,14},{6,2},{... | collective-permute-start | bytes 589832 | tf_op jit(solution)/shard_map/ppermute | solution.py:71
  308.4 8.2 %collective-permute-start.27 = (f32[64,768]{1,0:T(8,128)S(1)}, f32[64,768]{1,0:T(8,128)S(1)}, u32[]{:S(2)}, u32[]{:S(2)}) collective-permute-start(f32[64,768]{1,0:T(8,128)S(1)} %collective-permute-done.25), channel_id=1, source_target_pairs={{0,4},{4,8},{8,12},{12,0},{1,5},{5,9},{9,13},{13,1},{2,6},{6,10},{... | collective-permute-start | bytes 589832 | tf_op jit(solution)/shard_map/ppermute | solution.py:70
  308.4 8.8 %collective-permute-start.28 = (f32[64,768]{1,0:T(8,128)S(1)}, f32[64,768]{1,0:T(8,128)S(1)}, u32[]{:S(2)}, u32[]{:S(2)}) collective-permute-start(f32[64,768]{1,0:T(8,128)S(1)} %collective-permute-done.26), channel_id=1, source_target_pairs={{0,12},{4,0},{8,4},{12,8},{1,13},{5,1},{9,5},{13,9},{2,14},{6,2},{... | collective-permute-start | bytes 589832 | tf_op jit(solution)/shard_map/ppermute | solution.py:71
  311.1 15.2 %collective-permute-start.43 = (f32[64,768]{1,0:T(8,128)S(1)}, f32[64,768]{1,0:T(8,128)S(1)}, u32[]{:S(2)}, u32[]{:S(2)}) collective-permute-start(f32[64,768]{1,0:T(8,128)S(1)} %collective-permute-done.41), channel_id=1, source_target_pairs={{0,4},{4,8},{8,12},{12,0},{1,5},{5,9},{9,13},{13,1},{2,6},{6,10},{... | collective-permute-start | bytes 589832 | tf_op jit(solution)/shard_map/ppermute | solution.py:70
  312.4 14.5 %collective-permute-start.44 = (f32[64,768]{1,0:T(8,128)S(1)}, f32[64,768]{1,0:T(8,128)S(1)}, u32[]{:S(2)}, u32[]{:S(2)}) collective-permute-start(f32[64,768]{1,0:T(8,128)S(1)} %collective-permute-done.42), channel_id=1, source_target_pairs={{0,12},{4,0},{8,4},{12,8},{1,13},{5,1},{9,5},{13,9},{2,14},{6,2},{... | collective-permute-start | bytes 589832 | tf_op jit(solution)/shard_map/ppermute | solution.py:71
  318.0 11.4 %collective-permute-start.29 = (f32[512,768]{1,0:T(8,128)S(1)}, f32[512,768]{1,0:T(8,128)}, u32[]{:S(2)}, u32[]{:S(2)}) collective-permute-start(f32[512,768]{1,0:T(8,128)S(1)} %bitcast.232), channel_id=1, source_target_pairs={{0,1},{1,0},{2,3},{3,2},{4,5},{5,4},{6,7},{7,6},{8,9},{9,8},{10,11... | collective-permute-start | bytes 4718600 | tf_op jit(solution)/shard_map/ppermute | solution.py:75
  327.7 4.0 %collective-permute-start.45 = (f32[512,768]{1,0:T(8,128)S(1)}, f32[512,768]{1,0:T(8,128)}, u32[]{:S(2)}, u32[]{:S(2)}) collective-permute-start(f32[512,768]{1,0:T(8,128)S(1)} %bitcast.230), channel_id=1, source_target_pairs={{0,1},{1,0},{2,3},{3,2},{4,5},{5,4},{6,7},{7,6},{8,9},{9,8},{10,11... | collective-permute-start | bytes 4718600 | tf_op jit(solution)/shard_map/ppermute | solution.py:75
Sparse Core Ops, SparseCore 0:
  9.7 53.2 all-gather.1

commit v2 on v1

--- a/solution.py
+++ b/solution.py
@@ -93,7 +93,7 @@
         got = got.at[(y - s - 1) % y_size, 0].set(right)
         got = got.at[(y + s + 1) % y_size, 1].set(left)
     ringed = got.transpose(2, 1, 0, 3).reshape(half, 2 * y_size * width)
-    return jnp.concatenate([offloaded, ringed], axis=0)
+    return lax.optimization_barrier(jnp.concatenate([offloaded, ringed], axis=0))
 
 
 def local(images, captions, bank, sizes):

time: 348 us -> 349 us (level)
  transfers between devices with their start and end apart: 47 -> 47, of which waited for: 22 -> 23; matrix products, arithmetic and copies ran while one was open for 31% -> 26% of each run, Pallas kernels for 0% -> 0%
where the time goes in v2:
time: 349 us; the launch traced here: 345 us
  matrix products  142 us (41%)
  starting transfers between devices  75.8 us (22%)
  waiting for transfers between devices  65.5 us (19%)
  other arithmetic  39.9 us (11%)
  between operations  14.4 us (4%)
  local copies, waits for them, and re-layouts  7.78 us (2%)
    dot_general x2, matrix products, similar(): lax.dot_general(query_factor, target_factor, (((1,), (1,)), ((), ())), pr...  98.2 us
    dot_general x2, matrix products, rescaled_affinity(): jnp.dot(weights, features, precision=lax.Precision.HIGHEST, preferred_ele...  43.5 us
    all_gather x1, waiting for transfers between devices, gather_features(): offloaded = lax.all_gather(captions[:half], IMG, axis=1, tiled=True)  24.5 us
    ppermute x6, starting transfers between devices, reduce_rows(): lax.ppermute(left, 'x', ring('x', x_size, -1))  18.4 us
    ppermute x6, starting transfers between devices, reduce_rows(): left = lax.ppermute(left, 'x', ring('x', x_size, -1))  16.1 us
    ppermute x7, waiting for transfers between devices, merge_peaks(): other = lax.ppermute(pair, axis, [(j, j ^ dist) for j in range(size)])  11.8 us
    ppermute x7, starting transfers between devices, merge_peaks(): other = lax.ppermute(pair, axis, [(j, j ^ dist) for j in range(size)])  11.8 us
    ppermute x2, starting transfers between devices, reduce_rows(): other = lax.ppermute(held, 'core', swap)  8.38 us
  transfers between devices with their start and end apart: 47, of which 23 were waited for; matrix products, arithmetic and copies ran while one was open for 26% of the time, Pallas kernels for 0%

profile of v2, /device:TPU:1, one launch (start us, length us, event | category | flops | bytes accessed | tf_op | source)
XLA Modules:
  0.0 345.0 jit_solution(7252317695703509640)
XLA Ops:
  6.5 1.8 fusion.61
  8.4 4.5 %collective-permute-start = (f32[512,96]{0,1:T(8,128)S(1)}, f32[512,96]{0,1:T(8,128)S(1)}, u32[]{:S(2)}, u32[]{:S(2)}) collective-permute-start(f32[512,96]{0,1:T(8,128)S(1)} %get-tuple-element.292), channel_id=1, source_target_pairs={{0,64},{64,0},{1,65},{65,1},{2,66},{66,2},{3,67},{67,3},{4,68},{68... | collective-permute-start | bytes 589832 | tf_op jit(solution)/shard_map/ppermute | solution.py:86
  12.9 0.8 and_reduce_fusion.10
  13.7 0.8 and_reduce_fusion.8
  15.2 2.3 collective-permute-done
  17.6 1.4 collective-permute-start.1
  19.0 1.5 collective-permute-start.2
  20.5 0.8 and_reduce_fusion.13
  22.2 2.0 collective-permute-done.1
  24.2 2.7 collective-permute-start.4
  28.2 2.3 collective-permute-done.3
  30.6 3.2 collective-permute-start.6
  35.2 2.1 collective-permute-done.5
  38.6 24.5 %all-gather.2.cloned.1.call-done = f32[512,768]{0,1:T(8,128)} async-done(((f32[512,96]{0,1:T(8,128)}), f32[512,768]{0,1:T(8,128)}) %all-gather.2.cloned.1.call-update) | async-done | bytes 1572880 | tf_op jit(solution)/shard_map/all_gather | solution.py:83
  63.0 1.8 pad_maximum_fusion.1
  64.9 1.4 copy-done.6
  66.3 56.8 %multiply_reduce_fusion = (f32[1024]{0:T(1024)S(1)}, f32[1024,2048]{1,0:T(8,128)S(1)}) fusion(f32[1024,768]{0,1:T(8,128)S(1)} %pad_maximum_fusion.1, f32[2048,768]{1,0:T(8,128)S(1)} %copy-done.6), kind=kOutput, calls=%fused_computation.4 | convolution fusion | flops 19331547136 | bytes 17829888 | tf_op jit(solution)/shard_map/dot_general | solution.py:14
  123.1 1.9 exponential_reduce_fusion
  125.2 3.9 %collective-permute-done.7 = f32[2,1024]{1,0:T(2,128)S(1)} collective-permute-done((f32[2,1024]{1,0:T(2,128)S(1)}, f32[2,1024]{1,0:T(2,128)S(1)}, u32[]{:S(2)}, u32[]{:S(2)}) %collective-permute-start.7) | collective-permute-done | bytes 8224 | tf_op jit(solution)/shard_map/ppermute | solution.py:32
  129.2 0.8 collective-permute-start.8
  130.0 2.0 collective-permute-done.8
  132.1 1.5 collective-permute-start.9
  133.6 41.4 %multiply_bitcast_fusion = f32[2048,1024]{0,1:T(8,128)S(1)} fusion(f32[1024,768]{0,1:T(8,128)S(1)} %pad_maximum_fusion.1, f32[2048,768]{1,0:T(8,128)S(1)} %bitcast.274), kind=kOutput, calls=%fused_computation.2 | convolution fusion | flops 19329449984 | bytes 17825792 | tf_op jit(solution)/shard_map/dot_general | solution.py:14
  175.7 4.3 %fusion.58 = (f32[2048]{0:T(1024)S(1)}, f32[2048,1024]{0,1:T(8,128)}) fusion(f32[2048]{0:T(1024)S(1)} %subtract_reduce_fusion, f32[2048,1024]{0,1:T(8,128)S(1)} %multiply_bitcast_fusion, f32[1024]{0:T(1024)S(1)} %bitcast.264), kind=kLoop, calls=%fused_computation.202 | loop fusion | flops 6289408 | bytes 16797696 | tf_op jit(solution)/shard_map/reduce_sum | solution.py:114
  180.0 4.8 %collective-permute-start.10 = (f32[2,2048]{1,0:T(2,128)S(1)}, f32[2,2048]{1,0:T(2,128)S(1)}, u32[]{:S(2)}, u32[]{:S(2)}) collective-permute-start(f32[2,2048]{1,0:T(2,128)S(1)} %pad_maximum_fusion.2), channel_id=1, source_target_pairs={{0,1},{1,0},{2,3},{3,2},{4,5},{5,4},{6,7},{7,6},{8,9},{9,8},{10,11... | collective-permute-start | bytes 49160 | tf_op jit(solution)/shard_map/ppermute | solution.py:32
  184.8 0.8 collective-permute-done.10
  186.1 2.2 collective-permute-done.11
  188.4 1.3 collective-permute-start.12
  189.7 1.4 collective-permute-done.12
  191.2 2.8 collective-permute-start.13
  193.9 1.4 collective-permute-done.13
  195.4 21.7 %fusion.4 = f32[1024,768]{1,0:T(8,128)S(1)} fusion(f32[1024,768]{0,1:T(8,128)S(1)} %copy-done.2, f32[2048,1024]{0,1:T(8,128)} %get-tuple-element.276, f32[1024]{0:T(1024)S(1)} %get-tuple-element.309), kind=kOutput, calls=%fused_computation.13 | convolution fusion | flops 9664462848 | bytes 10489856 | tf_op jit(solution)/shard_map/dot_general | solution.py:24
  217.1 1.3 dynamic-slice_bitcast_fusion.1
  218.4 1.1 copy-done
  219.5 3.8 %collective-permute-start.14 = (f32[512,768]{1,0:T(8,128)}, f32[512,768]{1,0:T(8,128)}, u32[]{:S(2)}, u32[]{:S(2)}) collective-permute-start(f32[512,768]{1,0:T(8,128)} %dynamic-slice_bitcast_fusion.1), channel_id=1, source_target_pairs={{0,1},{1,0},{2,3},{3,2},{4,5},{5,4},{6,7},{7,6},{8,9},{9,8},{10,11... | collective-permute-start | bytes 4718600 | tf_op jit(solution)/shard_map/ppermute | solution.py:55
  223.3 21.8 %fusion.7 = f32[1024,768]{1,0:T(8,128)S(1)} fusion(f32[1024,768]{0,1:T(8,128)S(1)} %copy-done.3, f32[2048,1024]{0,1:T(8,128)} %get-tuple-element.276, f32[1024]{0:T(1024)S(1)} %get-tuple-element.310), kind=kOutput, calls=%fused_computation.14 | convolution fusion | flops 9664462848 | bytes 10489856 | tf_op jit(solution)/shard_map/dot_general | solution.py:24
  245.1 1.3 dynamic-slice_bitcast_fusion
  246.3 1.2 collective-permute-start.30
  248.3 0.8 and_reduce_fusion.2
  249.9 2.1 bitcast_add_fusion.1
  252.1 2.5 collective-permute-start.18
  254.7 1.6 bitcast_add_fusion
  256.5 2.9 collective-permute-start.34
  259.6 2.9 collective-permute-start.19
  263.1 3.5 %collective-permute-start.35 = (f32[64,768]{1,0:T(8,128)S(1)}, f32[64,768]{1,0:T(8,128)S(1)}, u32[]{:S(2)}, u32[]{:S(2)}) collective-permute-start(f32[64,768]{1,0:T(8,128)S(1)} %bitcast_add_fusion.4), channel_id=1, source_target_pairs={{0,12},{4,0},{8,4},{12,8},{1,13},{5,1},{9,5},{13,9},{2,14},{6,2},{... | collective-permute-start | bytes 589832 | tf_op jit(solution)/shard_map/ppermute | solution.py:60
  267.4 3.5 %collective-permute-start.20 = (f32[64,768]{1,0:T(8,128)S(1)}, f32[64,768]{1,0:T(8,128)S(1)}, u32[]{:S(2)}, u32[]{:S(2)}) collective-permute-start(f32[64,768]{1,0:T(8,128)S(1)} %bitcast_add_fusion.9), channel_id=1, source_target_pairs={{0,12},{4,0},{8,4},{12,8},{1,13},{5,1},{9,5},{13,9},{2,14},{6,2},{... | collective-permute-start | bytes 589832 | tf_op jit(solution)/shard_map/ppermute | solution.py:60
  271.2 3.2 collective-permute-start.36
  274.4 0.9 collective-permute-done.20
  275.4 2.9 collective-permute-done.17
  279.4 2.8 collective-permute-done.33
  284.0 4.4 %collective-permute-done.37 = f32[64,768]{1,0:T(8,128)S(1)} collective-permute-done((f32[64,768]{1,0:T(8,128)S(1)}, f32[64,768]{1,0:T(8,128)S(1)}, u32[]{:S(2)}, u32[]{:S(2)}) %collective-permute-start.37) | collective-permute-done | bytes 196640 | tf_op jit(solution)/shard_map/ppermute | solution.py:62
  289.0 3.7 %collective-permute-done.22 = f32[64,768]{1,0:T(8,128)S(1)} collective-permute-done((f32[64,768]{1,0:T(8,128)S(1)}, f32[64,768]{1,0:T(8,128)S(1)}, u32[]{:S(2)}, u32[]{:S(2)}) %collective-permute-start.22) | collective-permute-done | bytes 196640 | tf_op jit(solution)/shard_map/ppermute | solution.py:65
  292.8 2.7 collective-permute-start.24
  295.5 1.4 collective-permute-done.38
  297.0 2.7 collective-permute-start.40
  301.4 2.7 collective-permute-start.26
  305.4 2.7 collective-permute-start.42
  309.6 2.7 collective-permute-start.28
  313.7 2.7 collective-permute-start.44
  318.9 8.3 %collective-permute-start.29 = (f32[512,768]{1,0:T(8,128)S(1)}, f32[512,768]{1,0:T(8,128)}, u32[]{:S(2)}, u32[]{:S(2)}) collective-permute-start(f32[512,768]{1,0:T(8,128)S(1)} %bitcast.237), channel_id=1, source_target_pairs={{0,1},{1,0},{2,3},{3,2},{4,5},{5,4},{6,7},{7,6},{8,9},{9,8},{10,11... | collective-permute-start | bytes 4718600 | tf_op jit(solution)/shard_map/ppermute | solution.py:75
  328.5 1.8 collective-permute-done.29
  330.3 2.2 maximum_select_fusion
  332.6 2.2 maximum_select_fusion.1
  334.8 3.1 pad_maximum_fusion
  (142 shorter events, 24.6 us)
Async XLA Ops:
  6.5 6.4 %copy-start.4 = (s32[4]{0:T(128)S(1)}, s32[4]{0:T(128)}, u32[]{:S(2)}) copy-start(s32[4]{0:T(128)} %constant.689.clone.1) | copy-start | bytes 52
  6.5 13.9 %copy-start.5 = (s32[4]{0:T(128)S(1)}, s32[4]{0:T(128)}, u32[]{:S(2)}) copy-start(s32[4]{0:T(128)} %constant.683.clone.1) | copy-start | bytes 52
  6.5 56.5 %all-gather.2.cloned.1.call-start = ((), (), s32[]{:S(2)}) async-start(), calls=%async_computation | async-start | bytes 1769472 | tf_op jit(solution)/shard_map/all_gather | solution.py:83
  8.4 9.1 %collective-permute-start = (f32[512,96]{0,1:T(8,128)S(1)}, f32[512,96]{0,1:T(8,128)S(1)}, u32[]{:S(2)}, u32[]{:S(2)}) collective-permute-start(f32[512,96]{0,1:T(8,128)S(1)} %get-tuple-element.292), channel_id=1, source_target_pairs={{0,64},{64,0},{1,65},{65,1},{2,66},{66,2},{3,67},{67,3},{4,68},{68... | collective-permute-start | bytes 589832 | tf_op jit(solution)/shard_map/ppermute | solution.py:86
  17.6 6.6 %collective-permute-start.1 = (f32[512,96]{0,1:T(8,128)S(1)}, f32[512,96]{0,1:T(8,128)S(1)}, u32[]{:S(2)}, u32[]{:S(2)}) collective-permute-start(f32[512,96]{0,1:T(8,128)S(1)} %get-tuple-element.294), channel_id=1, source_target_pairs={{0,16},{16,32},{32,48},{48,0},{1,17},{17,33},{33,49},{49,1},{2,18}... | collective-permute-start | bytes 589832 | tf_op jit(solution)/shard_map/ppermute | solution.py:91
  19.0 5.2 %collective-permute-start.2 = (f32[512,96]{0,1:T(8,128)S(1)}, f32[512,96]{0,1:T(8,128)S(1)}, u32[]{:S(2)}, u32[]{:S(2)}) collective-permute-start(f32[512,96]{0,1:T(8,128)S(1)} %get-tuple-element.293), channel_id=1, source_target_pairs={{0,48},{16,0},{32,16},{48,32},{1,49},{17,1},{33,17},{49,33},{2,50}... | collective-permute-start | bytes 589832 | tf_op jit(solution)/shard_map/ppermute | solution.py:92
  24.2 6.4 %collective-permute-start.3 = (f32[512,96]{0,1:T(8,128)S(1)}, f32[512,96]{0,1:T(8,128)S(1)}, u32[]{:S(2)}, u32[]{:S(2)}) collective-permute-start(f32[512,96]{0,1:T(8,128)S(1)} %collective-permute-done.1), channel_id=1, source_target_pairs={{0,16},{16,32},{32,48},{48,0},{1,17},{17,33},{33,49},{49,1},{2,18}... | collective-permute-start | bytes 589832 | tf_op jit(solution)/shard_map/ppermute | solution.py:91
  24.2 6.4 %collective-permute-start.4 = (f32[512,96]{0,1:T(8,128)S(1)}, f32[512,96]{0,1:T(8,128)S(1)}, u32[]{:S(2)}, u32[]{:S(2)}) collective-permute-start(f32[512,96]{0,1:T(8,128)S(1)} %collective-permute-done.2), channel_id=1, source_target_pairs={{0,48},{16,0},{32,16},{48,32},{1,49},{17,1},{33,17},{49,33},{2,50}... | collective-permute-start | bytes 589832 | tf_op jit(solution)/shard_map/ppermute | solution.py:92
  30.5 6.8 %collective-permute-start.5 = (f32[512,96]{0,1:T(8,128)S(1)}, f32[512,96]{0,1:T(8,128)S(1)}, u32[]{:S(2)}, u32[]{:S(2)}) collective-permute-start(f32[512,96]{0,1:T(8,128)S(1)} %collective-permute-done.3), channel_id=1, source_target_pairs={{0,16},{16,32},{32,48},{48,0},{1,17},{17,33},{33,49},{49,1},{2,18}... | collective-permute-start | bytes 589832 | tf_op jit(solution)/shard_map/ppermute | solution.py:91
  30.6 7.4 %collective-permute-start.6 = (f32[512,96]{0,1:T(8,128)S(1)}, f32[512,96]{0,1:T(8,128)S(1)}, u32[]{:S(2)}, u32[]{:S(2)}) collective-permute-start(f32[512,96]{0,1:T(8,128)S(1)} %collective-permute-done.4), channel_id=1, source_target_pairs={{0,48},{16,0},{32,16},{48,32},{1,49},{17,1},{33,17},{49,33},{2,50}... | collective-permute-start | bytes 589832 | tf_op jit(solution)/shard_map/ppermute | solution.py:92
  63.0 3.3 copy-start.6
  63.0 70.5 %slice-start = ((s8[6291456]{0:T(1024)(128)(4,1)}), s8[4194304]{0:T(1024)(128)(4,1)S(1)}, s32[]{:S(2)}) async-start(s8[6291456]{0:T(1024)(128)(4,1)} %bitcast.273), calls=%async_computation.1 | async-start | bytes 8388608
  66.3 67.3 %copy-start.1 = (f32[1024,768]{0,1:T(8,128)}, f32[1024,768]{0,1:T(8,128)S(1)}, u32[]{:S(2)}) copy-start(f32[1024,768]{0,1:T(8,128)S(1)} %pad_maximum_fusion.1) | copy-start | bytes 9437188
  66.3 67.3 %slice-start.1 = ((s8[6291456]{0:T(1024)(128)(4,1)}), s8[2097152]{0:T(1024)(128)(4,1)S(1)}, s32[]{:S(2)}) async-start(s8[6291456]{0:T(1024)(128)(4,1)} %bitcast.273), calls=%async_computation.2 | async-start | bytes 4194304
  125.0 4.1 %collective-permute-start.7 = (f32[2,1024]{1,0:T(2,128)S(1)}, f32[2,1024]{1,0:T(2,128)S(1)}, u32[]{:S(2)}, u32[]{:S(2)}) collective-permute-start(f32[2,1024]{1,0:T(2,128)S(1)} %pad_maximum_fusion.6), channel_id=1, source_target_pairs={{0,64},{64,0},{1,65},{65,1},{2,66},{66,2},{3,67},{67,3},{4,68},{68... | collective-permute-start | bytes 24584 | tf_op jit(solution)/shard_map/ppermute | solution.py:32
  129.2 2.9 collective-permute-start.8
  132.1 42.9 %collective-permute-start.9 = (f32[2,1024]{1,0:T(2,128)S(1)}, f32[2,1024]{1,0:T(2,128)S(1)}, u32[]{:S(2)}, u32[]{:S(2)}) collective-permute-start(f32[2,1024]{1,0:T(2,128)S(1)} %pad_maximum_fusion.8), channel_id=1, source_target_pairs={{0,32},{16,48},{32,0},{48,16},{1,33},{17,49},{33,1},{49,17},{2,34}... | collective-permute-start | bytes 24584 | tf_op jit(solution)/shard_map/ppermute | solution.py:32
  175.6 19.8 %copy-start.2 = (f32[1024,768]{0,1:T(8,128)S(1)}, f32[1024,768]{0,1:T(8,128)}, u32[]{:S(2)}) copy-start(f32[1024,768]{0,1:T(8,128)} %copy-done.1) | copy-start | bytes 9437188
  180.0 5.6 %collective-permute-start.10 = (f32[2,2048]{1,0:T(2,128)S(1)}, f32[2,2048]{1,0:T(2,128)S(1)}, u32[]{:S(2)}, u32[]{:S(2)}) collective-permute-start(f32[2,2048]{1,0:T(2,128)S(1)} %pad_maximum_fusion.2), channel_id=1, source_target_pairs={{0,1},{1,0},{2,3},{3,2},{4,5},{5,4},{6,7},{7,6},{8,9},{9,8},{10,11... | collective-permute-start | bytes 49160 | tf_op jit(solution)/shard_map/ppermute | solution.py:32
  185.7 2.7 collective-permute-start.11
  188.4 2.7 collective-permute-start.12
  191.2 4.2 %collective-permute-start.13 = (f32[2,2048]{1,0:T(2,128)S(1)}, f32[2,2048]{1,0:T(2,128)S(1)}, u32[]{:S(2)}, u32[]{:S(2)}) collective-permute-start(f32[2,2048]{1,0:T(2,128)S(1)} %pad_maximum_fusion.5), channel_id=1, source_target_pairs={{0,8},{4,12},{8,0},{12,4},{1,9},{5,13},{9,1},{13,5},{2,10},{6,14},... | collective-permute-start | bytes 49160 | tf_op jit(solution)/shard_map/ppermute | solution.py:32
  217.1 2.4 copy-start
  217.1 6.2 %copy-start.3 = (f32[1024,768]{0,1:T(8,128)S(1)}, f32[1024,768]{0,1:T(8,128)}, u32[]{:S(2)}) copy-start(f32[1024,768]{0,1:T(8,128)} %copy-done.1) | copy-start | bytes 9437188
  219.5 30.4 %collective-permute-start.14 = (f32[512,768]{1,0:T(8,128)}, f32[512,768]{1,0:T(8,128)}, u32[]{:S(2)}, u32[]{:S(2)}) collective-permute-start(f32[512,768]{1,0:T(8,128)} %dynamic-slice_bitcast_fusion.1), channel_id=1, source_target_pairs={{0,1},{1,0},{2,3},{3,2},{4,5},{5,4},{6,7},{7,6},{8,9},{9,8},{10,11... | collective-permute-start | bytes 4718600 | tf_op jit(solution)/shard_map/ppermute | solution.py:55
  246.3 8.4 %collective-permute-start.30 = (f32[512,768]{1,0:T(8,128)}, f32[512,768]{1,0:T(8,128)}, u32[]{:S(2)}, u32[]{:S(2)}) collective-permute-start(f32[512,768]{1,0:T(8,128)} %dynamic-slice_bitcast_fusion), channel_id=1, source_target_pairs={{0,1},{1,0},{2,3},{3,2},{4,5},{5,4},{6,7},{7,6},{8,9},{9,8},{10,11... | collective-permute-start | bytes 4718600 | tf_op jit(solution)/shard_map/ppermute | solution.py:55
  252.1 7.4 %collective-permute-start.18 = (f32[64,768]{1,0:T(8,128)S(1)}, f32[64,768]{1,0:T(8,128)S(1)}, u32[]{:S(2)}, u32[]{:S(2)}) collective-permute-start(f32[64,768]{1,0:T(8,128)S(1)} %dynamic-slice_bitcast_fusion.4), channel_id=1, source_target_pairs={{0,12},{4,0},{8,4},{12,8},{1,13},{5,1},{9,5},{13,9},{2,14},{6,2},{... | collective-permute-start | bytes 589832 | tf_op jit(solution)/shard_map/ppermute | solution.py:60
  254.6 7.8 %collective-permute-start.15 = (f32[64,768]{1,0:T(8,128)S(1)}, f32[64,768]{1,0:T(8,128)S(1)}, u32[]{:S(2)}, u32[]{:S(2)}) collective-permute-start(f32[64,768]{1,0:T(8,128)S(1)} %dynamic-slice_bitcast_fusion.5), channel_id=1, source_target_pairs={{0,4},{4,8},{8,12},{12,0},{1,5},{5,9},{9,13},{13,1},{2,6},{6,10},{... | collective-permute-start | bytes 589832 | tf_op jit(solution)/shard_map/ppermute | solution.py:59
  256.5 6.6 %collective-permute-start.34 = (f32[64,768]{1,0:T(8,128)S(1)}, f32[64,768]{1,0:T(8,128)S(1)}, u32[]{:S(2)}, u32[]{:S(2)}) collective-permute-start(f32[64,768]{1,0:T(8,128)S(1)} %dynamic-slice_bitcast_fusion.2), channel_id=1, source_target_pairs={{0,12},{4,0},{8,4},{12,8},{1,13},{5,1},{9,5},{13,9},{2,14},{6,2},{... | collective-permute-start | bytes 589832 | tf_op jit(solution)/shard_map/ppermute | solution.py:60
  259.4 7.2 %collective-permute-start.31 = (f32[64,768]{1,0:T(8,128)S(1)}, f32[64,768]{1,0:T(8,128)S(1)}, u32[]{:S(2)}, u32[]{:S(2)}) collective-permute-start(f32[64,768]{1,0:T(8,128)S(1)} %dynamic-slice_bitcast_fusion.3), channel_id=1, source_target_pairs={{0,4},{4,8},{8,12},{12,0},{1,5},{5,9},{9,13},{13,1},{2,6},{6,10},{... | collective-permute-start | bytes 589832 | tf_op jit(solution)/shard_map/ppermute | solution.py:59
  259.6 7.8 %collective-permute-start.19 = (f32[64,768]{1,0:T(8,128)S(1)}, f32[64,768]{1,0:T(8,128)S(1)}, u32[]{:S(2)}, u32[]{:S(2)}) collective-permute-start(f32[64,768]{1,0:T(8,128)S(1)} %bitcast_add_fusion.10), channel_id=1, source_target_pairs={{0,12},{4,0},{8,4},{12,8},{1,13},{5,1},{9,5},{13,9},{2,14},{6,2},{... | collective-permute-start | bytes 589832 | tf_op jit(solution)/shard_map/ppermute | solution.py:60
  262.5 8.3 %collective-permute-start.16 = (f32[64,768]{1,0:T(8,128)S(1)}, f32[64,768]{1,0:T(8,128)S(1)}, u32[]{:S(2)}, u32[]{:S(2)}) collective-permute-start(f32[64,768]{1,0:T(8,128)S(1)} %bitcast_add_fusion.13), channel_id=1, source_target_pairs={{0,4},{4,8},{8,12},{12,0},{1,5},{5,9},{9,13},{13,1},{2,6},{6,10},{... | collective-permute-start | bytes 589832 | tf_op jit(solution)/shard_map/ppermute | solution.py:59
  263.1 8.0 %collective-permute-start.35 = (f32[64,768]{1,0:T(8,128)S(1)}, f32[64,768]{1,0:T(8,128)S(1)}, u32[]{:S(2)}, u32[]{:S(2)}) collective-permute-start(f32[64,768]{1,0:T(8,128)S(1)} %bitcast_add_fusion.4), channel_id=1, source_target_pairs={{0,12},{4,0},{8,4},{12,8},{1,13},{5,1},{9,5},{13,9},{2,14},{6,2},{... | collective-permute-start | bytes 589832 | tf_op jit(solution)/shard_map/ppermute | solution.py:60
  266.7 7.7 %collective-permute-start.32 = (f32[64,768]{1,0:T(8,128)S(1)}, f32[64,768]{1,0:T(8,128)S(1)}, u32[]{:S(2)}, u32[]{:S(2)}) collective-permute-start(f32[64,768]{1,0:T(8,128)S(1)} %bitcast_add_fusion.7), channel_id=1, source_target_pairs={{0,4},{4,8},{8,12},{12,0},{1,5},{5,9},{9,13},{13,1},{2,6},{6,10},{... | collective-permute-start | bytes 589832 | tf_op jit(solution)/shard_map/ppermute | solution.py:59
  267.4 8.0 %collective-permute-start.20 = (f32[64,768]{1,0:T(8,128)S(1)}, f32[64,768]{1,0:T(8,128)S(1)}, u32[]{:S(2)}, u32[]{:S(2)}) collective-permute-start(f32[64,768]{1,0:T(8,128)S(1)} %bitcast_add_fusion.9), channel_id=1, source_target_pairs={{0,12},{4,0},{8,4},{12,8},{1,13},{5,1},{9,5},{13,9},{2,14},{6,2},{... | collective-permute-start | bytes 589832 | tf_op jit(solution)/shard_map/ppermute | solution.py:60
  270.9 7.4 %collective-permute-start.17 = (f32[64,768]{1,0:T(8,128)S(1)}, f32[64,768]{1,0:T(8,128)S(1)}, u32[]{:S(2)}, u32[]{:S(2)}) collective-permute-start(f32[64,768]{1,0:T(8,128)S(1)} %bitcast_add_fusion.12), channel_id=1, source_target_pairs={{0,4},{4,8},{8,12},{12,0},{1,5},{5,9},{9,13},{13,1},{2,6},{6,10},{... | collective-permute-start | bytes 589832 | tf_op jit(solution)/shard_map/ppermute | solution.py:59
  271.2 8.2 %collective-permute-start.36 = (f32[64,768]{1,0:T(8,128)S(1)}, f32[64,768]{1,0:T(8,128)S(1)}, u32[]{:S(2)}, u32[]{:S(2)}) collective-permute-start(f32[64,768]{1,0:T(8,128)S(1)} %bitcast_add_fusion.3), channel_id=1, source_target_pairs={{0,12},{4,0},{8,4},{12,8},{1,13},{5,1},{9,5},{13,9},{2,14},{6,2},{... | collective-permute-start | bytes 589832 | tf_op jit(solution)/shard_map/ppermute | solution.py:60
  274.4 7.8 %collective-permute-start.33 = (f32[64,768]{1,0:T(8,128)S(1)}, f32[64,768]{1,0:T(8,128)S(1)}, u32[]{:S(2)}, u32[]{:S(2)}) collective-permute-start(f32[64,768]{1,0:T(8,128)S(1)} %bitcast_add_fusion.6), channel_id=1, source_target_pairs={{0,4},{4,8},{8,12},{12,0},{1,5},{5,9},{9,13},{13,1},{2,6},{6,10},{... | collective-permute-start | bytes 589832 | tf_op jit(solution)/shard_map/ppermute | solution.py:59
  278.3 4.9 %collective-permute-start.21 = (f32[64,768]{1,0:T(8,128)S(1)}, f32[64,768]{1,0:T(8,128)S(1)}, u32[]{:S(2)}, u32[]{:S(2)}) collective-permute-start(f32[64,768]{1,0:T(8,128)S(1)} %fusion.23), channel_id=1, source_target_pairs={{0,2},{2,0},{1,3},{3,1},{4,6},{6,4},{5,7},{7,5},{8,10},{10,8},{9,1... | collective-permute-start | bytes 589832 | tf_op jit(solution)/shard_map/ppermute | solution.py:62
  282.3 6.2 %collective-permute-start.37 = (f32[64,768]{1,0:T(8,128)S(1)}, f32[64,768]{1,0:T(8,128)S(1)}, u32[]{:S(2)}, u32[]{:S(2)}) collective-permute-start(f32[64,768]{1,0:T(8,128)S(1)} %fusion.17), channel_id=1, source_target_pairs={{0,2},{2,0},{1,3},{3,1},{4,6},{6,4},{5,7},{7,5},{8,10},{10,8},{9,1... | collective-permute-start | bytes 589832 | tf_op jit(solution)/shard_map/ppermute | solution.py:62
  283.3 9.4 %collective-permute-start.22 = (f32[64,768]{1,0:T(8,128)S(1)}, f32[64,768]{1,0:T(8,128)S(1)}, u32[]{:S(2)}, u32[]{:S(2)}) collective-permute-start(f32[64,768]{1,0:T(8,128)S(1)} %fusion.27), channel_id=1, source_target_pairs={{0,2},{2,0},{1,3},{3,1},{4,6},{6,4},{5,7},{7,5},{8,10},{10,8},{9,1... | collective-permute-start | bytes 589832 | tf_op jit(solution)/shard_map/ppermute | solution.py:65
  288.5 8.3 %collective-permute-start.38 = (f32[64,768]{1,0:T(8,128)S(1)}, f32[64,768]{1,0:T(8,128)S(1)}, u32[]{:S(2)}, u32[]{:S(2)}) collective-permute-start(f32[64,768]{1,0:T(8,128)S(1)} %fusion.21), channel_id=1, source_target_pairs={{0,2},{2,0},{1,3},{3,1},{4,6},{6,4},{5,7},{7,5},{8,10},{10,8},{9,1... | collective-permute-start | bytes 589832 | tf_op jit(solution)/shard_map/ppermute | solution.py:65
  292.7 8.6 %collective-permute-start.23 = (f32[64,768]{1,0:T(8,128)S(1)}, f32[64,768]{1,0:T(8,128)S(1)}, u32[]{:S(2)}, u32[]{:S(2)}) collective-permute-start(f32[64,768]{1,0:T(8,128)S(1)} %get-tuple-element.286), channel_id=1, source_target_pairs={{0,4},{4,8},{8,12},{12,0},{1,5},{5,9},{9,13},{13,1},{2,6},{6,10},{... | collective-permute-start | bytes 589832 | tf_op jit(solution)/shard_map/ppermute | solution.py:70
  292.8 8.6 %collective-permute-start.24 = (f32[64,768]{1,0:T(8,128)S(1)}, f32[64,768]{1,0:T(8,128)S(1)}, u32[]{:S(2)}, u32[]{:S(2)}) collective-permute-start(f32[64,768]{1,0:T(8,128)S(1)} %get-tuple-element.285), channel_id=1, source_target_pairs={{0,12},{4,0},{8,4},{12,8},{1,13},{5,1},{9,5},{13,9},{2,14},{6,2},{... | collective-permute-start | bytes 589832 | tf_op jit(solution)/shard_map/ppermute | solution.py:71
  297.0 7.1 %collective-permute-start.39 = (f32[64,768]{1,0:T(8,128)S(1)}, f32[64,768]{1,0:T(8,128)S(1)}, u32[]{:S(2)}, u32[]{:S(2)}) collective-permute-start(f32[64,768]{1,0:T(8,128)S(1)} %get-tuple-element.288), channel_id=1, source_target_pairs={{0,4},{4,8},{8,12},{12,0},{1,5},{5,9},{9,13},{13,1},{2,6},{6,10},{... | collective-permute-start | bytes 589832 | tf_op jit(solution)/shard_map/ppermute | solution.py:70
  297.0 8.3 %collective-permute-start.40 = (f32[64,768]{1,0:T(8,128)S(1)}, f32[64,768]{1,0:T(8,128)S(1)}, u32[]{:S(2)}, u32[]{:S(2)}) collective-permute-start(f32[64,768]{1,0:T(8,128)S(1)} %get-tuple-element.287), channel_id=1, source_target_pairs={{0,12},{4,0},{8,4},{12,8},{1,13},{5,1},{9,5},{13,9},{2,14},{6,2},{... | collective-permute-start | bytes 589832 | tf_op jit(solution)/shard_map/ppermute | solution.py:71
  301.3 8.2 %collective-permute-start.25 = (f32[64,768]{1,0:T(8,128)S(1)}, f32[64,768]{1,0:T(8,128)S(1)}, u32[]{:S(2)}, u32[]{:S(2)}) collective-permute-start(f32[64,768]{1,0:T(8,128)S(1)} %collective-permute-done.23), channel_id=1, source_target_pairs={{0,4},{4,8},{8,12},{12,0},{1,5},{5,9},{9,13},{13,1},{2,6},{6,10},{... | collective-permute-start | bytes 589832 | tf_op jit(solution)/shard_map/ppermute | solution.py:70
  301.4 8.2 %collective-permute-start.26 = (f32[64,768]{1,0:T(8,128)S(1)}, f32[64,768]{1,0:T(8,128)S(1)}, u32[]{:S(2)}, u32[]{:S(2)}) collective-permute-start(f32[64,768]{1,0:T(8,128)S(1)} %collective-permute-done.24), channel_id=1, source_target_pairs={{0,12},{4,0},{8,4},{12,8},{1,13},{5,1},{9,5},{13,9},{2,14},{6,2},{... | collective-permute-start | bytes 589832 | tf_op jit(solution)/shard_map/ppermute | solution.py:71
  304.1 8.2 %collective-permute-start.41 = (f32[64,768]{1,0:T(8,128)S(1)}, f32[64,768]{1,0:T(8,128)S(1)}, u32[]{:S(2)}, u32[]{:S(2)}) collective-permute-start(f32[64,768]{1,0:T(8,128)S(1)} %collective-permute-done.39), channel_id=1, source_target_pairs={{0,4},{4,8},{8,12},{12,0},{1,5},{5,9},{9,13},{13,1},{2,6},{6,10},{... | collective-permute-start | bytes 589832 | tf_op jit(solution)/shard_map/ppermute | solution.py:70
  305.4 8.3 %collective-permute-start.42 = (f32[64,768]{1,0:T(8,128)S(1)}, f32[64,768]{1,0:T(8,128)S(1)}, u32[]{:S(2)}, u32[]{:S(2)}) collective-permute-start(f32[64,768]{1,0:T(8,128)S(1)} %collective-permute-done.40), channel_id=1, source_target_pairs={{0,12},{4,0},{8,4},{12,8},{1,13},{5,1},{9,5},{13,9},{2,14},{6,2},{... | collective-permute-start | bytes 589832 | tf_op jit(solution)/shard_map/ppermute | solution.py:71
  309.5 8.1 %collective-permute-start.27 = (f32[64,768]{1,0:T(8,128)S(1)}, f32[64,768]{1,0:T(8,128)S(1)}, u32[]{:S(2)}, u32[]{:S(2)}) collective-permute-start(f32[64,768]{1,0:T(8,128)S(1)} %collective-permute-done.25), channel_id=1, source_target_pairs={{0,4},{4,8},{8,12},{12,0},{1,5},{5,9},{9,13},{13,1},{2,6},{6,10},{... | collective-permute-start | bytes 589832 | tf_op jit(solution)/shard_map/ppermute | solution.py:70
  309.6 8.7 %collective-permute-start.28 = (f32[64,768]{1,0:T(8,128)S(1)}, f32[64,768]{1,0:T(8,128)S(1)}, u32[]{:S(2)}, u32[]{:S(2)}) collective-permute-start(f32[64,768]{1,0:T(8,128)S(1)} %collective-permute-done.26), channel_id=1, source_target_pairs={{0,12},{4,0},{8,4},{12,8},{1,13},{5,1},{9,5},{13,9},{2,14},{6,2},{... | collective-permute-start | bytes 589832 | tf_op jit(solution)/shard_map/ppermute | solution.py:71
  312.2 14.9 %collective-permute-start.43 = (f32[64,768]{1,0:T(8,128)S(1)}, f32[64,768]{1,0:T(8,128)S(1)}, u32[]{:S(2)}, u32[]{:S(2)}) collective-permute-start(f32[64,768]{1,0:T(8,128)S(1)} %collective-permute-done.41), channel_id=1, source_target_pairs={{0,4},{4,8},{8,12},{12,0},{1,5},{5,9},{9,13},{13,1},{2,6},{6,10},{... | collective-permute-start | bytes 589832 | tf_op jit(solution)/shard_map/ppermute | solution.py:70
  313.7 14.2 %collective-permute-start.44 = (f32[64,768]{1,0:T(8,128)S(1)}, f32[64,768]{1,0:T(8,128)S(1)}, u32[]{:S(2)}, u32[]{:S(2)}) collective-permute-start(f32[64,768]{1,0:T(8,128)S(1)} %collective-permute-done.42), channel_id=1, source_target_pairs={{0,12},{4,0},{8,4},{12,8},{1,13},{5,1},{9,5},{13,9},{2,14},{6,2},{... | collective-permute-start | bytes 589832 | tf_op jit(solution)/shard_map/ppermute | solution.py:71
  318.9 11.4 %collective-permute-start.29 = (f32[512,768]{1,0:T(8,128)S(1)}, f32[512,768]{1,0:T(8,128)}, u32[]{:S(2)}, u32[]{:S(2)}) collective-permute-start(f32[512,768]{1,0:T(8,128)S(1)} %bitcast.237), channel_id=1, source_target_pairs={{0,1},{1,0},{2,3},{3,2},{4,5},{5,4},{6,7},{7,6},{8,9},{9,8},{10,11... | collective-permute-start | bytes 4718600 | tf_op jit(solution)/shard_map/ppermute | solution.py:75
  328.4 4.2 %collective-permute-start.45 = (f32[512,768]{1,0:T(8,128)S(1)}, f32[512,768]{1,0:T(8,128)}, u32[]{:S(2)}, u32[]{:S(2)}) collective-permute-start(f32[512,768]{1,0:T(8,128)S(1)} %bitcast.234), channel_id=1, source_target_pairs={{0,1},{1,0},{2,3},{3,2},{4,5},{5,4},{6,7},{7,6},{8,9},{9,8},{10,11... | collective-permute-start | bytes 4718600 | tf_op jit(solution)/shard_map/ppermute | solution.py:75
Sparse Core Ops, SparseCore 0:
  9.7 53.3 all-gather.1

commit v3 on v2

--- a/solution.py
+++ b/solution.py
@@ -1,6 +1,7 @@
 import jax
 import jax.numpy as jnp
 from jax import lax
+from jax.experimental.layout import Layout, with_layout_constraint
 from jax.sharding import Mesh
 from jax.sharding import PartitionSpec as P
 
@@ -11,18 +12,23 @@
 
 
 def similar(query_factor, target_factor):
-    return exponent_divisor * lax.dot_general(
+    product = lax.dot_general(
         query_factor,
         target_factor,
+        (((1,), (0,)), ((), ())),
+        precision=lax.Precision.HIGHEST,
+        preferred_element_type=jnp.float32,
+    )
+    return exponent_divisor * with_layout_constraint(product, Layout((0, 1)))
+
+
+def rescaled_affinity(weights, features):
+    return lax.dot_general(
+        weights,
+        features,
         (((1,), (1,)), ((), ())),
         precision=lax.Precision.HIGHEST,
         preferred_element_type=jnp.float32,
-    )
-
-
-def rescaled_affinity(weights, features):
-    return jnp.dot(
-        weights, features, precision=lax.Precision.HIGHEST, preferred_element_type=jnp.float32
     )
 
 
@@ -79,21 +85,17 @@
 def gather_features(captions, sizes):
     y_size = sizes["y"]
     rows, width = captions.shape
-    half = rows // 2
-    offloaded = lax.all_gather(captions[:half], IMG, axis=1, tiled=True)
-    mine = captions[half:]
     h, y = lax.axis_index("zh"), lax.axis_index("y")
-    other = lax.ppermute(mine, "zh", [(0, 1), (1, 0)])
-    pair = jnp.where(h == 0, jnp.stack([mine, other]), jnp.stack([other, mine]))
-    got = jnp.zeros((y_size, 2, half, width), captions.dtype).at[y].set(pair)
+    other = lax.ppermute(captions, "zh", [(0, 1), (1, 0)])
+    pair = jnp.where(h == 0, jnp.stack([captions, other]), jnp.stack([other, captions]))
+    got = jnp.zeros((y_size, 2, rows, width), captions.dtype).at[y].set(pair)
     right, left = pair[0], pair[1]
     for s in range(y_size - 1):
         right = lax.ppermute(right, "y", ring("y", y_size, 1))
         left = lax.ppermute(left, "y", ring("y", y_size, -1))
         got = got.at[(y - s - 1) % y_size, 0].set(right)
         got = got.at[(y + s + 1) % y_size, 1].set(left)
-    ringed = got.transpose(2, 1, 0, 3).reshape(half, 2 * y_size * width)
-    return lax.optimization_barrier(jnp.concatenate([offloaded, ringed], axis=0))
+    return got.transpose(1, 0, 3, 2).reshape(2 * y_size * width, rows)
 
 
 def local(images, captions, bank, sizes):

time: 349 us -> 250 us (0.72)
  matrix products: 142 us -> 67.2 us
  waiting for transfers between devices: 65.5 us -> 51.5 us
  between operations: 14.4 us -> 0.93 us
    dot_general x4, matrix products: 142 us -> 67.2 us  [the longest x2 44.7 us: similar(): lax.dot_general(query_factor, target_factor, (((1,), (0,)), ((), ())), pr...]
    all_gather x1 -> x0, waiting for transfers between devices: 24.5 us -> none  [gather_features(): offloaded = lax.all_gather(captions[:half], IMG, axis=1, tiled=True)]
    ppermute x3, waiting for transfers between devices: 6.45 us -> 12.1 us  [gather_features(): right = lax.ppermute(right, 'y', ring('y', y_size, 1))]
    ppermute x1, waiting for transfers between devices: 2.35 us -> 7.65 us  [gather_features(): other = lax.ppermute(captions, 'zh', [(0, 1), (1, 0)])]
  transfers between devices with their start and end apart: 47 -> 46, of which waited for: 23 -> 22; matrix products, arithmetic and copies ran while one was open for 26% -> 25% of each run, Pallas kernels for 0% -> 0%
where the time goes in v3:
time: 250 us; the launch traced here: 246 us
  starting transfers between devices  77.7 us (31%)
  matrix products  67.2 us (27%)
  waiting for transfers between devices  51.5 us (21%)
  other arithmetic  42 us (17%)
  local copies, waits for them, and re-layouts  7.05 us (3%)
    dot_general x2, matrix products, similar(): lax.dot_general(query_factor, target_factor, (((1,), (0,)), ((), ())), pr...  44.7 us
    dot_general x2, matrix products, rescaled_affinity(): lax.dot_general(weights, features, (((1,), (1,)), ((), ())), precision=la...  22.6 us
    ppermute x6, starting transfers between devices, reduce_rows(): lax.ppermute(left, 'x', ring('x', x_size, -1))  18.5 us
    ppermute x6, starting transfers between devices, reduce_rows(): left = lax.ppermute(left, 'x', ring('x', x_size, -1))  16.1 us
    ppermute x7, starting transfers between devices, merge_peaks(): other = lax.ppermute(pair, axis, [(j, j ^ dist) for j in range(size)])  15 us
    ppermute x3, waiting for transfers between devices, gather_features(): right = lax.ppermute(right, 'y', ring('y', y_size, 1))  12.1 us
    ppermute x7, waiting for transfers between devices, merge_peaks(): other = lax.ppermute(pair, axis, [(j, j ^ dist) for j in range(size)])  11 us
    ppermute x2, starting transfers between devices, reduce_rows(): other = lax.ppermute(held, 'core', swap)  8.37 us
  transfers between devices with their start and end apart: 46, of which 22 were waited for; matrix products, arithmetic and copies ran while one was open for 25% of the time, Pallas kernels for 0%

profile of v3, /device:TPU:1, one launch (start us, length us, event | category | flops | bytes accessed | tf_op | source)
XLA Modules:
  0.0 246.4 jit_solution(3793897854555590797)
XLA Ops:
  0.0 4.4 %collective-permute-start = (f32[1024,96]{0,1:T(8,128)}, f32[1024,96]{0,1:T(8,128)S(1)}, u32[]{:S(2)}, u32[]{:S(2)}) collective-permute-start(f32[1024,96]{0,1:T(8,128)} %param.46), channel_id=1, source_target_pairs={{0,64},{64,0},{1,65},{65,1},{2,66},{66,2},{3,67},{67,3},{4,68},{68... | collective-permute-start | bytes 1179656 | tf_op jit(solution)/shard_map/ppermute | solution.py:89
  4.4 1.4 and_reduce_fusion.10
  5.8 7.6 %collective-permute-done = f32[1024,96]{0,1:T(8,128)S(1)} collective-permute-done((f32[1024,96]{0,1:T(8,128)}, f32[1024,96]{0,1:T(8,128)S(1)}, u32[]{:S(2)}, u32[]{:S(2)}) %collective-permute-start) | collective-permute-done | bytes 393248 | tf_op jit(solution)/shard_map/ppermute | solution.py:89
  13.5 1.4 maximum_select_fusion.3
  14.8 1.0 slice_bitcast_fusion
  15.9 1.3 collective-permute-start.1
  17.2 1.4 collective-permute-start.2
  22.7 4.2 %collective-permute-done.1 = f32[1024,96]{0,1:T(8,128)} collective-permute-done((f32[1024,96]{0,1:T(8,128)}, f32[1024,96]{0,1:T(8,128)}, u32[]{:S(2)}, u32[]{:S(2)}) %collective-permute-start.1) | collective-permute-done | bytes 393248 | tf_op jit(solution)/shard_map/ppermute | solution.py:94
  26.9 2.7 %collective-permute-start.4 = (f32[1024,96]{0,1:T(8,128)}, f32[1024,96]{0,1:T(8,128)S(1)}, u32[]{:S(2)}, u32[]{:S(2)}) collective-permute-start(f32[1024,96]{0,1:T(8,128)} %collective-permute-done.2), channel_id=1, source_target_pairs={{0,48},{16,0},{32,16},{48,32},{1,49},{17,1},{33,17},{49,33},{2,50}... | collective-permute-start | bytes 1179656 | tf_op jit(solution)/shard_map/ppermute | solution.py:95
  29.6 1.9 fusion.22
  31.5 1.7 fusion.21
  33.2 3.6 %collective-permute-done.3 = f32[1024,96]{0,1:T(8,128)S(1)} collective-permute-done((f32[1024,96]{0,1:T(8,128)}, f32[1024,96]{0,1:T(8,128)S(1)}, u32[]{:S(2)}, u32[]{:S(2)}) %collective-permute-start.3) | collective-permute-done | bytes 393248 | tf_op jit(solution)/shard_map/ppermute | solution.py:94
  36.8 3.1 %collective-permute-start.6 = (f32[1024,96]{0,1:T(8,128)S(1)}, f32[1024,96]{0,1:T(8,128)S(1)}, u32[]{:S(2)}, u32[]{:S(2)}) collective-permute-start(f32[1024,96]{0,1:T(8,128)S(1)} %collective-permute-done.4), channel_id=1, source_target_pairs={{0,48},{16,0},{32,16},{48,32},{1,49},{17,1},{33,17},{49,33},{2,50}... | collective-permute-start | bytes 1179656 | tf_op jit(solution)/shard_map/ppermute | solution.py:95
  41.4 4.2 %collective-permute-done.5 = f32[1024,96]{0,1:T(8,128)S(1)} collective-permute-done((f32[1024,96]{0,1:T(8,128)S(1)}, f32[1024,96]{0,1:T(8,128)S(1)}, u32[]{:S(2)}, u32[]{:S(2)}) %collective-permute-start.5) | collective-permute-done | bytes 393248 | tf_op jit(solution)/shard_map/ppermute | solution.py:94
  46.4 0.9 fusion.17
  47.3 22.5 %fusion = (f32[1024]{0:T(1024)S(1)}, f32[1024,2048]{0,1:T(8,128)S(1)}) fusion(f32[768,1024]{1,0:T(8,128)S(1)} %bitcast.236, f32[2048,768]{1,0:T(8,128)S(1)} %copy-done.10), kind=kOutput, calls=%fused_computation.4 | convolution fusion | flops 19331547136 | bytes 17829888 | tf_op jit(solution)/shard_map/dot_general | solution.py:15
  69.8 1.4 exponential_reduce_fusion
  71.2 1.8 collective-permute-start.7
  73.0 2.3 collective-permute-done.7
  75.4 2.5 %collective-permute-done.8 = f32[2,1024]{1,0:T(2,128)S(1)} collective-permute-done((f32[2,1024]{1,0:T(2,128)S(1)}, f32[2,1024]{1,0:T(2,128)S(1)}, u32[]{:S(2)}, u32[]{:S(2)}) %collective-permute-start.8) | collective-permute-done | bytes 8224 | tf_op jit(solution)/shard_map/ppermute | solution.py:38
  78.0 2.6 %collective-permute-start.9 = (f32[2,1024]{1,0:T(2,128)S(1)}, f32[2,1024]{1,0:T(2,128)S(1)}, u32[]{:S(2)}, u32[]{:S(2)}) collective-permute-start(f32[2,1024]{1,0:T(2,128)S(1)} %pad_maximum_fusion.7), channel_id=1, source_target_pairs={{0,32},{16,48},{32,0},{48,16},{1,33},{17,49},{33,1},{49,17},{2,34}... | collective-permute-start | bytes 24584 | tf_op jit(solution)/shard_map/ppermute | solution.py:38
  80.6 22.2 %bitcast_multiply_fusion.1 = f32[2048,1024]{1,0:T(8,128)S(1)} fusion(f32[768,1024]{1,0:T(8,128)S(1)} %bitcast.237, f32[2048,768]{1,0:T(8,128)S(1)} %bitcast.283), kind=kOutput, calls=%fused_computation.1 | convolution fusion | flops 19329449984 | bytes 17825792 | tf_op jit(solution)/shard_map/dot_general | solution.py:15
  103.5 4.2 %fusion.59 = (f32[2048]{0:T(1024)S(1)}, f32[2048,1024]{1,0:T(8,128)}) fusion(f32[2048]{0:T(1024)S(1)} %subtract_reduce_fusion, f32[2048,1024]{1,0:T(8,128)S(1)} %bitcast_multiply_fusion.1, f32[1024]{0:T(1024)S(1)} %bitcast.273), kind=kLoop, calls=%fused_computation.200 | loop fusion | flops 6289408 | bytes 16797696 | tf_op jit(solution)/shard_map/reduce_sum | solution.py:116
  107.7 6.3 %collective-permute-start.10 = (f32[2,2048]{1,0:T(2,128)S(1)}, f32[2,2048]{1,0:T(2,128)S(1)}, u32[]{:S(2)}, u32[]{:S(2)}) collective-permute-start(f32[2,2048]{1,0:T(2,128)S(1)} %pad_maximum_fusion.1), channel_id=1, source_target_pairs={{0,1},{1,0},{2,3},{3,2},{4,5},{5,4},{6,7},{7,6},{8,9},{9,8},{10,11... | collective-permute-start | bytes 49160 | tf_op jit(solution)/shard_map/ppermute | solution.py:38
  113.9 0.8 collective-permute-done.10
  115.0 2.5 %collective-permute-done.11 = f32[2,2048]{1,0:T(2,128)S(1)} collective-permute-done((f32[2,2048]{1,0:T(2,128)S(1)}, f32[2,2048]{1,0:T(2,128)S(1)}, u32[]{:S(2)}, u32[]{:S(2)}) %collective-permute-start.11) | collective-permute-done | bytes 16416 | tf_op jit(solution)/shard_map/ppermute | solution.py:38
  117.6 1.3 collective-permute-start.12
  118.9 1.4 collective-permute-done.12
  120.3 2.8 %collective-permute-start.13 = (f32[2,2048]{1,0:T(2,128)S(1)}, f32[2,2048]{1,0:T(2,128)S(1)}, u32[]{:S(2)}, u32[]{:S(2)}) collective-permute-start(f32[2,2048]{1,0:T(2,128)S(1)} %pad_maximum_fusion.4), channel_id=1, source_target_pairs={{0,8},{4,12},{8,0},{12,4},{1,9},{5,13},{9,1},{13,5},{2,10},{6,14},... | collective-permute-start | bytes 49160 | tf_op jit(solution)/shard_map/ppermute | solution.py:38
  123.2 1.4 collective-permute-done.13
  124.7 12.4 %fusion.5 = f32[1024,768]{1,0:T(8,128)S(1)} fusion(f32[768,1024]{1,0:T(8,128)S(1)} %bitcast.238, f32[2048,1024]{1,0:T(8,128)} %get-tuple-element.276, f32[1024]{0:T(1024)S(1)} %get-tuple-element.305), kind=kOutput, calls=%fused_computation.13 | convolution fusion | flops 9664462848 | bytes 10489856 | tf_op jit(solution)/shard_map/dot_general | solution.py:26
  137.1 1.4 dynamic-slice_bitcast_fusion.1
  138.4 4.1 %collective-permute-start.14 = (f32[512,768]{1,0:T(8,128)}, f32[512,768]{1,0:T(8,128)}, u32[]{:S(2)}, u32[]{:S(2)}) collective-permute-start(f32[512,768]{1,0:T(8,128)} %dynamic-slice_bitcast_fusion.1), channel_id=1, source_target_pairs={{0,1},{1,0},{2,3},{3,2},{4,5},{5,4},{6,7},{7,6},{8,9},{9,8},{10,11... | collective-permute-start | bytes 4718600 | tf_op jit(solution)/shard_map/ppermute | solution.py:61
  142.5 10.2 %fusion.8 = f32[1024,768]{1,0:T(8,128)S(1)} fusion(f32[768,1024]{1,0:T(8,128)S(1)} %bitcast.239, f32[2048,1024]{1,0:T(8,128)S(1)} %copy-done, f32[1024]{0:T(1024)S(1)} %get-tuple-element.306), kind=kOutput, calls=%fused_computation.14 | convolution fusion | flops 9664462848 | bytes 10489856 | tf_op jit(solution)/shard_map/dot_general | solution.py:26
  152.8 1.6 copy-done.1
  154.4 1.3 dynamic-slice_bitcast_fusion
  156.0 0.8 and_reduce_fusion.4
  158.5 1.6 bitcast_add_fusion.1
  160.2 2.8 %collective-permute-start.18 = (f32[64,768]{1,0:T(8,128)S(1)}, f32[64,768]{1,0:T(8,128)S(1)}, u32[]{:S(2)}, u32[]{:S(2)}) collective-permute-start(f32[64,768]{1,0:T(8,128)S(1)} %dynamic-slice_bitcast_fusion.4), channel_id=1, source_target_pairs={{0,12},{4,0},{8,4},{12,8},{1,13},{5,1},{9,5},{13,9},{2,14},{6,2},{... | collective-permute-start | bytes 589832 | tf_op jit(solution)/shard_map/ppermute | solution.py:66
  163.2 1.6 bitcast_add_fusion
  164.9 2.7 %collective-permute-start.34 = (f32[64,768]{1,0:T(8,128)S(1)}, f32[64,768]{1,0:T(8,128)S(1)}, u32[]{:S(2)}, u32[]{:S(2)}) collective-permute-start(f32[64,768]{1,0:T(8,128)S(1)} %dynamic-slice_bitcast_fusion.2), channel_id=1, source_target_pairs={{0,12},{4,0},{8,4},{12,8},{1,13},{5,1},{9,5},{13,9},{2,14},{6,2},{... | collective-permute-start | bytes 589832 | tf_op jit(solution)/shard_map/ppermute | solution.py:66
  167.8 2.9 %collective-permute-start.19 = (f32[64,768]{1,0:T(8,128)S(1)}, f32[64,768]{1,0:T(8,128)S(1)}, u32[]{:S(2)}, u32[]{:S(2)}) collective-permute-start(f32[64,768]{1,0:T(8,128)S(1)} %bitcast_add_fusion.10), channel_id=1, source_target_pairs={{0,12},{4,0},{8,4},{12,8},{1,13},{5,1},{9,5},{13,9},{2,14},{6,2},{... | collective-permute-start | bytes 589832 | tf_op jit(solution)/shard_map/ppermute | solution.py:66
  171.2 3.5 %collective-permute-start.35 = (f32[64,768]{1,0:T(8,128)S(1)}, f32[64,768]{1,0:T(8,128)S(1)}, u32[]{:S(2)}, u32[]{:S(2)}) collective-permute-start(f32[64,768]{1,0:T(8,128)S(1)} %bitcast_add_fusion.4), channel_id=1, source_target_pairs={{0,12},{4,0},{8,4},{12,8},{1,13},{5,1},{9,5},{13,9},{2,14},{6,2},{... | collective-permute-start | bytes 589832 | tf_op jit(solution)/shard_map/ppermute | solution.py:66
  175.5 3.5 %collective-permute-start.20 = (f32[64,768]{1,0:T(8,128)S(1)}, f32[64,768]{1,0:T(8,128)S(1)}, u32[]{:S(2)}, u32[]{:S(2)}) collective-permute-start(f32[64,768]{1,0:T(8,128)S(1)} %bitcast_add_fusion.9), channel_id=1, source_target_pairs={{0,12},{4,0},{8,4},{12,8},{1,13},{5,1},{9,5},{13,9},{2,14},{6,2},{... | collective-permute-start | bytes 589832 | tf_op jit(solution)/shard_map/ppermute | solution.py:66
  179.3 3.1 %collective-permute-start.36 = (f32[64,768]{1,0:T(8,128)S(1)}, f32[64,768]{1,0:T(8,128)S(1)}, u32[]{:S(2)}, u32[]{:S(2)}) collective-permute-start(f32[64,768]{1,0:T(8,128)S(1)} %bitcast_add_fusion.3), channel_id=1, source_target_pairs={{0,12},{4,0},{8,4},{12,8},{1,13},{5,1},{9,5},{13,9},{2,14},{6,2},{... | collective-permute-start | bytes 589832 | tf_op jit(solution)/shard_map/ppermute | solution.py:66
  182.6 0.9 collective-permute-done.20
  183.5 2.6 %collective-permute-done.17 = f32[64,768]{1,0:T(8,128)S(1)} collective-permute-done((f32[64,768]{1,0:T(8,128)S(1)}, f32[64,768]{1,0:T(8,128)S(1)}, u32[]{:S(2)}, u32[]{:S(2)}) %collective-permute-start.17) | collective-permute-done | bytes 196640 | tf_op jit(solution)/shard_map/ppermute | solution.py:65
  186.3 1.2 collective-permute-done.36
  187.6 2.9 %collective-permute-done.33 = f32[64,768]{1,0:T(8,128)S(1)} collective-permute-done((f32[64,768]{1,0:T(8,128)S(1)}, f32[64,768]{1,0:T(8,128)S(1)}, u32[]{:S(2)}, u32[]{:S(2)}) %collective-permute-start.33) | collective-permute-done | bytes 196640 | tf_op jit(solution)/shard_map/ppermute | solution.py:65
  191.2 1.1 collective-permute-start.22
  192.3 4.4 %collective-permute-done.37 = f32[64,768]{1,0:T(8,128)S(1)} collective-permute-done((f32[64,768]{1,0:T(8,128)S(1)}, f32[64,768]{1,0:T(8,128)S(1)}, u32[]{:S(2)}, u32[]{:S(2)}) %collective-permute-start.37) | collective-permute-done | bytes 196640 | tf_op jit(solution)/shard_map/ppermute | solution.py:68
  197.0 4.0 %collective-permute-done.22 = f32[64,768]{1,0:T(8,128)S(1)} collective-permute-done((f32[64,768]{1,0:T(8,128)S(1)}, f32[64,768]{1,0:T(8,128)S(1)}, u32[]{:S(2)}, u32[]{:S(2)}) %collective-permute-start.22) | collective-permute-done | bytes 196640 | tf_op jit(solution)/shard_map/ppermute | solution.py:71
  201.1 2.7 %collective-permute-start.24 = (f32[64,768]{1,0:T(8,128)S(1)}, f32[64,768]{1,0:T(8,128)S(1)}, u32[]{:S(2)}, u32[]{:S(2)}) collective-permute-start(f32[64,768]{1,0:T(8,128)S(1)} %get-tuple-element.287), channel_id=1, source_target_pairs={{0,12},{4,0},{8,4},{12,8},{1,13},{5,1},{9,5},{13,9},{2,14},{6,2},{... | collective-permute-start | bytes 589832 | tf_op jit(solution)/shard_map/ppermute | solution.py:77
  203.8 1.4 collective-permute-done.38
  205.3 2.7 %collective-permute-start.40 = (f32[64,768]{1,0:T(8,128)S(1)}, f32[64,768]{1,0:T(8,128)S(1)}, u32[]{:S(2)}, u32[]{:S(2)}) collective-permute-start(f32[64,768]{1,0:T(8,128)S(1)} %get-tuple-element.289), channel_id=1, source_target_pairs={{0,12},{4,0},{8,4},{12,8},{1,13},{5,1},{9,5},{13,9},{2,14},{6,2},{... | collective-permute-start | bytes 589832 | tf_op jit(solution)/shard_map/ppermute | solution.py:77
  209.7 2.7 %collective-permute-start.26 = (f32[64,768]{1,0:T(8,128)S(1)}, f32[64,768]{1,0:T(8,128)S(1)}, u32[]{:S(2)}, u32[]{:S(2)}) collective-permute-start(f32[64,768]{1,0:T(8,128)S(1)} %collective-permute-done.24), channel_id=1, source_target_pairs={{0,12},{4,0},{8,4},{12,8},{1,13},{5,1},{9,5},{13,9},{2,14},{6,2},{... | collective-permute-start | bytes 589832 | tf_op jit(solution)/shard_map/ppermute | solution.py:77
  213.8 2.7 %collective-permute-start.42 = (f32[64,768]{1,0:T(8,128)S(1)}, f32[64,768]{1,0:T(8,128)S(1)}, u32[]{:S(2)}, u32[]{:S(2)}) collective-permute-start(f32[64,768]{1,0:T(8,128)S(1)} %collective-permute-done.40), channel_id=1, source_target_pairs={{0,12},{4,0},{8,4},{12,8},{1,13},{5,1},{9,5},{13,9},{2,14},{6,2},{... | collective-permute-start | bytes 589832 | tf_op jit(solution)/shard_map/ppermute | solution.py:77
  218.0 2.7 %collective-permute-start.28 = (f32[64,768]{1,0:T(8,128)S(1)}, f32[64,768]{1,0:T(8,128)S(1)}, u32[]{:S(2)}, u32[]{:S(2)}) collective-permute-start(f32[64,768]{1,0:T(8,128)S(1)} %collective-permute-done.26), channel_id=1, source_target_pairs={{0,12},{4,0},{8,4},{12,8},{1,13},{5,1},{9,5},{13,9},{2,14},{6,2},{... | collective-permute-start | bytes 589832 | tf_op jit(solution)/shard_map/ppermute | solution.py:77
  222.0 2.7 %collective-permute-start.44 = (f32[64,768]{1,0:T(8,128)S(1)}, f32[64,768]{1,0:T(8,128)S(1)}, u32[]{:S(2)}, u32[]{:S(2)}) collective-permute-start(f32[64,768]{1,0:T(8,128)S(1)} %collective-permute-done.42), channel_id=1, source_target_pairs={{0,12},{4,0},{8,4},{12,8},{1,13},{5,1},{9,5},{13,9},{2,14},{6,2},{... | collective-permute-start | bytes 589832 | tf_op jit(solution)/shard_map/ppermute | solution.py:77
  227.3 8.3 %collective-permute-start.29 = (f32[512,768]{1,0:T(8,128)S(1)}, f32[512,768]{1,0:T(8,128)}, u32[]{:S(2)}, u32[]{:S(2)}) collective-permute-start(f32[512,768]{1,0:T(8,128)S(1)} %bitcast.248), channel_id=1, source_target_pairs={{0,1},{1,0},{2,3},{3,2},{4,5},{5,4},{6,7},{7,6},{8,9},{9,8},{10,11... | collective-permute-start | bytes 4718600 | tf_op jit(solution)/shard_map/ppermute | solution.py:81
  237.0 1.7 collective-permute-done.29
  238.7 2.2 maximum_select_fusion
  241.0 2.2 maximum_select_fusion.1
  243.1 3.1 %pad_maximum_fusion = f32[2048,768]{1,0:T(8,128)} fusion(f32[1024,768]{1,0:T(8,128)S(1)} %bitcast.245, f32[1024,768]{1,0:T(8,128)S(1)} %bitcast.244), kind=kLoop, calls=%fused_computation.6 | loop fusion | flops 1572864 | bytes 12582912 | tf_op jit(solution)/shard_map/concatenate | solution.py:126
  (145 shorter events, 22.9 us)
Async XLA Ops:
  0.0 19.4 %copy-start.8 = (s32[4]{0:T(128)S(1)}, s32[4]{0:T(128)}, u32[]{:S(2)}) copy-start(s32[4]{0:T(128)} %constant.689.clone.1) | copy-start | bytes 52
  0.0 18.6 %copy-start.9 = (s32[4]{0:T(128)S(1)}, s32[4]{0:T(128)}, u32[]{:S(2)}) copy-start(s32[4]{0:T(128)} %constant.683.clone.1) | copy-start | bytes 52
  0.0 13.5 %collective-permute-start = (f32[1024,96]{0,1:T(8,128)}, f32[1024,96]{0,1:T(8,128)S(1)}, u32[]{:S(2)}, u32[]{:S(2)}) collective-permute-start(f32[1024,96]{0,1:T(8,128)} %param.46), channel_id=1, source_target_pairs={{0,64},{64,0},{1,65},{65,1},{2,66},{66,2},{3,67},{67,3},{4,68},{68... | collective-permute-start | bytes 1179656 | tf_op jit(solution)/shard_map/ppermute | solution.py:89
  13.5 7.5 %copy-start.6 = (f32[1024,96]{0,1:T(8,128)}, f32[1024,96]{0,1:T(8,128)S(1)}, u32[]{:S(2)}) copy-start(f32[1024,96]{0,1:T(8,128)S(1)} %collective-permute-done) | copy-start | bytes 1179652
  13.5 7.9 %copy-start.5 = (f32[1024,96]{0,1:T(8,128)S(1)}, f32[1024,96]{0,1:T(8,128)}, u32[]{:S(2)}) copy-start(f32[1024,96]{0,1:T(8,128)} %param.46) | copy-start | bytes 1179652
  15.9 11.0 %collective-permute-start.1 = (f32[1024,96]{0,1:T(8,128)}, f32[1024,96]{0,1:T(8,128)}, u32[]{:S(2)}, u32[]{:S(2)}) collective-permute-start(f32[1024,96]{0,1:T(8,128)} %get-tuple-element.286), channel_id=1, source_target_pairs={{0,16},{16,32},{32,48},{48,0},{1,17},{17,33},{33,49},{49,1},{2,18}... | collective-permute-start | bytes 1179656 | tf_op jit(solution)/shard_map/ppermute | solution.py:94
  17.2 9.7 %collective-permute-start.2 = (f32[1024,96]{0,1:T(8,128)}, f32[1024,96]{0,1:T(8,128)}, u32[]{:S(2)}, u32[]{:S(2)}) collective-permute-start(f32[1024,96]{0,1:T(8,128)} %get-tuple-element.285), channel_id=1, source_target_pairs={{0,48},{16,0},{32,16},{48,32},{1,49},{17,1},{33,17},{49,33},{2,50}... | collective-permute-start | bytes 1179656 | tf_op jit(solution)/shard_map/ppermute | solution.py:95
  21.0 1.0 copy-start.7
  26.9 9.9 %collective-permute-start.3 = (f32[1024,96]{0,1:T(8,128)}, f32[1024,96]{0,1:T(8,128)S(1)}, u32[]{:S(2)}, u32[]{:S(2)}) collective-permute-start(f32[1024,96]{0,1:T(8,128)} %collective-permute-done.1), channel_id=1, source_target_pairs={{0,16},{16,32},{32,48},{48,0},{1,17},{17,33},{33,49},{49,1},{2,18}... | collective-permute-start | bytes 1179656 | tf_op jit(solution)/shard_map/ppermute | solution.py:94
  26.9 9.9 %collective-permute-start.4 = (f32[1024,96]{0,1:T(8,128)}, f32[1024,96]{0,1:T(8,128)S(1)}, u32[]{:S(2)}, u32[]{:S(2)}) collective-permute-start(f32[1024,96]{0,1:T(8,128)} %collective-permute-done.2), channel_id=1, source_target_pairs={{0,48},{16,0},{32,16},{48,32},{1,49},{17,1},{33,17},{49,33},{2,50}... | collective-permute-start | bytes 1179656 | tf_op jit(solution)/shard_map/ppermute | solution.py:95
  29.6 17.7 %copy-start.10 = (f32[2048,768]{1,0:T(8,128)S(1)}, f32[2048,768]{1,0:T(8,128)}, u32[]{:S(2)}) copy-start(f32[2048,768]{1,0:T(8,128)} %param.47) | copy-start | bytes 18874372
  36.8 8.8 %collective-permute-start.5 = (f32[1024,96]{0,1:T(8,128)S(1)}, f32[1024,96]{0,1:T(8,128)S(1)}, u32[]{:S(2)}, u32[]{:S(2)}) collective-permute-start(f32[1024,96]{0,1:T(8,128)S(1)} %collective-permute-done.3), channel_id=1, source_target_pairs={{0,16},{16,32},{32,48},{48,0},{1,17},{17,33},{33,49},{49,1},{2,18}... | collective-permute-start | bytes 1179656 | tf_op jit(solution)/shard_map/ppermute | solution.py:94
  36.8 9.5 %collective-permute-start.6 = (f32[1024,96]{0,1:T(8,128)S(1)}, f32[1024,96]{0,1:T(8,128)S(1)}, u32[]{:S(2)}, u32[]{:S(2)}) collective-permute-start(f32[1024,96]{0,1:T(8,128)S(1)} %collective-permute-done.4), channel_id=1, source_target_pairs={{0,48},{16,0},{32,16},{48,32},{1,49},{17,1},{33,17},{49,33},{2,50}... | collective-permute-start | bytes 1179656 | tf_op jit(solution)/shard_map/ppermute | solution.py:95
  46.4 34.2 %slice-start = ((s8[6291456]{0:T(1024)(128)(4,1)}), s8[4194304]{0:T(1024)(128)(4,1)S(1)}, s32[]{:S(2)}) async-start(s8[6291456]{0:T(1024)(128)(4,1)} %bitcast.282), calls=%async_computation | async-start | bytes 8388608
  47.3 33.3 %slice-start.1 = ((s8[6291456]{0:T(1024)(128)(4,1)}), s8[2097152]{0:T(1024)(128)(4,1)S(1)}, s32[]{:S(2)}) async-start(s8[6291456]{0:T(1024)(128)(4,1)} %bitcast.282), calls=%async_computation.1 | async-start | bytes 4194304
  71.2 4.1 %collective-permute-start.7 = (f32[2,1024]{1,0:T(2,128)S(1)}, f32[2,1024]{1,0:T(2,128)S(1)}, u32[]{:S(2)}, u32[]{:S(2)}) collective-permute-start(f32[2,1024]{1,0:T(2,128)S(1)} %pad_maximum_fusion.5), channel_id=1, source_target_pairs={{0,64},{64,0},{1,65},{65,1},{2,66},{66,2},{3,67},{67,3},{4,68},{68... | collective-permute-start | bytes 24584 | tf_op jit(solution)/shard_map/ppermute | solution.py:38
  75.3 2.6 %collective-permute-start.8 = (f32[2,1024]{1,0:T(2,128)S(1)}, f32[2,1024]{1,0:T(2,128)S(1)}, u32[]{:S(2)}, u32[]{:S(2)}) collective-permute-start(f32[2,1024]{1,0:T(2,128)S(1)} %pad_maximum_fusion.6), channel_id=1, source_target_pairs={{0,16},{16,0},{32,48},{48,32},{1,17},{17,1},{33,49},{49,33},{2,18}... | collective-permute-start | bytes 24584 | tf_op jit(solution)/shard_map/ppermute | solution.py:38
  78.0 24.8 %collective-permute-start.9 = (f32[2,1024]{1,0:T(2,128)S(1)}, f32[2,1024]{1,0:T(2,128)S(1)}, u32[]{:S(2)}, u32[]{:S(2)}) collective-permute-start(f32[2,1024]{1,0:T(2,128)S(1)} %pad_maximum_fusion.7), channel_id=1, source_target_pairs={{0,32},{16,48},{32,0},{48,16},{1,33},{17,49},{33,1},{49,17},{2,34}... | collective-permute-start | bytes 24584 | tf_op jit(solution)/shard_map/ppermute | solution.py:38
  107.7 7.1 %collective-permute-start.10 = (f32[2,2048]{1,0:T(2,128)S(1)}, f32[2,2048]{1,0:T(2,128)S(1)}, u32[]{:S(2)}, u32[]{:S(2)}) collective-permute-start(f32[2,2048]{1,0:T(2,128)S(1)} %pad_maximum_fusion.1), channel_id=1, source_target_pairs={{0,1},{1,0},{2,3},{3,2},{4,5},{5,4},{6,7},{7,6},{8,9},{9,8},{10,11... | collective-permute-start | bytes 49160 | tf_op jit(solution)/shard_map/ppermute | solution.py:38
  114.9 2.7 %collective-permute-start.11 = (f32[2,2048]{1,0:T(2,128)S(1)}, f32[2,2048]{1,0:T(2,128)S(1)}, u32[]{:S(2)}, u32[]{:S(2)}) collective-permute-start(f32[2,2048]{1,0:T(2,128)S(1)} %pad_maximum_fusion.2), channel_id=1, source_target_pairs={{0,2},{2,0},{1,3},{3,1},{4,6},{6,4},{5,7},{7,5},{8,10},{10,8},{9,1... | collective-permute-start | bytes 49160 | tf_op jit(solution)/shard_map/ppermute | solution.py:38
  117.6 2.7 %collective-permute-start.12 = (f32[2,2048]{1,0:T(2,128)S(1)}, f32[2,2048]{1,0:T(2,128)S(1)}, u32[]{:S(2)}, u32[]{:S(2)}) collective-permute-start(f32[2,2048]{1,0:T(2,128)S(1)} %pad_maximum_fusion.3), channel_id=1, source_target_pairs={{0,4},{4,0},{8,12},{12,8},{1,5},{5,1},{9,13},{13,9},{2,6},{6,2},{1... | collective-permute-start | bytes 49160 | tf_op jit(solution)/shard_map/ppermute | solution.py:38
  120.3 4.3 %collective-permute-start.13 = (f32[2,2048]{1,0:T(2,128)S(1)}, f32[2,2048]{1,0:T(2,128)S(1)}, u32[]{:S(2)}, u32[]{:S(2)}) collective-permute-start(f32[2,2048]{1,0:T(2,128)S(1)} %pad_maximum_fusion.4), channel_id=1, source_target_pairs={{0,8},{4,12},{8,0},{12,4},{1,9},{5,13},{9,1},{13,5},{2,10},{6,14},... | collective-permute-start | bytes 49160 | tf_op jit(solution)/shard_map/ppermute | solution.py:38
  124.6 17.9 %copy-start = (f32[2048,1024]{1,0:T(8,128)S(1)}, f32[2048,1024]{1,0:T(8,128)}, u32[]{:S(2)}) copy-start(f32[2048,1024]{1,0:T(8,128)} %get-tuple-element.276) | copy-start | bytes 25165828
  137.1 5.5 %copy-start.3 = (f32[1024,768]{1,0:T(8,128)}, f32[1024,768]{1,0:T(8,128)S(1)}, u32[]{:S(2)}) copy-start(f32[1024,768]{1,0:T(8,128)S(1)} %fusion.5) | copy-start | bytes 9437188
  138.4 20.0 %collective-permute-start.14 = (f32[512,768]{1,0:T(8,128)}, f32[512,768]{1,0:T(8,128)}, u32[]{:S(2)}, u32[]{:S(2)}) collective-permute-start(f32[512,768]{1,0:T(8,128)} %dynamic-slice_bitcast_fusion.1), channel_id=1, source_target_pairs={{0,1},{1,0},{2,3},{3,2},{4,5},{5,4},{6,7},{7,6},{8,9},{9,8},{10,11... | collective-permute-start | bytes 4718600 | tf_op jit(solution)/shard_map/ppermute | solution.py:61
  152.7 1.7 copy-start.1
  152.7 5.7 %copy-start.4 = (f32[1024,768]{1,0:T(8,128)S(1)}, f32[1024,768]{1,0:T(8,128)}, u32[]{:S(2)}) copy-start(f32[1024,768]{1,0:T(8,128)} %copy-done.3) | copy-start | bytes 9437188
  155.7 7.4 %collective-permute-start.30 = (f32[512,768]{1,0:T(8,128)}, f32[512,768]{1,0:T(8,128)}, u32[]{:S(2)}, u32[]{:S(2)}) collective-permute-start(f32[512,768]{1,0:T(8,128)} %dynamic-slice_bitcast_fusion), channel_id=1, source_target_pairs={{0,1},{1,0},{2,3},{3,2},{4,5},{5,4},{6,7},{7,6},{8,9},{9,8},{10,11... | collective-permute-start | bytes 4718600 | tf_op jit(solution)/shard_map/ppermute | solution.py:61
  160.1 3.1 %copy-start.2 = (f32[1024,768]{1,0:T(8,128)S(1)}, f32[1024,768]{1,0:T(8,128)}, u32[]{:S(2)}) copy-start(f32[1024,768]{1,0:T(8,128)} %copy-done.1) | copy-start | bytes 9437188
  160.2 7.5 %collective-permute-start.18 = (f32[64,768]{1,0:T(8,128)S(1)}, f32[64,768]{1,0:T(8,128)S(1)}, u32[]{:S(2)}, u32[]{:S(2)}) collective-permute-start(f32[64,768]{1,0:T(8,128)S(1)} %dynamic-slice_bitcast_fusion.4), channel_id=1, source_target_pairs={{0,12},{4,0},{8,4},{12,8},{1,13},{5,1},{9,5},{13,9},{2,14},{6,2},{... | collective-permute-start | bytes 589832 | tf_op jit(solution)/shard_map/ppermute | solution.py:66
  163.0 7.6 %collective-permute-start.15 = (f32[64,768]{1,0:T(8,128)S(1)}, f32[64,768]{1,0:T(8,128)S(1)}, u32[]{:S(2)}, u32[]{:S(2)}) collective-permute-start(f32[64,768]{1,0:T(8,128)S(1)} %dynamic-slice_bitcast_fusion.5), channel_id=1, source_target_pairs={{0,4},{4,8},{8,12},{12,0},{1,5},{5,9},{9,13},{13,1},{2,6},{6,10},{... | collective-permute-start | bytes 589832 | tf_op jit(solution)/shard_map/ppermute | solution.py:65
  164.9 6.2 %collective-permute-start.34 = (f32[64,768]{1,0:T(8,128)S(1)}, f32[64,768]{1,0:T(8,128)S(1)}, u32[]{:S(2)}, u32[]{:S(2)}) collective-permute-start(f32[64,768]{1,0:T(8,128)S(1)} %dynamic-slice_bitcast_fusion.2), channel_id=1, source_target_pairs={{0,12},{4,0},{8,4},{12,8},{1,13},{5,1},{9,5},{13,9},{2,14},{6,2},{... | collective-permute-start | bytes 589832 | tf_op jit(solution)/shard_map/ppermute | solution.py:66
  167.6 7.0 %collective-permute-start.31 = (f32[64,768]{1,0:T(8,128)S(1)}, f32[64,768]{1,0:T(8,128)S(1)}, u32[]{:S(2)}, u32[]{:S(2)}) collective-permute-start(f32[64,768]{1,0:T(8,128)S(1)} %dynamic-slice_bitcast_fusion.3), channel_id=1, source_target_pairs={{0,4},{4,8},{8,12},{12,0},{1,5},{5,9},{9,13},{13,1},{2,6},{6,10},{... | collective-permute-start | bytes 589832 | tf_op jit(solution)/shard_map/ppermute | solution.py:65
  167.8 7.7 %collective-permute-start.19 = (f32[64,768]{1,0:T(8,128)S(1)}, f32[64,768]{1,0:T(8,128)S(1)}, u32[]{:S(2)}, u32[]{:S(2)}) collective-permute-start(f32[64,768]{1,0:T(8,128)S(1)} %bitcast_add_fusion.10), channel_id=1, source_target_pairs={{0,12},{4,0},{8,4},{12,8},{1,13},{5,1},{9,5},{13,9},{2,14},{6,2},{... | collective-permute-start | bytes 589832 | tf_op jit(solution)/shard_map/ppermute | solution.py:66
  170.7 8.3 %collective-permute-start.16 = (f32[64,768]{1,0:T(8,128)S(1)}, f32[64,768]{1,0:T(8,128)S(1)}, u32[]{:S(2)}, u32[]{:S(2)}) collective-permute-start(f32[64,768]{1,0:T(8,128)S(1)} %bitcast_add_fusion.13), channel_id=1, source_target_pairs={{0,4},{4,8},{8,12},{12,0},{1,5},{5,9},{9,13},{13,1},{2,6},{6,10},{... | collective-permute-start | bytes 589832 | tf_op jit(solution)/shard_map/ppermute | solution.py:65
  171.2 8.1 %collective-permute-start.35 = (f32[64,768]{1,0:T(8,128)S(1)}, f32[64,768]{1,0:T(8,128)S(1)}, u32[]{:S(2)}, u32[]{:S(2)}) collective-permute-start(f32[64,768]{1,0:T(8,128)S(1)} %bitcast_add_fusion.4), channel_id=1, source_target_pairs={{0,12},{4,0},{8,4},{12,8},{1,13},{5,1},{9,5},{13,9},{2,14},{6,2},{... | collective-permute-start | bytes 589832 | tf_op jit(solution)/shard_map/ppermute | solution.py:66
  174.7 7.8 %collective-permute-start.32 = (f32[64,768]{1,0:T(8,128)S(1)}, f32[64,768]{1,0:T(8,128)S(1)}, u32[]{:S(2)}, u32[]{:S(2)}) collective-permute-start(f32[64,768]{1,0:T(8,128)S(1)} %bitcast_add_fusion.7), channel_id=1, source_target_pairs={{0,4},{4,8},{8,12},{12,0},{1,5},{5,9},{9,13},{13,1},{2,6},{6,10},{... | collective-permute-start | bytes 589832 | tf_op jit(solution)/shard_map/ppermute | solution.py:65
  175.5 8.0 %collective-permute-start.20 = (f32[64,768]{1,0:T(8,128)S(1)}, f32[64,768]{1,0:T(8,128)S(1)}, u32[]{:S(2)}, u32[]{:S(2)}) collective-permute-start(f32[64,768]{1,0:T(8,128)S(1)} %bitcast_add_fusion.9), channel_id=1, source_target_pairs={{0,12},{4,0},{8,4},{12,8},{1,13},{5,1},{9,5},{13,9},{2,14},{6,2},{... | collective-permute-start | bytes 589832 | tf_op jit(solution)/shard_map/ppermute | solution.py:66
  179.0 7.1 %collective-permute-start.17 = (f32[64,768]{1,0:T(8,128)S(1)}, f32[64,768]{1,0:T(8,128)S(1)}, u32[]{:S(2)}, u32[]{:S(2)}) collective-permute-start(f32[64,768]{1,0:T(8,128)S(1)} %bitcast_add_fusion.12), channel_id=1, source_target_pairs={{0,4},{4,8},{8,12},{12,0},{1,5},{5,9},{9,13},{13,1},{2,6},{6,10},{... | collective-permute-start | bytes 589832 | tf_op jit(solution)/shard_map/ppermute | solution.py:65
  179.3 8.2 %collective-permute-start.36 = (f32[64,768]{1,0:T(8,128)S(1)}, f32[64,768]{1,0:T(8,128)S(1)}, u32[]{:S(2)}, u32[]{:S(2)}) collective-permute-start(f32[64,768]{1,0:T(8,128)S(1)} %bitcast_add_fusion.3), channel_id=1, source_target_pairs={{0,12},{4,0},{8,4},{12,8},{1,13},{5,1},{9,5},{13,9},{2,14},{6,2},{... | collective-permute-start | bytes 589832 | tf_op jit(solution)/shard_map/ppermute | solution.py:66
  182.5 8.0 %collective-permute-start.33 = (f32[64,768]{1,0:T(8,128)S(1)}, f32[64,768]{1,0:T(8,128)S(1)}, u32[]{:S(2)}, u32[]{:S(2)}) collective-permute-start(f32[64,768]{1,0:T(8,128)S(1)} %bitcast_add_fusion.6), channel_id=1, source_target_pairs={{0,4},{4,8},{8,12},{12,0},{1,5},{5,9},{9,13},{13,1},{2,6},{6,10},{... | collective-permute-start | bytes 589832 | tf_op jit(solution)/shard_map/ppermute | solution.py:65
  186.2 4.9 %collective-permute-start.21 = (f32[64,768]{1,0:T(8,128)S(1)}, f32[64,768]{1,0:T(8,128)S(1)}, u32[]{:S(2)}, u32[]{:S(2)}) collective-permute-start(f32[64,768]{1,0:T(8,128)S(1)} %fusion.30), channel_id=1, source_target_pairs={{0,2},{2,0},{1,3},{3,1},{4,6},{6,4},{5,7},{7,5},{8,10},{10,8},{9,1... | collective-permute-start | bytes 589832 | tf_op jit(solution)/shard_map/ppermute | solution.py:68
  190.6 6.2 %collective-permute-start.37 = (f32[64,768]{1,0:T(8,128)S(1)}, f32[64,768]{1,0:T(8,128)S(1)}, u32[]{:S(2)}, u32[]{:S(2)}) collective-permute-start(f32[64,768]{1,0:T(8,128)S(1)} %fusion.24), channel_id=1, source_target_pairs={{0,2},{2,0},{1,3},{3,1},{4,6},{6,4},{5,7},{7,5},{8,10},{10,8},{9,1... | collective-permute-start | bytes 589832 | tf_op jit(solution)/shard_map/ppermute | solution.py:68
  191.2 9.8 %collective-permute-start.22 = (f32[64,768]{1,0:T(8,128)S(1)}, f32[64,768]{1,0:T(8,128)S(1)}, u32[]{:S(2)}, u32[]{:S(2)}) collective-permute-start(f32[64,768]{1,0:T(8,128)S(1)} %fusion.34), channel_id=1, source_target_pairs={{0,2},{2,0},{1,3},{3,1},{4,6},{6,4},{5,7},{7,5},{8,10},{10,8},{9,1... | collective-permute-start | bytes 589832 | tf_op jit(solution)/shard_map/ppermute | solution.py:71
  196.8 8.3 %collective-permute-start.38 = (f32[64,768]{1,0:T(8,128)S(1)}, f32[64,768]{1,0:T(8,128)S(1)}, u32[]{:S(2)}, u32[]{:S(2)}) collective-permute-start(f32[64,768]{1,0:T(8,128)S(1)} %fusion.28), channel_id=1, source_target_pairs={{0,2},{2,0},{1,3},{3,1},{4,6},{6,4},{5,7},{7,5},{8,10},{10,8},{9,1... | collective-permute-start | bytes 589832 | tf_op jit(solution)/shard_map/ppermute | solution.py:71
  201.0 8.6 %collective-permute-start.23 = (f32[64,768]{1,0:T(8,128)S(1)}, f32[64,768]{1,0:T(8,128)S(1)}, u32[]{:S(2)}, u32[]{:S(2)}) collective-permute-start(f32[64,768]{1,0:T(8,128)S(1)} %get-tuple-element.288), channel_id=1, source_target_pairs={{0,4},{4,8},{8,12},{12,0},{1,5},{5,9},{9,13},{13,1},{2,6},{6,10},{... | collective-permute-start | bytes 589832 | tf_op jit(solution)/shard_map/ppermute | solution.py:76
  201.1 8.6 %collective-permute-start.24 = (f32[64,768]{1,0:T(8,128)S(1)}, f32[64,768]{1,0:T(8,128)S(1)}, u32[]{:S(2)}, u32[]{:S(2)}) collective-permute-start(f32[64,768]{1,0:T(8,128)S(1)} %get-tuple-element.287), channel_id=1, source_target_pairs={{0,12},{4,0},{8,4},{12,8},{1,13},{5,1},{9,5},{13,9},{2,14},{6,2},{... | collective-permute-start | bytes 589832 | tf_op jit(solution)/shard_map/ppermute | solution.py:77
  205.2 7.1 %collective-permute-start.39 = (f32[64,768]{1,0:T(8,128)S(1)}, f32[64,768]{1,0:T(8,128)S(1)}, u32[]{:S(2)}, u32[]{:S(2)}) collective-permute-start(f32[64,768]{1,0:T(8,128)S(1)} %get-tuple-element.290), channel_id=1, source_target_pairs={{0,4},{4,8},{8,12},{12,0},{1,5},{5,9},{9,13},{13,1},{2,6},{6,10},{... | collective-permute-start | bytes 589832 | tf_op jit(solution)/shard_map/ppermute | solution.py:76
  205.3 8.5 %collective-permute-start.40 = (f32[64,768]{1,0:T(8,128)S(1)}, f32[64,768]{1,0:T(8,128)S(1)}, u32[]{:S(2)}, u32[]{:S(2)}) collective-permute-start(f32[64,768]{1,0:T(8,128)S(1)} %get-tuple-element.289), channel_id=1, source_target_pairs={{0,12},{4,0},{8,4},{12,8},{1,13},{5,1},{9,5},{13,9},{2,14},{6,2},{... | collective-permute-start | bytes 589832 | tf_op jit(solution)/shard_map/ppermute | solution.py:77
  209.6 8.3 %collective-permute-start.25 = (f32[64,768]{1,0:T(8,128)S(1)}, f32[64,768]{1,0:T(8,128)S(1)}, u32[]{:S(2)}, u32[]{:S(2)}) collective-permute-start(f32[64,768]{1,0:T(8,128)S(1)} %collective-permute-done.23), channel_id=1, source_target_pairs={{0,4},{4,8},{8,12},{12,0},{1,5},{5,9},{9,13},{13,1},{2,6},{6,10},{... | collective-permute-start | bytes 589832 | tf_op jit(solution)/shard_map/ppermute | solution.py:76
  209.7 8.3 %collective-permute-start.26 = (f32[64,768]{1,0:T(8,128)S(1)}, f32[64,768]{1,0:T(8,128)S(1)}, u32[]{:S(2)}, u32[]{:S(2)}) collective-permute-start(f32[64,768]{1,0:T(8,128)S(1)} %collective-permute-done.24), channel_id=1, source_target_pairs={{0,12},{4,0},{8,4},{12,8},{1,13},{5,1},{9,5},{13,9},{2,14},{6,2},{... | collective-permute-start | bytes 589832 | tf_op jit(solution)/shard_map/ppermute | solution.py:77
  212.3 8.3 %collective-permute-start.41 = (f32[64,768]{1,0:T(8,128)S(1)}, f32[64,768]{1,0:T(8,128)S(1)}, u32[]{:S(2)}, u32[]{:S(2)}) collective-permute-start(f32[64,768]{1,0:T(8,128)S(1)} %collective-permute-done.39), channel_id=1, source_target_pairs={{0,4},{4,8},{8,12},{12,0},{1,5},{5,9},{9,13},{13,1},{2,6},{6,10},{... | collective-permute-start | bytes 589832 | tf_op jit(solution)/shard_map/ppermute | solution.py:76
  213.8 8.1 %collective-permute-start.42 = (f32[64,768]{1,0:T(8,128)S(1)}, f32[64,768]{1,0:T(8,128)S(1)}, u32[]{:S(2)}, u32[]{:S(2)}) collective-permute-start(f32[64,768]{1,0:T(8,128)S(1)} %collective-permute-done.40), channel_id=1, source_target_pairs={{0,12},{4,0},{8,4},{12,8},{1,13},{5,1},{9,5},{13,9},{2,14},{6,2},{... | collective-permute-start | bytes 589832 | tf_op jit(solution)/shard_map/ppermute | solution.py:77
  217.9 8.0 %collective-permute-start.27 = (f32[64,768]{1,0:T(8,128)S(1)}, f32[64,768]{1,0:T(8,128)S(1)}, u32[]{:S(2)}, u32[]{:S(2)}) collective-permute-start(f32[64,768]{1,0:T(8,128)S(1)} %collective-permute-done.25), channel_id=1, source_target_pairs={{0,4},{4,8},{8,12},{12,0},{1,5},{5,9},{9,13},{13,1},{2,6},{6,10},{... | collective-permute-start | bytes 589832 | tf_op jit(solution)/shard_map/ppermute | solution.py:76
  218.0 8.6 %collective-permute-start.28 = (f32[64,768]{1,0:T(8,128)S(1)}, f32[64,768]{1,0:T(8,128)S(1)}, u32[]{:S(2)}, u32[]{:S(2)}) collective-permute-start(f32[64,768]{1,0:T(8,128)S(1)} %collective-permute-done.26), channel_id=1, source_target_pairs={{0,12},{4,0},{8,4},{12,8},{1,13},{5,1},{9,5},{13,9},{2,14},{6,2},{... | collective-permute-start | bytes 589832 | tf_op jit(solution)/shard_map/ppermute | solution.py:77
  220.6 14.9 %collective-permute-start.43 = (f32[64,768]{1,0:T(8,128)S(1)}, f32[64,768]{1,0:T(8,128)S(1)}, u32[]{:S(2)}, u32[]{:S(2)}) collective-permute-start(f32[64,768]{1,0:T(8,128)S(1)} %collective-permute-done.41), channel_id=1, source_target_pairs={{0,4},{4,8},{8,12},{12,0},{1,5},{5,9},{9,13},{13,1},{2,6},{6,10},{... | collective-permute-start | bytes 589832 | tf_op jit(solution)/shard_map/ppermute | solution.py:76
  222.0 14.3 %collective-permute-start.44 = (f32[64,768]{1,0:T(8,128)S(1)}, f32[64,768]{1,0:T(8,128)S(1)}, u32[]{:S(2)}, u32[]{:S(2)}) collective-permute-start(f32[64,768]{1,0:T(8,128)S(1)} %collective-permute-done.42), channel_id=1, source_target_pairs={{0,12},{4,0},{8,4},{12,8},{1,13},{5,1},{9,5},{13,9},{2,14},{6,2},{... | collective-permute-start | bytes 589832 | tf_op jit(solution)/shard_map/ppermute | solution.py:77
  227.3 11.4 %collective-permute-start.29 = (f32[512,768]{1,0:T(8,128)S(1)}, f32[512,768]{1,0:T(8,128)}, u32[]{:S(2)}, u32[]{:S(2)}) collective-permute-start(f32[512,768]{1,0:T(8,128)S(1)} %bitcast.248), channel_id=1, source_target_pairs={{0,1},{1,0},{2,3},{3,2},{4,5},{5,4},{6,7},{7,6},{8,9},{9,8},{10,11... | collective-permute-start | bytes 4718600 | tf_op jit(solution)/shard_map/ppermute | solution.py:81
  236.9 4.0 %collective-permute-start.45 = (f32[512,768]{1,0:T(8,128)S(1)}, f32[512,768]{1,0:T(8,128)}, u32[]{:S(2)}, u32[]{:S(2)}) collective-permute-start(f32[512,768]{1,0:T(8,128)S(1)} %bitcast.246), channel_id=1, source_target_pairs={{0,1},{1,0},{2,3},{3,2},{4,5},{5,4},{6,7},{7,6},{8,9},{9,8},{10,11... | collective-permute-start | bytes 4718600 | tf_op jit(solution)/shard_map/ppermute | solution.py:81

commit v4 on v3

--- a/solution.py
+++ b/solution.py
@@ -9,6 +9,7 @@
 
 IMG = ("zh", "y")
 CAP = ("x", "zl", "core")
+CHUNKS = 1
 
 
 def similar(query_factor, target_factor):
@@ -117,9 +118,9 @@
     top, row_total = merge_peaks(cap_rounds, row_peak, row_sum)
     scale = jnp.exp(row_peak - top)
     rows = weights.shape[0]
-    chunk = rows // 2
+    chunk = rows // CHUNKS
     parts = []
-    for k in range(2):
+    for k in range(CHUNKS):
         part = slice(k * chunk, (k + 1) * chunk)
         summed = rescaled_affinity(weights[part], features) * scale[part, None]
         parts.append(reduce_rows(summed, row_total, k * chunk, sizes))

time: 250 us -> 275 us (1.10)
  waiting for transfers between devices: 51.5 us -> 90.9 us
  starting transfers between devices: 77.7 us -> 58.4 us
  local copies, waits for them, and re-layouts: 7.05 us -> 10.6 us
    ppermute x6 -> x3, waiting for transfers between devices: 0.02 us -> 14 us  [reduce_rows(): right = lax.ppermute(right, 'x', ring('x', x_size, 1))]
    ppermute x6 -> x3, waiting for transfers between devices: 3.39 us -> 17.3 us  [reduce_rows(): lax.ppermute(left, 'x', ring('x', x_size, -1))]
    ppermute x6 -> x3, starting transfers between devices: 18.5 us -> 9.27 us  [reduce_rows(): lax.ppermute(left, 'x', ring('x', x_size, -1))]
    ppermute x6 -> x3, starting transfers between devices: 16.1 us -> 8.29 us  [reduce_rows(): left = lax.ppermute(left, 'x', ring('x', x_size, -1))]
    ppermute x2 -> x1, waiting for transfers between devices: 0.01 us -> 5.42 us  [reduce_rows(): held = pick(halves, c) + lax.ppermute(pick(halves, 1 - c), 'core', swap)]
    unnamed x26 -> x28, local copies, waits for them, and re-layouts: 2.3 us -> 6.38 us
    ppermute x2 -> x1, waiting for transfers between devices: 1.71 us -> 5.42 us  [reduce_rows(): other = lax.ppermute(held, 'core', swap)]
    add x4 -> x2, other arithmetic: 0.1 us -> 3.57 us  [reduce_rows(): lax.ppermute(right, 'x', ring('x', x_size, 1))]
  transfers between devices with their start and end apart: 46 -> 30, of which waited for: 22 -> 22; matrix products, arithmetic and copies ran while one was open for 25% -> 18% of each run, Pallas kernels for 0% -> 0%
where the time goes in v4:
time: 275 us; the launch traced here: 271 us
  waiting for transfers between devices  90.9 us (33%)
  matrix products  66.8 us (24%)
  starting transfers between devices  58.4 us (21%)
  other arithmetic  43.8 us (16%)
  local copies, waits for them, and re-layouts  10.6 us (4%)
    dot_general x2, matrix products, similar(): lax.dot_general(query_factor, target_factor, (((1,), (0,)), ((), ())), pr...  43 us
    dot_general x1, matrix products, rescaled_affinity(): lax.dot_general(weights, features, (((1,), (1,)), ((), ())), precision=la...  23.8 us
    ppermute x3, waiting for transfers between devices, reduce_rows(): lax.ppermute(left, 'x', ring('x', x_size, -1))  17.3 us
    ppermute x7, starting transfers between devices, merge_peaks(): other = lax.ppermute(pair, axis, [(j, j ^ dist) for j in range(size)])  15 us
    ppermute x3, waiting for transfers between devices, reduce_rows(): right = lax.ppermute(right, 'x', ring('x', x_size, 1))  14 us
    ppermute x3, waiting for transfers between devices, gather_features(): right = lax.ppermute(right, 'y', ring('y', y_size, 1))  12.4 us
    ppermute x7, waiting for transfers between devices, merge_peaks(): other = lax.ppermute(pair, axis, [(j, j ^ dist) for j in range(size)])  9.69 us
    ppermute x3, starting transfers between devices, reduce_rows(): lax.ppermute(left, 'x', ring('x', x_size, -1))  9.27 us
  transfers between devices with their start and end apart: 30, of which 22 were waited for; matrix products, arithmetic and copies ran while one was open for 18% of the time, Pallas kernels for 0%

profile of v4, /device:TPU:1, one launch (start us, length us, event | category | flops | bytes accessed | tf_op | source)
XLA Modules:
  0.0 271.2 jit_solution(2999421756122914536)
XLA Ops:
  0.0 4.4 %collective-permute-start = (f32[1024,96]{0,1:T(8,128)}, f32[1024,96]{0,1:T(8,128)S(1)}, u32[]{:S(2)}, u32[]{:S(2)}) collective-permute-start(f32[1024,96]{0,1:T(8,128)} %param.32), channel_id=1, source_target_pairs={{0,64},{64,0},{1,65},{65,1},{2,66},{66,2},{3,67},{67,3},{4,68},{68... | collective-permute-start | bytes 1179656 | tf_op jit(solution)/shard_map/ppermute | solution.py:90
  4.4 1.4 and_reduce_fusion.10
  5.8 7.7 %collective-permute-done = f32[1024,96]{0,1:T(8,128)S(1)} collective-permute-done((f32[1024,96]{0,1:T(8,128)}, f32[1024,96]{0,1:T(8,128)S(1)}, u32[]{:S(2)}, u32[]{:S(2)}) %collective-permute-start) | collective-permute-done | bytes 393248 | tf_op jit(solution)/shard_map/ppermute | solution.py:90
  13.5 1.4 maximum_select_fusion.2
  14.9 1.0 slice_bitcast_fusion.2
  15.8 1.3 collective-permute-start.1
  17.1 1.4 collective-permute-start.2
  19.3 0.8 and_reduce_fusion.8
  20.1 0.8 and_reduce_fusion.6
  22.5 4.3 %collective-permute-done.1 = f32[1024,96]{0,1:T(8,128)} collective-permute-done((f32[1024,96]{0,1:T(8,128)}, f32[1024,96]{0,1:T(8,128)}, u32[]{:S(2)}, u32[]{:S(2)}) %collective-permute-start.1) | collective-permute-done | bytes 393248 | tf_op jit(solution)/shard_map/ppermute | solution.py:95
  26.8 2.7 collective-permute-start.4
  29.5 1.9 fusion.21
  31.4 1.7 fusion.20
  33.1 3.7 %collective-permute-done.3 = f32[1024,96]{0,1:T(8,128)S(1)} collective-permute-done((f32[1024,96]{0,1:T(8,128)}, f32[1024,96]{0,1:T(8,128)S(1)}, u32[]{:S(2)}, u32[]{:S(2)}) %collective-permute-start.3) | collective-permute-done | bytes 393248 | tf_op jit(solution)/shard_map/ppermute | solution.py:95
  36.8 2.9 %collective-permute-start.6 = (f32[1024,96]{0,1:T(8,128)S(1)}, f32[1024,96]{0,1:T(8,128)S(1)}, u32[]{:S(2)}, u32[]{:S(2)}) collective-permute-start(f32[1024,96]{0,1:T(8,128)S(1)} %collective-permute-done.4), channel_id=1, source_target_pairs={{0,48},{16,0},{32,16},{48,32},{1,49},{17,1},{33,17},{49,33},{2,50}... | collective-permute-start | bytes 1179656 | tf_op jit(solution)/shard_map/ppermute | solution.py:96
  41.1 4.4 %collective-permute-done.5 = f32[1024,96]{0,1:T(8,128)S(1)} collective-permute-done((f32[1024,96]{0,1:T(8,128)S(1)}, f32[1024,96]{0,1:T(8,128)S(1)}, u32[]{:S(2)}, u32[]{:S(2)}) %collective-permute-start.5) | collective-permute-done | bytes 393248 | tf_op jit(solution)/shard_map/ppermute | solution.py:95
  47.1 20.8 %fusion = (f32[1024]{0:T(1024)S(1)}, f32[1024,2048]{0,1:T(8,128)S(1)}) fusion(f32[768,1024]{1,0:T(8,128)S(1)} %bitcast.164, f32[2048,768]{1,0:T(8,128)S(1)} %copy-done.11), kind=kOutput, calls=%fused_computation.4 | convolution fusion | flops 19331547136 | bytes 17829888 | tf_op jit(solution)/shard_map/dot_general | solution.py:16
  67.9 1.4 exponential_reduce_fusion
  69.4 1.8 collective-permute-start.7
  71.2 2.3 collective-permute-done.7
  73.6 2.5 collective-permute-done.8
  76.1 2.2 collective-permute-start.9
  78.3 22.1 %bitcast_multiply_fusion.1 = f32[2048,1024]{1,0:T(8,128)S(1)} fusion(f32[768,1024]{1,0:T(8,128)S(1)} %bitcast.165, f32[2048,768]{1,0:T(8,128)S(1)} %bitcast.200), kind=kOutput, calls=%fused_computation.1 | convolution fusion | flops 19329449984 | bytes 17825792 | tf_op jit(solution)/shard_map/dot_general | solution.py:16
  101.2 2.5 copy-done
  103.7 1.9 fusion.1
  105.6 6.3 %collective-permute-start.10 = (f32[2,2048]{1,0:T(2,128)S(1)}, f32[2,2048]{1,0:T(2,128)S(1)}, u32[]{:S(2)}, u32[]{:S(2)}) collective-permute-start(f32[2,2048]{1,0:T(2,128)S(1)} %pad_maximum_fusion), channel_id=1, source_target_pairs={{0,1},{1,0},{2,3},{3,2},{4,5},{5,4},{6,7},{7,6},{8,9},{9,8},{10,11... | collective-permute-start | bytes 49160 | tf_op jit(solution)/shard_map/ppermute | solution.py:39
  111.9 0.8 collective-permute-done.10
  112.9 2.5 collective-permute-done.11
  116.1 1.3 collective-permute-start.12
  118.0 0.8 collective-permute-done.12
  119.4 3.2 %collective-permute-start.13 = (f32[2,2048]{1,0:T(2,128)S(1)}, f32[2,2048]{1,0:T(2,128)S(1)}, u32[]{:S(2)}, u32[]{:S(2)}) collective-permute-start(f32[2,2048]{1,0:T(2,128)S(1)} %pad_maximum_fusion.3), channel_id=1, source_target_pairs={{0,8},{4,12},{8,0},{12,4},{1,9},{5,13},{9,1},{13,5},{2,10},{6,14},... | collective-permute-start | bytes 49160 | tf_op jit(solution)/shard_map/ppermute | solution.py:39
  125.2 23.8 %fusion.5 = f32[2048,768]{1,0:T(8,128)S(1)} fusion(f32[768,1024]{1,0:T(8,128)S(1)} %bitcast.166, f32[2048,1024]{1,0:T(8,128)} %copy-done, f32[2048]{0:T(1024)S(1)} %subtract_reduce_fusion, f32[1024]{0:T(1024)S(1)} %bitcast.189, f32[2048]{0:T(1024)S(1)} %get-tuple-element.191), kind=kOutput, calls=%fused_computation.11 | convolution fusion | flops 19333120000 | bytes 17846272 | tf_op jit(solution)/shard_map/dot_general | solution.py:27
  149.3 2.5 copy-done.1
  151.8 3.8 %collective-permute-start.14 = (f32[1024,768]{1,0:T(8,128)S(1)}, f32[1024,768]{1,0:T(8,128)}, u32[]{:S(2)}, u32[]{:S(2)}) collective-permute-start(f32[1024,768]{1,0:T(8,128)S(1)} %dynamic-slice_bitcast_fusion), channel_id=1, source_target_pairs={{0,1},{1,0},{2,3},{3,2},{4,5},{5,4},{6,7},{7,6},{8,9},{9,8},{10,11... | collective-permute-start | bytes 9437192 | tf_op jit(solution)/shard_map/ppermute | solution.py:62
  155.6 5.4 %collective-permute-done.14 = f32[1024,768]{1,0:T(8,128)} collective-permute-done((f32[1024,768]{1,0:T(8,128)S(1)}, f32[1024,768]{1,0:T(8,128)}, u32[]{:S(2)}, u32[]{:S(2)}) %collective-permute-start.14) | collective-permute-done | bytes 3145760 | tf_op jit(solution)/shard_map/ppermute | solution.py:62
  161.0 3.2 %bitcast_add_fusion = f32[1024,768]{1,0:T(8,128)S(1)} fusion(f32[1024,768]{1,0:T(8,128)} %collective-permute-done.14, f32[2,1024,768]{2,1,0:T(8,128)} %bitcast.168, s32[]{:T(128)S(6)} %select_n.215), kind=kLoop, calls=%fused_computation.12 | loop fusion | flops 786432 | bytes 9437188 | tf_op jit(solution)/shard_map/add | solution.py:62
  164.5 0.8 dynamic-slice_bitcast_fusion.1
  165.2 2.5 collective-permute-start.18
  167.7 0.8 dynamic-slice_bitcast_fusion.2
  168.7 7.5 %collective-permute-done.18 = f32[128,768]{1,0:T(8,128)S(1)} collective-permute-done((f32[128,768]{1,0:T(8,128)}, f32[128,768]{1,0:T(8,128)S(1)}, u32[]{:S(2)}, u32[]{:S(2)}) %collective-permute-start.18) | collective-permute-done | bytes 393248 | tf_op jit(solution)/shard_map/ppermute | solution.py:67
  176.2 0.8 bitcast_add_fusion.3
  176.9 3.3 %collective-permute-start.19 = (f32[128,768]{1,0:T(8,128)}, f32[128,768]{1,0:T(8,128)}, u32[]{:S(2)}, u32[]{:S(2)}) collective-permute-start(f32[128,768]{1,0:T(8,128)} %bitcast_add_fusion.3), channel_id=1, source_target_pairs={{0,12},{4,0},{8,4},{12,8},{1,13},{5,1},{9,5},{13,9},{2,14},{6,2},{... | collective-permute-start | bytes 1179656 | tf_op jit(solution)/shard_map/ppermute | solution.py:67
  180.2 1.8 bitcast_add_fusion.6
  182.0 5.7 %collective-permute-done.19 = f32[128,768]{1,0:T(8,128)} collective-permute-done((f32[128,768]{1,0:T(8,128)}, f32[128,768]{1,0:T(8,128)}, u32[]{:S(2)}, u32[]{:S(2)}) %collective-permute-start.19) | collective-permute-done | bytes 393248 | tf_op jit(solution)/shard_map/ppermute | solution.py:67
  187.8 1.0 bitcast_add_fusion.2
  188.8 3.5 %collective-permute-start.20 = (f32[128,768]{1,0:T(8,128)S(1)}, f32[128,768]{1,0:T(8,128)}, u32[]{:S(2)}, u32[]{:S(2)}) collective-permute-start(f32[128,768]{1,0:T(8,128)S(1)} %bitcast_add_fusion.2), channel_id=1, source_target_pairs={{0,12},{4,0},{8,4},{12,8},{1,13},{5,1},{9,5},{13,9},{2,14},{6,2},{... | collective-permute-start | bytes 1179656 | tf_op jit(solution)/shard_map/ppermute | solution.py:67
  192.7 1.8 bitcast_add_fusion.5
  194.5 4.1 %collective-permute-done.20 = f32[128,768]{1,0:T(8,128)} collective-permute-done((f32[128,768]{1,0:T(8,128)S(1)}, f32[128,768]{1,0:T(8,128)}, u32[]{:S(2)}, u32[]{:S(2)}) %collective-permute-start.20) | collective-permute-done | bytes 393248 | tf_op jit(solution)/shard_map/ppermute | solution.py:67
  198.6 1.0 fusion.28
  199.6 4.6 %collective-permute-done.17 = f32[128,768]{1,0:T(8,128)} collective-permute-done((f32[128,768]{1,0:T(8,128)}, f32[128,768]{1,0:T(8,128)}, u32[]{:S(2)}, u32[]{:S(2)}) %collective-permute-start.17) | collective-permute-done | bytes 393248 | tf_op jit(solution)/shard_map/ppermute | solution.py:66
  204.2 1.0 fusion.29
  205.5 0.8 fusion.35
  206.3 6.4 %collective-permute-done.21 = f32[128,768]{1,0:T(8,128)S(1)} collective-permute-done((f32[128,768]{1,0:T(8,128)S(1)}, f32[128,768]{1,0:T(8,128)S(1)}, u32[]{:S(2)}, u32[]{:S(2)}) %collective-permute-start.21) | collective-permute-done | bytes 393248 | tf_op jit(solution)/shard_map/ppermute | solution.py:69
  213.0 7.5 %collective-permute-done.22 = f32[128,768]{1,0:T(8,128)S(1)} collective-permute-done((f32[128,768]{1,0:T(8,128)S(1)}, f32[128,768]{1,0:T(8,128)S(1)}, u32[]{:S(2)}, u32[]{:S(2)}) %collective-permute-start.22) | collective-permute-done | bytes 393248 | tf_op jit(solution)/shard_map/ppermute | solution.py:72
  220.7 2.7 collective-permute-start.24
  224.1 0.8 and_reduce_fusion.2
  227.2 1.3 collective-permute-done.23
  228.5 2.7 collective-permute-start.26
  232.5 6.0 %collective-permute-done.25 = f32[128,768]{1,0:T(8,128)S(1)} collective-permute-done((f32[128,768]{1,0:T(8,128)S(1)}, f32[128,768]{1,0:T(8,128)S(1)}, u32[]{:S(2)}, u32[]{:S(2)}) %collective-permute-start.25) | collective-permute-done | bytes 393248 | tf_op jit(solution)/shard_map/ppermute | solution.py:77
  238.5 3.0 %collective-permute-start.28 = (f32[128,768]{1,0:T(8,128)S(1)}, f32[128,768]{1,0:T(8,128)S(1)}, u32[]{:S(2)}, u32[]{:S(2)}) collective-permute-start(f32[128,768]{1,0:T(8,128)S(1)} %collective-permute-done.26), channel_id=1, source_target_pairs={{0,12},{4,0},{8,4},{12,8},{1,13},{5,1},{9,5},{13,9},{2,14},{6,2},{... | collective-permute-start | bytes 1179656 | tf_op jit(solution)/shard_map/ppermute | solution.py:78
  242.9 6.7 %collective-permute-done.27 = f32[128,768]{1,0:T(8,128)S(1)} collective-permute-done((f32[128,768]{1,0:T(8,128)S(1)}, f32[128,768]{1,0:T(8,128)S(1)}, u32[]{:S(2)}, u32[]{:S(2)}) %collective-permute-start.27) | collective-permute-done | bytes 393248 | tf_op jit(solution)/shard_map/ppermute | solution.py:77
  250.9 8.8 %collective-permute-start.29 = (f32[1024,768]{1,0:T(8,128)S(1)}, f32[1024,768]{1,0:T(8,128)}, u32[]{:S(2)}, u32[]{:S(2)}) collective-permute-start(f32[1024,768]{1,0:T(8,128)S(1)} %bitcast.161), channel_id=1, source_target_pairs={{0,1},{1,0},{2,3},{3,2},{4,5},{5,4},{6,7},{7,6},{8,9},{9,8},{10,11... | collective-permute-start | bytes 9437192 | tf_op jit(solution)/shard_map/ppermute | solution.py:82
  259.7 5.4 %collective-permute-done.29 = f32[1024,768]{1,0:T(8,128)} collective-permute-done((f32[1024,768]{1,0:T(8,128)S(1)}, f32[1024,768]{1,0:T(8,128)}, u32[]{:S(2)}, u32[]{:S(2)}) %collective-permute-start.29) | collective-permute-done | bytes 3145760 | tf_op jit(solution)/shard_map/ppermute | solution.py:82
  265.1 5.9 %maximum_select_fusion = f32[2,1024,768]{2,1,0:T(8,128)} fusion(f32[1,1024,768]{2,1,0:T(8,128)} %bitcast.80, f32[1,1024,768]{2,1,0:T(8,128)S(1)} %bitcast.162, pred[]{:T(512)S(6)} %eq.30), kind=kLoop, calls=%fused_computation.8 | loop fusion | flops 4718592 | bytes 12582913 | tf_op jit(solution)/shard_map/jit(_where)/select_n | solution.py:83
  (90 shorter events, 19.6 us)
Async XLA Ops:
  0.0 19.3 %copy-start.8 = (s32[4]{0:T(128)S(1)}, s32[4]{0:T(128)}, u32[]{:S(2)}) copy-start(s32[4]{0:T(128)} %constant.483.clone.1) | copy-start | bytes 52
  0.0 18.5 %copy-start.10 = (s32[4]{0:T(128)S(1)}, s32[4]{0:T(128)}, u32[]{:S(2)}) copy-start(s32[4]{0:T(128)} %constant.477.clone.1) | copy-start | bytes 52
  0.0 13.5 %collective-permute-start = (f32[1024,96]{0,1:T(8,128)}, f32[1024,96]{0,1:T(8,128)S(1)}, u32[]{:S(2)}, u32[]{:S(2)}) collective-permute-start(f32[1024,96]{0,1:T(8,128)} %param.32), channel_id=1, source_target_pairs={{0,64},{64,0},{1,65},{65,1},{2,66},{66,2},{3,67},{67,3},{4,68},{68... | collective-permute-start | bytes 1179656 | tf_op jit(solution)/shard_map/ppermute | solution.py:90
  13.5 7.4 %copy-start.5 = (f32[1024,96]{0,1:T(8,128)}, f32[1024,96]{0,1:T(8,128)S(1)}, u32[]{:S(2)}) copy-start(f32[1024,96]{0,1:T(8,128)S(1)} %collective-permute-done) | copy-start | bytes 1179652
  13.5 7.8 %copy-start.4 = (f32[1024,96]{0,1:T(8,128)S(1)}, f32[1024,96]{0,1:T(8,128)}, u32[]{:S(2)}) copy-start(f32[1024,96]{0,1:T(8,128)} %param.32) | copy-start | bytes 1179652
  15.8 11.0 %collective-permute-start.1 = (f32[1024,96]{0,1:T(8,128)}, f32[1024,96]{0,1:T(8,128)}, u32[]{:S(2)}, u32[]{:S(2)}) collective-permute-start(f32[1024,96]{0,1:T(8,128)} %get-tuple-element.207), channel_id=1, source_target_pairs={{0,16},{16,32},{32,48},{48,0},{1,17},{17,33},{33,49},{49,1},{2,18}... | collective-permute-start | bytes 1179656 | tf_op jit(solution)/shard_map/ppermute | solution.py:95
  17.1 9.7 %collective-permute-start.2 = (f32[1024,96]{0,1:T(8,128)}, f32[1024,96]{0,1:T(8,128)}, u32[]{:S(2)}, u32[]{:S(2)}) collective-permute-start(f32[1024,96]{0,1:T(8,128)} %get-tuple-element.206), channel_id=1, source_target_pairs={{0,48},{16,0},{32,16},{48,32},{1,49},{17,1},{33,17},{49,33},{2,50}... | collective-permute-start | bytes 1179656 | tf_op jit(solution)/shard_map/ppermute | solution.py:96
  20.9 1.0 copy-start.6
  26.8 9.9 %collective-permute-start.3 = (f32[1024,96]{0,1:T(8,128)}, f32[1024,96]{0,1:T(8,128)S(1)}, u32[]{:S(2)}, u32[]{:S(2)}) collective-permute-start(f32[1024,96]{0,1:T(8,128)} %collective-permute-done.1), channel_id=1, source_target_pairs={{0,16},{16,32},{32,48},{48,0},{1,17},{17,33},{33,49},{49,1},{2,18}... | collective-permute-start | bytes 1179656 | tf_op jit(solution)/shard_map/ppermute | solution.py:95
  26.8 9.9 %collective-permute-start.4 = (f32[1024,96]{0,1:T(8,128)}, f32[1024,96]{0,1:T(8,128)S(1)}, u32[]{:S(2)}, u32[]{:S(2)}) collective-permute-start(f32[1024,96]{0,1:T(8,128)} %collective-permute-done.2), channel_id=1, source_target_pairs={{0,48},{16,0},{32,16},{48,32},{1,49},{17,1},{33,17},{49,33},{2,50}... | collective-permute-start | bytes 1179656 | tf_op jit(solution)/shard_map/ppermute | solution.py:96
  29.5 17.6 %copy-start.11 = (f32[2048,768]{1,0:T(8,128)S(1)}, f32[2048,768]{1,0:T(8,128)}, u32[]{:S(2)}) copy-start(f32[2048,768]{1,0:T(8,128)} %param.33) | copy-start | bytes 18874372
  36.8 8.8 %collective-permute-start.5 = (f32[1024,96]{0,1:T(8,128)S(1)}, f32[1024,96]{0,1:T(8,128)S(1)}, u32[]{:S(2)}, u32[]{:S(2)}) collective-permute-start(f32[1024,96]{0,1:T(8,128)S(1)} %collective-permute-done.3), channel_id=1, source_target_pairs={{0,16},{16,32},{32,48},{48,0},{1,17},{17,33},{33,49},{49,1},{2,18}... | collective-permute-start | bytes 1179656 | tf_op jit(solution)/shard_map/ppermute | solution.py:95
  36.8 9.5 %collective-permute-start.6 = (f32[1024,96]{0,1:T(8,128)S(1)}, f32[1024,96]{0,1:T(8,128)S(1)}, u32[]{:S(2)}, u32[]{:S(2)}) collective-permute-start(f32[1024,96]{0,1:T(8,128)S(1)} %collective-permute-done.4), channel_id=1, source_target_pairs={{0,48},{16,0},{32,16},{48,32},{1,49},{17,1},{33,17},{49,33},{2,50}... | collective-permute-start | bytes 1179656 | tf_op jit(solution)/shard_map/ppermute | solution.py:96
  46.3 32.0 %slice-start = ((s8[6291456]{0:T(1024)(128)(4,1)}), s8[4194304]{0:T(1024)(128)(4,1)S(1)}, s32[]{:S(2)}) async-start(s8[6291456]{0:T(1024)(128)(4,1)} %bitcast.199), calls=%async_computation | async-start | bytes 8388608
  47.1 31.2 %slice-start.1 = ((s8[6291456]{0:T(1024)(128)(4,1)}), s8[2097152]{0:T(1024)(128)(4,1)S(1)}, s32[]{:S(2)}) async-start(s8[6291456]{0:T(1024)(128)(4,1)} %bitcast.199), calls=%async_computation.1 | async-start | bytes 4194304
  69.4 4.1 %collective-permute-start.7 = (f32[2,1024]{1,0:T(2,128)S(1)}, f32[2,1024]{1,0:T(2,128)S(1)}, u32[]{:S(2)}, u32[]{:S(2)}) collective-permute-start(f32[2,1024]{1,0:T(2,128)S(1)} %pad_maximum_fusion.4), channel_id=1, source_target_pairs={{0,64},{64,0},{1,65},{65,1},{2,66},{66,2},{3,67},{67,3},{4,68},{68... | collective-permute-start | bytes 24584 | tf_op jit(solution)/shard_map/ppermute | solution.py:39
  73.5 2.6 collective-permute-start.8
  76.1 24.4 %collective-permute-start.9 = (f32[2,1024]{1,0:T(2,128)S(1)}, f32[2,1024]{1,0:T(2,128)S(1)}, u32[]{:S(2)}, u32[]{:S(2)}) collective-permute-start(f32[2,1024]{1,0:T(2,128)S(1)} %pad_maximum_fusion.6), channel_id=1, source_target_pairs={{0,32},{16,48},{32,0},{48,16},{1,33},{17,49},{33,1},{49,17},{2,34}... | collective-permute-start | bytes 24584 | tf_op jit(solution)/shard_map/ppermute | solution.py:39
  100.5 3.2 %copy-start = (f32[2048,1024]{1,0:T(8,128)}, f32[2048,1024]{1,0:T(8,128)S(1)}, u32[]{:S(2)}) copy-start(f32[2048,1024]{1,0:T(8,128)S(1)} %bitcast_multiply_fusion.1) | copy-start | bytes 25165828
  105.6 7.1 %collective-permute-start.10 = (f32[2,2048]{1,0:T(2,128)S(1)}, f32[2,2048]{1,0:T(2,128)S(1)}, u32[]{:S(2)}, u32[]{:S(2)}) collective-permute-start(f32[2,2048]{1,0:T(2,128)S(1)} %pad_maximum_fusion), channel_id=1, source_target_pairs={{0,1},{1,0},{2,3},{3,2},{4,5},{5,4},{6,7},{7,6},{8,9},{9,8},{10,11... | collective-permute-start | bytes 49160 | tf_op jit(solution)/shard_map/ppermute | solution.py:39
  112.8 2.7 collective-permute-start.11
  116.1 2.7 collective-permute-start.12
  119.4 5.8 %copy-start.7 = (f32[1,2048]{1,0:T(1,128)}, f32[1,2048]{1,0:T(1,128)S(1)}, u32[]{:S(2)}) copy-start(f32[1,2048]{1,0:T(1,128)S(1)} %get-tuple-element.214) | copy-start | bytes 24580
  119.4 4.6 %collective-permute-start.13 = (f32[2,2048]{1,0:T(2,128)S(1)}, f32[2,2048]{1,0:T(2,128)S(1)}, u32[]{:S(2)}, u32[]{:S(2)}) collective-permute-start(f32[2,2048]{1,0:T(2,128)S(1)} %pad_maximum_fusion.3), channel_id=1, source_target_pairs={{0,8},{4,12},{8,0},{12,4},{1,9},{5,13},{9,1},{13,5},{2,10},{6,14},... | collective-permute-start | bytes 49160 | tf_op jit(solution)/shard_map/ppermute | solution.py:39
  149.1 2.7 copy-start.1
  151.8 9.2 %collective-permute-start.14 = (f32[1024,768]{1,0:T(8,128)S(1)}, f32[1024,768]{1,0:T(8,128)}, u32[]{:S(2)}, u32[]{:S(2)}) collective-permute-start(f32[1024,768]{1,0:T(8,128)S(1)} %dynamic-slice_bitcast_fusion), channel_id=1, source_target_pairs={{0,1},{1,0},{2,3},{3,2},{4,5},{5,4},{6,7},{7,6},{8,9},{9,8},{10,11... | collective-permute-start | bytes 9437192 | tf_op jit(solution)/shard_map/ppermute | solution.py:62
  165.2 10.9 %collective-permute-start.18 = (f32[128,768]{1,0:T(8,128)}, f32[128,768]{1,0:T(8,128)S(1)}, u32[]{:S(2)}, u32[]{:S(2)}) collective-permute-start(f32[128,768]{1,0:T(8,128)} %dynamic-slice_bitcast_fusion.1), channel_id=1, source_target_pairs={{0,12},{4,0},{8,4},{12,8},{1,13},{5,1},{9,5},{13,9},{2,14},{6,2},{... | collective-permute-start | bytes 1179656 | tf_op jit(solution)/shard_map/ppermute | solution.py:67
  168.5 11.8 %collective-permute-start.15 = (f32[128,768]{1,0:T(8,128)}, f32[128,768]{1,0:T(8,128)}, u32[]{:S(2)}, u32[]{:S(2)}) collective-permute-start(f32[128,768]{1,0:T(8,128)} %dynamic-slice_bitcast_fusion.2), channel_id=1, source_target_pairs={{0,4},{4,8},{8,12},{12,0},{1,5},{5,9},{9,13},{13,1},{2,6},{6,10},{... | collective-permute-start | bytes 1179656 | tf_op jit(solution)/shard_map/ppermute | solution.py:66
  176.9 10.8 %collective-permute-start.19 = (f32[128,768]{1,0:T(8,128)}, f32[128,768]{1,0:T(8,128)}, u32[]{:S(2)}, u32[]{:S(2)}) collective-permute-start(f32[128,768]{1,0:T(8,128)} %bitcast_add_fusion.3), channel_id=1, source_target_pairs={{0,12},{4,0},{8,4},{12,8},{1,13},{5,1},{9,5},{13,9},{2,14},{6,2},{... | collective-permute-start | bytes 1179656 | tf_op jit(solution)/shard_map/ppermute | solution.py:67
  182.0 10.7 %collective-permute-start.16 = (f32[128,768]{1,0:T(8,128)}, f32[128,768]{1,0:T(8,128)}, u32[]{:S(2)}, u32[]{:S(2)}) collective-permute-start(f32[128,768]{1,0:T(8,128)} %bitcast_add_fusion.6), channel_id=1, source_target_pairs={{0,4},{4,8},{8,12},{12,0},{1,5},{5,9},{9,13},{13,1},{2,6},{6,10},{... | collective-permute-start | bytes 1179656 | tf_op jit(solution)/shard_map/ppermute | solution.py:66
  188.8 9.8 %collective-permute-start.20 = (f32[128,768]{1,0:T(8,128)S(1)}, f32[128,768]{1,0:T(8,128)}, u32[]{:S(2)}, u32[]{:S(2)}) collective-permute-start(f32[128,768]{1,0:T(8,128)S(1)} %bitcast_add_fusion.2), channel_id=1, source_target_pairs={{0,12},{4,0},{8,4},{12,8},{1,13},{5,1},{9,5},{13,9},{2,14},{6,2},{... | collective-permute-start | bytes 1179656 | tf_op jit(solution)/shard_map/ppermute | solution.py:67
  194.5 9.7 %collective-permute-start.17 = (f32[128,768]{1,0:T(8,128)}, f32[128,768]{1,0:T(8,128)}, u32[]{:S(2)}, u32[]{:S(2)}) collective-permute-start(f32[128,768]{1,0:T(8,128)} %bitcast_add_fusion.5), channel_id=1, source_target_pairs={{0,4},{4,8},{8,12},{12,0},{1,5},{5,9},{9,13},{13,1},{2,6},{6,10},{... | collective-permute-start | bytes 1179656 | tf_op jit(solution)/shard_map/ppermute | solution.py:66
  205.2 18.1 %copy-start.9 = (s32[4]{0:T(128)S(1)}, s32[4]{0:T(128)}, u32[]{:S(2)}) copy-start(s32[4]{0:T(128)} %constant.483.clone.1) | copy-start | bytes 52
  205.3 7.4 %collective-permute-start.21 = (f32[128,768]{1,0:T(8,128)S(1)}, f32[128,768]{1,0:T(8,128)S(1)}, u32[]{:S(2)}, u32[]{:S(2)}) collective-permute-start(f32[128,768]{1,0:T(8,128)S(1)} %fusion.11), channel_id=1, source_target_pairs={{0,2},{2,0},{1,3},{3,1},{4,6},{6,4},{5,7},{7,5},{8,10},{10,8},{9,1... | collective-permute-start | bytes 1179656 | tf_op jit(solution)/shard_map/ppermute | solution.py:69
  212.8 12.8 %copy-start.2 = (f32[128,768]{1,0:T(8,128)}, f32[128,768]{1,0:T(8,128)S(1)}, u32[]{:S(2)}) copy-start(f32[128,768]{1,0:T(8,128)S(1)} %fusion.15) | copy-start | bytes 1179652
  212.8 7.6 %collective-permute-start.22 = (f32[128,768]{1,0:T(8,128)S(1)}, f32[128,768]{1,0:T(8,128)S(1)}, u32[]{:S(2)}, u32[]{:S(2)}) collective-permute-start(f32[128,768]{1,0:T(8,128)S(1)} %fusion.15), channel_id=1, source_target_pairs={{0,2},{2,0},{1,3},{3,1},{4,6},{6,4},{5,7},{7,5},{8,10},{10,8},{9,1... | collective-permute-start | bytes 1179656 | tf_op jit(solution)/shard_map/ppermute | solution.py:72
  220.6 7.9 %collective-permute-start.23 = (f32[128,768]{1,0:T(8,128)S(1)}, f32[128,768]{1,0:T(8,128)S(1)}, u32[]{:S(2)}, u32[]{:S(2)}) collective-permute-start(f32[128,768]{1,0:T(8,128)S(1)} %get-tuple-element.205), channel_id=1, source_target_pairs={{0,4},{4,8},{8,12},{12,0},{1,5},{5,9},{9,13},{13,1},{2,6},{6,10},{... | collective-permute-start | bytes 1179656 | tf_op jit(solution)/shard_map/ppermute | solution.py:77
  220.7 7.8 %collective-permute-start.24 = (f32[128,768]{1,0:T(8,128)S(1)}, f32[128,768]{1,0:T(8,128)S(1)}, u32[]{:S(2)}, u32[]{:S(2)}) collective-permute-start(f32[128,768]{1,0:T(8,128)S(1)} %get-tuple-element.204), channel_id=1, source_target_pairs={{0,12},{4,0},{8,4},{12,8},{1,13},{5,1},{9,5},{13,9},{2,14},{6,2},{... | collective-permute-start | bytes 1179656 | tf_op jit(solution)/shard_map/ppermute | solution.py:78
  225.6 1.0 copy-start.3
  228.5 10.0 %collective-permute-start.25 = (f32[128,768]{1,0:T(8,128)S(1)}, f32[128,768]{1,0:T(8,128)S(1)}, u32[]{:S(2)}, u32[]{:S(2)}) collective-permute-start(f32[128,768]{1,0:T(8,128)S(1)} %collective-permute-done.23), channel_id=1, source_target_pairs={{0,4},{4,8},{8,12},{12,0},{1,5},{5,9},{9,13},{13,1},{2,6},{6,10},{... | collective-permute-start | bytes 1179656 | tf_op jit(solution)/shard_map/ppermute | solution.py:77
  228.5 10.0 %collective-permute-start.26 = (f32[128,768]{1,0:T(8,128)S(1)}, f32[128,768]{1,0:T(8,128)S(1)}, u32[]{:S(2)}, u32[]{:S(2)}) collective-permute-start(f32[128,768]{1,0:T(8,128)S(1)} %collective-permute-done.24), channel_id=1, source_target_pairs={{0,12},{4,0},{8,4},{12,8},{1,13},{5,1},{9,5},{13,9},{2,14},{6,2},{... | collective-permute-start | bytes 1179656 | tf_op jit(solution)/shard_map/ppermute | solution.py:78
  238.5 11.1 %collective-permute-start.27 = (f32[128,768]{1,0:T(8,128)S(1)}, f32[128,768]{1,0:T(8,128)S(1)}, u32[]{:S(2)}, u32[]{:S(2)}) collective-permute-start(f32[128,768]{1,0:T(8,128)S(1)} %collective-permute-done.25), channel_id=1, source_target_pairs={{0,4},{4,8},{8,12},{12,0},{1,5},{5,9},{9,13},{13,1},{2,6},{6,10},{... | collective-permute-start | bytes 1179656 | tf_op jit(solution)/shard_map/ppermute | solution.py:77
  238.5 11.7 %collective-permute-start.28 = (f32[128,768]{1,0:T(8,128)S(1)}, f32[128,768]{1,0:T(8,128)S(1)}, u32[]{:S(2)}, u32[]{:S(2)}) collective-permute-start(f32[128,768]{1,0:T(8,128)S(1)} %collective-permute-done.26), channel_id=1, source_target_pairs={{0,12},{4,0},{8,4},{12,8},{1,13},{5,1},{9,5},{13,9},{2,14},{6,2},{... | collective-permute-start | bytes 1179656 | tf_op jit(solution)/shard_map/ppermute | solution.py:78
  250.9 14.2 %collective-permute-start.29 = (f32[1024,768]{1,0:T(8,128)S(1)}, f32[1024,768]{1,0:T(8,128)}, u32[]{:S(2)}, u32[]{:S(2)}) collective-permute-start(f32[1024,768]{1,0:T(8,128)S(1)} %bitcast.161), channel_id=1, source_target_pairs={{0,1},{1,0},{2,3},{3,2},{4,5},{5,4},{6,7},{7,6},{8,9},{9,8},{10,11... | collective-permute-start | bytes 9437192 | tf_op jit(solution)/shard_map/ppermute | solution.py:82

commit v5 on v4

--- a/solution.py
+++ b/solution.py
@@ -9,7 +9,7 @@
 
 IMG = ("zh", "y")
 CAP = ("x", "zl", "core")
-CHUNKS = 1
+CHUNKS = 4
 
 
 def similar(query_factor, target_factor):

time: 275 us -> 281 us (1.022)
  starting transfers between devices: 58.4 us -> 120 us
  waiting for transfers between devices: 90.9 us -> 35.6 us
  local copies, waits for them, and re-layouts: 10.6 us -> 2.94 us
  other arithmetic: 43.8 us -> 49.9 us
    ppermute x3 -> x12, starting transfers between devices: 9.27 us -> 32.5 us  [reduce_rows(): lax.ppermute(left, 'x', ring('x', x_size, -1))]
    ppermute x3 -> x12, starting transfers between devices: 8.29 us -> 31.4 us  [reduce_rows(): left = lax.ppermute(left, 'x', ring('x', x_size, -1))]
    ppermute x3 -> x12, waiting for transfers between devices: 17.3 us -> 0.03 us  [reduce_rows(): lax.ppermute(left, 'x', ring('x', x_size, -1))]
    ppermute x3 -> x12, waiting for transfers between devices: 14 us -> 0.03 us  [reduce_rows(): right = lax.ppermute(right, 'x', ring('x', x_size, 1))]
    ppermute x1 -> x4, starting transfers between devices: 8.79 us -> 15.9 us  [reduce_rows(): other = lax.ppermute(held, 'core', swap)]
    ppermute x1 -> x4, waiting for transfers between devices: 6.43 us -> 0.01 us  [reduce_rows(): mine = pick(block, z) + lax.ppermute(pick(block, 1 - z), 'zl', swap)]
    scatter x3 -> x12, other arithmetic: 2.09 us -> 8.25 us  [reduce_rows(): gathered = gathered.at[(p + s + 1) % x_size, 1].set(left)]
    unnamed x28 -> x18, local copies, waits for them, and re-layouts: 6.38 us -> 0.64 us
  transfers between devices with their start and end apart: 30 -> 78, of which waited for: 22 -> 16; matrix products, arithmetic and copies ran while one was open for 18% -> 27% of each run, Pallas kernels for 0% -> 0%
where the time goes in v5:
time: 281 us; the launch traced here: 277 us
  starting transfers between devices  120 us (43%)
  matrix products  67.8 us (24%)
  other arithmetic  49.9 us (18%)
  waiting for transfers between devices  35.6 us (13%)
  local copies, waits for them, and re-layouts  2.94 us (1%)
    dot_general x2, matrix products, similar(): lax.dot_general(query_factor, target_factor, (((1,), (0,)), ((), ())), pr...  44.7 us
    ppermute x12, starting transfers between devices, reduce_rows(): lax.ppermute(left, 'x', ring('x', x_size, -1))  32.5 us
    ppermute x12, starting transfers between devices, reduce_rows(): left = lax.ppermute(left, 'x', ring('x', x_size, -1))  31.4 us
    dot_general x4, matrix products, rescaled_affinity(): lax.dot_general(weights, features, (((1,), (1,)), ((), ())), precision=la...  23.1 us
    ppermute x4, starting transfers between devices, reduce_rows(): other = lax.ppermute(held, 'core', swap)  15.9 us
    ppermute x7, starting transfers between devices, merge_peaks(): other = lax.ppermute(pair, axis, [(j, j ^ dist) for j in range(size)])  15 us
    ppermute x3, waiting for transfers between devices, gather_features(): right = lax.ppermute(right, 'y', ring('y', y_size, 1))  12.4 us
    ppermute x7, waiting for transfers between devices, merge_peaks(): other = lax.ppermute(pair, axis, [(j, j ^ dist) for j in range(size)])  8.56 us
  transfers between devices with their start and end apart: 78, of which 16 were waited for; matrix products, arithmetic and copies ran while one was open for 27% of the time, Pallas kernels for 0%

profile of v5, /device:TPU:1, one launch (start us, length us, event | category | flops | bytes accessed | tf_op | source)
XLA Modules:
  0.0 277.5 jit_solution(4489652137227256801)
XLA Ops:
  0.0 4.4 %collective-permute-start = (f32[1024,96]{0,1:T(8,128)}, f32[1024,96]{0,1:T(8,128)S(1)}, u32[]{:S(2)}, u32[]{:S(2)}) collective-permute-start(f32[1024,96]{0,1:T(8,128)} %param.74), channel_id=1, source_target_pairs={{0,64},{64,0},{1,65},{65,1},{2,66},{66,2},{3,67},{67,3},{4,68},{68... | collective-permute-start | bytes 1179656 | tf_op jit(solution)/shard_map/ppermute | solution.py:90
  4.4 1.4 and_reduce_fusion.10
  5.9 7.6 %collective-permute-done = f32[1024,96]{0,1:T(8,128)S(1)} collective-permute-done((f32[1024,96]{0,1:T(8,128)}, f32[1024,96]{0,1:T(8,128)S(1)}, u32[]{:S(2)}, u32[]{:S(2)}) %collective-permute-start) | collective-permute-done | bytes 393248 | tf_op jit(solution)/shard_map/ppermute | solution.py:90
  13.5 1.4 maximum_select_fusion.5
  15.8 1.3 collective-permute-start.1
  17.1 1.4 collective-permute-start.2
  22.6 4.2 %collective-permute-done.1 = f32[1024,96]{0,1:T(8,128)} collective-permute-done((f32[1024,96]{0,1:T(8,128)}, f32[1024,96]{0,1:T(8,128)}, u32[]{:S(2)}, u32[]{:S(2)}) %collective-permute-start.1) | collective-permute-done | bytes 393248 | tf_op jit(solution)/shard_map/ppermute | solution.py:95
  26.8 2.7 collective-permute-start.4
  29.5 1.9 fusion.28
  31.4 1.8 fusion.27
  33.1 3.6 %collective-permute-done.3 = f32[1024,96]{0,1:T(8,128)S(1)} collective-permute-done((f32[1024,96]{0,1:T(8,128)}, f32[1024,96]{0,1:T(8,128)S(1)}, u32[]{:S(2)}, u32[]{:S(2)}) %collective-permute-start.3) | collective-permute-done | bytes 393248 | tf_op jit(solution)/shard_map/ppermute | solution.py:95
  36.8 2.8 %collective-permute-start.6 = (f32[1024,96]{0,1:T(8,128)S(1)}, f32[1024,96]{0,1:T(8,128)S(1)}, u32[]{:S(2)}, u32[]{:S(2)}) collective-permute-start(f32[1024,96]{0,1:T(8,128)S(1)} %collective-permute-done.4), channel_id=1, source_target_pairs={{0,48},{16,0},{32,16},{48,32},{1,49},{17,1},{33,17},{49,33},{2,50}... | collective-permute-start | bytes 1179656 | tf_op jit(solution)/shard_map/ppermute | solution.py:96
  41.0 4.6 %collective-permute-done.5 = f32[1024,96]{0,1:T(8,128)S(1)} collective-permute-done((f32[1024,96]{0,1:T(8,128)S(1)}, f32[1024,96]{0,1:T(8,128)S(1)}, u32[]{:S(2)}, u32[]{:S(2)}) %collective-permute-start.5) | collective-permute-done | bytes 393248 | tf_op jit(solution)/shard_map/ppermute | solution.py:95
  47.2 22.5 %fusion = (f32[1024]{0:T(1024)S(1)}, f32[1024,2048]{0,1:T(8,128)S(1)}) fusion(f32[768,1024]{1,0:T(8,128)S(1)} %bitcast.386, f32[2048,768]{1,0:T(8,128)S(1)} %copy-done.6), kind=kOutput, calls=%fused_computation.4 | convolution fusion | flops 19331547136 | bytes 17829888 | tf_op jit(solution)/shard_map/dot_general | solution.py:16
  69.7 1.4 exponential_reduce_fusion
  71.1 1.8 collective-permute-start.7
  72.9 2.3 collective-permute-done.7
  75.4 2.5 collective-permute-done.8
  77.9 2.4 collective-permute-start.9
  80.3 22.2 %bitcast_multiply_fusion.1 = f32[2048,1024]{1,0:T(8,128)S(1)} fusion(f32[768,1024]{1,0:T(8,128)S(1)} %bitcast.387, f32[2048,768]{1,0:T(8,128)S(1)} %bitcast.455), kind=kOutput, calls=%fused_computation.1 | convolution fusion | flops 19329449984 | bytes 17825792 | tf_op jit(solution)/shard_map/dot_general | solution.py:16
  103.2 4.2 %fusion.101 = (f32[2048]{0:T(1024)S(1)}, f32[2048,1024]{1,0:T(8,128)}) fusion(f32[2048]{0:T(1024)S(1)} %subtract_reduce_fusion, f32[2048,1024]{1,0:T(8,128)S(1)} %bitcast_multiply_fusion.1, f32[1024]{0:T(1024)S(1)} %bitcast.445), kind=kLoop, calls=%fused_computation.288 | loop fusion | flops 6289408 | bytes 16797696 | tf_op jit(solution)/shard_map/reduce_sum | solution.py:117
  107.4 6.3 %collective-permute-start.10 = (f32[2,2048]{1,0:T(2,128)S(1)}, f32[2,2048]{1,0:T(2,128)S(1)}, u32[]{:S(2)}, u32[]{:S(2)}) collective-permute-start(f32[2,2048]{1,0:T(2,128)S(1)} %pad_maximum_fusion.1), channel_id=1, source_target_pairs={{0,1},{1,0},{2,3},{3,2},{4,5},{5,4},{6,7},{7,6},{8,9},{9,8},{10,11... | collective-permute-start | bytes 49160 | tf_op jit(solution)/shard_map/ppermute | solution.py:39
  115.5 1.8 collective-permute-done.11
  120.1 3.0 %collective-permute-start.13 = (f32[2,2048]{1,0:T(2,128)S(1)}, f32[2,2048]{1,0:T(2,128)S(1)}, u32[]{:S(2)}, u32[]{:S(2)}) collective-permute-start(f32[2,2048]{1,0:T(2,128)S(1)} %pad_maximum_fusion.4), channel_id=1, source_target_pairs={{0,8},{4,12},{8,0},{12,4},{1,9},{5,13},{9,1},{13,5},{2,10},{6,14},... | collective-permute-start | bytes 49160 | tf_op jit(solution)/shard_map/ppermute | solution.py:39
  124.5 7.1 %fusion.9 = f32[512,768]{1,0:T(8,128)S(1)} fusion(f32[768,1024]{1,0:T(8,128)S(1)} %bitcast.388, f32[2048,1024]{1,0:T(8,128)} %get-tuple-element.444, f32[512]{0:T(512)S(1)} %get-tuple-element.483), kind=kOutput, calls=%fused_computation.19 | convolution fusion | flops 4832231424 | bytes 6817792 | tf_op jit(solution)/shard_map/dot_general | solution.py:27
  131.7 3.9 %collective-permute-start.14 = (f32[256,768]{1,0:T(8,128)S(1)}, f32[256,768]{1,0:T(8,128)S(1)}, u32[]{:S(2)}, u32[]{:S(2)}) collective-permute-start(f32[256,768]{1,0:T(8,128)S(1)} %dynamic-slice_bitcast_fusion.3), channel_id=1, source_target_pairs={{0,1},{1,0},{2,3},{3,2},{4,5},{5,4},{6,7},{7,6},{8,9},{9,8},{10,11... | collective-permute-start | bytes 2359304 | tf_op jit(solution)/shard_map/ppermute | solution.py:62
  135.5 5.3 %fusion.12 = f32[512,768]{1,0:T(8,128)S(1)} fusion(f32[768,1024]{1,0:T(8,128)S(1)} %bitcast.389, f32[2048,1024]{1,0:T(8,128)S(1)} %copy-done, f32[512]{0:T(512)S(1)} %get-tuple-element.486), kind=kOutput, calls=%fused_computation.20 | convolution fusion | flops 4832231424 | bytes 6817792 | tf_op jit(solution)/shard_map/dot_general | solution.py:27
  141.5 5.3 %fusion.15 = f32[512,768]{1,0:T(8,128)S(1)} fusion(f32[768,1024]{1,0:T(8,128)S(1)} %bitcast.390, f32[2048,1024]{1,0:T(8,128)S(1)} %copy-done, f32[512]{0:T(512)S(1)} %get-tuple-element.485), kind=kOutput, calls=%fused_computation.21 | convolution fusion | flops 4832231424 | bytes 6817792 | tf_op jit(solution)/shard_map/dot_general | solution.py:27
  147.5 5.3 %fusion.18 = f32[512,768]{1,0:T(8,128)S(1)} fusion(f32[768,1024]{1,0:T(8,128)S(1)} %bitcast.391, f32[2048,1024]{1,0:T(8,128)S(1)} %copy-done, f32[512]{0:T(512)S(1)} %get-tuple-element.484), kind=kOutput, calls=%fused_computation.22 | convolution fusion | flops 4832231424 | bytes 6817792 | tf_op jit(solution)/shard_map/dot_general | solution.py:27
  153.3 2.7 collective-permute-start.18
  156.3 2.7 collective-permute-start.34
  159.3 2.7 collective-permute-start.50
  162.4 2.7 collective-permute-start.66
  165.3 2.7 collective-permute-start.19
  168.2 2.7 collective-permute-start.35
  171.0 2.7 collective-permute-start.51
  174.1 2.5 collective-permute-start.67
  176.8 2.7 collective-permute-start.20
  179.6 2.7 collective-permute-start.36
  182.5 2.7 collective-permute-start.52
  185.4 2.7 collective-permute-start.68
  188.5 1.5 collective-permute-start.37
  190.0 1.3 collective-permute-done.49
  191.5 2.2 collective-permute-done.65
  194.0 1.5 collective-permute-start.22
  195.8 1.7 collective-permute-start.54
  199.0 2.7 collective-permute-start.24
  203.1 1.4 collective-permute-start.40
  208.1 2.7 collective-permute-start.56
  212.3 2.7 collective-permute-start.72
  216.5 2.7 collective-permute-start.26
  220.7 2.7 collective-permute-start.42
  224.9 2.7 collective-permute-start.58
  228.9 2.7 collective-permute-start.74
  233.2 2.7 collective-permute-start.28
  237.3 2.7 collective-permute-start.44
  241.5 2.7 collective-permute-start.60
  245.6 2.7 collective-permute-start.76
  249.0 15.1 %collective-permute-start.29 = (f32[256,768]{1,0:T(8,128)S(1)}, f32[256,768]{1,0:T(8,128)}, u32[]{:S(2)}, u32[]{:S(2)}) collective-permute-start(f32[256,768]{1,0:T(8,128)S(1)} %bitcast.406), channel_id=1, source_target_pairs={{0,1},{1,0},{2,3},{3,2},{4,5},{5,4},{6,7},{7,6},{8,9},{9,8},{10,11... | collective-permute-start | bytes 2359304 | tf_op jit(solution)/shard_map/ppermute | solution.py:82
  268.2 1.5 maximum_select_fusion
  269.7 1.5 maximum_select_fusion.1
  271.3 1.5 maximum_select_fusion.2
  272.8 1.5 maximum_select_fusion.3
  274.3 2.9 %pad_maximum_fusion = f32[2048,768]{1,0:T(8,128)} fusion(f32[512,768]{1,0:T(8,128)S(1)} %bitcast.403, f32[512,768]{1,0:T(8,128)S(1)} %bitcast.402, f32[512,768]{1,0:T(8,128)S(1)} %bitcast.401, f32[512,768]{1,0:T(8,128)S(1)} %bitcast.400), kind=kLoop, calls=%fused_computation.6 | loop fusion | flops 4718592 | bytes 12582912 | tf_op jit(solution)/shard_map/concatenate | solution.py:127
  (251 shorter events, 43.2 us)
Async XLA Ops:
  0.0 13.5 %collective-permute-start = (f32[1024,96]{0,1:T(8,128)}, f32[1024,96]{0,1:T(8,128)S(1)}, u32[]{:S(2)}, u32[]{:S(2)}) collective-permute-start(f32[1024,96]{0,1:T(8,128)} %param.74), channel_id=1, source_target_pairs={{0,64},{64,0},{1,65},{65,1},{2,66},{66,2},{3,67},{67,3},{4,68},{68... | collective-permute-start | bytes 1179656 | tf_op jit(solution)/shard_map/ppermute | solution.py:90
  15.8 11.0 %collective-permute-start.1 = (f32[1024,96]{0,1:T(8,128)}, f32[1024,96]{0,1:T(8,128)}, u32[]{:S(2)}, u32[]{:S(2)}) collective-permute-start(f32[1024,96]{0,1:T(8,128)} %get-tuple-element.458), channel_id=1, source_target_pairs={{0,16},{16,32},{32,48},{48,0},{1,17},{17,33},{33,49},{49,1},{2,18}... | collective-permute-start | bytes 1179656 | tf_op jit(solution)/shard_map/ppermute | solution.py:95
  17.1 9.7 %collective-permute-start.2 = (f32[1024,96]{0,1:T(8,128)}, f32[1024,96]{0,1:T(8,128)}, u32[]{:S(2)}, u32[]{:S(2)}) collective-permute-start(f32[1024,96]{0,1:T(8,128)} %get-tuple-element.457), channel_id=1, source_target_pairs={{0,48},{16,0},{32,16},{48,32},{1,49},{17,1},{33,17},{49,33},{2,50}... | collective-permute-start | bytes 1179656 | tf_op jit(solution)/shard_map/ppermute | solution.py:96
  26.8 9.9 %collective-permute-start.3 = (f32[1024,96]{0,1:T(8,128)}, f32[1024,96]{0,1:T(8,128)S(1)}, u32[]{:S(2)}, u32[]{:S(2)}) collective-permute-start(f32[1024,96]{0,1:T(8,128)} %collective-permute-done.1), channel_id=1, source_target_pairs={{0,16},{16,32},{32,48},{48,0},{1,17},{17,33},{33,49},{49,1},{2,18}... | collective-permute-start | bytes 1179656 | tf_op jit(solution)/shard_map/ppermute | solution.py:95
  26.8 9.9 %collective-permute-start.4 = (f32[1024,96]{0,1:T(8,128)}, f32[1024,96]{0,1:T(8,128)S(1)}, u32[]{:S(2)}, u32[]{:S(2)}) collective-permute-start(f32[1024,96]{0,1:T(8,128)} %collective-permute-done.2), channel_id=1, source_target_pairs={{0,48},{16,0},{32,16},{48,32},{1,49},{17,1},{33,17},{49,33},{2,50}... | collective-permute-start | bytes 1179656 | tf_op jit(solution)/shard_map/ppermute | solution.py:96
  36.8 8.8 %collective-permute-start.5 = (f32[1024,96]{0,1:T(8,128)S(1)}, f32[1024,96]{0,1:T(8,128)S(1)}, u32[]{:S(2)}, u32[]{:S(2)}) collective-permute-start(f32[1024,96]{0,1:T(8,128)S(1)} %collective-permute-done.3), channel_id=1, source_target_pairs={{0,16},{16,32},{32,48},{48,0},{1,17},{17,33},{33,49},{49,1},{2,18}... | collective-permute-start | bytes 1179656 | tf_op jit(solution)/shard_map/ppermute | solution.py:95
  36.8 9.5 %collective-permute-start.6 = (f32[1024,96]{0,1:T(8,128)S(1)}, f32[1024,96]{0,1:T(8,128)S(1)}, u32[]{:S(2)}, u32[]{:S(2)}) collective-permute-start(f32[1024,96]{0,1:T(8,128)S(1)} %collective-permute-done.4), channel_id=1, source_target_pairs={{0,48},{16,0},{32,16},{48,32},{1,49},{17,1},{33,17},{49,33},{2,50}... | collective-permute-start | bytes 1179656 | tf_op jit(solution)/shard_map/ppermute | solution.py:96
  77.9 24.6 %collective-permute-start.9 = (f32[2,1024]{1,0:T(2,128)S(1)}, f32[2,1024]{1,0:T(2,128)S(1)}, u32[]{:S(2)}, u32[]{:S(2)}) collective-permute-start(f32[2,1024]{1,0:T(2,128)S(1)} %pad_maximum_fusion.7), channel_id=1, source_target_pairs={{0,32},{16,48},{32,0},{48,16},{1,33},{17,49},{33,1},{49,17},{2,34}... | collective-permute-start | bytes 24584 | tf_op jit(solution)/shard_map/ppermute | solution.py:39
  107.4 7.1 %collective-permute-start.10 = (f32[2,2048]{1,0:T(2,128)S(1)}, f32[2,2048]{1,0:T(2,128)S(1)}, u32[]{:S(2)}, u32[]{:S(2)}) collective-permute-start(f32[2,2048]{1,0:T(2,128)S(1)} %pad_maximum_fusion.1), channel_id=1, source_target_pairs={{0,1},{1,0},{2,3},{3,2},{4,5},{5,4},{6,7},{7,6},{8,9},{9,8},{10,11... | collective-permute-start | bytes 49160 | tf_op jit(solution)/shard_map/ppermute | solution.py:39
  131.7 21.5 %collective-permute-start.14 = (f32[256,768]{1,0:T(8,128)S(1)}, f32[256,768]{1,0:T(8,128)S(1)}, u32[]{:S(2)}, u32[]{:S(2)}) collective-permute-start(f32[256,768]{1,0:T(8,128)S(1)} %dynamic-slice_bitcast_fusion.3), channel_id=1, source_target_pairs={{0,1},{1,0},{2,3},{3,2},{4,5},{5,4},{6,7},{7,6},{8,9},{9,8},{10,11... | collective-permute-start | bytes 2359304 | tf_op jit(solution)/shard_map/ppermute | solution.py:62
  141.0 15.1 %collective-permute-start.30 = (f32[256,768]{1,0:T(8,128)S(1)}, f32[256,768]{1,0:T(8,128)S(1)}, u32[]{:S(2)}, u32[]{:S(2)}) collective-permute-start(f32[256,768]{1,0:T(8,128)S(1)} %dynamic-slice_bitcast_fusion.2), channel_id=1, source_target_pairs={{0,1},{1,0},{2,3},{3,2},{4,5},{5,4},{6,7},{7,6},{8,9},{9,8},{10,11... | collective-permute-start | bytes 2359304 | tf_op jit(solution)/shard_map/ppermute | solution.py:62
  146.9 12.1 %collective-permute-start.46 = (f32[256,768]{1,0:T(8,128)S(1)}, f32[256,768]{1,0:T(8,128)S(1)}, u32[]{:S(2)}, u32[]{:S(2)}) collective-permute-start(f32[256,768]{1,0:T(8,128)S(1)} %dynamic-slice_bitcast_fusion.1), channel_id=1, source_target_pairs={{0,1},{1,0},{2,3},{3,2},{4,5},{5,4},{6,7},{7,6},{8,9},{9,8},{10,11... | collective-permute-start | bytes 2359304 | tf_op jit(solution)/shard_map/ppermute | solution.py:62
  152.9 6.4 %collective-permute-start.62 = (f32[256,768]{1,0:T(8,128)S(1)}, f32[256,768]{1,0:T(8,128)S(1)}, u32[]{:S(2)}, u32[]{:S(2)}) collective-permute-start(f32[256,768]{1,0:T(8,128)S(1)} %dynamic-slice_bitcast_fusion), channel_id=1, source_target_pairs={{0,1},{1,0},{2,3},{3,2},{4,5},{5,4},{6,7},{7,6},{8,9},{9,8},{10,11... | collective-permute-start | bytes 2359304 | tf_op jit(solution)/shard_map/ppermute | solution.py:62
  153.3 9.0 %collective-permute-start.18 = (f32[32,768]{1,0:T(8,128)S(1)}, f32[32,768]{1,0:T(8,128)S(1)}, u32[]{:S(2)}, u32[]{:S(2)}) collective-permute-start(f32[32,768]{1,0:T(8,128)S(1)} %dynamic-slice_bitcast_fusion.10), channel_id=1, source_target_pairs={{0,12},{4,0},{8,4},{12,8},{1,13},{5,1},{9,5},{13,9},{2,14},{6,2},{... | collective-permute-start | bytes 294920 | tf_op jit(solution)/shard_map/ppermute | solution.py:67
  156.0 6.4 %collective-permute-start.15 = (f32[32,768]{1,0:T(8,128)S(1)}, f32[32,768]{1,0:T(8,128)S(1)}, u32[]{:S(2)}, u32[]{:S(2)}) collective-permute-start(f32[32,768]{1,0:T(8,128)S(1)} %dynamic-slice_bitcast_fusion.11), channel_id=1, source_target_pairs={{0,4},{4,8},{8,12},{12,0},{1,5},{5,9},{9,13},{13,1},{2,6},{6,10},{... | collective-permute-start | bytes 294920 | tf_op jit(solution)/shard_map/ppermute | solution.py:66
  156.3 8.9 %collective-permute-start.34 = (f32[32,768]{1,0:T(8,128)S(1)}, f32[32,768]{1,0:T(8,128)S(1)}, u32[]{:S(2)}, u32[]{:S(2)}) collective-permute-start(f32[32,768]{1,0:T(8,128)S(1)} %dynamic-slice_bitcast_fusion.8), channel_id=1, source_target_pairs={{0,12},{4,0},{8,4},{12,8},{1,13},{5,1},{9,5},{13,9},{2,14},{6,2},{... | collective-permute-start | bytes 294920 | tf_op jit(solution)/shard_map/ppermute | solution.py:67
  159.0 6.3 %collective-permute-start.31 = (f32[32,768]{1,0:T(8,128)S(1)}, f32[32,768]{1,0:T(8,128)S(1)}, u32[]{:S(2)}, u32[]{:S(2)}) collective-permute-start(f32[32,768]{1,0:T(8,128)S(1)} %dynamic-slice_bitcast_fusion.9), channel_id=1, source_target_pairs={{0,4},{4,8},{8,12},{12,0},{1,5},{5,9},{9,13},{13,1},{2,6},{6,10},{... | collective-permute-start | bytes 294920 | tf_op jit(solution)/shard_map/ppermute | solution.py:66
  159.3 8.7 %collective-permute-start.50 = (f32[32,768]{1,0:T(8,128)S(1)}, f32[32,768]{1,0:T(8,128)S(1)}, u32[]{:S(2)}, u32[]{:S(2)}) collective-permute-start(f32[32,768]{1,0:T(8,128)S(1)} %dynamic-slice_bitcast_fusion.6), channel_id=1, source_target_pairs={{0,12},{4,0},{8,4},{12,8},{1,13},{5,1},{9,5},{13,9},{2,14},{6,2},{... | collective-permute-start | bytes 294920 | tf_op jit(solution)/shard_map/ppermute | solution.py:67
  162.3 5.8 %collective-permute-start.47 = (f32[32,768]{1,0:T(8,128)S(1)}, f32[32,768]{1,0:T(8,128)S(1)}, u32[]{:S(2)}, u32[]{:S(2)}) collective-permute-start(f32[32,768]{1,0:T(8,128)S(1)} %dynamic-slice_bitcast_fusion.7), channel_id=1, source_target_pairs={{0,4},{4,8},{8,12},{12,0},{1,5},{5,9},{9,13},{13,1},{2,6},{6,10},{... | collective-permute-start | bytes 294920 | tf_op jit(solution)/shard_map/ppermute | solution.py:66
  162.4 8.5 %collective-permute-start.66 = (f32[32,768]{1,0:T(8,128)S(1)}, f32[32,768]{1,0:T(8,128)S(1)}, u32[]{:S(2)}, u32[]{:S(2)}) collective-permute-start(f32[32,768]{1,0:T(8,128)S(1)} %dynamic-slice_bitcast_fusion.4), channel_id=1, source_target_pairs={{0,12},{4,0},{8,4},{12,8},{1,13},{5,1},{9,5},{13,9},{2,14},{6,2},{... | collective-permute-start | bytes 294920 | tf_op jit(solution)/shard_map/ppermute | solution.py:67
  165.2 5.8 %collective-permute-start.63 = (f32[32,768]{1,0:T(8,128)S(1)}, f32[32,768]{1,0:T(8,128)S(1)}, u32[]{:S(2)}, u32[]{:S(2)}) collective-permute-start(f32[32,768]{1,0:T(8,128)S(1)} %dynamic-slice_bitcast_fusion.5), channel_id=1, source_target_pairs={{0,4},{4,8},{8,12},{12,0},{1,5},{5,9},{9,13},{13,1},{2,6},{6,10},{... | collective-permute-start | bytes 294920 | tf_op jit(solution)/shard_map/ppermute | solution.py:66
  165.3 8.5 %collective-permute-start.19 = (f32[32,768]{1,0:T(8,128)S(1)}, f32[32,768]{1,0:T(8,128)S(1)}, u32[]{:S(2)}, u32[]{:S(2)}) collective-permute-start(f32[32,768]{1,0:T(8,128)S(1)} %bitcast_add_fusion.24), channel_id=1, source_target_pairs={{0,12},{4,0},{8,4},{12,8},{1,13},{5,1},{9,5},{13,9},{2,14},{6,2},{... | collective-permute-start | bytes 294920 | tf_op jit(solution)/shard_map/ppermute | solution.py:67
  168.0 6.1 %collective-permute-start.16 = (f32[32,768]{1,0:T(8,128)S(1)}, f32[32,768]{1,0:T(8,128)S(1)}, u32[]{:S(2)}, u32[]{:S(2)}) collective-permute-start(f32[32,768]{1,0:T(8,128)S(1)} %bitcast_add_fusion.27), channel_id=1, source_target_pairs={{0,4},{4,8},{8,12},{12,0},{1,5},{5,9},{9,13},{13,1},{2,6},{6,10},{... | collective-permute-start | bytes 294920 | tf_op jit(solution)/shard_map/ppermute | solution.py:66
  168.2 8.5 %collective-permute-start.35 = (f32[32,768]{1,0:T(8,128)S(1)}, f32[32,768]{1,0:T(8,128)S(1)}, u32[]{:S(2)}, u32[]{:S(2)}) collective-permute-start(f32[32,768]{1,0:T(8,128)S(1)} %bitcast_add_fusion.18), channel_id=1, source_target_pairs={{0,12},{4,0},{8,4},{12,8},{1,13},{5,1},{9,5},{13,9},{2,14},{6,2},{... | collective-permute-start | bytes 294920 | tf_op jit(solution)/shard_map/ppermute | solution.py:67
  170.9 5.8 %collective-permute-start.32 = (f32[32,768]{1,0:T(8,128)S(1)}, f32[32,768]{1,0:T(8,128)S(1)}, u32[]{:S(2)}, u32[]{:S(2)}) collective-permute-start(f32[32,768]{1,0:T(8,128)S(1)} %bitcast_add_fusion.21), channel_id=1, source_target_pairs={{0,4},{4,8},{8,12},{12,0},{1,5},{5,9},{9,13},{13,1},{2,6},{6,10},{... | collective-permute-start | bytes 294920 | tf_op jit(solution)/shard_map/ppermute | solution.py:66
  171.0 8.5 %collective-permute-start.51 = (f32[32,768]{1,0:T(8,128)S(1)}, f32[32,768]{1,0:T(8,128)S(1)}, u32[]{:S(2)}, u32[]{:S(2)}) collective-permute-start(f32[32,768]{1,0:T(8,128)S(1)} %bitcast_add_fusion.12), channel_id=1, source_target_pairs={{0,12},{4,0},{8,4},{12,8},{1,13},{5,1},{9,5},{13,9},{2,14},{6,2},{... | collective-permute-start | bytes 294920 | tf_op jit(solution)/shard_map/ppermute | solution.py:67
  173.8 5.8 %collective-permute-start.48 = (f32[32,768]{1,0:T(8,128)S(1)}, f32[32,768]{1,0:T(8,128)S(1)}, u32[]{:S(2)}, u32[]{:S(2)}) collective-permute-start(f32[32,768]{1,0:T(8,128)S(1)} %bitcast_add_fusion.15), channel_id=1, source_target_pairs={{0,4},{4,8},{8,12},{12,0},{1,5},{5,9},{9,13},{13,1},{2,6},{6,10},{... | collective-permute-start | bytes 294920 | tf_op jit(solution)/shard_map/ppermute | solution.py:66
  174.1 8.3 %collective-permute-start.67 = (f32[32,768]{1,0:T(8,128)S(1)}, f32[32,768]{1,0:T(8,128)S(1)}, u32[]{:S(2)}, u32[]{:S(2)}) collective-permute-start(f32[32,768]{1,0:T(8,128)S(1)} %bitcast_add_fusion.6), channel_id=1, source_target_pairs={{0,12},{4,0},{8,4},{12,8},{1,13},{5,1},{9,5},{13,9},{2,14},{6,2},{... | collective-permute-start | bytes 294920 | tf_op jit(solution)/shard_map/ppermute | solution.py:67
  176.6 5.8 %collective-permute-start.64 = (f32[32,768]{1,0:T(8,128)S(1)}, f32[32,768]{1,0:T(8,128)S(1)}, u32[]{:S(2)}, u32[]{:S(2)}) collective-permute-start(f32[32,768]{1,0:T(8,128)S(1)} %bitcast_add_fusion.9), channel_id=1, source_target_pairs={{0,4},{4,8},{8,12},{12,0},{1,5},{5,9},{9,13},{13,1},{2,6},{6,10},{... | collective-permute-start | bytes 294920 | tf_op jit(solution)/shard_map/ppermute | solution.py:66
  176.8 8.5 %collective-permute-start.20 = (f32[32,768]{1,0:T(8,128)S(1)}, f32[32,768]{1,0:T(8,128)S(1)}, u32[]{:S(2)}, u32[]{:S(2)}) collective-permute-start(f32[32,768]{1,0:T(8,128)S(1)} %bitcast_add_fusion.23), channel_id=1, source_target_pairs={{0,12},{4,0},{8,4},{12,8},{1,13},{5,1},{9,5},{13,9},{2,14},{6,2},{... | collective-permute-start | bytes 294920 | tf_op jit(solution)/shard_map/ppermute | solution.py:67
  179.5 8.6 %collective-permute-start.17 = (f32[32,768]{1,0:T(8,128)S(1)}, f32[32,768]{1,0:T(8,128)S(1)}, u32[]{:S(2)}, u32[]{:S(2)}) collective-permute-start(f32[32,768]{1,0:T(8,128)S(1)} %bitcast_add_fusion.26), channel_id=1, source_target_pairs={{0,4},{4,8},{8,12},{12,0},{1,5},{5,9},{9,13},{13,1},{2,6},{6,10},{... | collective-permute-start | bytes 294920 | tf_op jit(solution)/shard_map/ppermute | solution.py:66
  182.4 5.9 %collective-permute-start.33 = (f32[32,768]{1,0:T(8,128)S(1)}, f32[32,768]{1,0:T(8,128)S(1)}, u32[]{:S(2)}, u32[]{:S(2)}) collective-permute-start(f32[32,768]{1,0:T(8,128)S(1)} %bitcast_add_fusion.20), channel_id=1, source_target_pairs={{0,4},{4,8},{8,12},{12,0},{1,5},{5,9},{9,13},{13,1},{2,6},{6,10},{... | collective-permute-start | bytes 294920 | tf_op jit(solution)/shard_map/ppermute | solution.py:66
  182.5 6.0 %collective-permute-start.52 = (f32[32,768]{1,0:T(8,128)S(1)}, f32[32,768]{1,0:T(8,128)S(1)}, u32[]{:S(2)}, u32[]{:S(2)}) collective-permute-start(f32[32,768]{1,0:T(8,128)S(1)} %bitcast_add_fusion.11), channel_id=1, source_target_pairs={{0,12},{4,0},{8,4},{12,8},{1,13},{5,1},{9,5},{13,9},{2,14},{6,2},{... | collective-permute-start | bytes 294920 | tf_op jit(solution)/shard_map/ppermute | solution.py:67
  185.3 6.1 %collective-permute-start.49 = (f32[32,768]{1,0:T(8,128)S(1)}, f32[32,768]{1,0:T(8,128)S(1)}, u32[]{:S(2)}, u32[]{:S(2)}) collective-permute-start(f32[32,768]{1,0:T(8,128)S(1)} %bitcast_add_fusion.14), channel_id=1, source_target_pairs={{0,4},{4,8},{8,12},{12,0},{1,5},{5,9},{9,13},{13,1},{2,6},{6,10},{... | collective-permute-start | bytes 294920 | tf_op jit(solution)/shard_map/ppermute | solution.py:66
  185.4 6.1 %collective-permute-start.68 = (f32[32,768]{1,0:T(8,128)S(1)}, f32[32,768]{1,0:T(8,128)S(1)}, u32[]{:S(2)}, u32[]{:S(2)}) collective-permute-start(f32[32,768]{1,0:T(8,128)S(1)} %bitcast_add_fusion.5), channel_id=1, source_target_pairs={{0,12},{4,0},{8,4},{12,8},{1,13},{5,1},{9,5},{13,9},{2,14},{6,2},{... | collective-permute-start | bytes 294920 | tf_op jit(solution)/shard_map/ppermute | solution.py:67
  188.5 7.1 %collective-permute-start.37 = (f32[32,768]{1,0:T(8,128)S(1)}, f32[32,768]{1,0:T(8,128)S(1)}, u32[]{:S(2)}, u32[]{:S(2)}) collective-permute-start(f32[32,768]{1,0:T(8,128)S(1)} %fusion.50), channel_id=1, source_target_pairs={{0,2},{2,0},{1,3},{3,1},{4,6},{6,4},{5,7},{7,5},{8,10},{10,8},{9,1... | collective-permute-start | bytes 294920 | tf_op jit(solution)/shard_map/ppermute | solution.py:69
  195.6 6.1 %collective-permute-start.38 = (f32[32,768]{1,0:T(8,128)S(1)}, f32[32,768]{1,0:T(8,128)S(1)}, u32[]{:S(2)}, u32[]{:S(2)}) collective-permute-start(f32[32,768]{1,0:T(8,128)S(1)} %fusion.54), channel_id=1, source_target_pairs={{0,2},{2,0},{1,3},{3,1},{4,6},{6,4},{5,7},{7,5},{8,10},{10,8},{9,1... | collective-permute-start | bytes 294920 | tf_op jit(solution)/shard_map/ppermute | solution.py:72
  195.8 7.3 %collective-permute-start.54 = (f32[32,768]{1,0:T(8,128)S(1)}, f32[32,768]{1,0:T(8,128)S(1)}, u32[]{:S(2)}, u32[]{:S(2)}) collective-permute-start(f32[32,768]{1,0:T(8,128)S(1)} %fusion.48), channel_id=1, source_target_pairs={{0,2},{2,0},{1,3},{3,1},{4,6},{6,4},{5,7},{7,5},{8,10},{10,8},{9,1... | collective-permute-start | bytes 294920 | tf_op jit(solution)/shard_map/ppermute | solution.py:72
  197.6 7.6 %collective-permute-start.70 = (f32[32,768]{1,0:T(8,128)S(1)}, f32[32,768]{1,0:T(8,128)S(1)}, u32[]{:S(2)}, u32[]{:S(2)}) collective-permute-start(f32[32,768]{1,0:T(8,128)S(1)} %fusion.42), channel_id=1, source_target_pairs={{0,2},{2,0},{1,3},{3,1},{4,6},{6,4},{5,7},{7,5},{8,10},{10,8},{9,1... | collective-permute-start | bytes 294920 | tf_op jit(solution)/shard_map/ppermute | solution.py:72
  198.9 9.2 %collective-permute-start.23 = (f32[32,768]{1,0:T(8,128)S(1)}, f32[32,768]{1,0:T(8,128)S(1)}, u32[]{:S(2)}, u32[]{:S(2)}) collective-permute-start(f32[32,768]{1,0:T(8,128)S(1)} %get-tuple-element.460), channel_id=1, source_target_pairs={{0,4},{4,8},{8,12},{12,0},{1,5},{5,9},{9,13},{13,1},{2,6},{6,10},{... | collective-permute-start | bytes 294920 | tf_op jit(solution)/shard_map/ppermute | solution.py:77
  199.0 13.3 %collective-permute-start.24 = (f32[32,768]{1,0:T(8,128)S(1)}, f32[32,768]{1,0:T(8,128)S(1)}, u32[]{:S(2)}, u32[]{:S(2)}) collective-permute-start(f32[32,768]{1,0:T(8,128)S(1)} %get-tuple-element.459), channel_id=1, source_target_pairs={{0,12},{4,0},{8,4},{12,8},{1,13},{5,1},{9,5},{13,9},{2,14},{6,2},{... | collective-permute-start | bytes 294920 | tf_op jit(solution)/shard_map/ppermute | solution.py:78
  201.7 9.8 %collective-permute-start.39 = (f32[32,768]{1,0:T(8,128)S(1)}, f32[32,768]{1,0:T(8,128)S(1)}, u32[]{:S(2)}, u32[]{:S(2)}) collective-permute-start(f32[32,768]{1,0:T(8,128)S(1)} %get-tuple-element.462), channel_id=1, source_target_pairs={{0,4},{4,8},{8,12},{12,0},{1,5},{5,9},{9,13},{13,1},{2,6},{6,10},{... | collective-permute-start | bytes 294920 | tf_op jit(solution)/shard_map/ppermute | solution.py:77
  203.1 12.6 %collective-permute-start.40 = (f32[32,768]{1,0:T(8,128)S(1)}, f32[32,768]{1,0:T(8,128)S(1)}, u32[]{:S(2)}, u32[]{:S(2)}) collective-permute-start(f32[32,768]{1,0:T(8,128)S(1)} %get-tuple-element.461), channel_id=1, source_target_pairs={{0,12},{4,0},{8,4},{12,8},{1,13},{5,1},{9,5},{13,9},{2,14},{6,2},{... | collective-permute-start | bytes 294920 | tf_op jit(solution)/shard_map/ppermute | solution.py:78
  205.2 11.3 %collective-permute-start.55 = (f32[32,768]{1,0:T(8,128)S(1)}, f32[32,768]{1,0:T(8,128)S(1)}, u32[]{:S(2)}, u32[]{:S(2)}) collective-permute-start(f32[32,768]{1,0:T(8,128)S(1)} %get-tuple-element.464), channel_id=1, source_target_pairs={{0,4},{4,8},{8,12},{12,0},{1,5},{5,9},{9,13},{13,1},{2,6},{6,10},{... | collective-permute-start | bytes 294920 | tf_op jit(solution)/shard_map/ppermute | solution.py:77
  208.1 11.8 %collective-permute-start.56 = (f32[32,768]{1,0:T(8,128)S(1)}, f32[32,768]{1,0:T(8,128)S(1)}, u32[]{:S(2)}, u32[]{:S(2)}) collective-permute-start(f32[32,768]{1,0:T(8,128)S(1)} %get-tuple-element.463), channel_id=1, source_target_pairs={{0,12},{4,0},{8,4},{12,8},{1,13},{5,1},{9,5},{13,9},{2,14},{6,2},{... | collective-permute-start | bytes 294920 | tf_op jit(solution)/shard_map/ppermute | solution.py:78
  211.5 9.2 %collective-permute-start.71 = (f32[32,768]{1,0:T(8,128)S(1)}, f32[32,768]{1,0:T(8,128)S(1)}, u32[]{:S(2)}, u32[]{:S(2)}) collective-permute-start(f32[32,768]{1,0:T(8,128)S(1)} %get-tuple-element.466), channel_id=1, source_target_pairs={{0,4},{4,8},{8,12},{12,0},{1,5},{5,9},{9,13},{13,1},{2,6},{6,10},{... | collective-permute-start | bytes 294920 | tf_op jit(solution)/shard_map/ppermute | solution.py:77
  212.3 11.8 %collective-permute-start.72 = (f32[32,768]{1,0:T(8,128)S(1)}, f32[32,768]{1,0:T(8,128)S(1)}, u32[]{:S(2)}, u32[]{:S(2)}) collective-permute-start(f32[32,768]{1,0:T(8,128)S(1)} %get-tuple-element.465), channel_id=1, source_target_pairs={{0,12},{4,0},{8,4},{12,8},{1,13},{5,1},{9,5},{13,9},{2,14},{6,2},{... | collective-permute-start | bytes 294920 | tf_op jit(solution)/shard_map/ppermute | solution.py:78
  215.7 9.2 %collective-permute-start.25 = (f32[32,768]{1,0:T(8,128)S(1)}, f32[32,768]{1,0:T(8,128)S(1)}, u32[]{:S(2)}, u32[]{:S(2)}) collective-permute-start(f32[32,768]{1,0:T(8,128)S(1)} %collective-permute-done.23), channel_id=1, source_target_pairs={{0,4},{4,8},{8,12},{12,0},{1,5},{5,9},{9,13},{13,1},{2,6},{6,10},{... | collective-permute-start | bytes 294920 | tf_op jit(solution)/shard_map/ppermute | solution.py:77
  216.5 12.4 %collective-permute-start.26 = (f32[32,768]{1,0:T(8,128)S(1)}, f32[32,768]{1,0:T(8,128)S(1)}, u32[]{:S(2)}, u32[]{:S(2)}) collective-permute-start(f32[32,768]{1,0:T(8,128)S(1)} %collective-permute-done.24), channel_id=1, source_target_pairs={{0,12},{4,0},{8,4},{12,8},{1,13},{5,1},{9,5},{13,9},{2,14},{6,2},{... | collective-permute-start | bytes 294920 | tf_op jit(solution)/shard_map/ppermute | solution.py:78
  219.9 8.3 %collective-permute-start.41 = (f32[32,768]{1,0:T(8,128)S(1)}, f32[32,768]{1,0:T(8,128)S(1)}, u32[]{:S(2)}, u32[]{:S(2)}) collective-permute-start(f32[32,768]{1,0:T(8,128)S(1)} %collective-permute-done.39), channel_id=1, source_target_pairs={{0,4},{4,8},{8,12},{12,0},{1,5},{5,9},{9,13},{13,1},{2,6},{6,10},{... | collective-permute-start | bytes 294920 | tf_op jit(solution)/shard_map/ppermute | solution.py:77
  220.7 11.6 %collective-permute-start.42 = (f32[32,768]{1,0:T(8,128)S(1)}, f32[32,768]{1,0:T(8,128)S(1)}, u32[]{:S(2)}, u32[]{:S(2)}) collective-permute-start(f32[32,768]{1,0:T(8,128)S(1)} %collective-permute-done.40), channel_id=1, source_target_pairs={{0,12},{4,0},{8,4},{12,8},{1,13},{5,1},{9,5},{13,9},{2,14},{6,2},{... | collective-permute-start | bytes 294920 | tf_op jit(solution)/shard_map/ppermute | solution.py:78
  224.1 9.1 %collective-permute-start.57 = (f32[32,768]{1,0:T(8,128)S(1)}, f32[32,768]{1,0:T(8,128)S(1)}, u32[]{:S(2)}, u32[]{:S(2)}) collective-permute-start(f32[32,768]{1,0:T(8,128)S(1)} %collective-permute-done.55), channel_id=1, source_target_pairs={{0,4},{4,8},{8,12},{12,0},{1,5},{5,9},{9,13},{13,1},{2,6},{6,10},{... | collective-permute-start | bytes 294920 | tf_op jit(solution)/shard_map/ppermute | solution.py:77
  224.9 11.6 %collective-permute-start.58 = (f32[32,768]{1,0:T(8,128)S(1)}, f32[32,768]{1,0:T(8,128)S(1)}, u32[]{:S(2)}, u32[]{:S(2)}) collective-permute-start(f32[32,768]{1,0:T(8,128)S(1)} %collective-permute-done.56), channel_id=1, source_target_pairs={{0,12},{4,0},{8,4},{12,8},{1,13},{5,1},{9,5},{13,9},{2,14},{6,2},{... | collective-permute-start | bytes 294920 | tf_op jit(solution)/shard_map/ppermute | solution.py:78
  228.3 9.1 %collective-permute-start.73 = (f32[32,768]{1,0:T(8,128)S(1)}, f32[32,768]{1,0:T(8,128)S(1)}, u32[]{:S(2)}, u32[]{:S(2)}) collective-permute-start(f32[32,768]{1,0:T(8,128)S(1)} %collective-permute-done.71), channel_id=1, source_target_pairs={{0,4},{4,8},{8,12},{12,0},{1,5},{5,9},{9,13},{13,1},{2,6},{6,10},{... | collective-permute-start | bytes 294920 | tf_op jit(solution)/shard_map/ppermute | solution.py:77
  228.9 11.7 %collective-permute-start.74 = (f32[32,768]{1,0:T(8,128)S(1)}, f32[32,768]{1,0:T(8,128)S(1)}, u32[]{:S(2)}, u32[]{:S(2)}) collective-permute-start(f32[32,768]{1,0:T(8,128)S(1)} %collective-permute-done.72), channel_id=1, source_target_pairs={{0,12},{4,0},{8,4},{12,8},{1,13},{5,1},{9,5},{13,9},{2,14},{6,2},{... | collective-permute-start | bytes 294920 | tf_op jit(solution)/shard_map/ppermute | solution.py:78
  232.4 9.1 %collective-permute-start.27 = (f32[32,768]{1,0:T(8,128)S(1)}, f32[32,768]{1,0:T(8,128)S(1)}, u32[]{:S(2)}, u32[]{:S(2)}) collective-permute-start(f32[32,768]{1,0:T(8,128)S(1)} %collective-permute-done.25), channel_id=1, source_target_pairs={{0,4},{4,8},{8,12},{12,0},{1,5},{5,9},{9,13},{13,1},{2,6},{6,10},{... | collective-permute-start | bytes 294920 | tf_op jit(solution)/shard_map/ppermute | solution.py:77
  233.2 12.4 %collective-permute-start.28 = (f32[32,768]{1,0:T(8,128)S(1)}, f32[32,768]{1,0:T(8,128)S(1)}, u32[]{:S(2)}, u32[]{:S(2)}) collective-permute-start(f32[32,768]{1,0:T(8,128)S(1)} %collective-permute-done.26), channel_id=1, source_target_pairs={{0,12},{4,0},{8,4},{12,8},{1,13},{5,1},{9,5},{13,9},{2,14},{6,2},{... | collective-permute-start | bytes 294920 | tf_op jit(solution)/shard_map/ppermute | solution.py:78
  236.5 8.3 %collective-permute-start.43 = (f32[32,768]{1,0:T(8,128)S(1)}, f32[32,768]{1,0:T(8,128)S(1)}, u32[]{:S(2)}, u32[]{:S(2)}) collective-permute-start(f32[32,768]{1,0:T(8,128)S(1)} %collective-permute-done.41), channel_id=1, source_target_pairs={{0,4},{4,8},{8,12},{12,0},{1,5},{5,9},{9,13},{13,1},{2,6},{6,10},{... | collective-permute-start | bytes 294920 | tf_op jit(solution)/shard_map/ppermute | solution.py:77
  237.3 11.7 %collective-permute-start.44 = (f32[32,768]{1,0:T(8,128)S(1)}, f32[32,768]{1,0:T(8,128)S(1)}, u32[]{:S(2)}, u32[]{:S(2)}) collective-permute-start(f32[32,768]{1,0:T(8,128)S(1)} %collective-permute-done.42), channel_id=1, source_target_pairs={{0,12},{4,0},{8,4},{12,8},{1,13},{5,1},{9,5},{13,9},{2,14},{6,2},{... | collective-permute-start | bytes 294920 | tf_op jit(solution)/shard_map/ppermute | solution.py:78
  240.7 24.1 %collective-permute-start.59 = (f32[32,768]{1,0:T(8,128)S(1)}, f32[32,768]{1,0:T(8,128)S(1)}, u32[]{:S(2)}, u32[]{:S(2)}) collective-permute-start(f32[32,768]{1,0:T(8,128)S(1)} %collective-permute-done.57), channel_id=1, source_target_pairs={{0,4},{4,8},{8,12},{12,0},{1,5},{5,9},{9,13},{13,1},{2,6},{6,10},{... | collective-permute-start | bytes 294920 | tf_op jit(solution)/shard_map/ppermute | solution.py:77
  241.5 24.1 %collective-permute-start.60 = (f32[32,768]{1,0:T(8,128)S(1)}, f32[32,768]{1,0:T(8,128)S(1)}, u32[]{:S(2)}, u32[]{:S(2)}) collective-permute-start(f32[32,768]{1,0:T(8,128)S(1)} %collective-permute-done.58), channel_id=1, source_target_pairs={{0,12},{4,0},{8,4},{12,8},{1,13},{5,1},{9,5},{13,9},{2,14},{6,2},{... | collective-permute-start | bytes 294920 | tf_op jit(solution)/shard_map/ppermute | solution.py:78
  244.9 21.9 %collective-permute-start.75 = (f32[32,768]{1,0:T(8,128)S(1)}, f32[32,768]{1,0:T(8,128)S(1)}, u32[]{:S(2)}, u32[]{:S(2)}) collective-permute-start(f32[32,768]{1,0:T(8,128)S(1)} %collective-permute-done.73), channel_id=1, source_target_pairs={{0,4},{4,8},{8,12},{12,0},{1,5},{5,9},{9,13},{13,1},{2,6},{6,10},{... | collective-permute-start | bytes 294920 | tf_op jit(solution)/shard_map/ppermute | solution.py:77
  245.6 21.8 %collective-permute-start.76 = (f32[32,768]{1,0:T(8,128)S(1)}, f32[32,768]{1,0:T(8,128)S(1)}, u32[]{:S(2)}, u32[]{:S(2)}) collective-permute-start(f32[32,768]{1,0:T(8,128)S(1)} %collective-permute-done.74), channel_id=1, source_target_pairs={{0,12},{4,0},{8,4},{12,8},{1,13},{5,1},{9,5},{13,9},{2,14},{6,2},{... | collective-permute-start | bytes 294920 | tf_op jit(solution)/shard_map/ppermute | solution.py:78
  249.0 19.2 %collective-permute-start.29 = (f32[256,768]{1,0:T(8,128)S(1)}, f32[256,768]{1,0:T(8,128)}, u32[]{:S(2)}, u32[]{:S(2)}) collective-permute-start(f32[256,768]{1,0:T(8,128)S(1)} %bitcast.406), channel_id=1, source_target_pairs={{0,1},{1,0},{2,3},{3,2},{4,5},{5,4},{6,7},{7,6},{8,9},{9,8},{10,11... | collective-permute-start | bytes 2359304 | tf_op jit(solution)/shard_map/ppermute | solution.py:82
  (23 other events, 211.0 us)

commit v6 on v3

--- a/solution.py
+++ b/solution.py
@@ -121,7 +121,8 @@
     parts = []
     for k in range(2):
         part = slice(k * chunk, (k + 1) * chunk)
-        summed = rescaled_affinity(weights[part], features) * scale[part, None]
+        summed = lax.optimization_barrier(rescaled_affinity(weights[part], features))
+        summed = summed * scale[part, None]
         parts.append(reduce_rows(summed, row_total, k * chunk, sizes))
     return jnp.concatenate(parts, axis=0)
 

time: 250 us -> 242 us (0.968)
  starting transfers between devices: 77.7 us -> 66.2 us
  waiting for transfers between devices: 51.5 us -> 55.9 us
    ppermute x6, starting transfers between devices: 18.5 us -> 6.41 us  [reduce_rows(): lax.ppermute(left, 'x', ring('x', x_size, -1))]
    ppermute x6, waiting for transfers between devices: 3.39 us -> 15 us  [reduce_rows(): lax.ppermute(left, 'x', ring('x', x_size, -1))]
    ppermute x6, waiting for transfers between devices: 5.48 us -> 0.93 us  [reduce_rows(): lax.ppermute(right, 'x', ring('x', x_size, 1))]
    ppermute x6, starting transfers between devices: 0.3 us -> 4.73 us  [reduce_rows(): right = lax.ppermute(right, 'x', ring('x', x_size, 1))]
    ppermute x6, starting transfers between devices: 16.1 us -> 11.7 us  [reduce_rows(): left = lax.ppermute(left, 'x', ring('x', x_size, -1))]
    ppermute x7, waiting for transfers between devices: 11 us -> 8.19 us  [merge_peaks(): other = lax.ppermute(pair, axis, [(j, j ^ dist) for j in range(size)])]
    ppermute x6, starting transfers between devices: 0.45 us -> 3.22 us  [reduce_rows(): lax.ppermute(right, 'x', ring('x', x_size, 1))]
  transfers between devices with their start and end apart: 46 -> 46, of which waited for: 22 -> 21; matrix products, arithmetic and copies ran while one was open for 25% -> 32% of each run, Pallas kernels for 0% -> 0%
where the time goes in v6:
time: 242 us; the launch traced here: 239 us
  matrix products  67.5 us (28%)
  starting transfers between devices  66.2 us (27%)
  waiting for transfers between devices  55.9 us (23%)
  other arithmetic  42.7 us (18%)
  local copies, waits for them, and re-layouts  5.39 us (2%)
    dot_general x2, matrix products, similar(): lax.dot_general(query_factor, target_factor, (((1,), (0,)), ((), ())), pr...  44.7 us
    dot_general x2, matrix products, rescaled_affinity(): lax.dot_general(weights, features, (((1,), (1,)), ((), ())), precision=la...  22.8 us
    ppermute x7, starting transfers between devices, merge_peaks(): other = lax.ppermute(pair, axis, [(j, j ^ dist) for j in range(size)])  15.1 us
    ppermute x6, waiting for transfers between devices, reduce_rows(): lax.ppermute(left, 'x', ring('x', x_size, -1))  15 us
    ppermute x3, waiting for transfers between devices, gather_features(): right = lax.ppermute(right, 'y', ring('y', y_size, 1))  12.1 us
    ppermute x6, starting transfers between devices, reduce_rows(): left = lax.ppermute(left, 'x', ring('x', x_size, -1))  11.7 us
    ppermute x2, starting transfers between devices, reduce_rows(): other = lax.ppermute(held, 'core', swap)  8.35 us
    ppermute x7, waiting for transfers between devices, merge_peaks(): other = lax.ppermute(pair, axis, [(j, j ^ dist) for j in range(size)])  8.19 us
  transfers between devices with their start and end apart: 46, of which 21 were waited for; matrix products, arithmetic and copies ran while one was open for 32% of the time, Pallas kernels for 0%

profile of v6, /device:TPU:1, one launch (start us, length us, event | category | flops | bytes accessed | tf_op | source)
XLA Modules:
  0.0 238.6 jit_solution(7937807359622549612)
XLA Ops:
  0.0 4.4 %collective-permute-start = (f32[1024,96]{0,1:T(8,128)}, f32[1024,96]{0,1:T(8,128)S(1)}, u32[]{:S(2)}, u32[]{:S(2)}) collective-permute-start(f32[1024,96]{0,1:T(8,128)} %param.46), channel_id=1, source_target_pairs={{0,64},{64,0},{1,65},{65,1},{2,66},{66,2},{3,67},{67,3},{4,68},{68... | collective-permute-start | bytes 1179656 | tf_op jit(solution)/shard_map/ppermute | solution.py:89
  4.4 1.4 and_reduce_fusion.10
  5.8 7.7 %collective-permute-done = f32[1024,96]{0,1:T(8,128)S(1)} collective-permute-done((f32[1024,96]{0,1:T(8,128)}, f32[1024,96]{0,1:T(8,128)S(1)}, u32[]{:S(2)}, u32[]{:S(2)}) %collective-permute-start) | collective-permute-done | bytes 393248 | tf_op jit(solution)/shard_map/ppermute | solution.py:89
  13.5 1.4 maximum_select_fusion.3
  14.8 1.0 slice_bitcast_fusion
  15.8 1.3 collective-permute-start.1
  17.1 1.4 collective-permute-start.2
  22.6 4.2 %collective-permute-done.1 = f32[1024,96]{0,1:T(8,128)} collective-permute-done((f32[1024,96]{0,1:T(8,128)}, f32[1024,96]{0,1:T(8,128)}, u32[]{:S(2)}, u32[]{:S(2)}) %collective-permute-start.1) | collective-permute-done | bytes 393248 | tf_op jit(solution)/shard_map/ppermute | solution.py:94
  26.9 2.7 %collective-permute-start.4 = (f32[1024,96]{0,1:T(8,128)}, f32[1024,96]{0,1:T(8,128)S(1)}, u32[]{:S(2)}, u32[]{:S(2)}) collective-permute-start(f32[1024,96]{0,1:T(8,128)} %collective-permute-done.2), channel_id=1, source_target_pairs={{0,48},{16,0},{32,16},{48,32},{1,49},{17,1},{33,17},{49,33},{2,50}... | collective-permute-start | bytes 1179656 | tf_op jit(solution)/shard_map/ppermute | solution.py:95
  29.6 1.9 fusion.16
  31.5 1.6 fusion.15
  33.1 3.7 %collective-permute-done.3 = f32[1024,96]{0,1:T(8,128)S(1)} collective-permute-done((f32[1024,96]{0,1:T(8,128)}, f32[1024,96]{0,1:T(8,128)S(1)}, u32[]{:S(2)}, u32[]{:S(2)}) %collective-permute-start.3) | collective-permute-done | bytes 393248 | tf_op jit(solution)/shard_map/ppermute | solution.py:94
  36.8 3.1 %collective-permute-start.6 = (f32[1024,96]{0,1:T(8,128)S(1)}, f32[1024,96]{0,1:T(8,128)S(1)}, u32[]{:S(2)}, u32[]{:S(2)}) collective-permute-start(f32[1024,96]{0,1:T(8,128)S(1)} %collective-permute-done.4), channel_id=1, source_target_pairs={{0,48},{16,0},{32,16},{48,32},{1,49},{17,1},{33,17},{49,33},{2,50}... | collective-permute-start | bytes 1179656 | tf_op jit(solution)/shard_map/ppermute | solution.py:95
  41.4 4.2 %collective-permute-done.5 = f32[1024,96]{0,1:T(8,128)S(1)} collective-permute-done((f32[1024,96]{0,1:T(8,128)S(1)}, f32[1024,96]{0,1:T(8,128)S(1)}, u32[]{:S(2)}, u32[]{:S(2)}) %collective-permute-start.5) | collective-permute-done | bytes 393248 | tf_op jit(solution)/shard_map/ppermute | solution.py:94
  46.4 0.8 fusion.11
  47.3 22.5 %fusion = (f32[1024]{0:T(1024)S(1)}, f32[1024,2048]{0,1:T(8,128)S(1)}) fusion(f32[768,1024]{1,0:T(8,128)S(1)} %bitcast.246, f32[2048,768]{1,0:T(8,128)S(1)} %copy-done.7), kind=kOutput, calls=%fused_computation.4 | convolution fusion | flops 19331547136 | bytes 17829888 | tf_op jit(solution)/shard_map/dot_general | solution.py:15
  69.7 1.4 exponential_reduce_fusion
  71.2 1.8 collective-permute-start.7
  73.0 2.3 collective-permute-done.7
  75.4 2.5 %collective-permute-done.8 = f32[2,1024]{1,0:T(2,128)S(1)} collective-permute-done((f32[2,1024]{1,0:T(2,128)S(1)}, f32[2,1024]{1,0:T(2,128)S(1)}, u32[]{:S(2)}, u32[]{:S(2)}) %collective-permute-start.8) | collective-permute-done | bytes 8224 | tf_op jit(solution)/shard_map/ppermute | solution.py:38
  77.9 2.6 %collective-permute-start.9 = (f32[2,1024]{1,0:T(2,128)S(1)}, f32[2,1024]{1,0:T(2,128)S(1)}, u32[]{:S(2)}, u32[]{:S(2)}) collective-permute-start(f32[2,1024]{1,0:T(2,128)S(1)} %pad_maximum_fusion.7), channel_id=1, source_target_pairs={{0,32},{16,48},{32,0},{48,16},{1,33},{17,49},{33,1},{49,17},{2,34}... | collective-permute-start | bytes 24584 | tf_op jit(solution)/shard_map/ppermute | solution.py:38
  80.5 22.2 %bitcast_multiply_fusion.1 = f32[2048,1024]{1,0:T(8,128)S(1)} fusion(f32[768,1024]{1,0:T(8,128)S(1)} %bitcast.247, f32[2048,768]{1,0:T(8,128)S(1)} %bitcast.283), kind=kOutput, calls=%fused_computation.1 | convolution fusion | flops 19329449984 | bytes 17825792 | tf_op jit(solution)/shard_map/dot_general | solution.py:15
  103.4 4.2 %fusion.53 = (f32[2048]{0:T(1024)S(1)}, f32[2048,1024]{1,0:T(8,128)}) fusion(f32[2048]{0:T(1024)S(1)} %subtract_reduce_fusion, f32[2048,1024]{1,0:T(8,128)S(1)} %bitcast_multiply_fusion.1, f32[1024]{0:T(1024)S(1)} %bitcast.273), kind=kLoop, calls=%fused_computation.200 | loop fusion | flops 6289408 | bytes 16797696 | tf_op jit(solution)/shard_map/reduce_sum | solution.py:116
  107.6 6.3 %collective-permute-start.10 = (f32[2,2048]{1,0:T(2,128)S(1)}, f32[2,2048]{1,0:T(2,128)S(1)}, u32[]{:S(2)}, u32[]{:S(2)}) collective-permute-start(f32[2,2048]{1,0:T(2,128)S(1)} %pad_maximum_fusion.1), channel_id=1, source_target_pairs={{0,1},{1,0},{2,3},{3,2},{4,5},{5,4},{6,7},{7,6},{8,9},{9,8},{10,11... | collective-permute-start | bytes 49160 | tf_op jit(solution)/shard_map/ppermute | solution.py:38
  114.9 2.5 %collective-permute-done.11 = f32[2,2048]{1,0:T(2,128)S(1)} collective-permute-done((f32[2,2048]{1,0:T(2,128)S(1)}, f32[2,2048]{1,0:T(2,128)S(1)}, u32[]{:S(2)}, u32[]{:S(2)}) %collective-permute-start.11) | collective-permute-done | bytes 16416 | tf_op jit(solution)/shard_map/ppermute | solution.py:38
  117.5 1.3 collective-permute-start.12
  118.8 12.4 %fusion.3 = f32[1024,768]{1,0:T(8,128)S(1)} fusion(f32[768,1024]{1,0:T(8,128)S(1)} %bitcast.248, f32[2048,1024]{1,0:T(8,128)} %get-tuple-element.276), kind=kOutput, calls=%fused_computation.9 | convolution fusion | flops 9663676416 | bytes 10485760 | tf_op jit(solution)/shard_map/dot_general | solution.py:26
  131.3 2.9 %collective-permute-start.13 = (f32[2,2048]{1,0:T(2,128)S(1)}, f32[2,2048]{1,0:T(2,128)S(1)}, u32[]{:S(2)}, u32[]{:S(2)}) collective-permute-start(f32[2,2048]{1,0:T(2,128)S(1)} %pad_maximum_fusion.4), channel_id=1, source_target_pairs={{0,8},{4,12},{8,0},{12,4},{1,9},{5,13},{9,1},{13,5},{2,10},{6,14},... | collective-permute-start | bytes 49160 | tf_op jit(solution)/shard_map/ppermute | solution.py:38
  134.3 10.4 %fusion.1 = f32[1024,768]{1,0:T(8,128)S(1)} fusion(f32[768,1024]{1,0:T(8,128)S(1)} %bitcast.249, f32[2048,1024]{1,0:T(8,128)S(1)} %copy-done.1), kind=kOutput, calls=%fused_computation.7 | convolution fusion | flops 9663676416 | bytes 10485760 | tf_op jit(solution)/shard_map/dot_general | solution.py:26
  145.2 1.4 dynamic-slice_bitcast_fusion.1
  146.7 2.1 collective-permute-start.14
  148.7 1.3 dynamic-slice_bitcast_fusion
  152.6 2.1 bitcast_add_fusion.1
  155.1 1.3 collective-permute-start.15
  156.5 1.6 bitcast_add_fusion
  158.2 1.5 collective-permute-start.34
  159.8 1.2 collective-permute-done.18
  161.1 1.5 collective-permute-start.19
  162.7 2.6 %collective-permute-done.34 = f32[64,768]{1,0:T(8,128)S(1)} collective-permute-done((f32[64,768]{1,0:T(8,128)S(1)}, f32[64,768]{1,0:T(8,128)S(1)}, u32[]{:S(2)}, u32[]{:S(2)}) %collective-permute-start.34) | collective-permute-done | bytes 196640 | tf_op jit(solution)/shard_map/ppermute | solution.py:66
  165.3 1.2 collective-permute-start.35
  166.9 2.6 %collective-permute-done.19 = f32[64,768]{1,0:T(8,128)S(1)} collective-permute-done((f32[64,768]{1,0:T(8,128)S(1)}, f32[64,768]{1,0:T(8,128)S(1)}, u32[]{:S(2)}, u32[]{:S(2)}) %collective-permute-start.19) | collective-permute-done | bytes 196640 | tf_op jit(solution)/shard_map/ppermute | solution.py:66
  169.5 1.3 collective-permute-start.20
  171.1 2.5 %collective-permute-done.35 = f32[64,768]{1,0:T(8,128)S(1)} collective-permute-done((f32[64,768]{1,0:T(8,128)S(1)}, f32[64,768]{1,0:T(8,128)S(1)}, u32[]{:S(2)}, u32[]{:S(2)}) %collective-permute-start.35) | collective-permute-done | bytes 196640 | tf_op jit(solution)/shard_map/ppermute | solution.py:66
  174.4 1.0 collective-permute-start.33
  175.4 2.6 %collective-permute-done.20 = f32[64,768]{1,0:T(8,128)S(1)} collective-permute-done((f32[64,768]{1,0:T(8,128)S(1)}, f32[64,768]{1,0:T(8,128)S(1)}, u32[]{:S(2)}, u32[]{:S(2)}) %collective-permute-start.20) | collective-permute-done | bytes 196640 | tf_op jit(solution)/shard_map/ppermute | solution.py:66
  178.5 3.6 %collective-permute-done.36 = f32[64,768]{1,0:T(8,128)S(1)} collective-permute-done((f32[64,768]{1,0:T(8,128)S(1)}, f32[64,768]{1,0:T(8,128)S(1)}, u32[]{:S(2)}, u32[]{:S(2)}) %collective-permute-start.36) | collective-permute-done | bytes 196640 | tf_op jit(solution)/shard_map/ppermute | solution.py:66
  183.4 1.2 collective-permute-start.22
  184.5 4.4 %collective-permute-done.37 = f32[64,768]{1,0:T(8,128)S(1)} collective-permute-done((f32[64,768]{1,0:T(8,128)S(1)}, f32[64,768]{1,0:T(8,128)S(1)}, u32[]{:S(2)}, u32[]{:S(2)}) %collective-permute-start.37) | collective-permute-done | bytes 196640 | tf_op jit(solution)/shard_map/ppermute | solution.py:68
  189.1 4.0 %collective-permute-done.22 = f32[64,768]{1,0:T(8,128)S(1)} collective-permute-done((f32[64,768]{1,0:T(8,128)S(1)}, f32[64,768]{1,0:T(8,128)S(1)}, u32[]{:S(2)}, u32[]{:S(2)}) %collective-permute-start.22) | collective-permute-done | bytes 196640 | tf_op jit(solution)/shard_map/ppermute | solution.py:71
  193.2 1.3 collective-permute-start.23
  194.5 1.4 collective-permute-start.24
  195.9 1.4 collective-permute-done.38
  197.4 1.3 collective-permute-start.39
  198.7 1.4 collective-permute-start.40
  202.0 2.6 %collective-permute-start.26 = (f32[64,768]{1,0:T(8,128)S(1)}, f32[64,768]{1,0:T(8,128)S(1)}, u32[]{:S(2)}, u32[]{:S(2)}) collective-permute-start(f32[64,768]{1,0:T(8,128)S(1)} %collective-permute-done.24), channel_id=1, source_target_pairs={{0,12},{4,0},{8,4},{12,8},{1,13},{5,1},{9,5},{13,9},{2,14},{6,2},{... | collective-permute-start | bytes 589832 | tf_op jit(solution)/shard_map/ppermute | solution.py:77
  206.7 1.9 collective-permute-start.42
  210.1 2.7 %collective-permute-start.28 = (f32[64,768]{1,0:T(8,128)S(1)}, f32[64,768]{1,0:T(8,128)S(1)}, u32[]{:S(2)}, u32[]{:S(2)}) collective-permute-start(f32[64,768]{1,0:T(8,128)S(1)} %collective-permute-done.26), channel_id=1, source_target_pairs={{0,12},{4,0},{8,4},{12,8},{1,13},{5,1},{9,5},{13,9},{2,14},{6,2},{... | collective-permute-start | bytes 589832 | tf_op jit(solution)/shard_map/ppermute | solution.py:77
  212.8 1.0 collective-permute-start.43
  215.3 1.7 collective-permute-start.44
  219.5 8.2 %collective-permute-start.29 = (f32[512,768]{1,0:T(8,128)S(1)}, f32[512,768]{1,0:T(8,128)}, u32[]{:S(2)}, u32[]{:S(2)}) collective-permute-start(f32[512,768]{1,0:T(8,128)S(1)} %bitcast.244), channel_id=1, source_target_pairs={{0,1},{1,0},{2,3},{3,2},{4,5},{5,4},{6,7},{7,6},{8,9},{9,8},{10,11... | collective-permute-start | bytes 4718600 | tf_op jit(solution)/shard_map/ppermute | solution.py:81
  229.1 1.8 collective-permute-done.29
  230.9 2.2 maximum_select_fusion
  233.1 2.2 maximum_select_fusion.1
  235.3 3.1 %pad_maximum_fusion = f32[2048,768]{1,0:T(8,128)} fusion(f32[1024,768]{1,0:T(8,128)S(1)} %bitcast.241, f32[1024,768]{1,0:T(8,128)S(1)} %bitcast.240), kind=kLoop, calls=%fused_computation.6 | loop fusion | flops 1572864 | bytes 12582912 | tf_op jit(solution)/shard_map/concatenate | solution.py:127
  (140 shorter events, 26.3 us)
Async XLA Ops:
  0.0 19.4 %copy-start.5 = (s32[4]{0:T(128)S(1)}, s32[4]{0:T(128)}, u32[]{:S(2)}) copy-start(s32[4]{0:T(128)} %constant.689.clone.1) | copy-start | bytes 52
  0.0 18.6 %copy-start.6 = (s32[4]{0:T(128)S(1)}, s32[4]{0:T(128)}, u32[]{:S(2)}) copy-start(s32[4]{0:T(128)} %constant.683.clone.1) | copy-start | bytes 52
  0.0 13.5 %collective-permute-start = (f32[1024,96]{0,1:T(8,128)}, f32[1024,96]{0,1:T(8,128)S(1)}, u32[]{:S(2)}, u32[]{:S(2)}) collective-permute-start(f32[1024,96]{0,1:T(8,128)} %param.46), channel_id=1, source_target_pairs={{0,64},{64,0},{1,65},{65,1},{2,66},{66,2},{3,67},{67,3},{4,68},{68... | collective-permute-start | bytes 1179656 | tf_op jit(solution)/shard_map/ppermute | solution.py:89
  13.5 7.5 %copy-start.3 = (f32[1024,96]{0,1:T(8,128)}, f32[1024,96]{0,1:T(8,128)S(1)}, u32[]{:S(2)}) copy-start(f32[1024,96]{0,1:T(8,128)S(1)} %collective-permute-done) | copy-start | bytes 1179652
  13.5 7.8 %copy-start.2 = (f32[1024,96]{0,1:T(8,128)S(1)}, f32[1024,96]{0,1:T(8,128)}, u32[]{:S(2)}) copy-start(f32[1024,96]{0,1:T(8,128)} %param.46) | copy-start | bytes 1179652
  15.8 11.0 %collective-permute-start.1 = (f32[1024,96]{0,1:T(8,128)}, f32[1024,96]{0,1:T(8,128)}, u32[]{:S(2)}, u32[]{:S(2)}) collective-permute-start(f32[1024,96]{0,1:T(8,128)} %get-tuple-element.286), channel_id=1, source_target_pairs={{0,16},{16,32},{32,48},{48,0},{1,17},{17,33},{33,49},{49,1},{2,18}... | collective-permute-start | bytes 1179656 | tf_op jit(solution)/shard_map/ppermute | solution.py:94
  17.1 9.7 %collective-permute-start.2 = (f32[1024,96]{0,1:T(8,128)}, f32[1024,96]{0,1:T(8,128)}, u32[]{:S(2)}, u32[]{:S(2)}) collective-permute-start(f32[1024,96]{0,1:T(8,128)} %get-tuple-element.285), channel_id=1, source_target_pairs={{0,48},{16,0},{32,16},{48,32},{1,49},{17,1},{33,17},{49,33},{2,50}... | collective-permute-start | bytes 1179656 | tf_op jit(solution)/shard_map/ppermute | solution.py:95
  20.9 1.0 copy-start.4
  26.9 9.9 %collective-permute-start.3 = (f32[1024,96]{0,1:T(8,128)}, f32[1024,96]{0,1:T(8,128)S(1)}, u32[]{:S(2)}, u32[]{:S(2)}) collective-permute-start(f32[1024,96]{0,1:T(8,128)} %collective-permute-done.1), channel_id=1, source_target_pairs={{0,16},{16,32},{32,48},{48,0},{1,17},{17,33},{33,49},{49,1},{2,18}... | collective-permute-start | bytes 1179656 | tf_op jit(solution)/shard_map/ppermute | solution.py:94
  26.9 9.9 %collective-permute-start.4 = (f32[1024,96]{0,1:T(8,128)}, f32[1024,96]{0,1:T(8,128)S(1)}, u32[]{:S(2)}, u32[]{:S(2)}) collective-permute-start(f32[1024,96]{0,1:T(8,128)} %collective-permute-done.2), channel_id=1, source_target_pairs={{0,48},{16,0},{32,16},{48,32},{1,49},{17,1},{33,17},{49,33},{2,50}... | collective-permute-start | bytes 1179656 | tf_op jit(solution)/shard_map/ppermute | solution.py:95
  29.6 17.7 %copy-start.7 = (f32[2048,768]{1,0:T(8,128)S(1)}, f32[2048,768]{1,0:T(8,128)}, u32[]{:S(2)}) copy-start(f32[2048,768]{1,0:T(8,128)} %param.47) | copy-start | bytes 18874372
  36.8 8.8 %collective-permute-start.5 = (f32[1024,96]{0,1:T(8,128)S(1)}, f32[1024,96]{0,1:T(8,128)S(1)}, u32[]{:S(2)}, u32[]{:S(2)}) collective-permute-start(f32[1024,96]{0,1:T(8,128)S(1)} %collective-permute-done.3), channel_id=1, source_target_pairs={{0,16},{16,32},{32,48},{48,0},{1,17},{17,33},{33,49},{49,1},{2,18}... | collective-permute-start | bytes 1179656 | tf_op jit(solution)/shard_map/ppermute | solution.py:94
  36.8 9.6 %collective-permute-start.6 = (f32[1024,96]{0,1:T(8,128)S(1)}, f32[1024,96]{0,1:T(8,128)S(1)}, u32[]{:S(2)}, u32[]{:S(2)}) collective-permute-start(f32[1024,96]{0,1:T(8,128)S(1)} %collective-permute-done.4), channel_id=1, source_target_pairs={{0,48},{16,0},{32,16},{48,32},{1,49},{17,1},{33,17},{49,33},{2,50}... | collective-permute-start | bytes 1179656 | tf_op jit(solution)/shard_map/ppermute | solution.py:95
  46.4 34.1 %slice-start = ((s8[6291456]{0:T(1024)(128)(4,1)}), s8[4194304]{0:T(1024)(128)(4,1)S(1)}, s32[]{:S(2)}) async-start(s8[6291456]{0:T(1024)(128)(4,1)} %bitcast.282), calls=%async_computation | async-start | bytes 8388608
  47.3 33.3 %slice-start.1 = ((s8[6291456]{0:T(1024)(128)(4,1)}), s8[2097152]{0:T(1024)(128)(4,1)S(1)}, s32[]{:S(2)}) async-start(s8[6291456]{0:T(1024)(128)(4,1)} %bitcast.282), calls=%async_computation.1 | async-start | bytes 4194304
  71.2 4.1 %collective-permute-start.7 = (f32[2,1024]{1,0:T(2,128)S(1)}, f32[2,1024]{1,0:T(2,128)S(1)}, u32[]{:S(2)}, u32[]{:S(2)}) collective-permute-start(f32[2,1024]{1,0:T(2,128)S(1)} %pad_maximum_fusion.5), channel_id=1, source_target_pairs={{0,64},{64,0},{1,65},{65,1},{2,66},{66,2},{3,67},{67,3},{4,68},{68... | collective-permute-start | bytes 24584 | tf_op jit(solution)/shard_map/ppermute | solution.py:38
  75.3 2.6 %collective-permute-start.8 = (f32[2,1024]{1,0:T(2,128)S(1)}, f32[2,1024]{1,0:T(2,128)S(1)}, u32[]{:S(2)}, u32[]{:S(2)}) collective-permute-start(f32[2,1024]{1,0:T(2,128)S(1)} %pad_maximum_fusion.6), channel_id=1, source_target_pairs={{0,16},{16,0},{32,48},{48,32},{1,17},{17,1},{33,49},{49,33},{2,18}... | collective-permute-start | bytes 24584 | tf_op jit(solution)/shard_map/ppermute | solution.py:38
  77.9 24.8 %collective-permute-start.9 = (f32[2,1024]{1,0:T(2,128)S(1)}, f32[2,1024]{1,0:T(2,128)S(1)}, u32[]{:S(2)}, u32[]{:S(2)}) collective-permute-start(f32[2,1024]{1,0:T(2,128)S(1)} %pad_maximum_fusion.7), channel_id=1, source_target_pairs={{0,32},{16,48},{32,0},{48,16},{1,33},{17,49},{33,1},{49,17},{2,34}... | collective-permute-start | bytes 24584 | tf_op jit(solution)/shard_map/ppermute | solution.py:38
  107.6 7.1 %collective-permute-start.10 = (f32[2,2048]{1,0:T(2,128)S(1)}, f32[2,2048]{1,0:T(2,128)S(1)}, u32[]{:S(2)}, u32[]{:S(2)}) collective-permute-start(f32[2,2048]{1,0:T(2,128)S(1)} %pad_maximum_fusion.1), channel_id=1, source_target_pairs={{0,1},{1,0},{2,3},{3,2},{4,5},{5,4},{6,7},{7,6},{8,9},{9,8},{10,11... | collective-permute-start | bytes 49160 | tf_op jit(solution)/shard_map/ppermute | solution.py:38
  114.8 2.7 %collective-permute-start.11 = (f32[2,2048]{1,0:T(2,128)S(1)}, f32[2,2048]{1,0:T(2,128)S(1)}, u32[]{:S(2)}, u32[]{:S(2)}) collective-permute-start(f32[2,2048]{1,0:T(2,128)S(1)} %pad_maximum_fusion.2), channel_id=1, source_target_pairs={{0,2},{2,0},{1,3},{3,1},{4,6},{6,4},{5,7},{7,5},{8,10},{10,8},{9,1... | collective-permute-start | bytes 49160 | tf_op jit(solution)/shard_map/ppermute | solution.py:38
  117.5 13.7 %collective-permute-start.12 = (f32[2,2048]{1,0:T(2,128)S(1)}, f32[2,2048]{1,0:T(2,128)S(1)}, u32[]{:S(2)}, u32[]{:S(2)}) collective-permute-start(f32[2,2048]{1,0:T(2,128)S(1)} %pad_maximum_fusion.3), channel_id=1, source_target_pairs={{0,4},{4,0},{8,12},{12,8},{1,5},{5,1},{9,13},{13,9},{2,6},{6,2},{1... | collective-permute-start | bytes 49160 | tf_op jit(solution)/shard_map/ppermute | solution.py:38
  118.8 15.5 %copy-start.1 = (f32[2048,1024]{1,0:T(8,128)S(1)}, f32[2048,1024]{1,0:T(8,128)}, u32[]{:S(2)}) copy-start(f32[2048,1024]{1,0:T(8,128)} %get-tuple-element.276) | copy-start | bytes 25165828
  131.3 13.3 %collective-permute-start.13 = (f32[2,2048]{1,0:T(2,128)S(1)}, f32[2,2048]{1,0:T(2,128)S(1)}, u32[]{:S(2)}, u32[]{:S(2)}) collective-permute-start(f32[2,2048]{1,0:T(2,128)S(1)} %pad_maximum_fusion.4), channel_id=1, source_target_pairs={{0,8},{4,12},{8,0},{12,4},{1,9},{5,13},{9,1},{13,5},{2,10},{6,14},... | collective-permute-start | bytes 49160 | tf_op jit(solution)/shard_map/ppermute | solution.py:38
  145.2 4.8 %copy-start = (f32[1024,768]{1,0:T(8,128)}, f32[1024,768]{1,0:T(8,128)S(1)}, u32[]{:S(2)}) copy-start(f32[1024,768]{1,0:T(8,128)S(1)} %get-tuple-element.310) | copy-start | bytes 9437188
  146.7 6.0 %collective-permute-start.14 = (f32[512,768]{1,0:T(8,128)}, f32[512,768]{1,0:T(8,128)}, u32[]{:S(2)}, u32[]{:S(2)}) collective-permute-start(f32[512,768]{1,0:T(8,128)} %dynamic-slice_bitcast_fusion.1), channel_id=1, source_target_pairs={{0,1},{1,0},{2,3},{3,2},{4,5},{5,4},{6,7},{7,6},{8,9},{9,8},{10,11... | collective-permute-start | bytes 4718600 | tf_op jit(solution)/shard_map/ppermute | solution.py:61
  150.0 6.5 %collective-permute-start.30 = (f32[512,768]{1,0:T(8,128)}, f32[512,768]{1,0:T(8,128)}, u32[]{:S(2)}, u32[]{:S(2)}) collective-permute-start(f32[512,768]{1,0:T(8,128)} %dynamic-slice_bitcast_fusion), channel_id=1, source_target_pairs={{0,1},{1,0},{2,3},{3,2},{4,5},{5,4},{6,7},{7,6},{8,9},{9,8},{10,11... | collective-permute-start | bytes 4718600 | tf_op jit(solution)/shard_map/ppermute | solution.py:61
  154.8 6.2 %collective-permute-start.18 = (f32[64,768]{1,0:T(8,128)S(1)}, f32[64,768]{1,0:T(8,128)S(1)}, u32[]{:S(2)}, u32[]{:S(2)}) collective-permute-start(f32[64,768]{1,0:T(8,128)S(1)} %dynamic-slice_bitcast_fusion.4), channel_id=1, source_target_pairs={{0,12},{4,0},{8,4},{12,8},{1,13},{5,1},{9,5},{13,9},{2,14},{6,2},{... | collective-permute-start | bytes 589832 | tf_op jit(solution)/shard_map/ppermute | solution.py:66
  155.1 7.4 %collective-permute-start.15 = (f32[64,768]{1,0:T(8,128)S(1)}, f32[64,768]{1,0:T(8,128)S(1)}, u32[]{:S(2)}, u32[]{:S(2)}) collective-permute-start(f32[64,768]{1,0:T(8,128)S(1)} %dynamic-slice_bitcast_fusion.5), channel_id=1, source_target_pairs={{0,4},{4,8},{8,12},{12,0},{1,5},{5,9},{9,13},{13,1},{2,6},{6,10},{... | collective-permute-start | bytes 589832 | tf_op jit(solution)/shard_map/ppermute | solution.py:65
  158.2 7.0 %collective-permute-start.34 = (f32[64,768]{1,0:T(8,128)S(1)}, f32[64,768]{1,0:T(8,128)S(1)}, u32[]{:S(2)}, u32[]{:S(2)}) collective-permute-start(f32[64,768]{1,0:T(8,128)S(1)} %dynamic-slice_bitcast_fusion.2), channel_id=1, source_target_pairs={{0,12},{4,0},{8,4},{12,8},{1,13},{5,1},{9,5},{13,9},{2,14},{6,2},{... | collective-permute-start | bytes 589832 | tf_op jit(solution)/shard_map/ppermute | solution.py:66
  159.7 6.8 %collective-permute-start.31 = (f32[64,768]{1,0:T(8,128)S(1)}, f32[64,768]{1,0:T(8,128)S(1)}, u32[]{:S(2)}, u32[]{:S(2)}) collective-permute-start(f32[64,768]{1,0:T(8,128)S(1)} %dynamic-slice_bitcast_fusion.3), channel_id=1, source_target_pairs={{0,4},{4,8},{8,12},{12,0},{1,5},{5,9},{9,13},{13,1},{2,6},{6,10},{... | collective-permute-start | bytes 589832 | tf_op jit(solution)/shard_map/ppermute | solution.py:65
  161.1 8.4 %collective-permute-start.19 = (f32[64,768]{1,0:T(8,128)S(1)}, f32[64,768]{1,0:T(8,128)S(1)}, u32[]{:S(2)}, u32[]{:S(2)}) collective-permute-start(f32[64,768]{1,0:T(8,128)S(1)} %bitcast_add_fusion.10), channel_id=1, source_target_pairs={{0,12},{4,0},{8,4},{12,8},{1,13},{5,1},{9,5},{13,9},{2,14},{6,2},{... | collective-permute-start | bytes 589832 | tf_op jit(solution)/shard_map/ppermute | solution.py:66
  162.6 8.3 %collective-permute-start.16 = (f32[64,768]{1,0:T(8,128)S(1)}, f32[64,768]{1,0:T(8,128)S(1)}, u32[]{:S(2)}, u32[]{:S(2)}) collective-permute-start(f32[64,768]{1,0:T(8,128)S(1)} %bitcast_add_fusion.13), channel_id=1, source_target_pairs={{0,4},{4,8},{8,12},{12,0},{1,5},{5,9},{9,13},{13,1},{2,6},{6,10},{... | collective-permute-start | bytes 589832 | tf_op jit(solution)/shard_map/ppermute | solution.py:65
  165.3 8.4 %collective-permute-start.35 = (f32[64,768]{1,0:T(8,128)S(1)}, f32[64,768]{1,0:T(8,128)S(1)}, u32[]{:S(2)}, u32[]{:S(2)}) collective-permute-start(f32[64,768]{1,0:T(8,128)S(1)} %bitcast_add_fusion.4), channel_id=1, source_target_pairs={{0,12},{4,0},{8,4},{12,8},{1,13},{5,1},{9,5},{13,9},{2,14},{6,2},{... | collective-permute-start | bytes 589832 | tf_op jit(solution)/shard_map/ppermute | solution.py:66
  166.5 7.8 %collective-permute-start.32 = (f32[64,768]{1,0:T(8,128)S(1)}, f32[64,768]{1,0:T(8,128)S(1)}, u32[]{:S(2)}, u32[]{:S(2)}) collective-permute-start(f32[64,768]{1,0:T(8,128)S(1)} %bitcast_add_fusion.7), channel_id=1, source_target_pairs={{0,4},{4,8},{8,12},{12,0},{1,5},{5,9},{9,13},{13,1},{2,6},{6,10},{... | collective-permute-start | bytes 589832 | tf_op jit(solution)/shard_map/ppermute | solution.py:65
  169.5 8.4 %collective-permute-start.20 = (f32[64,768]{1,0:T(8,128)S(1)}, f32[64,768]{1,0:T(8,128)S(1)}, u32[]{:S(2)}, u32[]{:S(2)}) collective-permute-start(f32[64,768]{1,0:T(8,128)S(1)} %bitcast_add_fusion.9), channel_id=1, source_target_pairs={{0,12},{4,0},{8,4},{12,8},{1,13},{5,1},{9,5},{13,9},{2,14},{6,2},{... | collective-permute-start | bytes 589832 | tf_op jit(solution)/shard_map/ppermute | solution.py:66
  170.9 7.4 %collective-permute-start.17 = (f32[64,768]{1,0:T(8,128)S(1)}, f32[64,768]{1,0:T(8,128)S(1)}, u32[]{:S(2)}, u32[]{:S(2)}) collective-permute-start(f32[64,768]{1,0:T(8,128)S(1)} %bitcast_add_fusion.12), channel_id=1, source_target_pairs={{0,4},{4,8},{8,12},{12,0},{1,5},{5,9},{9,13},{13,1},{2,6},{6,10},{... | collective-permute-start | bytes 589832 | tf_op jit(solution)/shard_map/ppermute | solution.py:65
  173.7 8.4 %collective-permute-start.36 = (f32[64,768]{1,0:T(8,128)S(1)}, f32[64,768]{1,0:T(8,128)S(1)}, u32[]{:S(2)}, u32[]{:S(2)}) collective-permute-start(f32[64,768]{1,0:T(8,128)S(1)} %bitcast_add_fusion.3), channel_id=1, source_target_pairs={{0,12},{4,0},{8,4},{12,8},{1,13},{5,1},{9,5},{13,9},{2,14},{6,2},{... | collective-permute-start | bytes 589832 | tf_op jit(solution)/shard_map/ppermute | solution.py:66
  174.4 8.3 %collective-permute-start.33 = (f32[64,768]{1,0:T(8,128)S(1)}, f32[64,768]{1,0:T(8,128)S(1)}, u32[]{:S(2)}, u32[]{:S(2)}) collective-permute-start(f32[64,768]{1,0:T(8,128)S(1)} %bitcast_add_fusion.6), channel_id=1, source_target_pairs={{0,4},{4,8},{8,12},{12,0},{1,5},{5,9},{9,13},{13,1},{2,6},{6,10},{... | collective-permute-start | bytes 589832 | tf_op jit(solution)/shard_map/ppermute | solution.py:65
  178.4 4.9 %collective-permute-start.21 = (f32[64,768]{1,0:T(8,128)S(1)}, f32[64,768]{1,0:T(8,128)S(1)}, u32[]{:S(2)}, u32[]{:S(2)}) collective-permute-start(f32[64,768]{1,0:T(8,128)S(1)} %fusion.24), channel_id=1, source_target_pairs={{0,2},{2,0},{1,3},{3,1},{4,6},{6,4},{5,7},{7,5},{8,10},{10,8},{9,1... | collective-permute-start | bytes 589832 | tf_op jit(solution)/shard_map/ppermute | solution.py:68
  182.8 6.1 %collective-permute-start.37 = (f32[64,768]{1,0:T(8,128)S(1)}, f32[64,768]{1,0:T(8,128)S(1)}, u32[]{:S(2)}, u32[]{:S(2)}) collective-permute-start(f32[64,768]{1,0:T(8,128)S(1)} %fusion.18), channel_id=1, source_target_pairs={{0,2},{2,0},{1,3},{3,1},{4,6},{6,4},{5,7},{7,5},{8,10},{10,8},{9,1... | collective-permute-start | bytes 589832 | tf_op jit(solution)/shard_map/ppermute | solution.py:68
  183.4 9.7 %collective-permute-start.22 = (f32[64,768]{1,0:T(8,128)S(1)}, f32[64,768]{1,0:T(8,128)S(1)}, u32[]{:S(2)}, u32[]{:S(2)}) collective-permute-start(f32[64,768]{1,0:T(8,128)S(1)} %fusion.28), channel_id=1, source_target_pairs={{0,2},{2,0},{1,3},{3,1},{4,6},{6,4},{5,7},{7,5},{8,10},{10,8},{9,1... | collective-permute-start | bytes 589832 | tf_op jit(solution)/shard_map/ppermute | solution.py:71
  189.0 8.3 %collective-permute-start.38 = (f32[64,768]{1,0:T(8,128)S(1)}, f32[64,768]{1,0:T(8,128)S(1)}, u32[]{:S(2)}, u32[]{:S(2)}) collective-permute-start(f32[64,768]{1,0:T(8,128)S(1)} %fusion.22), channel_id=1, source_target_pairs={{0,2},{2,0},{1,3},{3,1},{4,6},{6,4},{5,7},{7,5},{8,10},{10,8},{9,1... | collective-permute-start | bytes 589832 | tf_op jit(solution)/shard_map/ppermute | solution.py:71
  193.2 8.7 %collective-permute-start.23 = (f32[64,768]{1,0:T(8,128)S(1)}, f32[64,768]{1,0:T(8,128)S(1)}, u32[]{:S(2)}, u32[]{:S(2)}) collective-permute-start(f32[64,768]{1,0:T(8,128)S(1)} %get-tuple-element.288), channel_id=1, source_target_pairs={{0,4},{4,8},{8,12},{12,0},{1,5},{5,9},{9,13},{13,1},{2,6},{6,10},{... | collective-permute-start | bytes 589832 | tf_op jit(solution)/shard_map/ppermute | solution.py:76
  194.5 7.5 %collective-permute-start.24 = (f32[64,768]{1,0:T(8,128)S(1)}, f32[64,768]{1,0:T(8,128)S(1)}, u32[]{:S(2)}, u32[]{:S(2)}) collective-permute-start(f32[64,768]{1,0:T(8,128)S(1)} %get-tuple-element.287), channel_id=1, source_target_pairs={{0,12},{4,0},{8,4},{12,8},{1,13},{5,1},{9,5},{13,9},{2,14},{6,2},{... | collective-permute-start | bytes 589832 | tf_op jit(solution)/shard_map/ppermute | solution.py:77
  197.4 7.2 %collective-permute-start.39 = (f32[64,768]{1,0:T(8,128)S(1)}, f32[64,768]{1,0:T(8,128)S(1)}, u32[]{:S(2)}, u32[]{:S(2)}) collective-permute-start(f32[64,768]{1,0:T(8,128)S(1)} %get-tuple-element.290), channel_id=1, source_target_pairs={{0,4},{4,8},{8,12},{12,0},{1,5},{5,9},{9,13},{13,1},{2,6},{6,10},{... | collective-permute-start | bytes 589832 | tf_op jit(solution)/shard_map/ppermute | solution.py:76
  198.7 8.0 %collective-permute-start.40 = (f32[64,768]{1,0:T(8,128)S(1)}, f32[64,768]{1,0:T(8,128)S(1)}, u32[]{:S(2)}, u32[]{:S(2)}) collective-permute-start(f32[64,768]{1,0:T(8,128)S(1)} %get-tuple-element.289), channel_id=1, source_target_pairs={{0,12},{4,0},{8,4},{12,8},{1,13},{5,1},{9,5},{13,9},{2,14},{6,2},{... | collective-permute-start | bytes 589832 | tf_op jit(solution)/shard_map/ppermute | solution.py:77
  201.8 8.2 %collective-permute-start.25 = (f32[64,768]{1,0:T(8,128)S(1)}, f32[64,768]{1,0:T(8,128)S(1)}, u32[]{:S(2)}, u32[]{:S(2)}) collective-permute-start(f32[64,768]{1,0:T(8,128)S(1)} %collective-permute-done.23), channel_id=1, source_target_pairs={{0,4},{4,8},{8,12},{12,0},{1,5},{5,9},{9,13},{13,1},{2,6},{6,10},{... | collective-permute-start | bytes 589832 | tf_op jit(solution)/shard_map/ppermute | solution.py:76
  202.0 8.2 %collective-permute-start.26 = (f32[64,768]{1,0:T(8,128)S(1)}, f32[64,768]{1,0:T(8,128)S(1)}, u32[]{:S(2)}, u32[]{:S(2)}) collective-permute-start(f32[64,768]{1,0:T(8,128)S(1)} %collective-permute-done.24), channel_id=1, source_target_pairs={{0,12},{4,0},{8,4},{12,8},{1,13},{5,1},{9,5},{13,9},{2,14},{6,2},{... | collective-permute-start | bytes 589832 | tf_op jit(solution)/shard_map/ppermute | solution.py:77
  204.6 8.2 %collective-permute-start.41 = (f32[64,768]{1,0:T(8,128)S(1)}, f32[64,768]{1,0:T(8,128)S(1)}, u32[]{:S(2)}, u32[]{:S(2)}) collective-permute-start(f32[64,768]{1,0:T(8,128)S(1)} %collective-permute-done.39), channel_id=1, source_target_pairs={{0,4},{4,8},{8,12},{12,0},{1,5},{5,9},{9,13},{13,1},{2,6},{6,10},{... | collective-permute-start | bytes 589832 | tf_op jit(solution)/shard_map/ppermute | solution.py:76
  206.7 8.5 %collective-permute-start.42 = (f32[64,768]{1,0:T(8,128)S(1)}, f32[64,768]{1,0:T(8,128)S(1)}, u32[]{:S(2)}, u32[]{:S(2)}) collective-permute-start(f32[64,768]{1,0:T(8,128)S(1)} %collective-permute-done.40), channel_id=1, source_target_pairs={{0,12},{4,0},{8,4},{12,8},{1,13},{5,1},{9,5},{13,9},{2,14},{6,2},{... | collective-permute-start | bytes 589832 | tf_op jit(solution)/shard_map/ppermute | solution.py:77
  210.0 8.1 %collective-permute-start.27 = (f32[64,768]{1,0:T(8,128)S(1)}, f32[64,768]{1,0:T(8,128)S(1)}, u32[]{:S(2)}, u32[]{:S(2)}) collective-permute-start(f32[64,768]{1,0:T(8,128)S(1)} %collective-permute-done.25), channel_id=1, source_target_pairs={{0,4},{4,8},{8,12},{12,0},{1,5},{5,9},{9,13},{13,1},{2,6},{6,10},{... | collective-permute-start | bytes 589832 | tf_op jit(solution)/shard_map/ppermute | solution.py:76
  210.1 8.7 %collective-permute-start.28 = (f32[64,768]{1,0:T(8,128)S(1)}, f32[64,768]{1,0:T(8,128)S(1)}, u32[]{:S(2)}, u32[]{:S(2)}) collective-permute-start(f32[64,768]{1,0:T(8,128)S(1)} %collective-permute-done.26), channel_id=1, source_target_pairs={{0,12},{4,0},{8,4},{12,8},{1,13},{5,1},{9,5},{13,9},{2,14},{6,2},{... | collective-permute-start | bytes 589832 | tf_op jit(solution)/shard_map/ppermute | solution.py:77
  212.8 14.9 %collective-permute-start.43 = (f32[64,768]{1,0:T(8,128)S(1)}, f32[64,768]{1,0:T(8,128)S(1)}, u32[]{:S(2)}, u32[]{:S(2)}) collective-permute-start(f32[64,768]{1,0:T(8,128)S(1)} %collective-permute-done.41), channel_id=1, source_target_pairs={{0,4},{4,8},{8,12},{12,0},{1,5},{5,9},{9,13},{13,1},{2,6},{6,10},{... | collective-permute-start | bytes 589832 | tf_op jit(solution)/shard_map/ppermute | solution.py:76
  215.3 13.1 %collective-permute-start.44 = (f32[64,768]{1,0:T(8,128)S(1)}, f32[64,768]{1,0:T(8,128)S(1)}, u32[]{:S(2)}, u32[]{:S(2)}) collective-permute-start(f32[64,768]{1,0:T(8,128)S(1)} %collective-permute-done.42), channel_id=1, source_target_pairs={{0,12},{4,0},{8,4},{12,8},{1,13},{5,1},{9,5},{13,9},{2,14},{6,2},{... | collective-permute-start | bytes 589832 | tf_op jit(solution)/shard_map/ppermute | solution.py:77
  219.5 11.4 %collective-permute-start.29 = (f32[512,768]{1,0:T(8,128)S(1)}, f32[512,768]{1,0:T(8,128)}, u32[]{:S(2)}, u32[]{:S(2)}) collective-permute-start(f32[512,768]{1,0:T(8,128)S(1)} %bitcast.244), channel_id=1, source_target_pairs={{0,1},{1,0},{2,3},{3,2},{4,5},{5,4},{6,7},{7,6},{8,9},{9,8},{10,11... | collective-permute-start | bytes 4718600 | tf_op jit(solution)/shard_map/ppermute | solution.py:81
  229.0 4.1 %collective-permute-start.45 = (f32[512,768]{1,0:T(8,128)S(1)}, f32[512,768]{1,0:T(8,128)}, u32[]{:S(2)}, u32[]{:S(2)}) collective-permute-start(f32[512,768]{1,0:T(8,128)S(1)} %bitcast.242), channel_id=1, source_target_pairs={{0,1},{1,0},{2,3},{3,2},{4,5},{5,4},{6,7},{7,6},{8,9},{9,8},{10,11... | collective-permute-start | bytes 4718600 | tf_op jit(solution)/shard_map/ppermute | solution.py:81

commit v7 on v6

--- a/solution.py
+++ b/solution.py
@@ -107,7 +107,12 @@
     querybank_similarity = similar(bank, features)
     local_peak = jnp.max(querybank_similarity, axis=0)
     local_total = jnp.sum(jnp.exp(querybank_similarity - local_peak[None, :]), axis=0)
-    raw = lax.optimization_barrier(similar(images, features))
+    split = images.shape[0] // 2
+    raw = jnp.concatenate(
+        [lax.optimization_barrier(similar(images[:split], features)),
+         lax.optimization_barrier(similar(images[split:], features))],
+        axis=0,
+    )
     peak, total = merge_peaks(img_rounds, local_peak, local_total)
     col_log = peak + jnp.log(total)
     logits = raw - col_log[None, :]

time: 242 us -> 241 us (level)
  waiting for transfers between devices: 55.9 us -> 53.4 us
    ppermute x7, waiting for transfers between devices: 8.19 us -> 5.72 us  [merge_peaks(): other = lax.ppermute(pair, axis, [(j, j ^ dist) for j in range(size)])]
    dot_general x2 -> x3, matrix products: 44.7 us -> 44.5 us  [similar(): lax.dot_general(query_factor, target_factor, (((1,), (0,)), ((), ())), pr...]
  transfers between devices with their start and end apart: 46 -> 46, of which waited for: 21 -> 20; matrix products, arithmetic and copies ran while one was open for 32% -> 32% of each run, Pallas kernels for 0% -> 0%
where the time goes in v7:
time: 241 us; the launch traced here: 238 us
  starting transfers between devices  67.3 us (28%)
  matrix products  67.3 us (28%)
  waiting for transfers between devices  53.4 us (22%)
  other arithmetic  43.5 us (18%)
  local copies, waits for them, and re-layouts  5.39 us (2%)
    dot_general x3, matrix products, similar(): lax.dot_general(query_factor, target_factor, (((1,), (0,)), ((), ())), pr...  44.5 us
    dot_general x2, matrix products, rescaled_affinity(): lax.dot_general(weights, features, (((1,), (1,)), ((), ())), precision=la...  22.8 us
    ppermute x7, starting transfers between devices, merge_peaks(): other = lax.ppermute(pair, axis, [(j, j ^ dist) for j in range(size)])  16.1 us
    ppermute x6, waiting for transfers between devices, reduce_rows(): lax.ppermute(left, 'x', ring('x', x_size, -1))  15 us
    ppermute x3, waiting for transfers between devices, gather_features(): right = lax.ppermute(right, 'y', ring('y', y_size, 1))  12.1 us
    ppermute x6, starting transfers between devices, reduce_rows(): left = lax.ppermute(left, 'x', ring('x', x_size, -1))  12 us
    ppermute x2, starting transfers between devices, reduce_rows(): other = lax.ppermute(held, 'core', swap)  8.35 us
    ppermute x1, waiting for transfers between devices, gather_features(): other = lax.ppermute(captions, 'zh', [(0, 1), (1, 0)])  7.67 us
  transfers between devices with their start and end apart: 46, of which 20 were waited for; matrix products, arithmetic and copies ran while one was open for 32% of the time, Pallas kernels for 0%

profile of v7, /device:TPU:1, one launch (start us, length us, event | category | flops | bytes accessed | tf_op | source)
XLA Modules:
  0.0 238.2 jit_solution(7876026790906097846)
XLA Ops:
  0.0 4.4 %collective-permute-start = (f32[1024,96]{0,1:T(8,128)}, f32[1024,96]{0,1:T(8,128)S(1)}, u32[]{:S(2)}, u32[]{:S(2)}) collective-permute-start(f32[1024,96]{0,1:T(8,128)} %param.46), channel_id=1, source_target_pairs={{0,64},{64,0},{1,65},{65,1},{2,66},{66,2},{3,67},{67,3},{4,68},{68... | collective-permute-start | bytes 1179656 | tf_op jit(solution)/shard_map/ppermute | solution.py:89
  4.4 1.4 and_reduce_fusion.10
  5.8 7.7 %collective-permute-done = f32[1024,96]{0,1:T(8,128)S(1)} collective-permute-done((f32[1024,96]{0,1:T(8,128)}, f32[1024,96]{0,1:T(8,128)S(1)}, u32[]{:S(2)}, u32[]{:S(2)}) %collective-permute-start) | collective-permute-done | bytes 393248 | tf_op jit(solution)/shard_map/ppermute | solution.py:89
  13.5 1.4 maximum_select_fusion.3
  14.8 1.0 slice_bitcast_fusion
  15.8 1.3 collective-permute-start.1
  17.1 1.4 collective-permute-start.2
  22.6 4.2 %collective-permute-done.1 = f32[1024,96]{0,1:T(8,128)} collective-permute-done((f32[1024,96]{0,1:T(8,128)}, f32[1024,96]{0,1:T(8,128)}, u32[]{:S(2)}, u32[]{:S(2)}) %collective-permute-start.1) | collective-permute-done | bytes 393248 | tf_op jit(solution)/shard_map/ppermute | solution.py:94
  26.9 2.7 %collective-permute-start.4 = (f32[1024,96]{0,1:T(8,128)}, f32[1024,96]{0,1:T(8,128)S(1)}, u32[]{:S(2)}, u32[]{:S(2)}) collective-permute-start(f32[1024,96]{0,1:T(8,128)} %collective-permute-done.2), channel_id=1, source_target_pairs={{0,48},{16,0},{32,16},{48,32},{1,49},{17,1},{33,17},{49,33},{2,50}... | collective-permute-start | bytes 1179656 | tf_op jit(solution)/shard_map/ppermute | solution.py:95
  29.6 1.9 fusion.25
  31.5 1.6 fusion.24
  33.1 3.7 %collective-permute-done.3 = f32[1024,96]{0,1:T(8,128)S(1)} collective-permute-done((f32[1024,96]{0,1:T(8,128)}, f32[1024,96]{0,1:T(8,128)S(1)}, u32[]{:S(2)}, u32[]{:S(2)}) %collective-permute-start.3) | collective-permute-done | bytes 393248 | tf_op jit(solution)/shard_map/ppermute | solution.py:94
  36.8 3.1 %collective-permute-start.6 = (f32[1024,96]{0,1:T(8,128)S(1)}, f32[1024,96]{0,1:T(8,128)S(1)}, u32[]{:S(2)}, u32[]{:S(2)}) collective-permute-start(f32[1024,96]{0,1:T(8,128)S(1)} %collective-permute-done.4), channel_id=1, source_target_pairs={{0,48},{16,0},{32,16},{48,32},{1,49},{17,1},{33,17},{49,33},{2,50}... | collective-permute-start | bytes 1179656 | tf_op jit(solution)/shard_map/ppermute | solution.py:95
  41.4 4.2 %collective-permute-done.5 = f32[1024,96]{0,1:T(8,128)S(1)} collective-permute-done((f32[1024,96]{0,1:T(8,128)S(1)}, f32[1024,96]{0,1:T(8,128)S(1)}, u32[]{:S(2)}, u32[]{:S(2)}) %collective-permute-start.5) | collective-permute-done | bytes 393248 | tf_op jit(solution)/shard_map/ppermute | solution.py:94
  46.4 0.8 fusion.20
  47.3 22.4 %fusion = (f32[1024]{0:T(1024)S(1)}, f32[1024,2048]{0,1:T(8,128)S(1)}) fusion(f32[768,1024]{1,0:T(8,128)S(1)} %bitcast.248, f32[2048,768]{1,0:T(8,128)S(1)} %copy-done.7), kind=kOutput, calls=%fused_computation.4 | convolution fusion | flops 19331547136 | bytes 17829888 | tf_op jit(solution)/shard_map/dot_general | solution.py:15
  69.7 1.4 exponential_reduce_fusion
  71.2 1.8 collective-permute-start.7
  72.9 2.3 collective-permute-done.7
  75.6 11.0 %bitcast_multiply_fusion.2 = f32[1024,1024]{1,0:T(8,128)S(1)} fusion(f32[768,1024]{1,0:T(8,128)S(1)} %bitcast.249, f32[2048,768]{1,0:T(8,128)S(1)} %bitcast.286), kind=kOutput, calls=%fused_computation.12 | convolution fusion | flops 9664724992 | bytes 10485760 | tf_op jit(solution)/shard_map/dot_general | solution.py:15
  86.7 3.7 %collective-permute-start.9 = (f32[2,1024]{1,0:T(2,128)S(1)}, f32[2,1024]{1,0:T(2,128)S(1)}, u32[]{:S(2)}, u32[]{:S(2)}) collective-permute-start(f32[2,1024]{1,0:T(2,128)S(1)} %pad_maximum_fusion.7), channel_id=1, source_target_pairs={{0,32},{16,48},{32,0},{48,16},{1,33},{17,49},{33,1},{49,17},{2,34}... | collective-permute-start | bytes 24584 | tf_op jit(solution)/shard_map/ppermute | solution.py:38
  90.4 11.0 %bitcast_multiply_fusion.1 = f32[1024,1024]{1,0:T(8,128)S(1)} fusion(f32[768,1024]{1,0:T(8,128)S(1)} %bitcast.250, f32[2048,768]{1,0:T(8,128)S(1)} %bitcast.286), kind=kOutput, calls=%fused_computation.11 | convolution fusion | flops 9664724992 | bytes 10485760 | tf_op jit(solution)/shard_map/dot_general | solution.py:15
  102.2 4.9 %fusion.62 = (f32[2048]{0:T(1024)S(1)}, f32[2048,1024]{1,0:T(8,128)}) fusion(f32[2048]{0:T(1024)S(1)} %fusion.1, f32[1024]{0:T(1024)S(1)} %bitcast.276, f32[1024,1024]{1,0:T(8,128)S(1)} %bitcast_multiply_fusion.1, f32[1024,1024]{1,0:T(8,128)S(1)} %bitcast_multiply_fusion.2), kind=kLoop, calls=%fused_computation.206 | loop fusion | flops 8386560 | bytes 16797696 | tf_op jit(solution)/shard_map/reduce_sum | solution.py:121
  107.1 6.2 %collective-permute-start.10 = (f32[2,2048]{1,0:T(2,128)S(1)}, f32[2,2048]{1,0:T(2,128)S(1)}, u32[]{:S(2)}, u32[]{:S(2)}) collective-permute-start(f32[2,2048]{1,0:T(2,128)S(1)} %pad_maximum_fusion.1), channel_id=1, source_target_pairs={{0,1},{1,0},{2,3},{3,2},{4,5},{5,4},{6,7},{7,6},{8,9},{9,8},{10,11... | collective-permute-start | bytes 49160 | tf_op jit(solution)/shard_map/ppermute | solution.py:38
  114.3 2.5 %collective-permute-done.11 = f32[2,2048]{1,0:T(2,128)S(1)} collective-permute-done((f32[2,2048]{1,0:T(2,128)S(1)}, f32[2,2048]{1,0:T(2,128)S(1)}, u32[]{:S(2)}, u32[]{:S(2)}) %collective-permute-start.11) | collective-permute-done | bytes 16416 | tf_op jit(solution)/shard_map/ppermute | solution.py:38
  116.9 1.3 collective-permute-start.12
  118.2 12.4 %fusion.4 = f32[1024,768]{1,0:T(8,128)S(1)} fusion(f32[768,1024]{1,0:T(8,128)S(1)} %bitcast.251, f32[2048,1024]{1,0:T(8,128)} %get-tuple-element.276), kind=kOutput, calls=%fused_computation.9 | convolution fusion | flops 9663676416 | bytes 10485760 | tf_op jit(solution)/shard_map/dot_general | solution.py:26
  130.7 2.7 %collective-permute-start.13 = (f32[2,2048]{1,0:T(2,128)S(1)}, f32[2,2048]{1,0:T(2,128)S(1)}, u32[]{:S(2)}, u32[]{:S(2)}) collective-permute-start(f32[2,2048]{1,0:T(2,128)S(1)} %pad_maximum_fusion.4), channel_id=1, source_target_pairs={{0,8},{4,12},{8,0},{12,4},{1,9},{5,13},{9,1},{13,5},{2,10},{6,14},... | collective-permute-start | bytes 49160 | tf_op jit(solution)/shard_map/ppermute | solution.py:38
  133.5 10.4 %fusion.2 = f32[1024,768]{1,0:T(8,128)S(1)} fusion(f32[768,1024]{1,0:T(8,128)S(1)} %bitcast.252, f32[2048,1024]{1,0:T(8,128)S(1)} %copy-done.1), kind=kOutput, calls=%fused_computation.7 | convolution fusion | flops 9663676416 | bytes 10485760 | tf_op jit(solution)/shard_map/dot_general | solution.py:26
  144.5 1.4 dynamic-slice_bitcast_fusion.1
  145.9 2.1 collective-permute-start.14
  147.9 1.3 dynamic-slice_bitcast_fusion
  151.9 2.1 bitcast_add_fusion.1
  154.4 1.3 collective-permute-start.15
  155.8 1.6 bitcast_add_fusion
  157.5 1.5 collective-permute-start.34
  159.1 1.2 collective-permute-done.18
  160.4 1.5 collective-permute-start.19
  162.0 2.6 %collective-permute-done.34 = f32[64,768]{1,0:T(8,128)S(1)} collective-permute-done((f32[64,768]{1,0:T(8,128)S(1)}, f32[64,768]{1,0:T(8,128)S(1)}, u32[]{:S(2)}, u32[]{:S(2)}) %collective-permute-start.34) | collective-permute-done | bytes 196640 | tf_op jit(solution)/shard_map/ppermute | solution.py:66
  164.6 1.2 collective-permute-start.35
  166.2 2.6 %collective-permute-done.19 = f32[64,768]{1,0:T(8,128)S(1)} collective-permute-done((f32[64,768]{1,0:T(8,128)S(1)}, f32[64,768]{1,0:T(8,128)S(1)}, u32[]{:S(2)}, u32[]{:S(2)}) %collective-permute-start.19) | collective-permute-done | bytes 196640 | tf_op jit(solution)/shard_map/ppermute | solution.py:66
  168.8 1.4 collective-permute-start.20
  170.4 2.5 %collective-permute-done.35 = f32[64,768]{1,0:T(8,128)S(1)} collective-permute-done((f32[64,768]{1,0:T(8,128)S(1)}, f32[64,768]{1,0:T(8,128)S(1)}, u32[]{:S(2)}, u32[]{:S(2)}) %collective-permute-start.35) | collective-permute-done | bytes 196640 | tf_op jit(solution)/shard_map/ppermute | solution.py:66
  173.7 1.0 collective-permute-start.33
  174.6 2.6 %collective-permute-done.20 = f32[64,768]{1,0:T(8,128)S(1)} collective-permute-done((f32[64,768]{1,0:T(8,128)S(1)}, f32[64,768]{1,0:T(8,128)S(1)}, u32[]{:S(2)}, u32[]{:S(2)}) %collective-permute-start.20) | collective-permute-done | bytes 196640 | tf_op jit(solution)/shard_map/ppermute | solution.py:66
  177.8 3.6 %collective-permute-done.36 = f32[64,768]{1,0:T(8,128)S(1)} collective-permute-done((f32[64,768]{1,0:T(8,128)S(1)}, f32[64,768]{1,0:T(8,128)S(1)}, u32[]{:S(2)}, u32[]{:S(2)}) %collective-permute-start.36) | collective-permute-done | bytes 196640 | tf_op jit(solution)/shard_map/ppermute | solution.py:66
  182.7 1.2 collective-permute-start.22
  183.8 4.4 %collective-permute-done.37 = f32[64,768]{1,0:T(8,128)S(1)} collective-permute-done((f32[64,768]{1,0:T(8,128)S(1)}, f32[64,768]{1,0:T(8,128)S(1)}, u32[]{:S(2)}, u32[]{:S(2)}) %collective-permute-start.37) | collective-permute-done | bytes 196640 | tf_op jit(solution)/shard_map/ppermute | solution.py:68
  188.4 4.0 %collective-permute-done.22 = f32[64,768]{1,0:T(8,128)S(1)} collective-permute-done((f32[64,768]{1,0:T(8,128)S(1)}, f32[64,768]{1,0:T(8,128)S(1)}, u32[]{:S(2)}, u32[]{:S(2)}) %collective-permute-start.22) | collective-permute-done | bytes 196640 | tf_op jit(solution)/shard_map/ppermute | solution.py:71
  192.5 1.3 collective-permute-start.23
  193.8 1.4 collective-permute-start.24
  195.2 1.4 collective-permute-done.38
  196.7 1.3 collective-permute-start.39
  198.0 1.4 collective-permute-start.40
  201.2 2.7 %collective-permute-start.26 = (f32[64,768]{1,0:T(8,128)S(1)}, f32[64,768]{1,0:T(8,128)S(1)}, u32[]{:S(2)}, u32[]{:S(2)}) collective-permute-start(f32[64,768]{1,0:T(8,128)S(1)} %collective-permute-done.24), channel_id=1, source_target_pairs={{0,12},{4,0},{8,4},{12,8},{1,13},{5,1},{9,5},{13,9},{2,14},{6,2},{... | collective-permute-start | bytes 589832 | tf_op jit(solution)/shard_map/ppermute | solution.py:77
  206.0 2.0 collective-permute-start.42
  209.4 2.7 %collective-permute-start.28 = (f32[64,768]{1,0:T(8,128)S(1)}, f32[64,768]{1,0:T(8,128)S(1)}, u32[]{:S(2)}, u32[]{:S(2)}) collective-permute-start(f32[64,768]{1,0:T(8,128)S(1)} %collective-permute-done.26), channel_id=1, source_target_pairs={{0,12},{4,0},{8,4},{12,8},{1,13},{5,1},{9,5},{13,9},{2,14},{6,2},{... | collective-permute-start | bytes 589832 | tf_op jit(solution)/shard_map/ppermute | solution.py:77
  212.1 1.0 collective-permute-start.43
  214.5 1.8 collective-permute-start.44
  218.8 8.2 %collective-permute-start.29 = (f32[512,768]{1,0:T(8,128)S(1)}, f32[512,768]{1,0:T(8,128)}, u32[]{:S(2)}, u32[]{:S(2)}) collective-permute-start(f32[512,768]{1,0:T(8,128)S(1)} %bitcast.246), channel_id=1, source_target_pairs={{0,1},{1,0},{2,3},{3,2},{4,5},{5,4},{6,7},{7,6},{8,9},{9,8},{10,11... | collective-permute-start | bytes 4718600 | tf_op jit(solution)/shard_map/ppermute | solution.py:81
  228.4 1.8 collective-permute-done.29
  230.2 2.2 maximum_select_fusion
  232.4 2.2 maximum_select_fusion.1
  234.6 3.1 %pad_maximum_fusion = f32[2048,768]{1,0:T(8,128)} fusion(f32[1024,768]{1,0:T(8,128)S(1)} %bitcast.243, f32[1024,768]{1,0:T(8,128)S(1)} %bitcast.242), kind=kLoop, calls=%fused_computation.6 | loop fusion | flops 1572864 | bytes 12582912 | tf_op jit(solution)/shard_map/concatenate | solution.py:132
  (141 shorter events, 26.6 us)
Async XLA Ops:
  0.0 19.4 %copy-start.5 = (s32[4]{0:T(128)S(1)}, s32[4]{0:T(128)}, u32[]{:S(2)}) copy-start(s32[4]{0:T(128)} %constant.690.clone.1) | copy-start | bytes 52
  0.0 18.6 %copy-start.6 = (s32[4]{0:T(128)S(1)}, s32[4]{0:T(128)}, u32[]{:S(2)}) copy-start(s32[4]{0:T(128)} %constant.684.clone.1) | copy-start | bytes 52
  0.0 13.5 %collective-permute-start = (f32[1024,96]{0,1:T(8,128)}, f32[1024,96]{0,1:T(8,128)S(1)}, u32[]{:S(2)}, u32[]{:S(2)}) collective-permute-start(f32[1024,96]{0,1:T(8,128)} %param.46), channel_id=1, source_target_pairs={{0,64},{64,0},{1,65},{65,1},{2,66},{66,2},{3,67},{67,3},{4,68},{68... | collective-permute-start | bytes 1179656 | tf_op jit(solution)/shard_map/ppermute | solution.py:89
  13.5 7.5 %copy-start.3 = (f32[1024,96]{0,1:T(8,128)}, f32[1024,96]{0,1:T(8,128)S(1)}, u32[]{:S(2)}) copy-start(f32[1024,96]{0,1:T(8,128)S(1)} %collective-permute-done) | copy-start | bytes 1179652
  13.5 7.8 %copy-start.2 = (f32[1024,96]{0,1:T(8,128)S(1)}, f32[1024,96]{0,1:T(8,128)}, u32[]{:S(2)}) copy-start(f32[1024,96]{0,1:T(8,128)} %param.46) | copy-start | bytes 1179652
  15.8 11.0 %collective-permute-start.1 = (f32[1024,96]{0,1:T(8,128)}, f32[1024,96]{0,1:T(8,128)}, u32[]{:S(2)}, u32[]{:S(2)}) collective-permute-start(f32[1024,96]{0,1:T(8,128)} %get-tuple-element.286), channel_id=1, source_target_pairs={{0,16},{16,32},{32,48},{48,0},{1,17},{17,33},{33,49},{49,1},{2,18}... | collective-permute-start | bytes 1179656 | tf_op jit(solution)/shard_map/ppermute | solution.py:94
  17.1 9.7 %collective-permute-start.2 = (f32[1024,96]{0,1:T(8,128)}, f32[1024,96]{0,1:T(8,128)}, u32[]{:S(2)}, u32[]{:S(2)}) collective-permute-start(f32[1024,96]{0,1:T(8,128)} %get-tuple-element.285), channel_id=1, source_target_pairs={{0,48},{16,0},{32,16},{48,32},{1,49},{17,1},{33,17},{49,33},{2,50}... | collective-permute-start | bytes 1179656 | tf_op jit(solution)/shard_map/ppermute | solution.py:95
  20.9 1.0 copy-start.4
  26.9 9.9 %collective-permute-start.3 = (f32[1024,96]{0,1:T(8,128)}, f32[1024,96]{0,1:T(8,128)S(1)}, u32[]{:S(2)}, u32[]{:S(2)}) collective-permute-start(f32[1024,96]{0,1:T(8,128)} %collective-permute-done.1), channel_id=1, source_target_pairs={{0,16},{16,32},{32,48},{48,0},{1,17},{17,33},{33,49},{49,1},{2,18}... | collective-permute-start | bytes 1179656 | tf_op jit(solution)/shard_map/ppermute | solution.py:94
  26.9 9.9 %collective-permute-start.4 = (f32[1024,96]{0,1:T(8,128)}, f32[1024,96]{0,1:T(8,128)S(1)}, u32[]{:S(2)}, u32[]{:S(2)}) collective-permute-start(f32[1024,96]{0,1:T(8,128)} %collective-permute-done.2), channel_id=1, source_target_pairs={{0,48},{16,0},{32,16},{48,32},{1,49},{17,1},{33,17},{49,33},{2,50}... | collective-permute-start | bytes 1179656 | tf_op jit(solution)/shard_map/ppermute | solution.py:95
  29.6 17.7 %copy-start.7 = (f32[2048,768]{1,0:T(8,128)S(1)}, f32[2048,768]{1,0:T(8,128)}, u32[]{:S(2)}) copy-start(f32[2048,768]{1,0:T(8,128)} %param.47) | copy-start | bytes 18874372
  36.8 8.8 %collective-permute-start.5 = (f32[1024,96]{0,1:T(8,128)S(1)}, f32[1024,96]{0,1:T(8,128)S(1)}, u32[]{:S(2)}, u32[]{:S(2)}) collective-permute-start(f32[1024,96]{0,1:T(8,128)S(1)} %collective-permute-done.3), channel_id=1, source_target_pairs={{0,16},{16,32},{32,48},{48,0},{1,17},{17,33},{33,49},{49,1},{2,18}... | collective-permute-start | bytes 1179656 | tf_op jit(solution)/shard_map/ppermute | solution.py:94
  36.8 9.6 %collective-permute-start.6 = (f32[1024,96]{0,1:T(8,128)S(1)}, f32[1024,96]{0,1:T(8,128)S(1)}, u32[]{:S(2)}, u32[]{:S(2)}) collective-permute-start(f32[1024,96]{0,1:T(8,128)S(1)} %collective-permute-done.4), channel_id=1, source_target_pairs={{0,48},{16,0},{32,16},{48,32},{1,49},{17,1},{33,17},{49,33},{2,50}... | collective-permute-start | bytes 1179656 | tf_op jit(solution)/shard_map/ppermute | solution.py:95
  46.4 29.2 %slice-start = ((s8[6291456]{0:T(1024)(128)(4,1)}), s8[4194304]{0:T(1024)(128)(4,1)S(1)}, s32[]{:S(2)}) async-start(s8[6291456]{0:T(1024)(128)(4,1)} %bitcast.285), calls=%async_computation | async-start | bytes 8388608
  47.3 28.4 %slice-start.1 = ((s8[6291456]{0:T(1024)(128)(4,1)}), s8[2097152]{0:T(1024)(128)(4,1)S(1)}, s32[]{:S(2)}) async-start(s8[6291456]{0:T(1024)(128)(4,1)} %bitcast.285), calls=%async_computation.1 | async-start | bytes 4194304
  71.2 4.1 %collective-permute-start.7 = (f32[2,1024]{1,0:T(2,128)S(1)}, f32[2,1024]{1,0:T(2,128)S(1)}, u32[]{:S(2)}, u32[]{:S(2)}) collective-permute-start(f32[2,1024]{1,0:T(2,128)S(1)} %pad_maximum_fusion.5), channel_id=1, source_target_pairs={{0,64},{64,0},{1,65},{65,1},{2,66},{66,2},{3,67},{67,3},{4,68},{68... | collective-permute-start | bytes 24584 | tf_op jit(solution)/shard_map/ppermute | solution.py:38
  75.3 11.4 %collective-permute-start.8 = (f32[2,1024]{1,0:T(2,128)S(1)}, f32[2,1024]{1,0:T(2,128)S(1)}, u32[]{:S(2)}, u32[]{:S(2)}) collective-permute-start(f32[2,1024]{1,0:T(2,128)S(1)} %pad_maximum_fusion.6), channel_id=1, source_target_pairs={{0,16},{16,0},{32,48},{48,32},{1,17},{17,1},{33,49},{49,33},{2,18}... | collective-permute-start | bytes 24584 | tf_op jit(solution)/shard_map/ppermute | solution.py:38
  86.7 14.7 %collective-permute-start.9 = (f32[2,1024]{1,0:T(2,128)S(1)}, f32[2,1024]{1,0:T(2,128)S(1)}, u32[]{:S(2)}, u32[]{:S(2)}) collective-permute-start(f32[2,1024]{1,0:T(2,128)S(1)} %pad_maximum_fusion.7), channel_id=1, source_target_pairs={{0,32},{16,48},{32,0},{48,16},{1,33},{17,49},{33,1},{49,17},{2,34}... | collective-permute-start | bytes 24584 | tf_op jit(solution)/shard_map/ppermute | solution.py:38
  107.1 7.0 %collective-permute-start.10 = (f32[2,2048]{1,0:T(2,128)S(1)}, f32[2,2048]{1,0:T(2,128)S(1)}, u32[]{:S(2)}, u32[]{:S(2)}) collective-permute-start(f32[2,2048]{1,0:T(2,128)S(1)} %pad_maximum_fusion.1), channel_id=1, source_target_pairs={{0,1},{1,0},{2,3},{3,2},{4,5},{5,4},{6,7},{7,6},{8,9},{9,8},{10,11... | collective-permute-start | bytes 49160 | tf_op jit(solution)/shard_map/ppermute | solution.py:38
  114.2 2.7 %collective-permute-start.11 = (f32[2,2048]{1,0:T(2,128)S(1)}, f32[2,2048]{1,0:T(2,128)S(1)}, u32[]{:S(2)}, u32[]{:S(2)}) collective-permute-start(f32[2,2048]{1,0:T(2,128)S(1)} %pad_maximum_fusion.2), channel_id=1, source_target_pairs={{0,2},{2,0},{1,3},{3,1},{4,6},{6,4},{5,7},{7,5},{8,10},{10,8},{9,1... | collective-permute-start | bytes 49160 | tf_op jit(solution)/shard_map/ppermute | solution.py:38
  116.9 13.7 %collective-permute-start.12 = (f32[2,2048]{1,0:T(2,128)S(1)}, f32[2,2048]{1,0:T(2,128)S(1)}, u32[]{:S(2)}, u32[]{:S(2)}) collective-permute-start(f32[2,2048]{1,0:T(2,128)S(1)} %pad_maximum_fusion.3), channel_id=1, source_target_pairs={{0,4},{4,0},{8,12},{12,8},{1,5},{5,1},{9,13},{13,9},{2,6},{6,2},{1... | collective-permute-start | bytes 49160 | tf_op jit(solution)/shard_map/ppermute | solution.py:38
  118.2 15.3 %copy-start.1 = (f32[2048,1024]{1,0:T(8,128)S(1)}, f32[2048,1024]{1,0:T(8,128)}, u32[]{:S(2)}) copy-start(f32[2048,1024]{1,0:T(8,128)} %get-tuple-element.276) | copy-start | bytes 25165828
  130.7 13.1 %collective-permute-start.13 = (f32[2,2048]{1,0:T(2,128)S(1)}, f32[2,2048]{1,0:T(2,128)S(1)}, u32[]{:S(2)}, u32[]{:S(2)}) collective-permute-start(f32[2,2048]{1,0:T(2,128)S(1)} %pad_maximum_fusion.4), channel_id=1, source_target_pairs={{0,8},{4,12},{8,0},{12,4},{1,9},{5,13},{9,1},{13,5},{2,10},{6,14},... | collective-permute-start | bytes 49160 | tf_op jit(solution)/shard_map/ppermute | solution.py:38
  144.4 4.8 %copy-start = (f32[1024,768]{1,0:T(8,128)}, f32[1024,768]{1,0:T(8,128)S(1)}, u32[]{:S(2)}) copy-start(f32[1024,768]{1,0:T(8,128)S(1)} %get-tuple-element.310) | copy-start | bytes 9437188
  145.9 6.0 %collective-permute-start.14 = (f32[512,768]{1,0:T(8,128)}, f32[512,768]{1,0:T(8,128)}, u32[]{:S(2)}, u32[]{:S(2)}) collective-permute-start(f32[512,768]{1,0:T(8,128)} %dynamic-slice_bitcast_fusion.1), channel_id=1, source_target_pairs={{0,1},{1,0},{2,3},{3,2},{4,5},{5,4},{6,7},{7,6},{8,9},{9,8},{10,11... | collective-permute-start | bytes 4718600 | tf_op jit(solution)/shard_map/ppermute | solution.py:61
  149.2 6.6 %collective-permute-start.30 = (f32[512,768]{1,0:T(8,128)}, f32[512,768]{1,0:T(8,128)}, u32[]{:S(2)}, u32[]{:S(2)}) collective-permute-start(f32[512,768]{1,0:T(8,128)} %dynamic-slice_bitcast_fusion), channel_id=1, source_target_pairs={{0,1},{1,0},{2,3},{3,2},{4,5},{5,4},{6,7},{7,6},{8,9},{9,8},{10,11... | collective-permute-start | bytes 4718600 | tf_op jit(solution)/shard_map/ppermute | solution.py:61
  154.1 6.2 %collective-permute-start.18 = (f32[64,768]{1,0:T(8,128)S(1)}, f32[64,768]{1,0:T(8,128)S(1)}, u32[]{:S(2)}, u32[]{:S(2)}) collective-permute-start(f32[64,768]{1,0:T(8,128)S(1)} %dynamic-slice_bitcast_fusion.4), channel_id=1, source_target_pairs={{0,12},{4,0},{8,4},{12,8},{1,13},{5,1},{9,5},{13,9},{2,14},{6,2},{... | collective-permute-start | bytes 589832 | tf_op jit(solution)/shard_map/ppermute | solution.py:66
  154.4 7.4 %collective-permute-start.15 = (f32[64,768]{1,0:T(8,128)S(1)}, f32[64,768]{1,0:T(8,128)S(1)}, u32[]{:S(2)}, u32[]{:S(2)}) collective-permute-start(f32[64,768]{1,0:T(8,128)S(1)} %dynamic-slice_bitcast_fusion.5), channel_id=1, source_target_pairs={{0,4},{4,8},{8,12},{12,0},{1,5},{5,9},{9,13},{13,1},{2,6},{6,10},{... | collective-permute-start | bytes 589832 | tf_op jit(solution)/shard_map/ppermute | solution.py:65
  157.5 7.0 %collective-permute-start.34 = (f32[64,768]{1,0:T(8,128)S(1)}, f32[64,768]{1,0:T(8,128)S(1)}, u32[]{:S(2)}, u32[]{:S(2)}) collective-permute-start(f32[64,768]{1,0:T(8,128)S(1)} %dynamic-slice_bitcast_fusion.2), channel_id=1, source_target_pairs={{0,12},{4,0},{8,4},{12,8},{1,13},{5,1},{9,5},{13,9},{2,14},{6,2},{... | collective-permute-start | bytes 589832 | tf_op jit(solution)/shard_map/ppermute | solution.py:66
  159.0 6.8 %collective-permute-start.31 = (f32[64,768]{1,0:T(8,128)S(1)}, f32[64,768]{1,0:T(8,128)S(1)}, u32[]{:S(2)}, u32[]{:S(2)}) collective-permute-start(f32[64,768]{1,0:T(8,128)S(1)} %dynamic-slice_bitcast_fusion.3), channel_id=1, source_target_pairs={{0,4},{4,8},{8,12},{12,0},{1,5},{5,9},{9,13},{13,1},{2,6},{6,10},{... | collective-permute-start | bytes 589832 | tf_op jit(solution)/shard_map/ppermute | solution.py:65
  160.4 8.4 %collective-permute-start.19 = (f32[64,768]{1,0:T(8,128)S(1)}, f32[64,768]{1,0:T(8,128)S(1)}, u32[]{:S(2)}, u32[]{:S(2)}) collective-permute-start(f32[64,768]{1,0:T(8,128)S(1)} %bitcast_add_fusion.10), channel_id=1, source_target_pairs={{0,12},{4,0},{8,4},{12,8},{1,13},{5,1},{9,5},{13,9},{2,14},{6,2},{... | collective-permute-start | bytes 589832 | tf_op jit(solution)/shard_map/ppermute | solution.py:66
  161.9 8.3 %collective-permute-start.16 = (f32[64,768]{1,0:T(8,128)S(1)}, f32[64,768]{1,0:T(8,128)S(1)}, u32[]{:S(2)}, u32[]{:S(2)}) collective-permute-start(f32[64,768]{1,0:T(8,128)S(1)} %bitcast_add_fusion.13), channel_id=1, source_target_pairs={{0,4},{4,8},{8,12},{12,0},{1,5},{5,9},{9,13},{13,1},{2,6},{6,10},{... | collective-permute-start | bytes 589832 | tf_op jit(solution)/shard_map/ppermute | solution.py:65
  164.6 8.4 %collective-permute-start.35 = (f32[64,768]{1,0:T(8,128)S(1)}, f32[64,768]{1,0:T(8,128)S(1)}, u32[]{:S(2)}, u32[]{:S(2)}) collective-permute-start(f32[64,768]{1,0:T(8,128)S(1)} %bitcast_add_fusion.4), channel_id=1, source_target_pairs={{0,12},{4,0},{8,4},{12,8},{1,13},{5,1},{9,5},{13,9},{2,14},{6,2},{... | collective-permute-start | bytes 589832 | tf_op jit(solution)/shard_map/ppermute | solution.py:66
  165.8 7.8 %collective-permute-start.32 = (f32[64,768]{1,0:T(8,128)S(1)}, f32[64,768]{1,0:T(8,128)S(1)}, u32[]{:S(2)}, u32[]{:S(2)}) collective-permute-start(f32[64,768]{1,0:T(8,128)S(1)} %bitcast_add_fusion.7), channel_id=1, source_target_pairs={{0,4},{4,8},{8,12},{12,0},{1,5},{5,9},{9,13},{13,1},{2,6},{6,10},{... | collective-permute-start | bytes 589832 | tf_op jit(solution)/shard_map/ppermute | solution.py:65
  168.8 8.4 %collective-permute-start.20 = (f32[64,768]{1,0:T(8,128)S(1)}, f32[64,768]{1,0:T(8,128)S(1)}, u32[]{:S(2)}, u32[]{:S(2)}) collective-permute-start(f32[64,768]{1,0:T(8,128)S(1)} %bitcast_add_fusion.9), channel_id=1, source_target_pairs={{0,12},{4,0},{8,4},{12,8},{1,13},{5,1},{9,5},{13,9},{2,14},{6,2},{... | collective-permute-start | bytes 589832 | tf_op jit(solution)/shard_map/ppermute | solution.py:66
  170.2 7.4 %collective-permute-start.17 = (f32[64,768]{1,0:T(8,128)S(1)}, f32[64,768]{1,0:T(8,128)S(1)}, u32[]{:S(2)}, u32[]{:S(2)}) collective-permute-start(f32[64,768]{1,0:T(8,128)S(1)} %bitcast_add_fusion.12), channel_id=1, source_target_pairs={{0,4},{4,8},{8,12},{12,0},{1,5},{5,9},{9,13},{13,1},{2,6},{6,10},{... | collective-permute-start | bytes 589832 | tf_op jit(solution)/shard_map/ppermute | solution.py:65
  173.0 8.4 %collective-permute-start.36 = (f32[64,768]{1,0:T(8,128)S(1)}, f32[64,768]{1,0:T(8,128)S(1)}, u32[]{:S(2)}, u32[]{:S(2)}) collective-permute-start(f32[64,768]{1,0:T(8,128)S(1)} %bitcast_add_fusion.3), channel_id=1, source_target_pairs={{0,12},{4,0},{8,4},{12,8},{1,13},{5,1},{9,5},{13,9},{2,14},{6,2},{... | collective-permute-start | bytes 589832 | tf_op jit(solution)/shard_map/ppermute | solution.py:66
  173.7 8.3 %collective-permute-start.33 = (f32[64,768]{1,0:T(8,128)S(1)}, f32[64,768]{1,0:T(8,128)S(1)}, u32[]{:S(2)}, u32[]{:S(2)}) collective-permute-start(f32[64,768]{1,0:T(8,128)S(1)} %bitcast_add_fusion.6), channel_id=1, source_target_pairs={{0,4},{4,8},{8,12},{12,0},{1,5},{5,9},{9,13},{13,1},{2,6},{6,10},{... | collective-permute-start | bytes 589832 | tf_op jit(solution)/shard_map/ppermute | solution.py:65
  177.7 4.9 %collective-permute-start.21 = (f32[64,768]{1,0:T(8,128)S(1)}, f32[64,768]{1,0:T(8,128)S(1)}, u32[]{:S(2)}, u32[]{:S(2)}) collective-permute-start(f32[64,768]{1,0:T(8,128)S(1)} %fusion.33), channel_id=1, source_target_pairs={{0,2},{2,0},{1,3},{3,1},{4,6},{6,4},{5,7},{7,5},{8,10},{10,8},{9,1... | collective-permute-start | bytes 589832 | tf_op jit(solution)/shard_map/ppermute | solution.py:68
  182.1 6.1 %collective-permute-start.37 = (f32[64,768]{1,0:T(8,128)S(1)}, f32[64,768]{1,0:T(8,128)S(1)}, u32[]{:S(2)}, u32[]{:S(2)}) collective-permute-start(f32[64,768]{1,0:T(8,128)S(1)} %fusion.27), channel_id=1, source_target_pairs={{0,2},{2,0},{1,3},{3,1},{4,6},{6,4},{5,7},{7,5},{8,10},{10,8},{9,1... | collective-permute-start | bytes 589832 | tf_op jit(solution)/shard_map/ppermute | solution.py:68
  182.7 9.7 %collective-permute-start.22 = (f32[64,768]{1,0:T(8,128)S(1)}, f32[64,768]{1,0:T(8,128)S(1)}, u32[]{:S(2)}, u32[]{:S(2)}) collective-permute-start(f32[64,768]{1,0:T(8,128)S(1)} %fusion.37), channel_id=1, source_target_pairs={{0,2},{2,0},{1,3},{3,1},{4,6},{6,4},{5,7},{7,5},{8,10},{10,8},{9,1... | collective-permute-start | bytes 589832 | tf_op jit(solution)/shard_map/ppermute | solution.py:71
  188.3 8.3 %collective-permute-start.38 = (f32[64,768]{1,0:T(8,128)S(1)}, f32[64,768]{1,0:T(8,128)S(1)}, u32[]{:S(2)}, u32[]{:S(2)}) collective-permute-start(f32[64,768]{1,0:T(8,128)S(1)} %fusion.31), channel_id=1, source_target_pairs={{0,2},{2,0},{1,3},{3,1},{4,6},{6,4},{5,7},{7,5},{8,10},{10,8},{9,1... | collective-permute-start | bytes 589832 | tf_op jit(solution)/shard_map/ppermute | solution.py:71
  192.5 8.7 %collective-permute-start.23 = (f32[64,768]{1,0:T(8,128)S(1)}, f32[64,768]{1,0:T(8,128)S(1)}, u32[]{:S(2)}, u32[]{:S(2)}) collective-permute-start(f32[64,768]{1,0:T(8,128)S(1)} %get-tuple-element.288), channel_id=1, source_target_pairs={{0,4},{4,8},{8,12},{12,0},{1,5},{5,9},{9,13},{13,1},{2,6},{6,10},{... | collective-permute-start | bytes 589832 | tf_op jit(solution)/shard_map/ppermute | solution.py:76
  193.8 7.5 %collective-permute-start.24 = (f32[64,768]{1,0:T(8,128)S(1)}, f32[64,768]{1,0:T(8,128)S(1)}, u32[]{:S(2)}, u32[]{:S(2)}) collective-permute-start(f32[64,768]{1,0:T(8,128)S(1)} %get-tuple-element.287), channel_id=1, source_target_pairs={{0,12},{4,0},{8,4},{12,8},{1,13},{5,1},{9,5},{13,9},{2,14},{6,2},{... | collective-permute-start | bytes 589832 | tf_op jit(solution)/shard_map/ppermute | solution.py:77
  196.7 7.2 %collective-permute-start.39 = (f32[64,768]{1,0:T(8,128)S(1)}, f32[64,768]{1,0:T(8,128)S(1)}, u32[]{:S(2)}, u32[]{:S(2)}) collective-permute-start(f32[64,768]{1,0:T(8,128)S(1)} %get-tuple-element.290), channel_id=1, source_target_pairs={{0,4},{4,8},{8,12},{12,0},{1,5},{5,9},{9,13},{13,1},{2,6},{6,10},{... | collective-permute-start | bytes 589832 | tf_op jit(solution)/shard_map/ppermute | solution.py:76
  198.0 8.0 %collective-permute-start.40 = (f32[64,768]{1,0:T(8,128)S(1)}, f32[64,768]{1,0:T(8,128)S(1)}, u32[]{:S(2)}, u32[]{:S(2)}) collective-permute-start(f32[64,768]{1,0:T(8,128)S(1)} %get-tuple-element.289), channel_id=1, source_target_pairs={{0,12},{4,0},{8,4},{12,8},{1,13},{5,1},{9,5},{13,9},{2,14},{6,2},{... | collective-permute-start | bytes 589832 | tf_op jit(solution)/shard_map/ppermute | solution.py:77
  201.1 8.2 %collective-permute-start.25 = (f32[64,768]{1,0:T(8,128)S(1)}, f32[64,768]{1,0:T(8,128)S(1)}, u32[]{:S(2)}, u32[]{:S(2)}) collective-permute-start(f32[64,768]{1,0:T(8,128)S(1)} %collective-permute-done.23), channel_id=1, source_target_pairs={{0,4},{4,8},{8,12},{12,0},{1,5},{5,9},{9,13},{13,1},{2,6},{6,10},{... | collective-permute-start | bytes 589832 | tf_op jit(solution)/shard_map/ppermute | solution.py:76
  201.2 8.2 %collective-permute-start.26 = (f32[64,768]{1,0:T(8,128)S(1)}, f32[64,768]{1,0:T(8,128)S(1)}, u32[]{:S(2)}, u32[]{:S(2)}) collective-permute-start(f32[64,768]{1,0:T(8,128)S(1)} %collective-permute-done.24), channel_id=1, source_target_pairs={{0,12},{4,0},{8,4},{12,8},{1,13},{5,1},{9,5},{13,9},{2,14},{6,2},{... | collective-permute-start | bytes 589832 | tf_op jit(solution)/shard_map/ppermute | solution.py:77
  203.9 8.2 %collective-permute-start.41 = (f32[64,768]{1,0:T(8,128)S(1)}, f32[64,768]{1,0:T(8,128)S(1)}, u32[]{:S(2)}, u32[]{:S(2)}) collective-permute-start(f32[64,768]{1,0:T(8,128)S(1)} %collective-permute-done.39), channel_id=1, source_target_pairs={{0,4},{4,8},{8,12},{12,0},{1,5},{5,9},{9,13},{13,1},{2,6},{6,10},{... | collective-permute-start | bytes 589832 | tf_op jit(solution)/shard_map/ppermute | solution.py:76
  206.0 8.5 %collective-permute-start.42 = (f32[64,768]{1,0:T(8,128)S(1)}, f32[64,768]{1,0:T(8,128)S(1)}, u32[]{:S(2)}, u32[]{:S(2)}) collective-permute-start(f32[64,768]{1,0:T(8,128)S(1)} %collective-permute-done.40), channel_id=1, source_target_pairs={{0,12},{4,0},{8,4},{12,8},{1,13},{5,1},{9,5},{13,9},{2,14},{6,2},{... | collective-permute-start | bytes 589832 | tf_op jit(solution)/shard_map/ppermute | solution.py:77
  209.3 8.1 %collective-permute-start.27 = (f32[64,768]{1,0:T(8,128)S(1)}, f32[64,768]{1,0:T(8,128)S(1)}, u32[]{:S(2)}, u32[]{:S(2)}) collective-permute-start(f32[64,768]{1,0:T(8,128)S(1)} %collective-permute-done.25), channel_id=1, source_target_pairs={{0,4},{4,8},{8,12},{12,0},{1,5},{5,9},{9,13},{13,1},{2,6},{6,10},{... | collective-permute-start | bytes 589832 | tf_op jit(solution)/shard_map/ppermute | solution.py:76
  209.4 8.7 %collective-permute-start.28 = (f32[64,768]{1,0:T(8,128)S(1)}, f32[64,768]{1,0:T(8,128)S(1)}, u32[]{:S(2)}, u32[]{:S(2)}) collective-permute-start(f32[64,768]{1,0:T(8,128)S(1)} %collective-permute-done.26), channel_id=1, source_target_pairs={{0,12},{4,0},{8,4},{12,8},{1,13},{5,1},{9,5},{13,9},{2,14},{6,2},{... | collective-permute-start | bytes 589832 | tf_op jit(solution)/shard_map/ppermute | solution.py:77
  212.1 14.9 %collective-permute-start.43 = (f32[64,768]{1,0:T(8,128)S(1)}, f32[64,768]{1,0:T(8,128)S(1)}, u32[]{:S(2)}, u32[]{:S(2)}) collective-permute-start(f32[64,768]{1,0:T(8,128)S(1)} %collective-permute-done.41), channel_id=1, source_target_pairs={{0,4},{4,8},{8,12},{12,0},{1,5},{5,9},{9,13},{13,1},{2,6},{6,10},{... | collective-permute-start | bytes 589832 | tf_op jit(solution)/shard_map/ppermute | solution.py:76
  214.5 13.2 %collective-permute-start.44 = (f32[64,768]{1,0:T(8,128)S(1)}, f32[64,768]{1,0:T(8,128)S(1)}, u32[]{:S(2)}, u32[]{:S(2)}) collective-permute-start(f32[64,768]{1,0:T(8,128)S(1)} %collective-permute-done.42), channel_id=1, source_target_pairs={{0,12},{4,0},{8,4},{12,8},{1,13},{5,1},{9,5},{13,9},{2,14},{6,2},{... | collective-permute-start | bytes 589832 | tf_op jit(solution)/shard_map/ppermute | solution.py:77
  218.8 11.4 %collective-permute-start.29 = (f32[512,768]{1,0:T(8,128)S(1)}, f32[512,768]{1,0:T(8,128)}, u32[]{:S(2)}, u32[]{:S(2)}) collective-permute-start(f32[512,768]{1,0:T(8,128)S(1)} %bitcast.246), channel_id=1, source_target_pairs={{0,1},{1,0},{2,3},{3,2},{4,5},{5,4},{6,7},{7,6},{8,9},{9,8},{10,11... | collective-permute-start | bytes 4718600 | tf_op jit(solution)/shard_map/ppermute | solution.py:81
  228.3 4.1 %collective-permute-start.45 = (f32[512,768]{1,0:T(8,128)S(1)}, f32[512,768]{1,0:T(8,128)}, u32[]{:S(2)}, u32[]{:S(2)}) collective-permute-start(f32[512,768]{1,0:T(8,128)S(1)} %bitcast.244), channel_id=1, source_target_pairs={{0,1},{1,0},{2,3},{3,2},{4,5},{5,4},{6,7},{7,6},{8,9},{9,8},{10,11... | collective-permute-start | bytes 4718600 | tf_op jit(solution)/shard_map/ppermute | solution.py:81

commit v8 on v6

--- a/solution.py
+++ b/solution.py
@@ -121,7 +121,12 @@
     parts = []
     for k in range(2):
         part = slice(k * chunk, (k + 1) * chunk)
-        summed = lax.optimization_barrier(rescaled_affinity(weights[part], features))
+        quarter = chunk // 2
+        summed = jnp.concatenate(
+            [lax.optimization_barrier(rescaled_affinity(weights[k * chunk + j * quarter:][:quarter], features))
+             for j in range(2)],
+            axis=0,
+        )
         summed = summed * scale[part, None]
         parts.append(reduce_rows(summed, row_total, k * chunk, sizes))
     return jnp.concatenate(parts, axis=0)

time: 242 us -> 244 us (level)
  waiting for transfers between devices: 55.9 us -> 44.5 us
  starting transfers between devices: 66.2 us -> 75 us
    ppermute x6, waiting for transfers between devices: 15 us -> 5.66 us  [reduce_rows(): lax.ppermute(left, 'x', ring('x', x_size, -1))]
    ppermute x6, starting transfers between devices: 6.41 us -> 15.1 us  [reduce_rows(): lax.ppermute(left, 'x', ring('x', x_size, -1))]
    ppermute x6, starting transfers between devices: 4.73 us -> 0.3 us  [reduce_rows(): right = lax.ppermute(right, 'x', ring('x', x_size, 1))]
    ppermute x6, starting transfers between devices: 11.7 us -> 16.1 us  [reduce_rows(): left = lax.ppermute(left, 'x', ring('x', x_size, -1))]
    ppermute x6, waiting for transfers between devices: 0.93 us -> 4.37 us  [reduce_rows(): lax.ppermute(right, 'x', ring('x', x_size, 1))]
    ppermute x7, waiting for transfers between devices: 8.19 us -> 4.8 us  [merge_peaks(): other = lax.ppermute(pair, axis, [(j, j ^ dist) for j in range(size)])]
    ppermute x2, starting transfers between devices: 0.26 us -> 3.01 us  [reduce_rows(): mine = pick(block, z) + lax.ppermute(pick(block, 1 - z), 'zl', swap)]
    ppermute x6, starting transfers between devices: 3.22 us -> 0.66 us  [reduce_rows(): lax.ppermute(right, 'x', ring('x', x_size, 1))]
  transfers between devices with their start and end apart: 46 -> 46, of which waited for: 21 -> 17; matrix products, arithmetic and copies ran while one was open for 32% -> 33% of each run, Pallas kernels for 0% -> 0%
where the time goes in v8:
time: 244 us; the launch traced here: 240 us
  starting transfers between devices  75 us (31%)
  matrix products  69 us (28%)
  waiting for transfers between devices  44.5 us (18%)
  other arithmetic  43.9 us (18%)
  local copies, waits for them, and re-layouts  6.97 us (3%)
    dot_general x2, matrix products, similar(): lax.dot_general(query_factor, target_factor, (((1,), (0,)), ((), ())), pr...  45 us
    dot_general x4, matrix products, rescaled_affinity(): lax.dot_general(weights, features, (((1,), (1,)), ((), ())), precision=la...  24 us
    ppermute x6, starting transfers between devices, reduce_rows(): left = lax.ppermute(left, 'x', ring('x', x_size, -1))  16.1 us
    ppermute x6, starting transfers between devices, reduce_rows(): lax.ppermute(left, 'x', ring('x', x_size, -1))  15.1 us
    ppermute x7, starting transfers between devices, merge_peaks(): other = lax.ppermute(pair, axis, [(j, j ^ dist) for j in range(size)])  14.8 us
    ppermute x3, waiting for transfers between devices, gather_features(): right = lax.ppermute(right, 'y', ring('y', y_size, 1))  12.2 us
    ppermute x2, starting transfers between devices, reduce_rows(): other = lax.ppermute(held, 'core', swap)  8.59 us
    ppermute x1, waiting for transfers between devices, gather_features(): other = lax.ppermute(captions, 'zh', [(0, 1), (1, 0)])  7.6 us
  transfers between devices with their start and end apart: 46, of which 17 were waited for; matrix products, arithmetic and copies ran while one was open for 33% of the time, Pallas kernels for 0%

profile of v8, /device:TPU:1, one launch (start us, length us, event | category | flops | bytes accessed | tf_op | source)
XLA Modules:
  0.0 240.4 jit_solution(4149393601165130811)
XLA Ops:
  0.0 4.4 %collective-permute-start = (f32[1024,96]{0,1:T(8,128)}, f32[1024,96]{0,1:T(8,128)S(1)}, u32[]{:S(2)}, u32[]{:S(2)}) collective-permute-start(f32[1024,96]{0,1:T(8,128)} %param.46), channel_id=1, source_target_pairs={{0,64},{64,0},{1,65},{65,1},{2,66},{66,2},{3,67},{67,3},{4,68},{68... | collective-permute-start | bytes 1179656 | tf_op jit(solution)/shard_map/ppermute | solution.py:89
  4.4 1.5 and_reduce_fusion.10
  5.9 7.6 %collective-permute-done = f32[1024,96]{0,1:T(8,128)S(1)} collective-permute-done((f32[1024,96]{0,1:T(8,128)}, f32[1024,96]{0,1:T(8,128)S(1)}, u32[]{:S(2)}, u32[]{:S(2)}) %collective-permute-start) | collective-permute-done | bytes 393248 | tf_op jit(solution)/shard_map/ppermute | solution.py:89
  13.5 1.4 maximum_select_fusion.3
  15.8 1.3 collective-permute-start.1
  17.1 1.4 collective-permute-start.2
  22.6 4.2 %collective-permute-done.1 = f32[1024,96]{0,1:T(8,128)} collective-permute-done((f32[1024,96]{0,1:T(8,128)}, f32[1024,96]{0,1:T(8,128)}, u32[]{:S(2)}, u32[]{:S(2)}) %collective-permute-start.1) | collective-permute-done | bytes 393248 | tf_op jit(solution)/shard_map/ppermute | solution.py:94
  26.9 2.7 %collective-permute-start.4 = (f32[1024,96]{0,1:T(8,128)}, f32[1024,96]{0,1:T(8,128)S(1)}, u32[]{:S(2)}, u32[]{:S(2)}) collective-permute-start(f32[1024,96]{0,1:T(8,128)} %collective-permute-done.2), channel_id=1, source_target_pairs={{0,48},{16,0},{32,16},{48,32},{1,49},{17,1},{33,17},{49,33},{2,50}... | collective-permute-start | bytes 1179656 | tf_op jit(solution)/shard_map/ppermute | solution.py:95
  29.5 1.9 fusion.20
  31.4 1.8 fusion.19
  33.2 3.6 %collective-permute-done.3 = f32[1024,96]{0,1:T(8,128)S(1)} collective-permute-done((f32[1024,96]{0,1:T(8,128)}, f32[1024,96]{0,1:T(8,128)S(1)}, u32[]{:S(2)}, u32[]{:S(2)}) %collective-permute-start.3) | collective-permute-done | bytes 393248 | tf_op jit(solution)/shard_map/ppermute | solution.py:94
  36.8 2.9 %collective-permute-start.6 = (f32[1024,96]{0,1:T(8,128)S(1)}, f32[1024,96]{0,1:T(8,128)S(1)}, u32[]{:S(2)}, u32[]{:S(2)}) collective-permute-start(f32[1024,96]{0,1:T(8,128)S(1)} %collective-permute-done.4), channel_id=1, source_target_pairs={{0,48},{16,0},{32,16},{48,32},{1,49},{17,1},{33,17},{49,33},{2,50}... | collective-permute-start | bytes 1179656 | tf_op jit(solution)/shard_map/ppermute | solution.py:95
  41.2 4.4 %collective-permute-done.5 = f32[1024,96]{0,1:T(8,128)S(1)} collective-permute-done((f32[1024,96]{0,1:T(8,128)S(1)}, f32[1024,96]{0,1:T(8,128)S(1)}, u32[]{:S(2)}, u32[]{:S(2)}) %collective-permute-start.5) | collective-permute-done | bytes 393248 | tf_op jit(solution)/shard_map/ppermute | solution.py:94
  47.1 22.8 %fusion = (f32[1024]{0:T(1024)S(1)}, f32[1024,2048]{0,1:T(8,128)S(1)}) fusion(f32[768,1024]{1,0:T(8,128)S(1)} %bitcast.238, f32[2048,768]{1,0:T(8,128)S(1)} %copy-done.8), kind=kOutput, calls=%fused_computation.4 | convolution fusion | flops 19331547136 | bytes 17829888 | tf_op jit(solution)/shard_map/dot_general | solution.py:15
  69.9 1.4 exponential_reduce_fusion
  71.3 1.8 collective-permute-start.7
  73.1 2.3 collective-permute-done.7
  75.6 2.5 %collective-permute-done.8 = f32[2,1024]{1,0:T(2,128)S(1)} collective-permute-done((f32[2,1024]{1,0:T(2,128)S(1)}, f32[2,1024]{1,0:T(2,128)S(1)}, u32[]{:S(2)}, u32[]{:S(2)}) %collective-permute-start.8) | collective-permute-done | bytes 8224 | tf_op jit(solution)/shard_map/ppermute | solution.py:38
  78.1 2.3 collective-permute-start.9
  80.3 22.2 %bitcast_multiply_fusion.1 = f32[2048,1024]{1,0:T(8,128)S(1)} fusion(f32[768,1024]{1,0:T(8,128)S(1)} %bitcast.239, f32[2048,768]{1,0:T(8,128)} %param.45), kind=kOutput, calls=%fused_computation.1 | convolution fusion | flops 19329449984 | bytes 17825792 | tf_op jit(solution)/shard_map/dot_general | solution.py:15
  103.2 1.8 fusion.65
  105.1 6.7 %collective-permute-start.10 = (f32[2,2048]{1,0:T(2,128)S(1)}, f32[2,2048]{1,0:T(2,128)S(1)}, u32[]{:S(2)}, u32[]{:S(2)}) collective-permute-start(f32[2,2048]{1,0:T(2,128)S(1)} %pad_maximum_fusion.3), channel_id=1, source_target_pairs={{0,1},{1,0},{2,3},{3,2},{4,5},{5,4},{6,7},{7,6},{8,9},{9,8},{10,11... | collective-permute-start | bytes 49160 | tf_op jit(solution)/shard_map/ppermute | solution.py:38
  111.8 5.3 %fusion.7 = f32[512,768]{1,0:T(8,128)S(1)} fusion(f32[768,1024]{1,0:T(8,128)S(1)} %bitcast.240, f32[2048,1024]{1,0:T(8,128)S(1)} %get-tuple-element.276), kind=kOutput, calls=%fused_computation.17 | convolution fusion | flops 4831838208 | bytes 6815744 | tf_op jit(solution)/shard_map/dot_general | solution.py:26
  117.3 5.3 %fusion.5 = f32[512,768]{1,0:T(8,128)S(1)} fusion(f32[768,1024]{1,0:T(8,128)S(1)} %bitcast.241, f32[2048,1024]{1,0:T(8,128)S(1)} %get-tuple-element.276), kind=kOutput, calls=%fused_computation.15 | convolution fusion | flops 4831838208 | bytes 6815744 | tf_op jit(solution)/shard_map/dot_general | solution.py:26
  122.7 1.3 collective-permute-start.12
  124.0 6.5 %fusion.3 = f32[512,768]{1,0:T(8,128)} fusion(f32[768,1024]{1,0:T(8,128)S(1)} %bitcast.242, f32[2048,1024]{1,0:T(8,128)S(1)} %get-tuple-element.276), kind=kOutput, calls=%fused_computation.13 | convolution fusion | flops 4831838208 | bytes 6815744 | tf_op jit(solution)/shard_map/dot_general | solution.py:26
  130.6 2.5 %collective-permute-start.13 = (f32[2,2048]{1,0:T(2,128)S(1)}, f32[2,2048]{1,0:T(2,128)S(1)}, u32[]{:S(2)}, u32[]{:S(2)}) collective-permute-start(f32[2,2048]{1,0:T(2,128)S(1)} %pad_maximum_fusion.6), channel_id=1, source_target_pairs={{0,8},{4,12},{8,0},{12,4},{1,9},{5,13},{9,1},{13,5},{2,10},{6,14},... | collective-permute-start | bytes 49160 | tf_op jit(solution)/shard_map/ppermute | solution.py:38
  133.1 1.9 pad_maximum_fusion.1
  135.1 2.2 broadcast_multiply_fusion.1
  137.3 1.7 copy-done.1
  139.0 1.3 dynamic-slice_bitcast_fusion.1
  140.3 1.6 collective-permute-start.14
  141.9 6.9 %fusion.1 = f32[512,768]{1,0:T(8,128)S(1)} fusion(f32[768,1024]{1,0:T(8,128)S(1)} %bitcast.243, f32[2048,1024]{1,0:T(8,128)} %copy-done), kind=kOutput, calls=%fused_computation.11 | convolution fusion | flops 4831838208 | bytes 6815744 | tf_op jit(solution)/shard_map/dot_general | solution.py:26
  149.3 1.3 dynamic-slice_bitcast_fusion
  153.0 2.1 bitcast_add_fusion.1
  155.2 1.9 collective-permute-start.18
  157.2 1.6 bitcast_add_fusion
  158.9 2.7 %collective-permute-start.34 = (f32[64,768]{1,0:T(8,128)S(1)}, f32[64,768]{1,0:T(8,128)S(1)}, u32[]{:S(2)}, u32[]{:S(2)}) collective-permute-start(f32[64,768]{1,0:T(8,128)S(1)} %dynamic-slice_bitcast_fusion.2), channel_id=1, source_target_pairs={{0,12},{4,0},{8,4},{12,8},{1,13},{5,1},{9,5},{13,9},{2,14},{6,2},{... | collective-permute-start | bytes 589832 | tf_op jit(solution)/shard_map/ppermute | solution.py:66
  161.8 2.7 %collective-permute-start.19 = (f32[64,768]{1,0:T(8,128)S(1)}, f32[64,768]{1,0:T(8,128)S(1)}, u32[]{:S(2)}, u32[]{:S(2)}) collective-permute-start(f32[64,768]{1,0:T(8,128)S(1)} %bitcast_add_fusion.10), channel_id=1, source_target_pairs={{0,12},{4,0},{8,4},{12,8},{1,13},{5,1},{9,5},{13,9},{2,14},{6,2},{... | collective-permute-start | bytes 589832 | tf_op jit(solution)/shard_map/ppermute | solution.py:66
  165.7 2.7 %collective-permute-start.35 = (f32[64,768]{1,0:T(8,128)S(1)}, f32[64,768]{1,0:T(8,128)S(1)}, u32[]{:S(2)}, u32[]{:S(2)}) collective-permute-start(f32[64,768]{1,0:T(8,128)S(1)} %bitcast_add_fusion.4), channel_id=1, source_target_pairs={{0,12},{4,0},{8,4},{12,8},{1,13},{5,1},{9,5},{13,9},{2,14},{6,2},{... | collective-permute-start | bytes 589832 | tf_op jit(solution)/shard_map/ppermute | solution.py:66
  168.5 1.4 collective-permute-done.19
  169.9 2.9 %collective-permute-start.20 = (f32[64,768]{1,0:T(8,128)S(1)}, f32[64,768]{1,0:T(8,128)S(1)}, u32[]{:S(2)}, u32[]{:S(2)}) collective-permute-start(f32[64,768]{1,0:T(8,128)S(1)} %bitcast_add_fusion.9), channel_id=1, source_target_pairs={{0,12},{4,0},{8,4},{12,8},{1,13},{5,1},{9,5},{13,9},{2,14},{6,2},{... | collective-permute-start | bytes 589832 | tf_op jit(solution)/shard_map/ppermute | solution.py:66
  172.9 1.1 collective-permute-done.35
  174.1 2.2 collective-permute-start.36
  176.6 1.6 collective-permute-done.20
  178.3 2.0 collective-permute-done.17
  180.3 1.5 collective-permute-start.21
  182.3 2.4 %collective-permute-done.33 = f32[64,768]{1,0:T(8,128)S(1)} collective-permute-done((f32[64,768]{1,0:T(8,128)S(1)}, f32[64,768]{1,0:T(8,128)S(1)}, u32[]{:S(2)}, u32[]{:S(2)}) %collective-permute-start.33) | collective-permute-done | bytes 196640 | tf_op jit(solution)/shard_map/ppermute | solution.py:65
  184.8 1.5 collective-permute-start.37
  186.8 4.0 %collective-permute-done.37 = f32[64,768]{1,0:T(8,128)S(1)} collective-permute-done((f32[64,768]{1,0:T(8,128)S(1)}, f32[64,768]{1,0:T(8,128)S(1)}, u32[]{:S(2)}, u32[]{:S(2)}) %collective-permute-start.37) | collective-permute-done | bytes 196640 | tf_op jit(solution)/shard_map/ppermute | solution.py:68
  190.9 1.5 collective-permute-start.38
  192.4 2.6 %collective-permute-done.22 = f32[64,768]{1,0:T(8,128)S(1)} collective-permute-done((f32[64,768]{1,0:T(8,128)S(1)}, f32[64,768]{1,0:T(8,128)S(1)}, u32[]{:S(2)}, u32[]{:S(2)}) %collective-permute-start.22) | collective-permute-done | bytes 196640 | tf_op jit(solution)/shard_map/ppermute | solution.py:71
  195.2 2.7 %collective-permute-start.24 = (f32[64,768]{1,0:T(8,128)S(1)}, f32[64,768]{1,0:T(8,128)S(1)}, u32[]{:S(2)}, u32[]{:S(2)}) collective-permute-start(f32[64,768]{1,0:T(8,128)S(1)} %get-tuple-element.287), channel_id=1, source_target_pairs={{0,12},{4,0},{8,4},{12,8},{1,13},{5,1},{9,5},{13,9},{2,14},{6,2},{... | collective-permute-start | bytes 589832 | tf_op jit(solution)/shard_map/ppermute | solution.py:77
  197.9 1.4 collective-permute-done.38
  199.4 2.7 %collective-permute-start.40 = (f32[64,768]{1,0:T(8,128)S(1)}, f32[64,768]{1,0:T(8,128)S(1)}, u32[]{:S(2)}, u32[]{:S(2)}) collective-permute-start(f32[64,768]{1,0:T(8,128)S(1)} %get-tuple-element.289), channel_id=1, source_target_pairs={{0,12},{4,0},{8,4},{12,8},{1,13},{5,1},{9,5},{13,9},{2,14},{6,2},{... | collective-permute-start | bytes 589832 | tf_op jit(solution)/shard_map/ppermute | solution.py:77
  203.7 2.7 %collective-permute-start.26 = (f32[64,768]{1,0:T(8,128)S(1)}, f32[64,768]{1,0:T(8,128)S(1)}, u32[]{:S(2)}, u32[]{:S(2)}) collective-permute-start(f32[64,768]{1,0:T(8,128)S(1)} %collective-permute-done.24), channel_id=1, source_target_pairs={{0,12},{4,0},{8,4},{12,8},{1,13},{5,1},{9,5},{13,9},{2,14},{6,2},{... | collective-permute-start | bytes 589832 | tf_op jit(solution)/shard_map/ppermute | solution.py:77
  207.5 2.7 %collective-permute-start.42 = (f32[64,768]{1,0:T(8,128)S(1)}, f32[64,768]{1,0:T(8,128)S(1)}, u32[]{:S(2)}, u32[]{:S(2)}) collective-permute-start(f32[64,768]{1,0:T(8,128)S(1)} %collective-permute-done.40), channel_id=1, source_target_pairs={{0,12},{4,0},{8,4},{12,8},{1,13},{5,1},{9,5},{13,9},{2,14},{6,2},{... | collective-permute-start | bytes 589832 | tf_op jit(solution)/shard_map/ppermute | solution.py:77
  211.7 2.7 %collective-permute-start.28 = (f32[64,768]{1,0:T(8,128)S(1)}, f32[64,768]{1,0:T(8,128)S(1)}, u32[]{:S(2)}, u32[]{:S(2)}) collective-permute-start(f32[64,768]{1,0:T(8,128)S(1)} %collective-permute-done.26), channel_id=1, source_target_pairs={{0,12},{4,0},{8,4},{12,8},{1,13},{5,1},{9,5},{13,9},{2,14},{6,2},{... | collective-permute-start | bytes 589832 | tf_op jit(solution)/shard_map/ppermute | solution.py:77
  215.6 2.7 %collective-permute-start.44 = (f32[64,768]{1,0:T(8,128)S(1)}, f32[64,768]{1,0:T(8,128)S(1)}, u32[]{:S(2)}, u32[]{:S(2)}) collective-permute-start(f32[64,768]{1,0:T(8,128)S(1)} %collective-permute-done.42), channel_id=1, source_target_pairs={{0,12},{4,0},{8,4},{12,8},{1,13},{5,1},{9,5},{13,9},{2,14},{6,2},{... | collective-permute-start | bytes 589832 | tf_op jit(solution)/shard_map/ppermute | solution.py:77
  220.9 8.5 %collective-permute-start.29 = (f32[512,768]{1,0:T(8,128)S(1)}, f32[512,768]{1,0:T(8,128)}, u32[]{:S(2)}, u32[]{:S(2)}) collective-permute-start(f32[512,768]{1,0:T(8,128)S(1)} %bitcast.250), channel_id=1, source_target_pairs={{0,1},{1,0},{2,3},{3,2},{4,5},{5,4},{6,7},{7,6},{8,9},{9,8},{10,11... | collective-permute-start | bytes 4718600 | tf_op jit(solution)/shard_map/ppermute | solution.py:81
  230.9 1.7 collective-permute-done.29
  232.6 2.2 maximum_select_fusion
  234.9 2.2 maximum_select_fusion.1
  237.0 3.1 %pad_maximum_fusion = f32[2048,768]{1,0:T(8,128)} fusion(f32[1024,768]{1,0:T(8,128)S(1)} %bitcast.247, f32[1024,768]{1,0:T(8,128)S(1)} %bitcast.245), kind=kLoop, calls=%fused_computation.6 | loop fusion | flops 1572864 | bytes 12582912 | tf_op jit(solution)/shard_map/concatenate | solution.py:132
  (148 shorter events, 25.2 us)
Async XLA Ops:
  0.0 19.4 %copy-start.6 = (s32[4]{0:T(128)S(1)}, s32[4]{0:T(128)}, u32[]{:S(2)}) copy-start(s32[4]{0:T(128)} %constant.689.clone.1) | copy-start | bytes 52
  0.0 18.6 %copy-start.7 = (s32[4]{0:T(128)S(1)}, s32[4]{0:T(128)}, u32[]{:S(2)}) copy-start(s32[4]{0:T(128)} %constant.683.clone.1) | copy-start | bytes 52
  0.0 13.5 %collective-permute-start = (f32[1024,96]{0,1:T(8,128)}, f32[1024,96]{0,1:T(8,128)S(1)}, u32[]{:S(2)}, u32[]{:S(2)}) collective-permute-start(f32[1024,96]{0,1:T(8,128)} %param.46), channel_id=1, source_target_pairs={{0,64},{64,0},{1,65},{65,1},{2,66},{66,2},{3,67},{67,3},{4,68},{68... | collective-permute-start | bytes 1179656 | tf_op jit(solution)/shard_map/ppermute | solution.py:89
  13.5 7.4 %copy-start.4 = (f32[1024,96]{0,1:T(8,128)}, f32[1024,96]{0,1:T(8,128)S(1)}, u32[]{:S(2)}) copy-start(f32[1024,96]{0,1:T(8,128)S(1)} %collective-permute-done) | copy-start | bytes 1179652
  13.5 7.8 %copy-start.3 = (f32[1024,96]{0,1:T(8,128)S(1)}, f32[1024,96]{0,1:T(8,128)}, u32[]{:S(2)}) copy-start(f32[1024,96]{0,1:T(8,128)} %param.46) | copy-start | bytes 1179652
  15.8 11.0 %collective-permute-start.1 = (f32[1024,96]{0,1:T(8,128)}, f32[1024,96]{0,1:T(8,128)}, u32[]{:S(2)}, u32[]{:S(2)}) collective-permute-start(f32[1024,96]{0,1:T(8,128)} %get-tuple-element.286), channel_id=1, source_target_pairs={{0,16},{16,32},{32,48},{48,0},{1,17},{17,33},{33,49},{49,1},{2,18}... | collective-permute-start | bytes 1179656 | tf_op jit(solution)/shard_map/ppermute | solution.py:94
  17.1 9.7 %collective-permute-start.2 = (f32[1024,96]{0,1:T(8,128)}, f32[1024,96]{0,1:T(8,128)}, u32[]{:S(2)}, u32[]{:S(2)}) collective-permute-start(f32[1024,96]{0,1:T(8,128)} %get-tuple-element.285), channel_id=1, source_target_pairs={{0,48},{16,0},{32,16},{48,32},{1,49},{17,1},{33,17},{49,33},{2,50}... | collective-permute-start | bytes 1179656 | tf_op jit(solution)/shard_map/ppermute | solution.py:95
  20.9 1.0 copy-start.5
  26.9 9.9 %collective-permute-start.3 = (f32[1024,96]{0,1:T(8,128)}, f32[1024,96]{0,1:T(8,128)S(1)}, u32[]{:S(2)}, u32[]{:S(2)}) collective-permute-start(f32[1024,96]{0,1:T(8,128)} %collective-permute-done.1), channel_id=1, source_target_pairs={{0,16},{16,32},{32,48},{48,0},{1,17},{17,33},{33,49},{49,1},{2,18}... | collective-permute-start | bytes 1179656 | tf_op jit(solution)/shard_map/ppermute | solution.py:94
  26.9 9.9 %collective-permute-start.4 = (f32[1024,96]{0,1:T(8,128)}, f32[1024,96]{0,1:T(8,128)S(1)}, u32[]{:S(2)}, u32[]{:S(2)}) collective-permute-start(f32[1024,96]{0,1:T(8,128)} %collective-permute-done.2), channel_id=1, source_target_pairs={{0,48},{16,0},{32,16},{48,32},{1,49},{17,1},{33,17},{49,33},{2,50}... | collective-permute-start | bytes 1179656 | tf_op jit(solution)/shard_map/ppermute | solution.py:95
  29.5 17.5 %copy-start.8 = (f32[2048,768]{1,0:T(8,128)S(1)}, f32[2048,768]{1,0:T(8,128)}, u32[]{:S(2)}) copy-start(f32[2048,768]{1,0:T(8,128)} %param.47) | copy-start | bytes 18874372
  36.8 8.8 %collective-permute-start.5 = (f32[1024,96]{0,1:T(8,128)S(1)}, f32[1024,96]{0,1:T(8,128)S(1)}, u32[]{:S(2)}, u32[]{:S(2)}) collective-permute-start(f32[1024,96]{0,1:T(8,128)S(1)} %collective-permute-done.3), channel_id=1, source_target_pairs={{0,16},{16,32},{32,48},{48,0},{1,17},{17,33},{33,49},{49,1},{2,18}... | collective-permute-start | bytes 1179656 | tf_op jit(solution)/shard_map/ppermute | solution.py:94
  36.8 9.5 %collective-permute-start.6 = (f32[1024,96]{0,1:T(8,128)S(1)}, f32[1024,96]{0,1:T(8,128)S(1)}, u32[]{:S(2)}, u32[]{:S(2)}) collective-permute-start(f32[1024,96]{0,1:T(8,128)S(1)} %collective-permute-done.4), channel_id=1, source_target_pairs={{0,48},{16,0},{32,16},{48,32},{1,49},{17,1},{33,17},{49,33},{2,50}... | collective-permute-start | bytes 1179656 | tf_op jit(solution)/shard_map/ppermute | solution.py:95
  71.3 4.1 %collective-permute-start.7 = (f32[2,1024]{1,0:T(2,128)S(1)}, f32[2,1024]{1,0:T(2,128)S(1)}, u32[]{:S(2)}, u32[]{:S(2)}) collective-permute-start(f32[2,1024]{1,0:T(2,128)S(1)} %pad_maximum_fusion.7), channel_id=1, source_target_pairs={{0,64},{64,0},{1,65},{65,1},{2,66},{66,2},{3,67},{67,3},{4,68},{68... | collective-permute-start | bytes 24584 | tf_op jit(solution)/shard_map/ppermute | solution.py:38
  75.5 2.6 %collective-permute-start.8 = (f32[2,1024]{1,0:T(2,128)S(1)}, f32[2,1024]{1,0:T(2,128)S(1)}, u32[]{:S(2)}, u32[]{:S(2)}) collective-permute-start(f32[2,1024]{1,0:T(2,128)S(1)} %pad_maximum_fusion.8), channel_id=1, source_target_pairs={{0,16},{16,0},{32,48},{48,32},{1,17},{17,1},{33,49},{49,33},{2,18}... | collective-permute-start | bytes 24584 | tf_op jit(solution)/shard_map/ppermute | solution.py:38
  78.1 24.5 %collective-permute-start.9 = (f32[2,1024]{1,0:T(2,128)S(1)}, f32[2,1024]{1,0:T(2,128)S(1)}, u32[]{:S(2)}, u32[]{:S(2)}) collective-permute-start(f32[2,1024]{1,0:T(2,128)S(1)} %pad_maximum_fusion.9), channel_id=1, source_target_pairs={{0,32},{16,48},{32,0},{48,16},{1,33},{17,49},{33,1},{49,17},{2,34}... | collective-permute-start | bytes 24584 | tf_op jit(solution)/shard_map/ppermute | solution.py:38
  105.0 19.0 %copy-start = (f32[2048,1024]{1,0:T(8,128)}, f32[2048,1024]{1,0:T(8,128)S(1)}, u32[]{:S(2)}) copy-start(f32[2048,1024]{1,0:T(8,128)S(1)} %get-tuple-element.276) | copy-start | bytes 25165828
  105.1 12.0 %collective-permute-start.10 = (f32[2,2048]{1,0:T(2,128)S(1)}, f32[2,2048]{1,0:T(2,128)S(1)}, u32[]{:S(2)}, u32[]{:S(2)}) collective-permute-start(f32[2,2048]{1,0:T(2,128)S(1)} %pad_maximum_fusion.3), channel_id=1, source_target_pairs={{0,1},{1,0},{2,3},{3,2},{4,5},{5,4},{6,7},{7,6},{8,9},{9,8},{10,11... | collective-permute-start | bytes 49160 | tf_op jit(solution)/shard_map/ppermute | solution.py:38
  117.2 5.4 %collective-permute-start.11 = (f32[2,2048]{1,0:T(2,128)S(1)}, f32[2,2048]{1,0:T(2,128)S(1)}, u32[]{:S(2)}, u32[]{:S(2)}) collective-permute-start(f32[2,2048]{1,0:T(2,128)S(1)} %pad_maximum_fusion.4), channel_id=1, source_target_pairs={{0,2},{2,0},{1,3},{3,1},{4,6},{6,4},{5,7},{7,5},{8,10},{10,8},{9,1... | collective-permute-start | bytes 49160 | tf_op jit(solution)/shard_map/ppermute | solution.py:38
  122.7 7.8 %collective-permute-start.12 = (f32[2,2048]{1,0:T(2,128)S(1)}, f32[2,2048]{1,0:T(2,128)S(1)}, u32[]{:S(2)}, u32[]{:S(2)}) collective-permute-start(f32[2,2048]{1,0:T(2,128)S(1)} %pad_maximum_fusion.5), channel_id=1, source_target_pairs={{0,4},{4,0},{8,12},{12,8},{1,5},{5,1},{9,13},{13,9},{2,6},{6,2},{1... | collective-permute-start | bytes 49160 | tf_op jit(solution)/shard_map/ppermute | solution.py:38
  130.6 4.4 %collective-permute-start.13 = (f32[2,2048]{1,0:T(2,128)S(1)}, f32[2,2048]{1,0:T(2,128)S(1)}, u32[]{:S(2)}, u32[]{:S(2)}) collective-permute-start(f32[2,2048]{1,0:T(2,128)S(1)} %pad_maximum_fusion.6), channel_id=1, source_target_pairs={{0,8},{4,12},{8,0},{12,4},{1,9},{5,13},{9,1},{13,5},{2,10},{6,14},... | collective-permute-start | bytes 49160 | tf_op jit(solution)/shard_map/ppermute | solution.py:38
  137.3 1.7 copy-start.1
  140.3 8.5 %copy-start.2 = (f32[512,768]{1,0:T(8,128)S(1)}, f32[512,768]{1,0:T(8,128)}, u32[]{:S(2)}) copy-start(f32[512,768]{1,0:T(8,128)} %fusion.3) | copy-start | bytes 4718596
  140.3 12.7 %collective-permute-start.14 = (f32[512,768]{1,0:T(8,128)}, f32[512,768]{1,0:T(8,128)}, u32[]{:S(2)}, u32[]{:S(2)}) collective-permute-start(f32[512,768]{1,0:T(8,128)} %dynamic-slice_bitcast_fusion.1), channel_id=1, source_target_pairs={{0,1},{1,0},{2,3},{3,2},{4,5},{5,4},{6,7},{7,6},{8,9},{9,8},{10,11... | collective-permute-start | bytes 4718600 | tf_op jit(solution)/shard_map/ppermute | solution.py:61
  150.5 6.6 %collective-permute-start.30 = (f32[512,768]{1,0:T(8,128)}, f32[512,768]{1,0:T(8,128)}, u32[]{:S(2)}, u32[]{:S(2)}) collective-permute-start(f32[512,768]{1,0:T(8,128)} %dynamic-slice_bitcast_fusion), channel_id=1, source_target_pairs={{0,1},{1,0},{2,3},{3,2},{4,5},{5,4},{6,7},{7,6},{8,9},{9,8},{10,11... | collective-permute-start | bytes 4718600 | tf_op jit(solution)/shard_map/ppermute | solution.py:61
  155.2 6.6 %collective-permute-start.18 = (f32[64,768]{1,0:T(8,128)S(1)}, f32[64,768]{1,0:T(8,128)S(1)}, u32[]{:S(2)}, u32[]{:S(2)}) collective-permute-start(f32[64,768]{1,0:T(8,128)S(1)} %dynamic-slice_bitcast_fusion.4), channel_id=1, source_target_pairs={{0,12},{4,0},{8,4},{12,8},{1,13},{5,1},{9,5},{13,9},{2,14},{6,2},{... | collective-permute-start | bytes 589832 | tf_op jit(solution)/shard_map/ppermute | solution.py:66
  157.1 7.4 %collective-permute-start.15 = (f32[64,768]{1,0:T(8,128)S(1)}, f32[64,768]{1,0:T(8,128)S(1)}, u32[]{:S(2)}, u32[]{:S(2)}) collective-permute-start(f32[64,768]{1,0:T(8,128)S(1)} %dynamic-slice_bitcast_fusion.5), channel_id=1, source_target_pairs={{0,4},{4,8},{8,12},{12,0},{1,5},{5,9},{9,13},{13,1},{2,6},{6,10},{... | collective-permute-start | bytes 589832 | tf_op jit(solution)/shard_map/ppermute | solution.py:65
  158.9 6.8 %collective-permute-start.34 = (f32[64,768]{1,0:T(8,128)S(1)}, f32[64,768]{1,0:T(8,128)S(1)}, u32[]{:S(2)}, u32[]{:S(2)}) collective-permute-start(f32[64,768]{1,0:T(8,128)S(1)} %dynamic-slice_bitcast_fusion.2), channel_id=1, source_target_pairs={{0,12},{4,0},{8,4},{12,8},{1,13},{5,1},{9,5},{13,9},{2,14},{6,2},{... | collective-permute-start | bytes 589832 | tf_op jit(solution)/shard_map/ppermute | solution.py:66
  161.7 6.7 %collective-permute-start.31 = (f32[64,768]{1,0:T(8,128)S(1)}, f32[64,768]{1,0:T(8,128)S(1)}, u32[]{:S(2)}, u32[]{:S(2)}) collective-permute-start(f32[64,768]{1,0:T(8,128)S(1)} %dynamic-slice_bitcast_fusion.3), channel_id=1, source_target_pairs={{0,4},{4,8},{8,12},{12,0},{1,5},{5,9},{9,13},{13,1},{2,6},{6,10},{... | collective-permute-start | bytes 589832 | tf_op jit(solution)/shard_map/ppermute | solution.py:65
  161.8 8.1 %collective-permute-start.19 = (f32[64,768]{1,0:T(8,128)S(1)}, f32[64,768]{1,0:T(8,128)S(1)}, u32[]{:S(2)}, u32[]{:S(2)}) collective-permute-start(f32[64,768]{1,0:T(8,128)S(1)} %bitcast_add_fusion.10), channel_id=1, source_target_pairs={{0,12},{4,0},{8,4},{12,8},{1,13},{5,1},{9,5},{13,9},{2,14},{6,2},{... | collective-permute-start | bytes 589832 | tf_op jit(solution)/shard_map/ppermute | solution.py:66
  164.5 8.3 %collective-permute-start.16 = (f32[64,768]{1,0:T(8,128)S(1)}, f32[64,768]{1,0:T(8,128)S(1)}, u32[]{:S(2)}, u32[]{:S(2)}) collective-permute-start(f32[64,768]{1,0:T(8,128)S(1)} %bitcast_add_fusion.13), channel_id=1, source_target_pairs={{0,4},{4,8},{8,12},{12,0},{1,5},{5,9},{9,13},{13,1},{2,6},{6,10},{... | collective-permute-start | bytes 589832 | tf_op jit(solution)/shard_map/ppermute | solution.py:65
  165.7 8.3 %collective-permute-start.35 = (f32[64,768]{1,0:T(8,128)S(1)}, f32[64,768]{1,0:T(8,128)S(1)}, u32[]{:S(2)}, u32[]{:S(2)}) collective-permute-start(f32[64,768]{1,0:T(8,128)S(1)} %bitcast_add_fusion.4), channel_id=1, source_target_pairs={{0,12},{4,0},{8,4},{12,8},{1,13},{5,1},{9,5},{13,9},{2,14},{6,2},{... | collective-permute-start | bytes 589832 | tf_op jit(solution)/shard_map/ppermute | solution.py:66
  168.4 7.9 %collective-permute-start.32 = (f32[64,768]{1,0:T(8,128)S(1)}, f32[64,768]{1,0:T(8,128)S(1)}, u32[]{:S(2)}, u32[]{:S(2)}) collective-permute-start(f32[64,768]{1,0:T(8,128)S(1)} %bitcast_add_fusion.7), channel_id=1, source_target_pairs={{0,4},{4,8},{8,12},{12,0},{1,5},{5,9},{9,13},{13,1},{2,6},{6,10},{... | collective-permute-start | bytes 589832 | tf_op jit(solution)/shard_map/ppermute | solution.py:65
  169.9 8.3 %collective-permute-start.20 = (f32[64,768]{1,0:T(8,128)S(1)}, f32[64,768]{1,0:T(8,128)S(1)}, u32[]{:S(2)}, u32[]{:S(2)}) collective-permute-start(f32[64,768]{1,0:T(8,128)S(1)} %bitcast_add_fusion.9), channel_id=1, source_target_pairs={{0,12},{4,0},{8,4},{12,8},{1,13},{5,1},{9,5},{13,9},{2,14},{6,2},{... | collective-permute-start | bytes 589832 | tf_op jit(solution)/shard_map/ppermute | solution.py:66
  172.8 7.4 %collective-permute-start.17 = (f32[64,768]{1,0:T(8,128)S(1)}, f32[64,768]{1,0:T(8,128)S(1)}, u32[]{:S(2)}, u32[]{:S(2)}) collective-permute-start(f32[64,768]{1,0:T(8,128)S(1)} %bitcast_add_fusion.12), channel_id=1, source_target_pairs={{0,4},{4,8},{8,12},{12,0},{1,5},{5,9},{9,13},{13,1},{2,6},{6,10},{... | collective-permute-start | bytes 589832 | tf_op jit(solution)/shard_map/ppermute | solution.py:65
  174.1 8.2 %collective-permute-start.36 = (f32[64,768]{1,0:T(8,128)S(1)}, f32[64,768]{1,0:T(8,128)S(1)}, u32[]{:S(2)}, u32[]{:S(2)}) collective-permute-start(f32[64,768]{1,0:T(8,128)S(1)} %bitcast_add_fusion.3), channel_id=1, source_target_pairs={{0,12},{4,0},{8,4},{12,8},{1,13},{5,1},{9,5},{13,9},{2,14},{6,2},{... | collective-permute-start | bytes 589832 | tf_op jit(solution)/shard_map/ppermute | solution.py:66
  176.3 8.4 %collective-permute-start.33 = (f32[64,768]{1,0:T(8,128)S(1)}, f32[64,768]{1,0:T(8,128)S(1)}, u32[]{:S(2)}, u32[]{:S(2)}) collective-permute-start(f32[64,768]{1,0:T(8,128)S(1)} %bitcast_add_fusion.6), channel_id=1, source_target_pairs={{0,4},{4,8},{8,12},{12,0},{1,5},{5,9},{9,13},{13,1},{2,6},{6,10},{... | collective-permute-start | bytes 589832 | tf_op jit(solution)/shard_map/ppermute | solution.py:65
  180.3 5.9 %collective-permute-start.21 = (f32[64,768]{1,0:T(8,128)S(1)}, f32[64,768]{1,0:T(8,128)S(1)}, u32[]{:S(2)}, u32[]{:S(2)}) collective-permute-start(f32[64,768]{1,0:T(8,128)S(1)} %fusion.28), channel_id=1, source_target_pairs={{0,2},{2,0},{1,3},{3,1},{4,6},{6,4},{5,7},{7,5},{8,10},{10,8},{9,1... | collective-permute-start | bytes 589832 | tf_op jit(solution)/shard_map/ppermute | solution.py:68
  184.8 6.1 %collective-permute-start.37 = (f32[64,768]{1,0:T(8,128)S(1)}, f32[64,768]{1,0:T(8,128)S(1)}, u32[]{:S(2)}, u32[]{:S(2)}) collective-permute-start(f32[64,768]{1,0:T(8,128)S(1)} %fusion.22), channel_id=1, source_target_pairs={{0,2},{2,0},{1,3},{3,1},{4,6},{6,4},{5,7},{7,5},{8,10},{10,8},{9,1... | collective-permute-start | bytes 589832 | tf_op jit(solution)/shard_map/ppermute | solution.py:68
  186.4 8.7 %collective-permute-start.22 = (f32[64,768]{1,0:T(8,128)S(1)}, f32[64,768]{1,0:T(8,128)S(1)}, u32[]{:S(2)}, u32[]{:S(2)}) collective-permute-start(f32[64,768]{1,0:T(8,128)S(1)} %fusion.32), channel_id=1, source_target_pairs={{0,2},{2,0},{1,3},{3,1},{4,6},{6,4},{5,7},{7,5},{8,10},{10,8},{9,1... | collective-permute-start | bytes 589832 | tf_op jit(solution)/shard_map/ppermute | solution.py:71
  190.9 8.3 %collective-permute-start.38 = (f32[64,768]{1,0:T(8,128)S(1)}, f32[64,768]{1,0:T(8,128)S(1)}, u32[]{:S(2)}, u32[]{:S(2)}) collective-permute-start(f32[64,768]{1,0:T(8,128)S(1)} %fusion.26), channel_id=1, source_target_pairs={{0,2},{2,0},{1,3},{3,1},{4,6},{6,4},{5,7},{7,5},{8,10},{10,8},{9,1... | collective-permute-start | bytes 589832 | tf_op jit(solution)/shard_map/ppermute | solution.py:71
  195.1 8.4 %collective-permute-start.23 = (f32[64,768]{1,0:T(8,128)S(1)}, f32[64,768]{1,0:T(8,128)S(1)}, u32[]{:S(2)}, u32[]{:S(2)}) collective-permute-start(f32[64,768]{1,0:T(8,128)S(1)} %get-tuple-element.288), channel_id=1, source_target_pairs={{0,4},{4,8},{8,12},{12,0},{1,5},{5,9},{9,13},{13,1},{2,6},{6,10},{... | collective-permute-start | bytes 589832 | tf_op jit(solution)/shard_map/ppermute | solution.py:76
  195.2 8.4 %collective-permute-start.24 = (f32[64,768]{1,0:T(8,128)S(1)}, f32[64,768]{1,0:T(8,128)S(1)}, u32[]{:S(2)}, u32[]{:S(2)}) collective-permute-start(f32[64,768]{1,0:T(8,128)S(1)} %get-tuple-element.287), channel_id=1, source_target_pairs={{0,12},{4,0},{8,4},{12,8},{1,13},{5,1},{9,5},{13,9},{2,14},{6,2},{... | collective-permute-start | bytes 589832 | tf_op jit(solution)/shard_map/ppermute | solution.py:77
  199.3 7.0 %collective-permute-start.39 = (f32[64,768]{1,0:T(8,128)S(1)}, f32[64,768]{1,0:T(8,128)S(1)}, u32[]{:S(2)}, u32[]{:S(2)}) collective-permute-start(f32[64,768]{1,0:T(8,128)S(1)} %get-tuple-element.290), channel_id=1, source_target_pairs={{0,4},{4,8},{8,12},{12,0},{1,5},{5,9},{9,13},{13,1},{2,6},{6,10},{... | collective-permute-start | bytes 589832 | tf_op jit(solution)/shard_map/ppermute | solution.py:76
  199.4 8.1 %collective-permute-start.40 = (f32[64,768]{1,0:T(8,128)S(1)}, f32[64,768]{1,0:T(8,128)S(1)}, u32[]{:S(2)}, u32[]{:S(2)}) collective-permute-start(f32[64,768]{1,0:T(8,128)S(1)} %get-tuple-element.289), channel_id=1, source_target_pairs={{0,12},{4,0},{8,4},{12,8},{1,13},{5,1},{9,5},{13,9},{2,14},{6,2},{... | collective-permute-start | bytes 589832 | tf_op jit(solution)/shard_map/ppermute | solution.py:77
  203.6 8.1 %collective-permute-start.25 = (f32[64,768]{1,0:T(8,128)S(1)}, f32[64,768]{1,0:T(8,128)S(1)}, u32[]{:S(2)}, u32[]{:S(2)}) collective-permute-start(f32[64,768]{1,0:T(8,128)S(1)} %collective-permute-done.23), channel_id=1, source_target_pairs={{0,4},{4,8},{8,12},{12,0},{1,5},{5,9},{9,13},{13,1},{2,6},{6,10},{... | collective-permute-start | bytes 589832 | tf_op jit(solution)/shard_map/ppermute | solution.py:76
  203.7 8.1 %collective-permute-start.26 = (f32[64,768]{1,0:T(8,128)S(1)}, f32[64,768]{1,0:T(8,128)S(1)}, u32[]{:S(2)}, u32[]{:S(2)}) collective-permute-start(f32[64,768]{1,0:T(8,128)S(1)} %collective-permute-done.24), channel_id=1, source_target_pairs={{0,12},{4,0},{8,4},{12,8},{1,13},{5,1},{9,5},{13,9},{2,14},{6,2},{... | collective-permute-start | bytes 589832 | tf_op jit(solution)/shard_map/ppermute | solution.py:77
  206.3 8.1 %collective-permute-start.41 = (f32[64,768]{1,0:T(8,128)S(1)}, f32[64,768]{1,0:T(8,128)S(1)}, u32[]{:S(2)}, u32[]{:S(2)}) collective-permute-start(f32[64,768]{1,0:T(8,128)S(1)} %collective-permute-done.39), channel_id=1, source_target_pairs={{0,4},{4,8},{8,12},{12,0},{1,5},{5,9},{9,13},{13,1},{2,6},{6,10},{... | collective-permute-start | bytes 589832 | tf_op jit(solution)/shard_map/ppermute | solution.py:76
  207.5 8.1 %collective-permute-start.42 = (f32[64,768]{1,0:T(8,128)S(1)}, f32[64,768]{1,0:T(8,128)S(1)}, u32[]{:S(2)}, u32[]{:S(2)}) collective-permute-start(f32[64,768]{1,0:T(8,128)S(1)} %collective-permute-done.40), channel_id=1, source_target_pairs={{0,12},{4,0},{8,4},{12,8},{1,13},{5,1},{9,5},{13,9},{2,14},{6,2},{... | collective-permute-start | bytes 589832 | tf_op jit(solution)/shard_map/ppermute | solution.py:77
  211.6 8.0 %collective-permute-start.27 = (f32[64,768]{1,0:T(8,128)S(1)}, f32[64,768]{1,0:T(8,128)S(1)}, u32[]{:S(2)}, u32[]{:S(2)}) collective-permute-start(f32[64,768]{1,0:T(8,128)S(1)} %collective-permute-done.25), channel_id=1, source_target_pairs={{0,4},{4,8},{8,12},{12,0},{1,5},{5,9},{9,13},{13,1},{2,6},{6,10},{... | collective-permute-start | bytes 589832 | tf_op jit(solution)/shard_map/ppermute | solution.py:76
  211.7 8.5 %collective-permute-start.28 = (f32[64,768]{1,0:T(8,128)S(1)}, f32[64,768]{1,0:T(8,128)S(1)}, u32[]{:S(2)}, u32[]{:S(2)}) collective-permute-start(f32[64,768]{1,0:T(8,128)S(1)} %collective-permute-done.26), channel_id=1, source_target_pairs={{0,12},{4,0},{8,4},{12,8},{1,13},{5,1},{9,5},{13,9},{2,14},{6,2},{... | collective-permute-start | bytes 589832 | tf_op jit(solution)/shard_map/ppermute | solution.py:77
  214.4 15.0 %collective-permute-start.43 = (f32[64,768]{1,0:T(8,128)S(1)}, f32[64,768]{1,0:T(8,128)S(1)}, u32[]{:S(2)}, u32[]{:S(2)}) collective-permute-start(f32[64,768]{1,0:T(8,128)S(1)} %collective-permute-done.41), channel_id=1, source_target_pairs={{0,4},{4,8},{8,12},{12,0},{1,5},{5,9},{9,13},{13,1},{2,6},{6,10},{... | collective-permute-start | bytes 589832 | tf_op jit(solution)/shard_map/ppermute | solution.py:76
  215.6 14.5 %collective-permute-start.44 = (f32[64,768]{1,0:T(8,128)S(1)}, f32[64,768]{1,0:T(8,128)S(1)}, u32[]{:S(2)}, u32[]{:S(2)}) collective-permute-start(f32[64,768]{1,0:T(8,128)S(1)} %collective-permute-done.42), channel_id=1, source_target_pairs={{0,12},{4,0},{8,4},{12,8},{1,13},{5,1},{9,5},{13,9},{2,14},{6,2},{... | collective-permute-start | bytes 589832 | tf_op jit(solution)/shard_map/ppermute | solution.py:77
  220.9 11.7 %collective-permute-start.29 = (f32[512,768]{1,0:T(8,128)S(1)}, f32[512,768]{1,0:T(8,128)}, u32[]{:S(2)}, u32[]{:S(2)}) collective-permute-start(f32[512,768]{1,0:T(8,128)S(1)} %bitcast.250), channel_id=1, source_target_pairs={{0,1},{1,0},{2,3},{3,2},{4,5},{5,4},{6,7},{7,6},{8,9},{9,8},{10,11... | collective-permute-start | bytes 4718600 | tf_op jit(solution)/shard_map/ppermute | solution.py:81
  230.8 4.1 %collective-permute-start.45 = (f32[512,768]{1,0:T(8,128)S(1)}, f32[512,768]{1,0:T(8,128)}, u32[]{:S(2)}, u32[]{:S(2)}) collective-permute-start(f32[512,768]{1,0:T(8,128)S(1)} %bitcast.248), channel_id=1, source_target_pairs={{0,1},{1,0},{2,3},{3,2},{4,5},{5,4},{6,7},{7,6},{8,9},{9,8},{10,11... | collective-permute-start | bytes 4718600 | tf_op jit(solution)/shard_map/ppermute | solution.py:81

commit v9 on v6

--- a/solution.py
+++ b/solution.py
@@ -77,9 +77,7 @@
         left = lax.ppermute(left, "x", ring("x", x_size, -1))
         gathered = gathered.at[(p - s - 1) % x_size, 0].set(right)
         gathered = gathered.at[(p + s + 1) % x_size, 1].set(left)
-    held = gathered.reshape(half, width)
-    other = lax.ppermute(held, "core", swap)
-    return jnp.where(c == 0, jnp.stack([held, other]), jnp.stack([other, held])).reshape(rows, width)
+    return gathered.reshape(half, width)
 
 
 def gather_features(captions, sizes):
@@ -124,7 +122,11 @@
         summed = lax.optimization_barrier(rescaled_affinity(weights[part], features))
         summed = summed * scale[part, None]
         parts.append(reduce_rows(summed, row_total, k * chunk, sizes))
-    return jnp.concatenate(parts, axis=0)
+    held = jnp.stack(parts)
+    other = jnp.stack([lax.ppermute(part, "core", [(0, 1), (1, 0)]) for part in parts])
+    c = lax.axis_index("core")
+    both = jnp.where(c == 0, jnp.stack([held, other], axis=1), jnp.stack([other, held], axis=1))
+    return both.reshape(rows, held.shape[-1])
 
 
 def solution(mesh):

time: 242 us -> 242 us (level)
    concatenate x1 -> x0, other arithmetic: 3.11 us -> none  [local(): return jnp.concatenate(parts, axis=0)]
    another operation x7 -> x9, other arithmetic: 5.97 us -> 8.26 us
  transfers between devices with their start and end apart: 46 -> 46, of which waited for: 21 -> 22; matrix products, arithmetic and copies ran while one was open for 32% -> 31% of each run, Pallas kernels for 0% -> 0%
where the time goes in v9:
time: 242 us; the launch traced here: 238 us
  matrix products  67.5 us (28%)
  starting transfers between devices  66.2 us (27%)
  waiting for transfers between devices  57.9 us (24%)
  other arithmetic  40.4 us (17%)
  local copies, waits for them, and re-layouts  5.39 us (2%)
    dot_general x2, matrix products, similar(): lax.dot_general(query_factor, target_factor, (((1,), (0,)), ((), ())), pr...  44.7 us
    dot_general x2, matrix products, rescaled_affinity(): lax.dot_general(weights, features, (((1,), (1,)), ((), ())), precision=la...  22.8 us
    ppermute x7, starting transfers between devices, merge_peaks(): other = lax.ppermute(pair, axis, [(j, j ^ dist) for j in range(size)])  15.1 us
    ppermute x6, waiting for transfers between devices, reduce_rows(): lax.ppermute(left, 'x', ring('x', x_size, -1))  15 us
    ppermute x3, waiting for transfers between devices, gather_features(): right = lax.ppermute(right, 'y', ring('y', y_size, 1))  12.1 us
    ppermute x6, starting transfers between devices, reduce_rows(): left = lax.ppermute(left, 'x', ring('x', x_size, -1))  11.7 us
    ppermute x2, starting transfers between devices, local(): lax.ppermute(part, 'core', [(0, 1), (1, 0)])  8.35 us
    ppermute x7, waiting for transfers between devices, merge_peaks(): other = lax.ppermute(pair, axis, [(j, j ^ dist) for j in range(size)])  8.19 us
  transfers between devices with their start and end apart: 46, of which 22 were waited for; matrix products, arithmetic and copies ran while one was open for 31% of the time, Pallas kernels for 0%

profile of v9, /device:TPU:1, one launch (start us, length us, event | category | flops | bytes accessed | tf_op | source)
XLA Modules:
  0.0 238.3 jit_solution(4830356431275234748)
XLA Ops:
  0.0 4.4 %collective-permute-start = (f32[1024,96]{0,1:T(8,128)}, f32[1024,96]{0,1:T(8,128)S(1)}, u32[]{:S(2)}, u32[]{:S(2)}) collective-permute-start(f32[1024,96]{0,1:T(8,128)} %param.46), channel_id=1, source_target_pairs={{0,64},{64,0},{1,65},{65,1},{2,66},{66,2},{3,67},{67,3},{4,68},{68... | collective-permute-start | bytes 1179656 | tf_op jit(solution)/shard_map/ppermute | solution.py:87
  4.4 1.4 and_reduce_fusion.10
  5.8 7.7 %collective-permute-done = f32[1024,96]{0,1:T(8,128)S(1)} collective-permute-done((f32[1024,96]{0,1:T(8,128)}, f32[1024,96]{0,1:T(8,128)S(1)}, u32[]{:S(2)}, u32[]{:S(2)}) %collective-permute-start) | collective-permute-done | bytes 393248 | tf_op jit(solution)/shard_map/ppermute | solution.py:87
  13.5 1.4 maximum_select_fusion.2
  14.8 1.0 slice_bitcast_fusion
  15.8 1.3 collective-permute-start.1
  17.1 1.4 collective-permute-start.2
  22.6 4.2 %collective-permute-done.1 = f32[1024,96]{0,1:T(8,128)} collective-permute-done((f32[1024,96]{0,1:T(8,128)}, f32[1024,96]{0,1:T(8,128)}, u32[]{:S(2)}, u32[]{:S(2)}) %collective-permute-start.1) | collective-permute-done | bytes 393248 | tf_op jit(solution)/shard_map/ppermute | solution.py:92
  26.9 2.7 %collective-permute-start.4 = (f32[1024,96]{0,1:T(8,128)}, f32[1024,96]{0,1:T(8,128)S(1)}, u32[]{:S(2)}, u32[]{:S(2)}) collective-permute-start(f32[1024,96]{0,1:T(8,128)} %collective-permute-done.2), channel_id=1, source_target_pairs={{0,48},{16,0},{32,16},{48,32},{1,49},{17,1},{33,17},{49,33},{2,50}... | collective-permute-start | bytes 1179656 | tf_op jit(solution)/shard_map/ppermute | solution.py:93
  29.6 1.9 fusion.16
  31.5 1.6 fusion.15
  33.1 3.7 %collective-permute-done.3 = f32[1024,96]{0,1:T(8,128)S(1)} collective-permute-done((f32[1024,96]{0,1:T(8,128)}, f32[1024,96]{0,1:T(8,128)S(1)}, u32[]{:S(2)}, u32[]{:S(2)}) %collective-permute-start.3) | collective-permute-done | bytes 393248 | tf_op jit(solution)/shard_map/ppermute | solution.py:92
  36.8 3.1 %collective-permute-start.6 = (f32[1024,96]{0,1:T(8,128)S(1)}, f32[1024,96]{0,1:T(8,128)S(1)}, u32[]{:S(2)}, u32[]{:S(2)}) collective-permute-start(f32[1024,96]{0,1:T(8,128)S(1)} %collective-permute-done.4), channel_id=1, source_target_pairs={{0,48},{16,0},{32,16},{48,32},{1,49},{17,1},{33,17},{49,33},{2,50}... | collective-permute-start | bytes 1179656 | tf_op jit(solution)/shard_map/ppermute | solution.py:93
  41.4 4.2 %collective-permute-done.5 = f32[1024,96]{0,1:T(8,128)S(1)} collective-permute-done((f32[1024,96]{0,1:T(8,128)S(1)}, f32[1024,96]{0,1:T(8,128)S(1)}, u32[]{:S(2)}, u32[]{:S(2)}) %collective-permute-start.5) | collective-permute-done | bytes 393248 | tf_op jit(solution)/shard_map/ppermute | solution.py:92
  46.4 0.8 fusion.11
  47.3 22.5 %fusion = (f32[1024]{0:T(1024)S(1)}, f32[1024,2048]{0,1:T(8,128)S(1)}) fusion(f32[768,1024]{1,0:T(8,128)S(1)} %bitcast.247, f32[2048,768]{1,0:T(8,128)S(1)} %copy-done.7), kind=kOutput, calls=%fused_computation.4 | convolution fusion | flops 19331547136 | bytes 17829888 | tf_op jit(solution)/shard_map/dot_general | solution.py:15
  69.7 1.4 exponential_reduce_fusion
  71.2 1.8 collective-permute-start.7
  73.0 2.3 collective-permute-done.7
  75.4 2.5 %collective-permute-done.8 = f32[2,1024]{1,0:T(2,128)S(1)} collective-permute-done((f32[2,1024]{1,0:T(2,128)S(1)}, f32[2,1024]{1,0:T(2,128)S(1)}, u32[]{:S(2)}, u32[]{:S(2)}) %collective-permute-start.8) | collective-permute-done | bytes 8224 | tf_op jit(solution)/shard_map/ppermute | solution.py:38
  77.9 2.6 %collective-permute-start.9 = (f32[2,1024]{1,0:T(2,128)S(1)}, f32[2,1024]{1,0:T(2,128)S(1)}, u32[]{:S(2)}, u32[]{:S(2)}) collective-permute-start(f32[2,1024]{1,0:T(2,128)S(1)} %pad_maximum_fusion.6), channel_id=1, source_target_pairs={{0,32},{16,48},{32,0},{48,16},{1,33},{17,49},{33,1},{49,17},{2,34}... | collective-permute-start | bytes 24584 | tf_op jit(solution)/shard_map/ppermute | solution.py:38
  80.5 22.2 %bitcast_multiply_fusion.1 = f32[2048,1024]{1,0:T(8,128)S(1)} fusion(f32[768,1024]{1,0:T(8,128)S(1)} %bitcast.248, f32[2048,768]{1,0:T(8,128)S(1)} %bitcast.284), kind=kOutput, calls=%fused_computation.1 | convolution fusion | flops 19329449984 | bytes 17825792 | tf_op jit(solution)/shard_map/dot_general | solution.py:15
  103.4 4.2 %fusion.53 = (f32[2048]{0:T(1024)S(1)}, f32[2048,1024]{1,0:T(8,128)}) fusion(f32[2048]{0:T(1024)S(1)} %subtract_reduce_fusion, f32[2048,1024]{1,0:T(8,128)S(1)} %bitcast_multiply_fusion.1, f32[1024]{0:T(1024)S(1)} %bitcast.274), kind=kLoop, calls=%fused_computation.200 | loop fusion | flops 6289408 | bytes 16797696 | tf_op jit(solution)/shard_map/reduce_sum | solution.py:114
  107.6 6.3 %collective-permute-start.10 = (f32[2,2048]{1,0:T(2,128)S(1)}, f32[2,2048]{1,0:T(2,128)S(1)}, u32[]{:S(2)}, u32[]{:S(2)}) collective-permute-start(f32[2,2048]{1,0:T(2,128)S(1)} %pad_maximum_fusion), channel_id=1, source_target_pairs={{0,1},{1,0},{2,3},{3,2},{4,5},{5,4},{6,7},{7,6},{8,9},{9,8},{10,11... | collective-permute-start | bytes 49160 | tf_op jit(solution)/shard_map/ppermute | solution.py:38
  114.9 2.5 %collective-permute-done.11 = f32[2,2048]{1,0:T(2,128)S(1)} collective-permute-done((f32[2,2048]{1,0:T(2,128)S(1)}, f32[2,2048]{1,0:T(2,128)S(1)}, u32[]{:S(2)}, u32[]{:S(2)}) %collective-permute-start.11) | collective-permute-done | bytes 16416 | tf_op jit(solution)/shard_map/ppermute | solution.py:38
  117.5 1.3 collective-permute-start.12
  118.8 12.4 %fusion.3 = f32[1024,768]{1,0:T(8,128)S(1)} fusion(f32[768,1024]{1,0:T(8,128)S(1)} %bitcast.249, f32[2048,1024]{1,0:T(8,128)} %get-tuple-element.276), kind=kOutput, calls=%fused_computation.9 | convolution fusion | flops 9663676416 | bytes 10485760 | tf_op jit(solution)/shard_map/dot_general | solution.py:26
  131.3 2.9 %collective-permute-start.13 = (f32[2,2048]{1,0:T(2,128)S(1)}, f32[2,2048]{1,0:T(2,128)S(1)}, u32[]{:S(2)}, u32[]{:S(2)}) collective-permute-start(f32[2,2048]{1,0:T(2,128)S(1)} %pad_maximum_fusion.3), channel_id=1, source_target_pairs={{0,8},{4,12},{8,0},{12,4},{1,9},{5,13},{9,1},{13,5},{2,10},{6,14},... | collective-permute-start | bytes 49160 | tf_op jit(solution)/shard_map/ppermute | solution.py:38
  134.3 10.4 %fusion.1 = f32[1024,768]{1,0:T(8,128)S(1)} fusion(f32[768,1024]{1,0:T(8,128)S(1)} %bitcast.250, f32[2048,1024]{1,0:T(8,128)S(1)} %copy-done.1), kind=kOutput, calls=%fused_computation.7 | convolution fusion | flops 9663676416 | bytes 10485760 | tf_op jit(solution)/shard_map/dot_general | solution.py:26
  145.2 1.4 dynamic-slice_bitcast_fusion.1
  146.7 2.1 collective-permute-start.14
  148.7 1.3 dynamic-slice_bitcast_fusion
  152.6 2.1 bitcast_add_fusion.1
  155.1 1.3 collective-permute-start.15
  156.5 1.6 bitcast_add_fusion
  158.2 1.5 collective-permute-start.33
  159.8 1.2 collective-permute-done.18
  161.1 1.5 collective-permute-start.19
  162.7 2.6 %collective-permute-done.33 = f32[64,768]{1,0:T(8,128)S(1)} collective-permute-done((f32[64,768]{1,0:T(8,128)S(1)}, f32[64,768]{1,0:T(8,128)S(1)}, u32[]{:S(2)}, u32[]{:S(2)}) %collective-permute-start.33) | collective-permute-done | bytes 196640 | tf_op jit(solution)/shard_map/ppermute | solution.py:66
  165.3 1.2 collective-permute-start.34
  166.9 2.6 %collective-permute-done.19 = f32[64,768]{1,0:T(8,128)S(1)} collective-permute-done((f32[64,768]{1,0:T(8,128)S(1)}, f32[64,768]{1,0:T(8,128)S(1)}, u32[]{:S(2)}, u32[]{:S(2)}) %collective-permute-start.19) | collective-permute-done | bytes 196640 | tf_op jit(solution)/shard_map/ppermute | solution.py:66
  169.5 1.3 collective-permute-start.20
  171.1 2.5 %collective-permute-done.34 = f32[64,768]{1,0:T(8,128)S(1)} collective-permute-done((f32[64,768]{1,0:T(8,128)S(1)}, f32[64,768]{1,0:T(8,128)S(1)}, u32[]{:S(2)}, u32[]{:S(2)}) %collective-permute-start.34) | collective-permute-done | bytes 196640 | tf_op jit(solution)/shard_map/ppermute | solution.py:66
  174.4 1.0 collective-permute-start.32
  175.4 2.6 %collective-permute-done.20 = f32[64,768]{1,0:T(8,128)S(1)} collective-permute-done((f32[64,768]{1,0:T(8,128)S(1)}, f32[64,768]{1,0:T(8,128)S(1)}, u32[]{:S(2)}, u32[]{:S(2)}) %collective-permute-start.20) | collective-permute-done | bytes 196640 | tf_op jit(solution)/shard_map/ppermute | solution.py:66
  178.5 3.6 %collective-permute-done.35 = f32[64,768]{1,0:T(8,128)S(1)} collective-permute-done((f32[64,768]{1,0:T(8,128)S(1)}, f32[64,768]{1,0:T(8,128)S(1)}, u32[]{:S(2)}, u32[]{:S(2)}) %collective-permute-start.35) | collective-permute-done | bytes 196640 | tf_op jit(solution)/shard_map/ppermute | solution.py:66
  183.4 1.2 collective-permute-start.22
  184.5 4.4 %collective-permute-done.36 = f32[64,768]{1,0:T(8,128)S(1)} collective-permute-done((f32[64,768]{1,0:T(8,128)S(1)}, f32[64,768]{1,0:T(8,128)S(1)}, u32[]{:S(2)}, u32[]{:S(2)}) %collective-permute-start.36) | collective-permute-done | bytes 196640 | tf_op jit(solution)/shard_map/ppermute | solution.py:68
  189.1 4.0 %collective-permute-done.22 = f32[64,768]{1,0:T(8,128)S(1)} collective-permute-done((f32[64,768]{1,0:T(8,128)S(1)}, f32[64,768]{1,0:T(8,128)S(1)}, u32[]{:S(2)}, u32[]{:S(2)}) %collective-permute-start.22) | collective-permute-done | bytes 196640 | tf_op jit(solution)/shard_map/ppermute | solution.py:71
  193.2 1.3 collective-permute-start.23
  194.5 1.4 collective-permute-start.24
  195.9 1.4 collective-permute-done.37
  197.4 1.3 collective-permute-start.38
  198.7 1.4 collective-permute-start.39
  202.0 2.6 %collective-permute-start.26 = (f32[64,768]{1,0:T(8,128)S(1)}, f32[64,768]{1,0:T(8,128)S(1)}, u32[]{:S(2)}, u32[]{:S(2)}) collective-permute-start(f32[64,768]{1,0:T(8,128)S(1)} %collective-permute-done.24), channel_id=1, source_target_pairs={{0,12},{4,0},{8,4},{12,8},{1,13},{5,1},{9,5},{13,9},{2,14},{6,2},{... | collective-permute-start | bytes 589832 | tf_op jit(solution)/shard_map/ppermute | solution.py:77
  206.7 1.9 collective-permute-start.41
  210.1 2.7 %collective-permute-start.28 = (f32[64,768]{1,0:T(8,128)S(1)}, f32[64,768]{1,0:T(8,128)S(1)}, u32[]{:S(2)}, u32[]{:S(2)}) collective-permute-start(f32[64,768]{1,0:T(8,128)S(1)} %collective-permute-done.26), channel_id=1, source_target_pairs={{0,12},{4,0},{8,4},{12,8},{1,13},{5,1},{9,5},{13,9},{2,14},{6,2},{... | collective-permute-start | bytes 589832 | tf_op jit(solution)/shard_map/ppermute | solution.py:77
  212.8 1.0 collective-permute-start.42
  215.3 1.7 collective-permute-start.43
  219.5 8.2 %collective-permute-start.44 = (f32[512,768]{1,0:T(8,128)S(1)}, f32[512,768]{1,0:T(8,128)}, u32[]{:S(2)}, u32[]{:S(2)}) collective-permute-start(f32[512,768]{1,0:T(8,128)S(1)} %bitcast.245), channel_id=1, source_target_pairs={{0,1},{1,0},{2,3},{3,2},{4,5},{5,4},{6,7},{7,6},{8,9},{9,8},{10,11... | collective-permute-start | bytes 4718600 | tf_op jit(solution)/shard_map/ppermute | solution.py:126
  229.3 1.6 collective-permute-done.44
  230.9 2.2 collective-permute-done.45
  233.1 2.1 maximum_bitcast_fusion.1
  235.2 2.9 %maximum_select_fusion = f32[2,2,512,768]{3,2,1,0:T(8,128)} fusion(f32[2,1,512,768]{3,2,1,0:T(8,128)S(1)} %maximum_bitcast_fusion.1, f32[2,1,512,768]{3,2,1,0:T(8,128)S(1)} %maximum_bitcast_fusion, pred[]{:T(512)S(6)} %eq.45), kind=kLoop, calls=%fused_computation.6 | loop fusion | flops 4718592 | bytes 12582913 | tf_op jit(solution)/shard_map/jit(_where)/select_n | solution.py:128
  (140 shorter events, 26.5 us)
Async XLA Ops:
  0.0 19.4 %copy-start.5 = (s32[4]{0:T(128)S(1)}, s32[4]{0:T(128)}, u32[]{:S(2)}) copy-start(s32[4]{0:T(128)} %constant.689.clone.1) | copy-start | bytes 52
  0.0 18.6 %copy-start.6 = (s32[4]{0:T(128)S(1)}, s32[4]{0:T(128)}, u32[]{:S(2)}) copy-start(s32[4]{0:T(128)} %constant.683.clone.1) | copy-start | bytes 52
  0.0 13.5 %collective-permute-start = (f32[1024,96]{0,1:T(8,128)}, f32[1024,96]{0,1:T(8,128)S(1)}, u32[]{:S(2)}, u32[]{:S(2)}) collective-permute-start(f32[1024,96]{0,1:T(8,128)} %param.46), channel_id=1, source_target_pairs={{0,64},{64,0},{1,65},{65,1},{2,66},{66,2},{3,67},{67,3},{4,68},{68... | collective-permute-start | bytes 1179656 | tf_op jit(solution)/shard_map/ppermute | solution.py:87
  13.5 7.5 %copy-start.3 = (f32[1024,96]{0,1:T(8,128)}, f32[1024,96]{0,1:T(8,128)S(1)}, u32[]{:S(2)}) copy-start(f32[1024,96]{0,1:T(8,128)S(1)} %collective-permute-done) | copy-start | bytes 1179652
  13.5 7.8 %copy-start.2 = (f32[1024,96]{0,1:T(8,128)S(1)}, f32[1024,96]{0,1:T(8,128)}, u32[]{:S(2)}) copy-start(f32[1024,96]{0,1:T(8,128)} %param.46) | copy-start | bytes 1179652
  15.8 11.0 %collective-permute-start.1 = (f32[1024,96]{0,1:T(8,128)}, f32[1024,96]{0,1:T(8,128)}, u32[]{:S(2)}, u32[]{:S(2)}) collective-permute-start(f32[1024,96]{0,1:T(8,128)} %get-tuple-element.286), channel_id=1, source_target_pairs={{0,16},{16,32},{32,48},{48,0},{1,17},{17,33},{33,49},{49,1},{2,18}... | collective-permute-start | bytes 1179656 | tf_op jit(solution)/shard_map/ppermute | solution.py:92
  17.1 9.7 %collective-permute-start.2 = (f32[1024,96]{0,1:T(8,128)}, f32[1024,96]{0,1:T(8,128)}, u32[]{:S(2)}, u32[]{:S(2)}) collective-permute-start(f32[1024,96]{0,1:T(8,128)} %get-tuple-element.285), channel_id=1, source_target_pairs={{0,48},{16,0},{32,16},{48,32},{1,49},{17,1},{33,17},{49,33},{2,50}... | collective-permute-start | bytes 1179656 | tf_op jit(solution)/shard_map/ppermute | solution.py:93
  20.9 1.0 copy-start.4
  26.9 9.9 %collective-permute-start.3 = (f32[1024,96]{0,1:T(8,128)}, f32[1024,96]{0,1:T(8,128)S(1)}, u32[]{:S(2)}, u32[]{:S(2)}) collective-permute-start(f32[1024,96]{0,1:T(8,128)} %collective-permute-done.1), channel_id=1, source_target_pairs={{0,16},{16,32},{32,48},{48,0},{1,17},{17,33},{33,49},{49,1},{2,18}... | collective-permute-start | bytes 1179656 | tf_op jit(solution)/shard_map/ppermute | solution.py:92
  26.9 9.9 %collective-permute-start.4 = (f32[1024,96]{0,1:T(8,128)}, f32[1024,96]{0,1:T(8,128)S(1)}, u32[]{:S(2)}, u32[]{:S(2)}) collective-permute-start(f32[1024,96]{0,1:T(8,128)} %collective-permute-done.2), channel_id=1, source_target_pairs={{0,48},{16,0},{32,16},{48,32},{1,49},{17,1},{33,17},{49,33},{2,50}... | collective-permute-start | bytes 1179656 | tf_op jit(solution)/shard_map/ppermute | solution.py:93
  29.6 17.7 %copy-start.7 = (f32[2048,768]{1,0:T(8,128)S(1)}, f32[2048,768]{1,0:T(8,128)}, u32[]{:S(2)}) copy-start(f32[2048,768]{1,0:T(8,128)} %param.47) | copy-start | bytes 18874372
  36.8 8.8 %collective-permute-start.5 = (f32[1024,96]{0,1:T(8,128)S(1)}, f32[1024,96]{0,1:T(8,128)S(1)}, u32[]{:S(2)}, u32[]{:S(2)}) collective-permute-start(f32[1024,96]{0,1:T(8,128)S(1)} %collective-permute-done.3), channel_id=1, source_target_pairs={{0,16},{16,32},{32,48},{48,0},{1,17},{17,33},{33,49},{49,1},{2,18}... | collective-permute-start | bytes 1179656 | tf_op jit(solution)/shard_map/ppermute | solution.py:92
  36.8 9.6 %collective-permute-start.6 = (f32[1024,96]{0,1:T(8,128)S(1)}, f32[1024,96]{0,1:T(8,128)S(1)}, u32[]{:S(2)}, u32[]{:S(2)}) collective-permute-start(f32[1024,96]{0,1:T(8,128)S(1)} %collective-permute-done.4), channel_id=1, source_target_pairs={{0,48},{16,0},{32,16},{48,32},{1,49},{17,1},{33,17},{49,33},{2,50}... | collective-permute-start | bytes 1179656 | tf_op jit(solution)/shard_map/ppermute | solution.py:93
  46.4 34.1 %slice-start = ((s8[6291456]{0:T(1024)(128)(4,1)}), s8[4194304]{0:T(1024)(128)(4,1)S(1)}, s32[]{:S(2)}) async-start(s8[6291456]{0:T(1024)(128)(4,1)} %bitcast.283), calls=%async_computation | async-start | bytes 8388608
  47.3 33.3 %slice-start.1 = ((s8[6291456]{0:T(1024)(128)(4,1)}), s8[2097152]{0:T(1024)(128)(4,1)S(1)}, s32[]{:S(2)}) async-start(s8[6291456]{0:T(1024)(128)(4,1)} %bitcast.283), calls=%async_computation.1 | async-start | bytes 4194304
  71.2 4.1 %collective-permute-start.7 = (f32[2,1024]{1,0:T(2,128)S(1)}, f32[2,1024]{1,0:T(2,128)S(1)}, u32[]{:S(2)}, u32[]{:S(2)}) collective-permute-start(f32[2,1024]{1,0:T(2,128)S(1)} %pad_maximum_fusion.4), channel_id=1, source_target_pairs={{0,64},{64,0},{1,65},{65,1},{2,66},{66,2},{3,67},{67,3},{4,68},{68... | collective-permute-start | bytes 24584 | tf_op jit(solution)/shard_map/ppermute | solution.py:38
  75.3 2.6 %collective-permute-start.8 = (f32[2,1024]{1,0:T(2,128)S(1)}, f32[2,1024]{1,0:T(2,128)S(1)}, u32[]{:S(2)}, u32[]{:S(2)}) collective-permute-start(f32[2,1024]{1,0:T(2,128)S(1)} %pad_maximum_fusion.5), channel_id=1, source_target_pairs={{0,16},{16,0},{32,48},{48,32},{1,17},{17,1},{33,49},{49,33},{2,18}... | collective-permute-start | bytes 24584 | tf_op jit(solution)/shard_map/ppermute | solution.py:38
  77.9 24.8 %collective-permute-start.9 = (f32[2,1024]{1,0:T(2,128)S(1)}, f32[2,1024]{1,0:T(2,128)S(1)}, u32[]{:S(2)}, u32[]{:S(2)}) collective-permute-start(f32[2,1024]{1,0:T(2,128)S(1)} %pad_maximum_fusion.6), channel_id=1, source_target_pairs={{0,32},{16,48},{32,0},{48,16},{1,33},{17,49},{33,1},{49,17},{2,34}... | collective-permute-start | bytes 24584 | tf_op jit(solution)/shard_map/ppermute | solution.py:38
  107.6 7.1 %collective-permute-start.10 = (f32[2,2048]{1,0:T(2,128)S(1)}, f32[2,2048]{1,0:T(2,128)S(1)}, u32[]{:S(2)}, u32[]{:S(2)}) collective-permute-start(f32[2,2048]{1,0:T(2,128)S(1)} %pad_maximum_fusion), channel_id=1, source_target_pairs={{0,1},{1,0},{2,3},{3,2},{4,5},{5,4},{6,7},{7,6},{8,9},{9,8},{10,11... | collective-permute-start | bytes 49160 | tf_op jit(solution)/shard_map/ppermute | solution.py:38
  114.8 2.7 %collective-permute-start.11 = (f32[2,2048]{1,0:T(2,128)S(1)}, f32[2,2048]{1,0:T(2,128)S(1)}, u32[]{:S(2)}, u32[]{:S(2)}) collective-permute-start(f32[2,2048]{1,0:T(2,128)S(1)} %pad_maximum_fusion.1), channel_id=1, source_target_pairs={{0,2},{2,0},{1,3},{3,1},{4,6},{6,4},{5,7},{7,5},{8,10},{10,8},{9,1... | collective-permute-start | bytes 49160 | tf_op jit(solution)/shard_map/ppermute | solution.py:38
  117.5 13.7 %collective-permute-start.12 = (f32[2,2048]{1,0:T(2,128)S(1)}, f32[2,2048]{1,0:T(2,128)S(1)}, u32[]{:S(2)}, u32[]{:S(2)}) collective-permute-start(f32[2,2048]{1,0:T(2,128)S(1)} %pad_maximum_fusion.2), channel_id=1, source_target_pairs={{0,4},{4,0},{8,12},{12,8},{1,5},{5,1},{9,13},{13,9},{2,6},{6,2},{1... | collective-permute-start | bytes 49160 | tf_op jit(solution)/shard_map/ppermute | solution.py:38
  118.8 15.5 %copy-start.1 = (f32[2048,1024]{1,0:T(8,128)S(1)}, f32[2048,1024]{1,0:T(8,128)}, u32[]{:S(2)}) copy-start(f32[2048,1024]{1,0:T(8,128)} %get-tuple-element.276) | copy-start | bytes 25165828
  131.3 13.3 %collective-permute-start.13 = (f32[2,2048]{1,0:T(2,128)S(1)}, f32[2,2048]{1,0:T(2,128)S(1)}, u32[]{:S(2)}, u32[]{:S(2)}) collective-permute-start(f32[2,2048]{1,0:T(2,128)S(1)} %pad_maximum_fusion.3), channel_id=1, source_target_pairs={{0,8},{4,12},{8,0},{12,4},{1,9},{5,13},{9,1},{13,5},{2,10},{6,14},... | collective-permute-start | bytes 49160 | tf_op jit(solution)/shard_map/ppermute | solution.py:38
  145.2 4.8 %copy-start = (f32[1024,768]{1,0:T(8,128)}, f32[1024,768]{1,0:T(8,128)S(1)}, u32[]{:S(2)}) copy-start(f32[1024,768]{1,0:T(8,128)S(1)} %get-tuple-element.310) | copy-start | bytes 9437188
  146.7 6.0 %collective-permute-start.14 = (f32[512,768]{1,0:T(8,128)}, f32[512,768]{1,0:T(8,128)}, u32[]{:S(2)}, u32[]{:S(2)}) collective-permute-start(f32[512,768]{1,0:T(8,128)} %dynamic-slice_bitcast_fusion.1), channel_id=1, source_target_pairs={{0,1},{1,0},{2,3},{3,2},{4,5},{5,4},{6,7},{7,6},{8,9},{9,8},{10,11... | collective-permute-start | bytes 4718600 | tf_op jit(solution)/shard_map/ppermute | solution.py:61
  150.0 6.5 %collective-permute-start.29 = (f32[512,768]{1,0:T(8,128)}, f32[512,768]{1,0:T(8,128)}, u32[]{:S(2)}, u32[]{:S(2)}) collective-permute-start(f32[512,768]{1,0:T(8,128)} %dynamic-slice_bitcast_fusion), channel_id=1, source_target_pairs={{0,1},{1,0},{2,3},{3,2},{4,5},{5,4},{6,7},{7,6},{8,9},{9,8},{10,11... | collective-permute-start | bytes 4718600 | tf_op jit(solution)/shard_map/ppermute | solution.py:61
  154.8 6.2 %collective-permute-start.18 = (f32[64,768]{1,0:T(8,128)S(1)}, f32[64,768]{1,0:T(8,128)S(1)}, u32[]{:S(2)}, u32[]{:S(2)}) collective-permute-start(f32[64,768]{1,0:T(8,128)S(1)} %dynamic-slice_bitcast_fusion.4), channel_id=1, source_target_pairs={{0,12},{4,0},{8,4},{12,8},{1,13},{5,1},{9,5},{13,9},{2,14},{6,2},{... | collective-permute-start | bytes 589832 | tf_op jit(solution)/shard_map/ppermute | solution.py:66
  155.1 7.4 %collective-permute-start.15 = (f32[64,768]{1,0:T(8,128)S(1)}, f32[64,768]{1,0:T(8,128)S(1)}, u32[]{:S(2)}, u32[]{:S(2)}) collective-permute-start(f32[64,768]{1,0:T(8,128)S(1)} %dynamic-slice_bitcast_fusion.5), channel_id=1, source_target_pairs={{0,4},{4,8},{8,12},{12,0},{1,5},{5,9},{9,13},{13,1},{2,6},{6,10},{... | collective-permute-start | bytes 589832 | tf_op jit(solution)/shard_map/ppermute | solution.py:65
  158.2 7.0 %collective-permute-start.33 = (f32[64,768]{1,0:T(8,128)S(1)}, f32[64,768]{1,0:T(8,128)S(1)}, u32[]{:S(2)}, u32[]{:S(2)}) collective-permute-start(f32[64,768]{1,0:T(8,128)S(1)} %dynamic-slice_bitcast_fusion.2), channel_id=1, source_target_pairs={{0,12},{4,0},{8,4},{12,8},{1,13},{5,1},{9,5},{13,9},{2,14},{6,2},{... | collective-permute-start | bytes 589832 | tf_op jit(solution)/shard_map/ppermute | solution.py:66
  159.7 6.8 %collective-permute-start.30 = (f32[64,768]{1,0:T(8,128)S(1)}, f32[64,768]{1,0:T(8,128)S(1)}, u32[]{:S(2)}, u32[]{:S(2)}) collective-permute-start(f32[64,768]{1,0:T(8,128)S(1)} %dynamic-slice_bitcast_fusion.3), channel_id=1, source_target_pairs={{0,4},{4,8},{8,12},{12,0},{1,5},{5,9},{9,13},{13,1},{2,6},{6,10},{... | collective-permute-start | bytes 589832 | tf_op jit(solution)/shard_map/ppermute | solution.py:65
  161.1 8.4 %collective-permute-start.19 = (f32[64,768]{1,0:T(8,128)S(1)}, f32[64,768]{1,0:T(8,128)S(1)}, u32[]{:S(2)}, u32[]{:S(2)}) collective-permute-start(f32[64,768]{1,0:T(8,128)S(1)} %bitcast_add_fusion.10), channel_id=1, source_target_pairs={{0,12},{4,0},{8,4},{12,8},{1,13},{5,1},{9,5},{13,9},{2,14},{6,2},{... | collective-permute-start | bytes 589832 | tf_op jit(solution)/shard_map/ppermute | solution.py:66
  162.6 8.3 %collective-permute-start.16 = (f32[64,768]{1,0:T(8,128)S(1)}, f32[64,768]{1,0:T(8,128)S(1)}, u32[]{:S(2)}, u32[]{:S(2)}) collective-permute-start(f32[64,768]{1,0:T(8,128)S(1)} %bitcast_add_fusion.13), channel_id=1, source_target_pairs={{0,4},{4,8},{8,12},{12,0},{1,5},{5,9},{9,13},{13,1},{2,6},{6,10},{... | collective-permute-start | bytes 589832 | tf_op jit(solution)/shard_map/ppermute | solution.py:65
  165.3 8.4 %collective-permute-start.34 = (f32[64,768]{1,0:T(8,128)S(1)}, f32[64,768]{1,0:T(8,128)S(1)}, u32[]{:S(2)}, u32[]{:S(2)}) collective-permute-start(f32[64,768]{1,0:T(8,128)S(1)} %bitcast_add_fusion.4), channel_id=1, source_target_pairs={{0,12},{4,0},{8,4},{12,8},{1,13},{5,1},{9,5},{13,9},{2,14},{6,2},{... | collective-permute-start | bytes 589832 | tf_op jit(solution)/shard_map/ppermute | solution.py:66
  166.5 7.8 %collective-permute-start.31 = (f32[64,768]{1,0:T(8,128)S(1)}, f32[64,768]{1,0:T(8,128)S(1)}, u32[]{:S(2)}, u32[]{:S(2)}) collective-permute-start(f32[64,768]{1,0:T(8,128)S(1)} %bitcast_add_fusion.7), channel_id=1, source_target_pairs={{0,4},{4,8},{8,12},{12,0},{1,5},{5,9},{9,13},{13,1},{2,6},{6,10},{... | collective-permute-start | bytes 589832 | tf_op jit(solution)/shard_map/ppermute | solution.py:65
  169.5 8.4 %collective-permute-start.20 = (f32[64,768]{1,0:T(8,128)S(1)}, f32[64,768]{1,0:T(8,128)S(1)}, u32[]{:S(2)}, u32[]{:S(2)}) collective-permute-start(f32[64,768]{1,0:T(8,128)S(1)} %bitcast_add_fusion.9), channel_id=1, source_target_pairs={{0,12},{4,0},{8,4},{12,8},{1,13},{5,1},{9,5},{13,9},{2,14},{6,2},{... | collective-permute-start | bytes 589832 | tf_op jit(solution)/shard_map/ppermute | solution.py:66
  170.9 7.4 %collective-permute-start.17 = (f32[64,768]{1,0:T(8,128)S(1)}, f32[64,768]{1,0:T(8,128)S(1)}, u32[]{:S(2)}, u32[]{:S(2)}) collective-permute-start(f32[64,768]{1,0:T(8,128)S(1)} %bitcast_add_fusion.12), channel_id=1, source_target_pairs={{0,4},{4,8},{8,12},{12,0},{1,5},{5,9},{9,13},{13,1},{2,6},{6,10},{... | collective-permute-start | bytes 589832 | tf_op jit(solution)/shard_map/ppermute | solution.py:65
  173.7 8.4 %collective-permute-start.35 = (f32[64,768]{1,0:T(8,128)S(1)}, f32[64,768]{1,0:T(8,128)S(1)}, u32[]{:S(2)}, u32[]{:S(2)}) collective-permute-start(f32[64,768]{1,0:T(8,128)S(1)} %bitcast_add_fusion.3), channel_id=1, source_target_pairs={{0,12},{4,0},{8,4},{12,8},{1,13},{5,1},{9,5},{13,9},{2,14},{6,2},{... | collective-permute-start | bytes 589832 | tf_op jit(solution)/shard_map/ppermute | solution.py:66
  174.4 8.3 %collective-permute-start.32 = (f32[64,768]{1,0:T(8,128)S(1)}, f32[64,768]{1,0:T(8,128)S(1)}, u32[]{:S(2)}, u32[]{:S(2)}) collective-permute-start(f32[64,768]{1,0:T(8,128)S(1)} %bitcast_add_fusion.6), channel_id=1, source_target_pairs={{0,4},{4,8},{8,12},{12,0},{1,5},{5,9},{9,13},{13,1},{2,6},{6,10},{... | collective-permute-start | bytes 589832 | tf_op jit(solution)/shard_map/ppermute | solution.py:65
  178.4 4.9 %collective-permute-start.21 = (f32[64,768]{1,0:T(8,128)S(1)}, f32[64,768]{1,0:T(8,128)S(1)}, u32[]{:S(2)}, u32[]{:S(2)}) collective-permute-start(f32[64,768]{1,0:T(8,128)S(1)} %fusion.24), channel_id=1, source_target_pairs={{0,2},{2,0},{1,3},{3,1},{4,6},{6,4},{5,7},{7,5},{8,10},{10,8},{9,1... | collective-permute-start | bytes 589832 | tf_op jit(solution)/shard_map/ppermute | solution.py:68
  182.8 6.1 %collective-permute-start.36 = (f32[64,768]{1,0:T(8,128)S(1)}, f32[64,768]{1,0:T(8,128)S(1)}, u32[]{:S(2)}, u32[]{:S(2)}) collective-permute-start(f32[64,768]{1,0:T(8,128)S(1)} %fusion.18), channel_id=1, source_target_pairs={{0,2},{2,0},{1,3},{3,1},{4,6},{6,4},{5,7},{7,5},{8,10},{10,8},{9,1... | collective-permute-start | bytes 589832 | tf_op jit(solution)/shard_map/ppermute | solution.py:68
  183.4 9.7 %collective-permute-start.22 = (f32[64,768]{1,0:T(8,128)S(1)}, f32[64,768]{1,0:T(8,128)S(1)}, u32[]{:S(2)}, u32[]{:S(2)}) collective-permute-start(f32[64,768]{1,0:T(8,128)S(1)} %fusion.28), channel_id=1, source_target_pairs={{0,2},{2,0},{1,3},{3,1},{4,6},{6,4},{5,7},{7,5},{8,10},{10,8},{9,1... | collective-permute-start | bytes 589832 | tf_op jit(solution)/shard_map/ppermute | solution.py:71
  189.0 8.3 %collective-permute-start.37 = (f32[64,768]{1,0:T(8,128)S(1)}, f32[64,768]{1,0:T(8,128)S(1)}, u32[]{:S(2)}, u32[]{:S(2)}) collective-permute-start(f32[64,768]{1,0:T(8,128)S(1)} %fusion.22), channel_id=1, source_target_pairs={{0,2},{2,0},{1,3},{3,1},{4,6},{6,4},{5,7},{7,5},{8,10},{10,8},{9,1... | collective-permute-start | bytes 589832 | tf_op jit(solution)/shard_map/ppermute | solution.py:71
  193.2 8.7 %collective-permute-start.23 = (f32[64,768]{1,0:T(8,128)S(1)}, f32[64,768]{1,0:T(8,128)S(1)}, u32[]{:S(2)}, u32[]{:S(2)}) collective-permute-start(f32[64,768]{1,0:T(8,128)S(1)} %get-tuple-element.288), channel_id=1, source_target_pairs={{0,4},{4,8},{8,12},{12,0},{1,5},{5,9},{9,13},{13,1},{2,6},{6,10},{... | collective-permute-start | bytes 589832 | tf_op jit(solution)/shard_map/ppermute | solution.py:76
  194.5 7.5 %collective-permute-start.24 = (f32[64,768]{1,0:T(8,128)S(1)}, f32[64,768]{1,0:T(8,128)S(1)}, u32[]{:S(2)}, u32[]{:S(2)}) collective-permute-start(f32[64,768]{1,0:T(8,128)S(1)} %get-tuple-element.287), channel_id=1, source_target_pairs={{0,12},{4,0},{8,4},{12,8},{1,13},{5,1},{9,5},{13,9},{2,14},{6,2},{... | collective-permute-start | bytes 589832 | tf_op jit(solution)/shard_map/ppermute | solution.py:77
  197.4 7.2 %collective-permute-start.38 = (f32[64,768]{1,0:T(8,128)S(1)}, f32[64,768]{1,0:T(8,128)S(1)}, u32[]{:S(2)}, u32[]{:S(2)}) collective-permute-start(f32[64,768]{1,0:T(8,128)S(1)} %get-tuple-element.290), channel_id=1, source_target_pairs={{0,4},{4,8},{8,12},{12,0},{1,5},{5,9},{9,13},{13,1},{2,6},{6,10},{... | collective-permute-start | bytes 589832 | tf_op jit(solution)/shard_map/ppermute | solution.py:76
  198.7 8.0 %collective-permute-start.39 = (f32[64,768]{1,0:T(8,128)S(1)}, f32[64,768]{1,0:T(8,128)S(1)}, u32[]{:S(2)}, u32[]{:S(2)}) collective-permute-start(f32[64,768]{1,0:T(8,128)S(1)} %get-tuple-element.289), channel_id=1, source_target_pairs={{0,12},{4,0},{8,4},{12,8},{1,13},{5,1},{9,5},{13,9},{2,14},{6,2},{... | collective-permute-start | bytes 589832 | tf_op jit(solution)/shard_map/ppermute | solution.py:77
  201.8 8.2 %collective-permute-start.25 = (f32[64,768]{1,0:T(8,128)S(1)}, f32[64,768]{1,0:T(8,128)S(1)}, u32[]{:S(2)}, u32[]{:S(2)}) collective-permute-start(f32[64,768]{1,0:T(8,128)S(1)} %collective-permute-done.23), channel_id=1, source_target_pairs={{0,4},{4,8},{8,12},{12,0},{1,5},{5,9},{9,13},{13,1},{2,6},{6,10},{... | collective-permute-start | bytes 589832 | tf_op jit(solution)/shard_map/ppermute | solution.py:76
  202.0 8.2 %collective-permute-start.26 = (f32[64,768]{1,0:T(8,128)S(1)}, f32[64,768]{1,0:T(8,128)S(1)}, u32[]{:S(2)}, u32[]{:S(2)}) collective-permute-start(f32[64,768]{1,0:T(8,128)S(1)} %collective-permute-done.24), channel_id=1, source_target_pairs={{0,12},{4,0},{8,4},{12,8},{1,13},{5,1},{9,5},{13,9},{2,14},{6,2},{... | collective-permute-start | bytes 589832 | tf_op jit(solution)/shard_map/ppermute | solution.py:77
  204.6 8.2 %collective-permute-start.40 = (f32[64,768]{1,0:T(8,128)S(1)}, f32[64,768]{1,0:T(8,128)S(1)}, u32[]{:S(2)}, u32[]{:S(2)}) collective-permute-start(f32[64,768]{1,0:T(8,128)S(1)} %collective-permute-done.38), channel_id=1, source_target_pairs={{0,4},{4,8},{8,12},{12,0},{1,5},{5,9},{9,13},{13,1},{2,6},{6,10},{... | collective-permute-start | bytes 589832 | tf_op jit(solution)/shard_map/ppermute | solution.py:76
  206.7 8.5 %collective-permute-start.41 = (f32[64,768]{1,0:T(8,128)S(1)}, f32[64,768]{1,0:T(8,128)S(1)}, u32[]{:S(2)}, u32[]{:S(2)}) collective-permute-start(f32[64,768]{1,0:T(8,128)S(1)} %collective-permute-done.39), channel_id=1, source_target_pairs={{0,12},{4,0},{8,4},{12,8},{1,13},{5,1},{9,5},{13,9},{2,14},{6,2},{... | collective-permute-start | bytes 589832 | tf_op jit(solution)/shard_map/ppermute | solution.py:77
  210.0 8.1 %collective-permute-start.27 = (f32[64,768]{1,0:T(8,128)S(1)}, f32[64,768]{1,0:T(8,128)S(1)}, u32[]{:S(2)}, u32[]{:S(2)}) collective-permute-start(f32[64,768]{1,0:T(8,128)S(1)} %collective-permute-done.25), channel_id=1, source_target_pairs={{0,4},{4,8},{8,12},{12,0},{1,5},{5,9},{9,13},{13,1},{2,6},{6,10},{... | collective-permute-start | bytes 589832 | tf_op jit(solution)/shard_map/ppermute | solution.py:76
  210.1 8.7 %collective-permute-start.28 = (f32[64,768]{1,0:T(8,128)S(1)}, f32[64,768]{1,0:T(8,128)S(1)}, u32[]{:S(2)}, u32[]{:S(2)}) collective-permute-start(f32[64,768]{1,0:T(8,128)S(1)} %collective-permute-done.26), channel_id=1, source_target_pairs={{0,12},{4,0},{8,4},{12,8},{1,13},{5,1},{9,5},{13,9},{2,14},{6,2},{... | collective-permute-start | bytes 589832 | tf_op jit(solution)/shard_map/ppermute | solution.py:77
  212.8 14.9 %collective-permute-start.42 = (f32[64,768]{1,0:T(8,128)S(1)}, f32[64,768]{1,0:T(8,128)S(1)}, u32[]{:S(2)}, u32[]{:S(2)}) collective-permute-start(f32[64,768]{1,0:T(8,128)S(1)} %collective-permute-done.40), channel_id=1, source_target_pairs={{0,4},{4,8},{8,12},{12,0},{1,5},{5,9},{9,13},{13,1},{2,6},{6,10},{... | collective-permute-start | bytes 589832 | tf_op jit(solution)/shard_map/ppermute | solution.py:76
  215.3 13.1 %collective-permute-start.43 = (f32[64,768]{1,0:T(8,128)S(1)}, f32[64,768]{1,0:T(8,128)S(1)}, u32[]{:S(2)}, u32[]{:S(2)}) collective-permute-start(f32[64,768]{1,0:T(8,128)S(1)} %collective-permute-done.41), channel_id=1, source_target_pairs={{0,12},{4,0},{8,4},{12,8},{1,13},{5,1},{9,5},{13,9},{2,14},{6,2},{... | collective-permute-start | bytes 589832 | tf_op jit(solution)/shard_map/ppermute | solution.py:77
  219.5 11.4 %collective-permute-start.44 = (f32[512,768]{1,0:T(8,128)S(1)}, f32[512,768]{1,0:T(8,128)}, u32[]{:S(2)}, u32[]{:S(2)}) collective-permute-start(f32[512,768]{1,0:T(8,128)S(1)} %bitcast.245), channel_id=1, source_target_pairs={{0,1},{1,0},{2,3},{3,2},{4,5},{5,4},{6,7},{7,6},{8,9},{9,8},{10,11... | collective-permute-start | bytes 4718600 | tf_op jit(solution)/shard_map/ppermute | solution.py:126
  229.0 4.1 %collective-permute-start.45 = (f32[512,768]{1,0:T(8,128)S(1)}, f32[512,768]{1,0:T(8,128)}, u32[]{:S(2)}, u32[]{:S(2)}) collective-permute-start(f32[512,768]{1,0:T(8,128)S(1)} %bitcast.243), channel_id=1, source_target_pairs={{0,1},{1,0},{2,3},{3,2},{4,5},{5,4},{6,7},{7,6},{8,9},{9,8},{10,11... | collective-permute-start | bytes 4718600 | tf_op jit(solution)/shard_map/ppermute | solution.py:126

commit v10 on v6

--- a/solution.py
+++ b/solution.py
@@ -117,13 +117,14 @@
     top, row_total = merge_peaks(cap_rounds, row_peak, row_sum)
     scale = jnp.exp(row_peak - top)
     rows = weights.shape[0]
-    chunk = rows // 2
+    first = 3 * rows // 8
+    bounds = ((0, first), (first, rows))
     parts = []
-    for k in range(2):
-        part = slice(k * chunk, (k + 1) * chunk)
+    for lo, hi in bounds:
+        part = slice(lo, hi)
         summed = lax.optimization_barrier(rescaled_affinity(weights[part], features))
         summed = summed * scale[part, None]
-        parts.append(reduce_rows(summed, row_total, k * chunk, sizes))
+        parts.append(reduce_rows(summed, row_total, lo, sizes))
     return jnp.concatenate(parts, axis=0)
 
 

time: 242 us -> 262 us (1.083)
  starting transfers between devices: 66.2 us -> 76.5 us
  waiting for transfers between devices: 55.9 us -> 65.1 us
    ppermute x6, waiting for transfers between devices: 0.02 us -> 12.1 us  [reduce_rows(): right = lax.ppermute(right, 'x', ring('x', x_size, 1))]
    ppermute x6, starting transfers between devices: 6.41 us -> 16.2 us  [reduce_rows(): lax.ppermute(left, 'x', ring('x', x_size, -1))]
    ppermute x2, waiting for transfers between devices: 4.69 us -> 0.01 us  [reduce_rows(): mine = pick(block, z) + lax.ppermute(pick(block, 1 - z), 'zl', swap)]
    ppermute x2, waiting for transfers between devices: 5.39 us -> 0.77 us  [reduce_rows(): other = lax.ppermute(mine, 'zl', swap)]
    ppermute x6, starting transfers between devices: 4.73 us -> 0.16 us  [reduce_rows(): right = lax.ppermute(right, 'x', ring('x', x_size, 1))]
    ppermute x6, starting transfers between devices: 11.7 us -> 16.2 us  [reduce_rows(): left = lax.ppermute(left, 'x', ring('x', x_size, -1))]
    ppermute x6, waiting for transfers between devices: 0.93 us -> 4.02 us  [reduce_rows(): lax.ppermute(right, 'x', ring('x', x_size, 1))]
    ppermute x2, starting transfers between devices: 8.35 us -> 11 us  [reduce_rows(): other = lax.ppermute(held, 'core', swap)]
  transfers between devices with their start and end apart: 46 -> 46, of which waited for: 21 -> 24; matrix products, arithmetic and copies ran while one was open for 32% -> 29% of each run, Pallas kernels for 0% -> 0%
where the time goes in v10:
time: 262 us; the launch traced here: 258 us
  starting transfers between devices  76.5 us (29%)
  matrix products  69.3 us (26%)
  waiting for transfers between devices  65.1 us (25%)
  other arithmetic  41 us (16%)
  local copies, waits for them, and re-layouts  5.26 us (2%)
    dot_general x2, matrix products, similar(): lax.dot_general(query_factor, target_factor, (((1,), (0,)), ((), ())), pr...  44.9 us
    dot_general x2, matrix products, rescaled_affinity(): lax.dot_general(weights, features, (((1,), (1,)), ((), ())), precision=la...  24.5 us
    ppermute x6, starting transfers between devices, reduce_rows(): left = lax.ppermute(left, 'x', ring('x', x_size, -1))  16.2 us
    ppermute x6, waiting for transfers between devices, reduce_rows(): lax.ppermute(left, 'x', ring('x', x_size, -1))  16.2 us
    ppermute x6, starting transfers between devices, reduce_rows(): lax.ppermute(left, 'x', ring('x', x_size, -1))  16.2 us
    ppermute x7, starting transfers between devices, merge_peaks(): other = lax.ppermute(pair, axis, [(j, j ^ dist) for j in range(size)])  15.1 us
    ppermute x3, waiting for transfers between devices, gather_features(): right = lax.ppermute(right, 'y', ring('y', y_size, 1))  12.2 us
    ppermute x6, waiting for transfers between devices, reduce_rows(): right = lax.ppermute(right, 'x', ring('x', x_size, 1))  12.1 us
  transfers between devices with their start and end apart: 46, of which 24 were waited for; matrix products, arithmetic and copies ran while one was open for 29% of the time, Pallas kernels for 0%

profile of v10, /device:TPU:1, one launch (start us, length us, event | category | flops | bytes accessed | tf_op | source)
XLA Modules:
  0.0 258.1 jit_solution(17001751264681766584)
XLA Ops:
  0.0 4.4 %collective-permute-start = (f32[1024,96]{0,1:T(8,128)}, f32[1024,96]{0,1:T(8,128)S(1)}, u32[]{:S(2)}, u32[]{:S(2)}) collective-permute-start(f32[1024,96]{0,1:T(8,128)} %param.46), channel_id=1, source_target_pairs={{0,64},{64,0},{1,65},{65,1},{2,66},{66,2},{3,67},{67,3},{4,68},{68... | collective-permute-start | bytes 1179656 | tf_op jit(solution)/shard_map/ppermute | solution.py:89
  4.4 1.4 and_reduce_fusion.10
  5.9 7.6 %collective-permute-done = f32[1024,96]{0,1:T(8,128)S(1)} collective-permute-done((f32[1024,96]{0,1:T(8,128)}, f32[1024,96]{0,1:T(8,128)S(1)}, u32[]{:S(2)}, u32[]{:S(2)}) %collective-permute-start) | collective-permute-done | bytes 393248 | tf_op jit(solution)/shard_map/ppermute | solution.py:89
  13.5 1.4 maximum_select_fusion.3
  14.8 1.0 slice_bitcast_fusion
  15.8 1.3 collective-permute-start.1
  17.1 1.4 collective-permute-start.2
  22.5 4.4 %collective-permute-done.1 = f32[1024,96]{0,1:T(8,128)} collective-permute-done((f32[1024,96]{0,1:T(8,128)}, f32[1024,96]{0,1:T(8,128)}, u32[]{:S(2)}, u32[]{:S(2)}) %collective-permute-start.1) | collective-permute-done | bytes 393248 | tf_op jit(solution)/shard_map/ppermute | solution.py:94
  26.9 2.7 %collective-permute-start.4 = (f32[1024,96]{0,1:T(8,128)}, f32[1024,96]{0,1:T(8,128)S(1)}, u32[]{:S(2)}, u32[]{:S(2)}) collective-permute-start(f32[1024,96]{0,1:T(8,128)} %collective-permute-done.2), channel_id=1, source_target_pairs={{0,48},{16,0},{32,16},{48,32},{1,49},{17,1},{33,17},{49,33},{2,50}... | collective-permute-start | bytes 1179656 | tf_op jit(solution)/shard_map/ppermute | solution.py:95
  29.6 2.0 fusion.14
  31.6 1.7 fusion.13
  33.3 3.5 %collective-permute-done.3 = f32[1024,96]{0,1:T(8,128)S(1)} collective-permute-done((f32[1024,96]{0,1:T(8,128)}, f32[1024,96]{0,1:T(8,128)S(1)}, u32[]{:S(2)}, u32[]{:S(2)}) %collective-permute-start.3) | collective-permute-done | bytes 393248 | tf_op jit(solution)/shard_map/ppermute | solution.py:94
  36.8 3.1 %collective-permute-start.6 = (f32[1024,96]{0,1:T(8,128)S(1)}, f32[1024,96]{0,1:T(8,128)S(1)}, u32[]{:S(2)}, u32[]{:S(2)}) collective-permute-start(f32[1024,96]{0,1:T(8,128)S(1)} %collective-permute-done.4), channel_id=1, source_target_pairs={{0,48},{16,0},{32,16},{48,32},{1,49},{17,1},{33,17},{49,33},{2,50}... | collective-permute-start | bytes 1179656 | tf_op jit(solution)/shard_map/ppermute | solution.py:95
  41.3 4.3 %collective-permute-done.5 = f32[1024,96]{0,1:T(8,128)S(1)} collective-permute-done((f32[1024,96]{0,1:T(8,128)S(1)}, f32[1024,96]{0,1:T(8,128)S(1)}, u32[]{:S(2)}, u32[]{:S(2)}) %collective-permute-start.5) | collective-permute-done | bytes 393248 | tf_op jit(solution)/shard_map/ppermute | solution.py:94
  46.3 0.8 fusion.9
  47.1 22.5 %fusion = (f32[1024]{0:T(1024)S(1)}, f32[1024,2048]{0,1:T(8,128)S(1)}) fusion(f32[768,1024]{1,0:T(8,128)S(1)} %bitcast.236, f32[2048,768]{1,0:T(8,128)S(1)} %copy-done.6), kind=kOutput, calls=%fused_computation.4 | convolution fusion | flops 19331547136 | bytes 17829888 | tf_op jit(solution)/shard_map/dot_general | solution.py:15
  69.6 1.4 exponential_reduce_fusion
  71.0 1.8 collective-permute-start.7
  72.8 2.3 collective-permute-done.7
  75.3 2.5 collective-permute-done.8
  77.8 2.5 collective-permute-start.9
  80.3 22.4 %bitcast_multiply_fusion.1 = f32[2048,1024]{1,0:T(8,128)S(1)} fusion(f32[768,1024]{1,0:T(8,128)S(1)} %bitcast.237, f32[2048,768]{1,0:T(8,128)S(1)} %bitcast.283), kind=kOutput, calls=%fused_computation.1 | convolution fusion | flops 19329449984 | bytes 17825792 | tf_op jit(solution)/shard_map/dot_general | solution.py:15
  103.4 4.1 %fusion.53 = (f32[2048]{0:T(1024)S(1)}, f32[2048,1024]{1,0:T(8,128)}) fusion(f32[2048]{0:T(1024)S(1)} %subtract_reduce_fusion, f32[2048,1024]{1,0:T(8,128)S(1)} %bitcast_multiply_fusion.1, f32[1024]{0:T(1024)S(1)} %bitcast.273), kind=kLoop, calls=%fused_computation.200 | loop fusion | flops 6289408 | bytes 16797696 | tf_op jit(solution)/shard_map/reduce_sum | solution.py:116
  107.5 6.3 %collective-permute-start.10 = (f32[2,2048]{1,0:T(2,128)S(1)}, f32[2,2048]{1,0:T(2,128)S(1)}, u32[]{:S(2)}, u32[]{:S(2)}) collective-permute-start(f32[2,2048]{1,0:T(2,128)S(1)} %pad_maximum_fusion.1), channel_id=1, source_target_pairs={{0,1},{1,0},{2,3},{3,2},{4,5},{5,4},{6,7},{7,6},{8,9},{9,8},{10,11... | collective-permute-start | bytes 49160 | tf_op jit(solution)/shard_map/ppermute | solution.py:38
  113.9 0.8 collective-permute-done.10
  114.9 2.5 collective-permute-done.11
  117.5 1.3 collective-permute-start.12
  120.2 3.0 %collective-permute-start.13 = (f32[2,2048]{1,0:T(2,128)S(1)}, f32[2,2048]{1,0:T(2,128)S(1)}, u32[]{:S(2)}, u32[]{:S(2)}) collective-permute-start(f32[2,2048]{1,0:T(2,128)S(1)} %pad_maximum_fusion.4), channel_id=1, source_target_pairs={{0,8},{4,12},{8,0},{12,4},{1,9},{5,13},{9,1},{13,5},{2,10},{6,14},... | collective-permute-start | bytes 49160 | tf_op jit(solution)/shard_map/ppermute | solution.py:38
  123.2 9.7 %fusion.3 = f32[768,768]{1,0:T(8,128)S(1)} fusion(f32[768,1024]{1,0:T(8,128)S(1)} %bitcast.238, f32[2048,1024]{1,0:T(8,128)} %get-tuple-element.276), kind=kOutput, calls=%fused_computation.10 | convolution fusion | flops 7247757312 | bytes 8650752 | tf_op jit(solution)/shard_map/dot_general | solution.py:26
  133.4 3.2 %collective-permute-start.14 = (f32[384,768]{1,0:T(8,128)S(1)}, f32[384,768]{1,0:T(8,128)S(1)}, u32[]{:S(2)}, u32[]{:S(2)}) collective-permute-start(f32[384,768]{1,0:T(8,128)S(1)} %dynamic-slice_bitcast_fusion.1), channel_id=1, source_target_pairs={{0,1},{1,0},{2,3},{3,2},{4,5},{5,4},{6,7},{7,6},{8,9},{9,8},{10,11... | collective-permute-start | bytes 3538952 | tf_op jit(solution)/shard_map/ppermute | solution.py:61
  136.6 14.7 %fusion.1 = f32[1280,768]{1,0:T(8,128)S(1)} fusion(f32[768,1024]{1,0:T(8,128)S(1)} %bitcast.239, f32[2048,1024]{1,0:T(8,128)} %get-tuple-element.276), kind=kOutput, calls=%fused_computation.7 | convolution fusion | flops 12079595520 | bytes 12320768 | tf_op jit(solution)/shard_map/dot_general | solution.py:26
  151.7 1.6 dynamic-slice_bitcast_fusion
  153.4 0.8 copy-done
  154.3 0.9 collective-permute-start.18
  155.3 0.8 and_reduce_fusion.2
  156.8 3.1 %collective-permute-done.18 = f32[48,768]{1,0:T(8,128)S(1)} collective-permute-done((f32[48,768]{1,0:T(8,128)S(1)}, f32[48,768]{1,0:T(8,128)S(1)}, u32[]{:S(2)}, u32[]{:S(2)}) %collective-permute-start.18) | collective-permute-done | bytes 147488 | tf_op jit(solution)/shard_map/ppermute | solution.py:66
  159.9 2.1 collective-permute-start.19
  162.7 1.9 collective-permute-done.19
  164.6 3.3 %collective-permute-start.20 = (f32[48,768]{1,0:T(8,128)S(1)}, f32[48,768]{1,0:T(8,128)S(1)}, u32[]{:S(2)}, u32[]{:S(2)}) collective-permute-start(f32[48,768]{1,0:T(8,128)S(1)} %bitcast_add_fusion.9), channel_id=1, source_target_pairs={{0,12},{4,0},{8,4},{12,8},{1,13},{5,1},{9,5},{13,9},{2,14},{6,2},{... | collective-permute-start | bytes 442376 | tf_op jit(solution)/shard_map/ppermute | solution.py:66
  168.0 2.0 collective-permute-done.20
  170.0 1.8 bitcast_add_fusion
  172.0 3.2 %collective-permute-start.34 = (f32[80,768]{1,0:T(8,128)S(1)}, f32[80,768]{1,0:T(8,128)S(1)}, u32[]{:S(2)}, u32[]{:S(2)}) collective-permute-start(f32[80,768]{1,0:T(8,128)S(1)} %dynamic-slice_bitcast_fusion.2), channel_id=1, source_target_pairs={{0,12},{4,0},{8,4},{12,8},{1,13},{5,1},{9,5},{13,9},{2,14},{6,2},{... | collective-permute-start | bytes 737288 | tf_op jit(solution)/shard_map/ppermute | solution.py:66
  175.5 2.8 %collective-permute-done.34 = f32[80,768]{1,0:T(8,128)S(1)} collective-permute-done((f32[80,768]{1,0:T(8,128)S(1)}, f32[80,768]{1,0:T(8,128)S(1)}, u32[]{:S(2)}, u32[]{:S(2)}) %collective-permute-start.34) | collective-permute-done | bytes 245792 | tf_op jit(solution)/shard_map/ppermute | solution.py:66
  178.4 3.4 %collective-permute-start.35 = (f32[80,768]{1,0:T(8,128)S(1)}, f32[80,768]{1,0:T(8,128)S(1)}, u32[]{:S(2)}, u32[]{:S(2)}) collective-permute-start(f32[80,768]{1,0:T(8,128)S(1)} %bitcast_add_fusion.4), channel_id=1, source_target_pairs={{0,12},{4,0},{8,4},{12,8},{1,13},{5,1},{9,5},{13,9},{2,14},{6,2},{... | collective-permute-start | bytes 737288 | tf_op jit(solution)/shard_map/ppermute | solution.py:66
  182.2 2.8 %collective-permute-done.35 = f32[80,768]{1,0:T(8,128)S(1)} collective-permute-done((f32[80,768]{1,0:T(8,128)S(1)}, f32[80,768]{1,0:T(8,128)S(1)}, u32[]{:S(2)}, u32[]{:S(2)}) %collective-permute-start.35) | collective-permute-done | bytes 245792 | tf_op jit(solution)/shard_map/ppermute | solution.py:66
  185.0 3.2 %collective-permute-start.36 = (f32[80,768]{1,0:T(8,128)S(1)}, f32[80,768]{1,0:T(8,128)S(1)}, u32[]{:S(2)}, u32[]{:S(2)}) collective-permute-start(f32[80,768]{1,0:T(8,128)S(1)} %bitcast_add_fusion.3), channel_id=1, source_target_pairs={{0,12},{4,0},{8,4},{12,8},{1,13},{5,1},{9,5},{13,9},{2,14},{6,2},{... | collective-permute-start | bytes 737288 | tf_op jit(solution)/shard_map/ppermute | solution.py:66
  188.3 3.7 %collective-permute-done.36 = f32[80,768]{1,0:T(8,128)S(1)} collective-permute-done((f32[80,768]{1,0:T(8,128)S(1)}, f32[80,768]{1,0:T(8,128)S(1)}, u32[]{:S(2)}, u32[]{:S(2)}) %collective-permute-start.36) | collective-permute-done | bytes 245792 | tf_op jit(solution)/shard_map/ppermute | solution.py:66
  192.1 3.5 %collective-permute-done.33 = f32[80,768]{1,0:T(8,128)S(1)} collective-permute-done((f32[80,768]{1,0:T(8,128)S(1)}, f32[80,768]{1,0:T(8,128)S(1)}, u32[]{:S(2)}, u32[]{:S(2)}) %collective-permute-start.33) | collective-permute-done | bytes 245792 | tf_op jit(solution)/shard_map/ppermute | solution.py:65
  195.9 2.7 %collective-permute-start.24 = (f32[48,768]{1,0:T(8,128)S(1)}, f32[48,768]{1,0:T(8,128)S(1)}, u32[]{:S(2)}, u32[]{:S(2)}) collective-permute-start(f32[48,768]{1,0:T(8,128)S(1)} %get-tuple-element.289), channel_id=1, source_target_pairs={{0,12},{4,0},{8,4},{12,8},{1,13},{5,1},{9,5},{13,9},{2,14},{6,2},{... | collective-permute-start | bytes 442376 | tf_op jit(solution)/shard_map/ppermute | solution.py:77
  200.1 2.8 %collective-permute-done.23 = f32[48,768]{1,0:T(8,128)S(1)} collective-permute-done((f32[48,768]{1,0:T(8,128)S(1)}, f32[48,768]{1,0:T(8,128)S(1)}, u32[]{:S(2)}, u32[]{:S(2)}) %collective-permute-start.23) | collective-permute-done | bytes 147488 | tf_op jit(solution)/shard_map/ppermute | solution.py:76
  202.9 2.7 %collective-permute-start.26 = (f32[48,768]{1,0:T(8,128)S(1)}, f32[48,768]{1,0:T(8,128)S(1)}, u32[]{:S(2)}, u32[]{:S(2)}) collective-permute-start(f32[48,768]{1,0:T(8,128)S(1)} %collective-permute-done.24), channel_id=1, source_target_pairs={{0,12},{4,0},{8,4},{12,8},{1,13},{5,1},{9,5},{13,9},{2,14},{6,2},{... | collective-permute-start | bytes 442376 | tf_op jit(solution)/shard_map/ppermute | solution.py:77
  207.2 1.3 collective-permute-done.25
  208.5 2.7 %collective-permute-start.28 = (f32[48,768]{1,0:T(8,128)S(1)}, f32[48,768]{1,0:T(8,128)S(1)}, u32[]{:S(2)}, u32[]{:S(2)}) collective-permute-start(f32[48,768]{1,0:T(8,128)S(1)} %collective-permute-done.26), channel_id=1, source_target_pairs={{0,12},{4,0},{8,4},{12,8},{1,13},{5,1},{9,5},{13,9},{2,14},{6,2},{... | collective-permute-start | bytes 442376 | tf_op jit(solution)/shard_map/ppermute | solution.py:77
  212.8 2.7 %collective-permute-start.40 = (f32[80,768]{1,0:T(8,128)S(1)}, f32[80,768]{1,0:T(8,128)S(1)}, u32[]{:S(2)}, u32[]{:S(2)}) collective-permute-start(f32[80,768]{1,0:T(8,128)S(1)} %get-tuple-element.287), channel_id=1, source_target_pairs={{0,12},{4,0},{8,4},{12,8},{1,13},{5,1},{9,5},{13,9},{2,14},{6,2},{... | collective-permute-start | bytes 737288 | tf_op jit(solution)/shard_map/ppermute | solution.py:77
  216.4 2.3 collective-permute-done.39
  219.4 2.7 %collective-permute-start.42 = (f32[80,768]{1,0:T(8,128)S(1)}, f32[80,768]{1,0:T(8,128)S(1)}, u32[]{:S(2)}, u32[]{:S(2)}) collective-permute-start(f32[80,768]{1,0:T(8,128)S(1)} %collective-permute-done.40), channel_id=1, source_target_pairs={{0,12},{4,0},{8,4},{12,8},{1,13},{5,1},{9,5},{13,9},{2,14},{6,2},{... | collective-permute-start | bytes 737288 | tf_op jit(solution)/shard_map/ppermute | solution.py:77
  222.8 3.6 %collective-permute-done.41 = f32[80,768]{1,0:T(8,128)S(1)} collective-permute-done((f32[80,768]{1,0:T(8,128)S(1)}, f32[80,768]{1,0:T(8,128)S(1)}, u32[]{:S(2)}, u32[]{:S(2)}) %collective-permute-start.41) | collective-permute-done | bytes 245792 | tf_op jit(solution)/shard_map/ppermute | solution.py:76
  227.2 2.7 %collective-permute-start.44 = (f32[80,768]{1,0:T(8,128)S(1)}, f32[80,768]{1,0:T(8,128)S(1)}, u32[]{:S(2)}, u32[]{:S(2)}) collective-permute-start(f32[80,768]{1,0:T(8,128)S(1)} %collective-permute-done.42), channel_id=1, source_target_pairs={{0,12},{4,0},{8,4},{12,8},{1,13},{5,1},{9,5},{13,9},{2,14},{6,2},{... | collective-permute-start | bytes 737288 | tf_op jit(solution)/shard_map/ppermute | solution.py:77
  230.6 2.0 collective-permute-done.43
  234.0 10.9 %collective-permute-start.45 = (f32[640,768]{1,0:T(8,128)S(1)}, f32[640,768]{1,0:T(8,128)}, u32[]{:S(2)}, u32[]{:S(2)}) collective-permute-start(f32[640,768]{1,0:T(8,128)S(1)} %bitcast.243), channel_id=1, source_target_pairs={{0,1},{1,0},{2,3},{3,2},{4,5},{5,4},{6,7},{7,6},{8,9},{9,8},{10,11... | collective-permute-start | bytes 5898248 | tf_op jit(solution)/shard_map/ppermute | solution.py:81
  247.0 3.3 %collective-permute-done.29 = f32[384,768]{1,0:T(8,128)} collective-permute-done((f32[384,768]{1,0:T(8,128)S(1)}, f32[384,768]{1,0:T(8,128)}, u32[]{:S(2)}, u32[]{:S(2)}) %collective-permute-start.29) | collective-permute-done | bytes 1179680 | tf_op jit(solution)/shard_map/ppermute | solution.py:81
  250.3 1.8 maximum_select_fusion.1
  252.2 2.5 maximum_select_fusion
  254.7 3.1 %pad_maximum_fusion = f32[2048,768]{1,0:T(8,128)} fusion(f32[1280,768]{1,0:T(8,128)S(1)} %bitcast.242, f32[768,768]{1,0:T(8,128)S(1)} %bitcast.247), kind=kLoop, calls=%fused_computation.6 | loop fusion | flops 1572864 | bytes 12582912 | tf_op jit(solution)/shard_map/concatenate | solution.py:128
  (141 shorter events, 24.0 us)
Async XLA Ops:
  0.0 19.4 %copy-start.4 = (s32[4]{0:T(128)S(1)}, s32[4]{0:T(128)}, u32[]{:S(2)}) copy-start(s32[4]{0:T(128)} %constant.699.clone.1) | copy-start | bytes 52
  0.0 18.6 %copy-start.5 = (s32[4]{0:T(128)S(1)}, s32[4]{0:T(128)}, u32[]{:S(2)}) copy-start(s32[4]{0:T(128)} %constant.693.clone.1) | copy-start | bytes 52
  0.0 13.5 %collective-permute-start = (f32[1024,96]{0,1:T(8,128)}, f32[1024,96]{0,1:T(8,128)S(1)}, u32[]{:S(2)}, u32[]{:S(2)}) collective-permute-start(f32[1024,96]{0,1:T(8,128)} %param.46), channel_id=1, source_target_pairs={{0,64},{64,0},{1,65},{65,1},{2,66},{66,2},{3,67},{67,3},{4,68},{68... | collective-permute-start | bytes 1179656 | tf_op jit(solution)/shard_map/ppermute | solution.py:89
  13.5 7.4 %copy-start.2 = (f32[1024,96]{0,1:T(8,128)}, f32[1024,96]{0,1:T(8,128)S(1)}, u32[]{:S(2)}) copy-start(f32[1024,96]{0,1:T(8,128)S(1)} %collective-permute-done) | copy-start | bytes 1179652
  13.5 7.8 %copy-start.1 = (f32[1024,96]{0,1:T(8,128)S(1)}, f32[1024,96]{0,1:T(8,128)}, u32[]{:S(2)}) copy-start(f32[1024,96]{0,1:T(8,128)} %param.46) | copy-start | bytes 1179652
  15.8 11.0 %collective-permute-start.1 = (f32[1024,96]{0,1:T(8,128)}, f32[1024,96]{0,1:T(8,128)}, u32[]{:S(2)}, u32[]{:S(2)}) collective-permute-start(f32[1024,96]{0,1:T(8,128)} %get-tuple-element.286), channel_id=1, source_target_pairs={{0,16},{16,32},{32,48},{48,0},{1,17},{17,33},{33,49},{49,1},{2,18}... | collective-permute-start | bytes 1179656 | tf_op jit(solution)/shard_map/ppermute | solution.py:94
  17.1 9.7 %collective-permute-start.2 = (f32[1024,96]{0,1:T(8,128)}, f32[1024,96]{0,1:T(8,128)}, u32[]{:S(2)}, u32[]{:S(2)}) collective-permute-start(f32[1024,96]{0,1:T(8,128)} %get-tuple-element.285), channel_id=1, source_target_pairs={{0,48},{16,0},{32,16},{48,32},{1,49},{17,1},{33,17},{49,33},{2,50}... | collective-permute-start | bytes 1179656 | tf_op jit(solution)/shard_map/ppermute | solution.py:95
  20.9 1.0 copy-start.3
  26.9 9.9 %collective-permute-start.3 = (f32[1024,96]{0,1:T(8,128)}, f32[1024,96]{0,1:T(8,128)S(1)}, u32[]{:S(2)}, u32[]{:S(2)}) collective-permute-start(f32[1024,96]{0,1:T(8,128)} %collective-permute-done.1), channel_id=1, source_target_pairs={{0,16},{16,32},{32,48},{48,0},{1,17},{17,33},{33,49},{49,1},{2,18}... | collective-permute-start | bytes 1179656 | tf_op jit(solution)/shard_map/ppermute | solution.py:94
  26.9 9.9 %collective-permute-start.4 = (f32[1024,96]{0,1:T(8,128)}, f32[1024,96]{0,1:T(8,128)S(1)}, u32[]{:S(2)}, u32[]{:S(2)}) collective-permute-start(f32[1024,96]{0,1:T(8,128)} %collective-permute-done.2), channel_id=1, source_target_pairs={{0,48},{16,0},{32,16},{48,32},{1,49},{17,1},{33,17},{49,33},{2,50}... | collective-permute-start | bytes 1179656 | tf_op jit(solution)/shard_map/ppermute | solution.py:95
  29.6 17.6 %copy-start.6 = (f32[2048,768]{1,0:T(8,128)S(1)}, f32[2048,768]{1,0:T(8,128)}, u32[]{:S(2)}) copy-start(f32[2048,768]{1,0:T(8,128)} %param.47) | copy-start | bytes 18874372
  36.8 8.8 %collective-permute-start.5 = (f32[1024,96]{0,1:T(8,128)S(1)}, f32[1024,96]{0,1:T(8,128)S(1)}, u32[]{:S(2)}, u32[]{:S(2)}) collective-permute-start(f32[1024,96]{0,1:T(8,128)S(1)} %collective-permute-done.3), channel_id=1, source_target_pairs={{0,16},{16,32},{32,48},{48,0},{1,17},{17,33},{33,49},{49,1},{2,18}... | collective-permute-start | bytes 1179656 | tf_op jit(solution)/shard_map/ppermute | solution.py:94
  36.8 9.4 %collective-permute-start.6 = (f32[1024,96]{0,1:T(8,128)S(1)}, f32[1024,96]{0,1:T(8,128)S(1)}, u32[]{:S(2)}, u32[]{:S(2)}) collective-permute-start(f32[1024,96]{0,1:T(8,128)S(1)} %collective-permute-done.4), channel_id=1, source_target_pairs={{0,48},{16,0},{32,16},{48,32},{1,49},{17,1},{33,17},{49,33},{2,50}... | collective-permute-start | bytes 1179656 | tf_op jit(solution)/shard_map/ppermute | solution.py:95
  46.3 34.0 %slice-start = ((s8[6291456]{0:T(1024)(128)(4,1)}), s8[4194304]{0:T(1024)(128)(4,1)S(1)}, s32[]{:S(2)}) async-start(s8[6291456]{0:T(1024)(128)(4,1)} %bitcast.282), calls=%async_computation | async-start | bytes 8388608
  47.1 33.2 %slice-start.1 = ((s8[6291456]{0:T(1024)(128)(4,1)}), s8[2097152]{0:T(1024)(128)(4,1)S(1)}, s32[]{:S(2)}) async-start(s8[6291456]{0:T(1024)(128)(4,1)} %bitcast.282), calls=%async_computation.1 | async-start | bytes 4194304
  71.0 4.1 %collective-permute-start.7 = (f32[2,1024]{1,0:T(2,128)S(1)}, f32[2,1024]{1,0:T(2,128)S(1)}, u32[]{:S(2)}, u32[]{:S(2)}) collective-permute-start(f32[2,1024]{1,0:T(2,128)S(1)} %pad_maximum_fusion.5), channel_id=1, source_target_pairs={{0,64},{64,0},{1,65},{65,1},{2,66},{66,2},{3,67},{67,3},{4,68},{68... | collective-permute-start | bytes 24584 | tf_op jit(solution)/shard_map/ppermute | solution.py:38
  75.2 2.6 %collective-permute-start.8 = (f32[2,1024]{1,0:T(2,128)S(1)}, f32[2,1024]{1,0:T(2,128)S(1)}, u32[]{:S(2)}, u32[]{:S(2)}) collective-permute-start(f32[2,1024]{1,0:T(2,128)S(1)} %pad_maximum_fusion.6), channel_id=1, source_target_pairs={{0,16},{16,0},{32,48},{48,32},{1,17},{17,1},{33,49},{49,33},{2,18}... | collective-permute-start | bytes 24584 | tf_op jit(solution)/shard_map/ppermute | solution.py:38
  77.8 24.9 %collective-permute-start.9 = (f32[2,1024]{1,0:T(2,128)S(1)}, f32[2,1024]{1,0:T(2,128)S(1)}, u32[]{:S(2)}, u32[]{:S(2)}) collective-permute-start(f32[2,1024]{1,0:T(2,128)S(1)} %pad_maximum_fusion.7), channel_id=1, source_target_pairs={{0,32},{16,48},{32,0},{48,16},{1,33},{17,49},{33,1},{49,17},{2,34}... | collective-permute-start | bytes 24584 | tf_op jit(solution)/shard_map/ppermute | solution.py:38
  107.5 7.1 %collective-permute-start.10 = (f32[2,2048]{1,0:T(2,128)S(1)}, f32[2,2048]{1,0:T(2,128)S(1)}, u32[]{:S(2)}, u32[]{:S(2)}) collective-permute-start(f32[2,2048]{1,0:T(2,128)S(1)} %pad_maximum_fusion.1), channel_id=1, source_target_pairs={{0,1},{1,0},{2,3},{3,2},{4,5},{5,4},{6,7},{7,6},{8,9},{9,8},{10,11... | collective-permute-start | bytes 49160 | tf_op jit(solution)/shard_map/ppermute | solution.py:38
  114.8 2.7 %collective-permute-start.11 = (f32[2,2048]{1,0:T(2,128)S(1)}, f32[2,2048]{1,0:T(2,128)S(1)}, u32[]{:S(2)}, u32[]{:S(2)}) collective-permute-start(f32[2,2048]{1,0:T(2,128)S(1)} %pad_maximum_fusion.2), channel_id=1, source_target_pairs={{0,2},{2,0},{1,3},{3,1},{4,6},{6,4},{5,7},{7,5},{8,10},{10,8},{9,1... | collective-permute-start | bytes 49160 | tf_op jit(solution)/shard_map/ppermute | solution.py:38
  117.5 2.7 %collective-permute-start.12 = (f32[2,2048]{1,0:T(2,128)S(1)}, f32[2,2048]{1,0:T(2,128)S(1)}, u32[]{:S(2)}, u32[]{:S(2)}) collective-permute-start(f32[2,2048]{1,0:T(2,128)S(1)} %pad_maximum_fusion.3), channel_id=1, source_target_pairs={{0,4},{4,0},{8,12},{12,8},{1,5},{5,1},{9,13},{13,9},{2,6},{6,2},{1... | collective-permute-start | bytes 49160 | tf_op jit(solution)/shard_map/ppermute | solution.py:38
  120.2 12.7 %collective-permute-start.13 = (f32[2,2048]{1,0:T(2,128)S(1)}, f32[2,2048]{1,0:T(2,128)S(1)}, u32[]{:S(2)}, u32[]{:S(2)}) collective-permute-start(f32[2,2048]{1,0:T(2,128)S(1)} %pad_maximum_fusion.4), channel_id=1, source_target_pairs={{0,8},{4,12},{8,0},{12,4},{1,9},{5,13},{9,1},{13,5},{2,10},{6,14},... | collective-permute-start | bytes 49160 | tf_op jit(solution)/shard_map/ppermute | solution.py:38
  133.4 19.9 %collective-permute-start.14 = (f32[384,768]{1,0:T(8,128)S(1)}, f32[384,768]{1,0:T(8,128)S(1)}, u32[]{:S(2)}, u32[]{:S(2)}) collective-permute-start(f32[384,768]{1,0:T(8,128)S(1)} %dynamic-slice_bitcast_fusion.1), channel_id=1, source_target_pairs={{0,1},{1,0},{2,3},{3,2},{4,5},{5,4},{6,7},{7,6},{8,9},{9,8},{10,11... | collective-permute-start | bytes 3538952 | tf_op jit(solution)/shard_map/ppermute | solution.py:61
  151.7 2.6 copy-start
  153.2 16.8 %collective-permute-start.30 = (f32[640,768]{1,0:T(8,128)}, f32[640,768]{1,0:T(8,128)S(1)}, u32[]{:S(2)}, u32[]{:S(2)}) collective-permute-start(f32[640,768]{1,0:T(8,128)} %dynamic-slice_bitcast_fusion), channel_id=1, source_target_pairs={{0,1},{1,0},{2,3},{3,2},{4,5},{5,4},{6,7},{7,6},{8,9},{9,8},{10,11... | collective-permute-start | bytes 5898248 | tf_op jit(solution)/shard_map/ppermute | solution.py:61
  154.3 5.5 %collective-permute-start.18 = (f32[48,768]{1,0:T(8,128)S(1)}, f32[48,768]{1,0:T(8,128)S(1)}, u32[]{:S(2)}, u32[]{:S(2)}) collective-permute-start(f32[48,768]{1,0:T(8,128)S(1)} %dynamic-slice_bitcast_fusion.4), channel_id=1, source_target_pairs={{0,12},{4,0},{8,4},{12,8},{1,13},{5,1},{9,5},{13,9},{2,14},{6,2},{... | collective-permute-start | bytes 442376 | tf_op jit(solution)/shard_map/ppermute | solution.py:66
  156.1 6.4 %collective-permute-start.15 = (f32[48,768]{1,0:T(8,128)S(1)}, f32[48,768]{1,0:T(8,128)S(1)}, u32[]{:S(2)}, u32[]{:S(2)}) collective-permute-start(f32[48,768]{1,0:T(8,128)S(1)} %dynamic-slice_bitcast_fusion.5), channel_id=1, source_target_pairs={{0,4},{4,8},{8,12},{12,0},{1,5},{5,9},{9,13},{13,1},{2,6},{6,10},{... | collective-permute-start | bytes 442376 | tf_op jit(solution)/shard_map/ppermute | solution.py:65
  159.9 4.6 %collective-permute-start.19 = (f32[48,768]{1,0:T(8,128)S(1)}, f32[48,768]{1,0:T(8,128)S(1)}, u32[]{:S(2)}, u32[]{:S(2)}) collective-permute-start(f32[48,768]{1,0:T(8,128)S(1)} %bitcast_add_fusion.10), channel_id=1, source_target_pairs={{0,12},{4,0},{8,4},{12,8},{1,13},{5,1},{9,5},{13,9},{2,14},{6,2},{... | collective-permute-start | bytes 442376 | tf_op jit(solution)/shard_map/ppermute | solution.py:66
  162.6 5.3 %collective-permute-start.16 = (f32[48,768]{1,0:T(8,128)S(1)}, f32[48,768]{1,0:T(8,128)S(1)}, u32[]{:S(2)}, u32[]{:S(2)}) collective-permute-start(f32[48,768]{1,0:T(8,128)S(1)} %bitcast_add_fusion.13), channel_id=1, source_target_pairs={{0,4},{4,8},{8,12},{12,0},{1,5},{5,9},{9,13},{13,1},{2,6},{6,10},{... | collective-permute-start | bytes 442376 | tf_op jit(solution)/shard_map/ppermute | solution.py:65
  164.6 5.4 %collective-permute-start.20 = (f32[48,768]{1,0:T(8,128)S(1)}, f32[48,768]{1,0:T(8,128)S(1)}, u32[]{:S(2)}, u32[]{:S(2)}) collective-permute-start(f32[48,768]{1,0:T(8,128)S(1)} %bitcast_add_fusion.9), channel_id=1, source_target_pairs={{0,12},{4,0},{8,4},{12,8},{1,13},{5,1},{9,5},{13,9},{2,14},{6,2},{... | collective-permute-start | bytes 442376 | tf_op jit(solution)/shard_map/ppermute | solution.py:66
  167.9 7.3 %collective-permute-start.17 = (f32[48,768]{1,0:T(8,128)S(1)}, f32[48,768]{1,0:T(8,128)S(1)}, u32[]{:S(2)}, u32[]{:S(2)}) collective-permute-start(f32[48,768]{1,0:T(8,128)S(1)} %bitcast_add_fusion.12), channel_id=1, source_target_pairs={{0,4},{4,8},{8,12},{12,0},{1,5},{5,9},{9,13},{13,1},{2,6},{6,10},{... | collective-permute-start | bytes 442376 | tf_op jit(solution)/shard_map/ppermute | solution.py:65
  172.0 6.3 %collective-permute-start.34 = (f32[80,768]{1,0:T(8,128)S(1)}, f32[80,768]{1,0:T(8,128)S(1)}, u32[]{:S(2)}, u32[]{:S(2)}) collective-permute-start(f32[80,768]{1,0:T(8,128)S(1)} %dynamic-slice_bitcast_fusion.2), channel_id=1, source_target_pairs={{0,12},{4,0},{8,4},{12,8},{1,13},{5,1},{9,5},{13,9},{2,14},{6,2},{... | collective-permute-start | bytes 737288 | tf_op jit(solution)/shard_map/ppermute | solution.py:66
  175.2 6.6 %collective-permute-start.31 = (f32[80,768]{1,0:T(8,128)S(1)}, f32[80,768]{1,0:T(8,128)S(1)}, u32[]{:S(2)}, u32[]{:S(2)}) collective-permute-start(f32[80,768]{1,0:T(8,128)S(1)} %dynamic-slice_bitcast_fusion.3), channel_id=1, source_target_pairs={{0,4},{4,8},{8,12},{12,0},{1,5},{5,9},{9,13},{13,1},{2,6},{6,10},{... | collective-permute-start | bytes 737288 | tf_op jit(solution)/shard_map/ppermute | solution.py:65
  175.4 6.5 %collective-permute-start.21 = (f32[48,768]{1,0:T(8,128)S(1)}, f32[48,768]{1,0:T(8,128)S(1)}, u32[]{:S(2)}, u32[]{:S(2)}) collective-permute-start(f32[48,768]{1,0:T(8,128)S(1)} %fusion.32), channel_id=1, source_target_pairs={{0,2},{2,0},{1,3},{3,1},{4,6},{6,4},{5,7},{7,5},{8,10},{10,8},{9,1... | collective-permute-start | bytes 442376 | tf_op jit(solution)/shard_map/ppermute | solution.py:68
  178.4 6.6 %collective-permute-start.35 = (f32[80,768]{1,0:T(8,128)S(1)}, f32[80,768]{1,0:T(8,128)S(1)}, u32[]{:S(2)}, u32[]{:S(2)}) collective-permute-start(f32[80,768]{1,0:T(8,128)S(1)} %bitcast_add_fusion.4), channel_id=1, source_target_pairs={{0,12},{4,0},{8,4},{12,8},{1,13},{5,1},{9,5},{13,9},{2,14},{6,2},{... | collective-permute-start | bytes 737288 | tf_op jit(solution)/shard_map/ppermute | solution.py:66
  181.8 6.3 %collective-permute-start.32 = (f32[80,768]{1,0:T(8,128)S(1)}, f32[80,768]{1,0:T(8,128)S(1)}, u32[]{:S(2)}, u32[]{:S(2)}) collective-permute-start(f32[80,768]{1,0:T(8,128)S(1)} %bitcast_add_fusion.7), channel_id=1, source_target_pairs={{0,4},{4,8},{8,12},{12,0},{1,5},{5,9},{9,13},{13,1},{2,6},{6,10},{... | collective-permute-start | bytes 737288 | tf_op jit(solution)/shard_map/ppermute | solution.py:65
  182.0 6.3 %collective-permute-start.22 = (f32[48,768]{1,0:T(8,128)S(1)}, f32[48,768]{1,0:T(8,128)S(1)}, u32[]{:S(2)}, u32[]{:S(2)}) collective-permute-start(f32[48,768]{1,0:T(8,128)S(1)} %fusion.36), channel_id=1, source_target_pairs={{0,2},{2,0},{1,3},{3,1},{4,6},{6,4},{5,7},{7,5},{8,10},{10,8},{9,1... | collective-permute-start | bytes 442376 | tf_op jit(solution)/shard_map/ppermute | solution.py:71
  185.0 7.0 %collective-permute-start.36 = (f32[80,768]{1,0:T(8,128)S(1)}, f32[80,768]{1,0:T(8,128)S(1)}, u32[]{:S(2)}, u32[]{:S(2)}) collective-permute-start(f32[80,768]{1,0:T(8,128)S(1)} %bitcast_add_fusion.3), channel_id=1, source_target_pairs={{0,12},{4,0},{8,4},{12,8},{1,13},{5,1},{9,5},{13,9},{2,14},{6,2},{... | collective-permute-start | bytes 737288 | tf_op jit(solution)/shard_map/ppermute | solution.py:66
  188.2 7.3 %collective-permute-start.33 = (f32[80,768]{1,0:T(8,128)S(1)}, f32[80,768]{1,0:T(8,128)S(1)}, u32[]{:S(2)}, u32[]{:S(2)}) collective-permute-start(f32[80,768]{1,0:T(8,128)S(1)} %bitcast_add_fusion.6), channel_id=1, source_target_pairs={{0,4},{4,8},{8,12},{12,0},{1,5},{5,9},{9,13},{13,1},{2,6},{6,10},{... | collective-permute-start | bytes 737288 | tf_op jit(solution)/shard_map/ppermute | solution.py:65
  195.6 10.0 %collective-permute-start.37 = (f32[80,768]{1,0:T(8,128)S(1)}, f32[80,768]{1,0:T(8,128)S(1)}, u32[]{:S(2)}, u32[]{:S(2)}) collective-permute-start(f32[80,768]{1,0:T(8,128)S(1)} %fusion.18), channel_id=1, source_target_pairs={{0,2},{2,0},{1,3},{3,1},{4,6},{6,4},{5,7},{7,5},{8,10},{10,8},{9,1... | collective-permute-start | bytes 737288 | tf_op jit(solution)/shard_map/ppermute | solution.py:68
  195.8 7.1 %collective-permute-start.23 = (f32[48,768]{1,0:T(8,128)S(1)}, f32[48,768]{1,0:T(8,128)S(1)}, u32[]{:S(2)}, u32[]{:S(2)}) collective-permute-start(f32[48,768]{1,0:T(8,128)S(1)} %get-tuple-element.290), channel_id=1, source_target_pairs={{0,4},{4,8},{8,12},{12,0},{1,5},{5,9},{9,13},{13,1},{2,6},{6,10},{... | collective-permute-start | bytes 442376 | tf_op jit(solution)/shard_map/ppermute | solution.py:76
  195.9 7.0 %collective-permute-start.24 = (f32[48,768]{1,0:T(8,128)S(1)}, f32[48,768]{1,0:T(8,128)S(1)}, u32[]{:S(2)}, u32[]{:S(2)}) collective-permute-start(f32[48,768]{1,0:T(8,128)S(1)} %get-tuple-element.289), channel_id=1, source_target_pairs={{0,12},{4,0},{8,4},{12,8},{1,13},{5,1},{9,5},{13,9},{2,14},{6,2},{... | collective-permute-start | bytes 442376 | tf_op jit(solution)/shard_map/ppermute | solution.py:77
  202.9 5.6 %collective-permute-start.25 = (f32[48,768]{1,0:T(8,128)S(1)}, f32[48,768]{1,0:T(8,128)S(1)}, u32[]{:S(2)}, u32[]{:S(2)}) collective-permute-start(f32[48,768]{1,0:T(8,128)S(1)} %collective-permute-done.23), channel_id=1, source_target_pairs={{0,4},{4,8},{8,12},{12,0},{1,5},{5,9},{9,13},{13,1},{2,6},{6,10},{... | collective-permute-start | bytes 442376 | tf_op jit(solution)/shard_map/ppermute | solution.py:76
  202.9 5.6 %collective-permute-start.26 = (f32[48,768]{1,0:T(8,128)S(1)}, f32[48,768]{1,0:T(8,128)S(1)}, u32[]{:S(2)}, u32[]{:S(2)}) collective-permute-start(f32[48,768]{1,0:T(8,128)S(1)} %collective-permute-done.24), channel_id=1, source_target_pairs={{0,12},{4,0},{8,4},{12,8},{1,13},{5,1},{9,5},{13,9},{2,14},{6,2},{... | collective-permute-start | bytes 442376 | tf_op jit(solution)/shard_map/ppermute | solution.py:77
  205.7 6.2 %collective-permute-start.38 = (f32[80,768]{1,0:T(8,128)S(1)}, f32[80,768]{1,0:T(8,128)S(1)}, u32[]{:S(2)}, u32[]{:S(2)}) collective-permute-start(f32[80,768]{1,0:T(8,128)S(1)} %fusion.22), channel_id=1, source_target_pairs={{0,2},{2,0},{1,3},{3,1},{4,6},{6,4},{5,7},{7,5},{8,10},{10,8},{9,1... | collective-permute-start | bytes 737288 | tf_op jit(solution)/shard_map/ppermute | solution.py:71
  208.5 37.2 %collective-permute-start.27 = (f32[48,768]{1,0:T(8,128)S(1)}, f32[48,768]{1,0:T(8,128)S(1)}, u32[]{:S(2)}, u32[]{:S(2)}) collective-permute-start(f32[48,768]{1,0:T(8,128)S(1)} %collective-permute-done.25), channel_id=1, source_target_pairs={{0,4},{4,8},{8,12},{12,0},{1,5},{5,9},{9,13},{13,1},{2,6},{6,10},{... | collective-permute-start | bytes 442376 | tf_op jit(solution)/shard_map/ppermute | solution.py:76
  208.5 37.8 %collective-permute-start.28 = (f32[48,768]{1,0:T(8,128)S(1)}, f32[48,768]{1,0:T(8,128)S(1)}, u32[]{:S(2)}, u32[]{:S(2)}) collective-permute-start(f32[48,768]{1,0:T(8,128)S(1)} %collective-permute-done.26), channel_id=1, source_target_pairs={{0,12},{4,0},{8,4},{12,8},{1,13},{5,1},{9,5},{13,9},{2,14},{6,2},{... | collective-permute-start | bytes 442376 | tf_op jit(solution)/shard_map/ppermute | solution.py:77
  212.0 6.7 %collective-permute-start.39 = (f32[80,768]{1,0:T(8,128)S(1)}, f32[80,768]{1,0:T(8,128)S(1)}, u32[]{:S(2)}, u32[]{:S(2)}) collective-permute-start(f32[80,768]{1,0:T(8,128)S(1)} %get-tuple-element.288), channel_id=1, source_target_pairs={{0,4},{4,8},{8,12},{12,0},{1,5},{5,9},{9,13},{13,1},{2,6},{6,10},{... | collective-permute-start | bytes 737288 | tf_op jit(solution)/shard_map/ppermute | solution.py:76
  212.8 6.6 %collective-permute-start.40 = (f32[80,768]{1,0:T(8,128)S(1)}, f32[80,768]{1,0:T(8,128)S(1)}, u32[]{:S(2)}, u32[]{:S(2)}) collective-permute-start(f32[80,768]{1,0:T(8,128)S(1)} %get-tuple-element.287), channel_id=1, source_target_pairs={{0,12},{4,0},{8,4},{12,8},{1,13},{5,1},{9,5},{13,9},{2,14},{6,2},{... | collective-permute-start | bytes 737288 | tf_op jit(solution)/shard_map/ppermute | solution.py:77
  218.7 7.8 %collective-permute-start.41 = (f32[80,768]{1,0:T(8,128)S(1)}, f32[80,768]{1,0:T(8,128)S(1)}, u32[]{:S(2)}, u32[]{:S(2)}) collective-permute-start(f32[80,768]{1,0:T(8,128)S(1)} %collective-permute-done.39), channel_id=1, source_target_pairs={{0,4},{4,8},{8,12},{12,0},{1,5},{5,9},{9,13},{13,1},{2,6},{6,10},{... | collective-permute-start | bytes 737288 | tf_op jit(solution)/shard_map/ppermute | solution.py:76
  219.4 7.8 %collective-permute-start.42 = (f32[80,768]{1,0:T(8,128)S(1)}, f32[80,768]{1,0:T(8,128)S(1)}, u32[]{:S(2)}, u32[]{:S(2)}) collective-permute-start(f32[80,768]{1,0:T(8,128)S(1)} %collective-permute-done.40), channel_id=1, source_target_pairs={{0,12},{4,0},{8,4},{12,8},{1,13},{5,1},{9,5},{13,9},{2,14},{6,2},{... | collective-permute-start | bytes 737288 | tf_op jit(solution)/shard_map/ppermute | solution.py:77
  226.4 6.3 %collective-permute-start.43 = (f32[80,768]{1,0:T(8,128)S(1)}, f32[80,768]{1,0:T(8,128)S(1)}, u32[]{:S(2)}, u32[]{:S(2)}) collective-permute-start(f32[80,768]{1,0:T(8,128)S(1)} %collective-permute-done.41), channel_id=1, source_target_pairs={{0,4},{4,8},{8,12},{12,0},{1,5},{5,9},{9,13},{13,1},{2,6},{6,10},{... | collective-permute-start | bytes 737288 | tf_op jit(solution)/shard_map/ppermute | solution.py:76
  227.2 6.1 %collective-permute-start.44 = (f32[80,768]{1,0:T(8,128)S(1)}, f32[80,768]{1,0:T(8,128)S(1)}, u32[]{:S(2)}, u32[]{:S(2)}) collective-permute-start(f32[80,768]{1,0:T(8,128)S(1)} %collective-permute-done.42), channel_id=1, source_target_pairs={{0,12},{4,0},{8,4},{12,8},{1,13},{5,1},{9,5},{13,9},{2,14},{6,2},{... | collective-permute-start | bytes 737288 | tf_op jit(solution)/shard_map/ppermute | solution.py:77
  234.0 18.2 %collective-permute-start.45 = (f32[640,768]{1,0:T(8,128)S(1)}, f32[640,768]{1,0:T(8,128)}, u32[]{:S(2)}, u32[]{:S(2)}) collective-permute-start(f32[640,768]{1,0:T(8,128)S(1)} %bitcast.243), channel_id=1, source_target_pairs={{0,1},{1,0},{2,3},{3,2},{4,5},{5,4},{6,7},{7,6},{8,9},{9,8},{10,11... | collective-permute-start | bytes 5898248 | tf_op jit(solution)/shard_map/ppermute | solution.py:81
  246.9 3.4 %collective-permute-start.29 = (f32[384,768]{1,0:T(8,128)S(1)}, f32[384,768]{1,0:T(8,128)}, u32[]{:S(2)}, u32[]{:S(2)}) collective-permute-start(f32[384,768]{1,0:T(8,128)S(1)} %bitcast.248), channel_id=1, source_target_pairs={{0,1},{1,0},{2,3},{3,2},{4,5},{5,4},{6,7},{7,6},{8,9},{9,8},{10,11... | collective-permute-start | bytes 3538952 | tf_op jit(solution)/shard_map/ppermute | solution.py:81

commit v11 on v9

--- a/solution.py
+++ b/solution.py
@@ -87,12 +87,12 @@
     other = lax.ppermute(captions, "zh", [(0, 1), (1, 0)])
     pair = jnp.where(h == 0, jnp.stack([captions, other]), jnp.stack([other, captions]))
     got = jnp.zeros((y_size, 2, rows, width), captions.dtype).at[y].set(pair)
-    right, left = pair[0], pair[1]
+    right, left = captions, other
     for s in range(y_size - 1):
         right = lax.ppermute(right, "y", ring("y", y_size, 1))
         left = lax.ppermute(left, "y", ring("y", y_size, -1))
-        got = got.at[(y - s - 1) % y_size, 0].set(right)
-        got = got.at[(y + s + 1) % y_size, 1].set(left)
+        got = lax.dynamic_update_slice(got, right[None, None], ((y - s - 1) % y_size, h, 0, 0))
+        got = lax.dynamic_update_slice(got, left[None, None], ((y + s + 1) % y_size, 1 - h, 0, 0))
     return got.transpose(1, 0, 3, 2).reshape(2 * y_size * width, rows)
 
 

time: 242 us -> 239 us (0.988)
  other arithmetic: 40.4 us -> 31.3 us
  starting transfers between devices: 66.2 us -> 70.4 us
    ppermute x3, waiting for transfers between devices: 0.01 us -> 12.7 us  [gather_features(): left = lax.ppermute(left, 'y', ring('y', y_size, -1))]
    ppermute x3, waiting for transfers between devices: 12.1 us -> 0.01 us  [gather_features(): right = lax.ppermute(right, 'y', ring('y', y_size, 1))]
    scatter x6 -> x0, other arithmetic: 6.63 us -> none  [the longest x3 3.41 us: gather_features(): got = got.at[(y - s - 1) % y_size, 0].set(right)]
    ppermute x3, starting transfers between devices: 7.23 us -> 9.89 us  [gather_features(): left = lax.ppermute(left, 'y', ring('y', y_size, -1))]
    another operation x7 -> x4, other arithmetic: 5.97 us -> 3.74 us
  transfers between devices with their start and end apart: 46 -> 46, of which waited for: 22 -> 22; matrix products, arithmetic and copies ran while one was open for 31% -> 29% of each run, Pallas kernels for 0% -> 0%
where the time goes in v11:
time: 239 us; the launch traced here: 235 us
  starting transfers between devices  70.4 us (29%)
  matrix products  67.5 us (28%)
  waiting for transfers between devices  58.6 us (25%)
  other arithmetic  31.3 us (13%)
  local copies, waits for them, and re-layouts  6.62 us (3%)
    dot_general x2, matrix products, similar(): lax.dot_general(query_factor, target_factor, (((1,), (0,)), ((), ())), pr...  44.7 us
    dot_general x2, matrix products, rescaled_affinity(): lax.dot_general(weights, features, (((1,), (1,)), ((), ())), precision=la...  22.9 us
    ppermute x7, starting transfers between devices, merge_peaks(): other = lax.ppermute(pair, axis, [(j, j ^ dist) for j in range(size)])  16.2 us
    ppermute x6, waiting for transfers between devices, reduce_rows(): lax.ppermute(left, 'x', ring('x', x_size, -1))  15.1 us
    ppermute x3, waiting for transfers between devices, gather_features(): left = lax.ppermute(left, 'y', ring('y', y_size, -1))  12.7 us
    ppermute x6, starting transfers between devices, reduce_rows(): left = lax.ppermute(left, 'x', ring('x', x_size, -1))  10.7 us
    ppermute x3, starting transfers between devices, gather_features(): left = lax.ppermute(left, 'y', ring('y', y_size, -1))  9.89 us
    ppermute x2, starting transfers between devices, local(): lax.ppermute(part, 'core', [(0, 1), (1, 0)])  8.64 us
  transfers between devices with their start and end apart: 46, of which 22 were waited for; matrix products, arithmetic and copies ran while one was open for 29% of the time, Pallas kernels for 0%

profile of v11, /device:TPU:1, one launch (start us, length us, event | category | flops | bytes accessed | tf_op | source)
XLA Modules:
  0.0 235.4 jit_solution(1494060936293987696)
XLA Ops:
  0.0 4.4 %collective-permute-start = (f32[1024,96]{0,1:T(8,128)}, f32[1024,96]{0,1:T(8,128)}, u32[]{:S(2)}, u32[]{:S(2)}) collective-permute-start(f32[1024,96]{0,1:T(8,128)} %param.34), channel_id=1, source_target_pairs={{0,64},{64,0},{1,65},{65,1},{2,66},{66,2},{3,67},{67,3},{4,68},{68... | collective-permute-start | bytes 1179656 | tf_op jit(solution)/shard_map/ppermute | solution.py:87
  4.4 1.3 collective-permute-start.1
  5.7 7.9 %collective-permute-done = f32[1024,96]{0,1:T(8,128)} collective-permute-done((f32[1024,96]{0,1:T(8,128)}, f32[1024,96]{0,1:T(8,128)}, u32[]{:S(2)}, u32[]{:S(2)}) %collective-permute-start) | collective-permute-done | bytes 393248 | tf_op jit(solution)/shard_map/ppermute | solution.py:87
  13.6 2.7 %collective-permute-start.2 = (f32[1024,96]{0,1:T(8,128)}, f32[1024,96]{0,1:T(8,128)}, u32[]{:S(2)}, u32[]{:S(2)}) collective-permute-start(f32[1024,96]{0,1:T(8,128)} %collective-permute-done), channel_id=1, source_target_pairs={{0,48},{16,0},{32,16},{48,32},{1,49},{17,1},{33,17},{49,33},{2,50}... | collective-permute-start | bytes 1179656 | tf_op jit(solution)/shard_map/ppermute | solution.py:93
  16.3 1.4 and_reduce_fusion.7
  18.7 2.0 fusion.7
  20.8 3.0 %collective-permute-done.2 = f32[1024,96]{0,1:T(8,128)} collective-permute-done((f32[1024,96]{0,1:T(8,128)}, f32[1024,96]{0,1:T(8,128)}, u32[]{:S(2)}, u32[]{:S(2)}) %collective-permute-start.2) | collective-permute-done | bytes 393248 | tf_op jit(solution)/shard_map/ppermute | solution.py:93
  23.8 3.4 %collective-permute-start.4 = (f32[1024,96]{0,1:T(8,128)}, f32[1024,96]{0,1:T(8,128)S(1)}, u32[]{:S(2)}, u32[]{:S(2)}) collective-permute-start(f32[1024,96]{0,1:T(8,128)} %collective-permute-done.2), channel_id=1, source_target_pairs={{0,48},{16,0},{32,16},{48,32},{1,49},{17,1},{33,17},{49,33},{2,50}... | collective-permute-start | bytes 1179656 | tf_op jit(solution)/shard_map/ppermute | solution.py:93
  27.2 1.1 bitcast_dynamic-update-slice_fusion.2
  28.3 1.0 bitcast_dynamic-update-slice_fusion.1
  29.3 4.5 %collective-permute-done.4 = f32[1024,96]{0,1:T(8,128)S(1)} collective-permute-done((f32[1024,96]{0,1:T(8,128)}, f32[1024,96]{0,1:T(8,128)S(1)}, u32[]{:S(2)}, u32[]{:S(2)}) %collective-permute-start.4) | collective-permute-done | bytes 393248 | tf_op jit(solution)/shard_map/ppermute | solution.py:93
  33.8 3.7 %collective-permute-start.6 = (f32[1024,96]{0,1:T(8,128)S(1)}, f32[1024,96]{0,1:T(8,128)S(1)}, u32[]{:S(2)}, u32[]{:S(2)}) collective-permute-start(f32[1024,96]{0,1:T(8,128)S(1)} %collective-permute-done.4), channel_id=1, source_target_pairs={{0,48},{16,0},{32,16},{48,32},{1,49},{17,1},{33,17},{49,33},{2,50}... | collective-permute-start | bytes 1179656 | tf_op jit(solution)/shard_map/ppermute | solution.py:93
  37.6 5.2 %collective-permute-done.6 = f32[1024,96]{0,1:T(8,128)S(1)} collective-permute-done((f32[1024,96]{0,1:T(8,128)S(1)}, f32[1024,96]{0,1:T(8,128)S(1)}, u32[]{:S(2)}, u32[]{:S(2)}) %collective-permute-start.6) | collective-permute-done | bytes 393248 | tf_op jit(solution)/shard_map/ppermute | solution.py:93
  43.0 22.4 %fusion = (f32[1024]{0:T(1024)S(1)}, f32[1024,2048]{0,1:T(8,128)S(1)}) fusion(f32[768,1024]{1,0:T(8,128)S(1)} %bitcast.225, f32[2048,768]{1,0:T(8,128)S(1)} %copy-done.4), kind=kOutput, calls=%fused_computation.4 | convolution fusion | flops 19331547136 | bytes 17829888 | tf_op jit(solution)/shard_map/dot_general | solution.py:15
  65.4 1.4 exponential_reduce_fusion
  66.9 1.8 collective-permute-start.7
  68.6 2.3 collective-permute-done.7
  71.1 2.5 %collective-permute-done.8 = f32[2,1024]{1,0:T(2,128)S(1)} collective-permute-done((f32[2,1024]{1,0:T(2,128)S(1)}, f32[2,1024]{1,0:T(2,128)S(1)}, u32[]{:S(2)}, u32[]{:S(2)}) %collective-permute-start.8) | collective-permute-done | bytes 8224 | tf_op jit(solution)/shard_map/ppermute | solution.py:38
  73.6 3.9 %collective-permute-start.9 = (f32[2,1024]{1,0:T(2,128)S(1)}, f32[2,1024]{1,0:T(2,128)S(1)}, u32[]{:S(2)}, u32[]{:S(2)}) collective-permute-start(f32[2,1024]{1,0:T(2,128)S(1)} %pad_maximum_fusion.6), channel_id=1, source_target_pairs={{0,32},{16,48},{32,0},{48,16},{1,33},{17,49},{33,1},{49,17},{2,34}... | collective-permute-start | bytes 24584 | tf_op jit(solution)/shard_map/ppermute | solution.py:38
  77.5 22.2 %bitcast_multiply_fusion.1 = f32[2048,1024]{1,0:T(8,128)S(1)} fusion(f32[768,1024]{1,0:T(8,128)S(1)} %bitcast.226, f32[2048,768]{1,0:T(8,128)S(1)} %bitcast.257), kind=kOutput, calls=%fused_computation.1 | convolution fusion | flops 19329449984 | bytes 17825792 | tf_op jit(solution)/shard_map/dot_general | solution.py:15
  100.4 4.2 %fusion.48 = (f32[2048]{0:T(1024)S(1)}, f32[2048,1024]{1,0:T(8,128)}) fusion(f32[2048]{0:T(1024)S(1)} %subtract_reduce_fusion, f32[2048,1024]{1,0:T(8,128)S(1)} %bitcast_multiply_fusion.1, f32[1024]{0:T(1024)S(1)} %bitcast.247), kind=kLoop, calls=%fused_computation.168 | loop fusion | flops 6289408 | bytes 16797696 | tf_op jit(solution)/shard_map/reduce_sum | solution.py:114
  104.6 6.1 %collective-permute-start.10 = (f32[2,2048]{1,0:T(2,128)S(1)}, f32[2,2048]{1,0:T(2,128)S(1)}, u32[]{:S(2)}, u32[]{:S(2)}) collective-permute-start(f32[2,2048]{1,0:T(2,128)S(1)} %pad_maximum_fusion), channel_id=1, source_target_pairs={{0,1},{1,0},{2,3},{3,2},{4,5},{5,4},{6,7},{7,6},{8,9},{9,8},{10,11... | collective-permute-start | bytes 49160 | tf_op jit(solution)/shard_map/ppermute | solution.py:38
  110.7 0.8 collective-permute-done.10
  111.7 2.5 %collective-permute-done.11 = f32[2,2048]{1,0:T(2,128)S(1)} collective-permute-done((f32[2,2048]{1,0:T(2,128)S(1)}, f32[2,2048]{1,0:T(2,128)S(1)}, u32[]{:S(2)}, u32[]{:S(2)}) %collective-permute-start.11) | collective-permute-done | bytes 16416 | tf_op jit(solution)/shard_map/ppermute | solution.py:38
  114.3 1.3 collective-permute-start.12
  115.6 12.5 %fusion.3 = f32[1024,768]{1,0:T(8,128)S(1)} fusion(f32[768,1024]{1,0:T(8,128)S(1)} %bitcast.227, f32[2048,1024]{1,0:T(8,128)} %get-tuple-element.198), kind=kOutput, calls=%fused_computation.9 | convolution fusion | flops 9663676416 | bytes 10485760 | tf_op jit(solution)/shard_map/dot_general | solution.py:26
  128.2 2.9 %collective-permute-start.13 = (f32[2,2048]{1,0:T(2,128)S(1)}, f32[2,2048]{1,0:T(2,128)S(1)}, u32[]{:S(2)}, u32[]{:S(2)}) collective-permute-start(f32[2,2048]{1,0:T(2,128)S(1)} %pad_maximum_fusion.3), channel_id=1, source_target_pairs={{0,8},{4,12},{8,0},{12,4},{1,9},{5,13},{9,1},{13,5},{2,10},{6,14},... | collective-permute-start | bytes 49160 | tf_op jit(solution)/shard_map/ppermute | solution.py:38
  131.1 10.4 %fusion.1 = f32[1024,768]{1,0:T(8,128)S(1)} fusion(f32[768,1024]{1,0:T(8,128)S(1)} %bitcast.228, f32[2048,1024]{1,0:T(8,128)S(1)} %copy-done.1), kind=kOutput, calls=%fused_computation.7 | convolution fusion | flops 9663676416 | bytes 10485760 | tf_op jit(solution)/shard_map/dot_general | solution.py:26
  142.1 1.4 dynamic-slice_bitcast_fusion.1
  143.5 2.1 collective-permute-start.14
  145.6 1.3 dynamic-slice_bitcast_fusion
  149.6 2.1 bitcast_add_fusion.1
  152.1 1.3 collective-permute-start.15
  153.5 1.6 bitcast_add_fusion
  155.2 1.5 collective-permute-start.33
  156.8 1.2 collective-permute-done.18
  158.1 1.5 collective-permute-start.19
  159.7 2.6 %collective-permute-done.33 = f32[64,768]{1,0:T(8,128)S(1)} collective-permute-done((f32[64,768]{1,0:T(8,128)S(1)}, f32[64,768]{1,0:T(8,128)S(1)}, u32[]{:S(2)}, u32[]{:S(2)}) %collective-permute-start.33) | collective-permute-done | bytes 196640 | tf_op jit(solution)/shard_map/ppermute | solution.py:66
  162.3 1.2 collective-permute-start.34
  163.9 2.6 %collective-permute-done.19 = f32[64,768]{1,0:T(8,128)S(1)} collective-permute-done((f32[64,768]{1,0:T(8,128)S(1)}, f32[64,768]{1,0:T(8,128)S(1)}, u32[]{:S(2)}, u32[]{:S(2)}) %collective-permute-start.19) | collective-permute-done | bytes 196640 | tf_op jit(solution)/shard_map/ppermute | solution.py:66
  166.5 1.3 collective-permute-start.20
  168.2 2.5 %collective-permute-done.34 = f32[64,768]{1,0:T(8,128)S(1)} collective-permute-done((f32[64,768]{1,0:T(8,128)S(1)}, f32[64,768]{1,0:T(8,128)S(1)}, u32[]{:S(2)}, u32[]{:S(2)}) %collective-permute-start.34) | collective-permute-done | bytes 196640 | tf_op jit(solution)/shard_map/ppermute | solution.py:66
  171.4 1.0 collective-permute-start.32
  172.4 2.6 %collective-permute-done.20 = f32[64,768]{1,0:T(8,128)S(1)} collective-permute-done((f32[64,768]{1,0:T(8,128)S(1)}, f32[64,768]{1,0:T(8,128)S(1)}, u32[]{:S(2)}, u32[]{:S(2)}) %collective-permute-start.20) | collective-permute-done | bytes 196640 | tf_op jit(solution)/shard_map/ppermute | solution.py:66
  175.5 3.6 %collective-permute-done.35 = f32[64,768]{1,0:T(8,128)S(1)} collective-permute-done((f32[64,768]{1,0:T(8,128)S(1)}, f32[64,768]{1,0:T(8,128)S(1)}, u32[]{:S(2)}, u32[]{:S(2)}) %collective-permute-start.35) | collective-permute-done | bytes 196640 | tf_op jit(solution)/shard_map/ppermute | solution.py:66
  180.3 1.2 collective-permute-start.22
  181.5 4.4 %collective-permute-done.36 = f32[64,768]{1,0:T(8,128)S(1)} collective-permute-done((f32[64,768]{1,0:T(8,128)S(1)}, f32[64,768]{1,0:T(8,128)S(1)}, u32[]{:S(2)}, u32[]{:S(2)}) %collective-permute-start.36) | collective-permute-done | bytes 196640 | tf_op jit(solution)/shard_map/ppermute | solution.py:68
  186.1 4.0 %collective-permute-done.22 = f32[64,768]{1,0:T(8,128)S(1)} collective-permute-done((f32[64,768]{1,0:T(8,128)S(1)}, f32[64,768]{1,0:T(8,128)S(1)}, u32[]{:S(2)}, u32[]{:S(2)}) %collective-permute-start.22) | collective-permute-done | bytes 196640 | tf_op jit(solution)/shard_map/ppermute | solution.py:71
  190.1 1.4 collective-permute-start.23
  191.6 1.3 collective-permute-start.24
  192.9 1.4 collective-permute-done.37
  194.4 1.4 collective-permute-start.38
  195.8 1.3 collective-permute-start.39
  198.8 2.5 %collective-permute-start.26 = (f32[64,768]{1,0:T(8,128)S(1)}, f32[64,768]{1,0:T(8,128)S(1)}, u32[]{:S(2)}, u32[]{:S(2)}) collective-permute-start(f32[64,768]{1,0:T(8,128)S(1)} %collective-permute-done.24), channel_id=1, source_target_pairs={{0,12},{4,0},{8,4},{12,8},{1,13},{5,1},{9,5},{13,9},{2,14},{6,2},{... | collective-permute-start | bytes 589832 | tf_op jit(solution)/shard_map/ppermute | solution.py:77
  201.3 1.2 collective-permute-start.40
  204.0 1.5 collective-permute-start.41
  206.9 2.7 %collective-permute-start.28 = (f32[64,768]{1,0:T(8,128)S(1)}, f32[64,768]{1,0:T(8,128)S(1)}, u32[]{:S(2)}, u32[]{:S(2)}) collective-permute-start(f32[64,768]{1,0:T(8,128)S(1)} %collective-permute-done.26), channel_id=1, source_target_pairs={{0,12},{4,0},{8,4},{12,8},{1,13},{5,1},{9,5},{13,9},{2,14},{6,2},{... | collective-permute-start | bytes 589832 | tf_op jit(solution)/shard_map/ppermute | solution.py:77
  209.5 1.4 collective-permute-start.42
  212.3 1.3 collective-permute-start.43
  216.3 8.5 %collective-permute-start.44 = (f32[512,768]{1,0:T(8,128)S(1)}, f32[512,768]{1,0:T(8,128)}, u32[]{:S(2)}, u32[]{:S(2)}) collective-permute-start(f32[512,768]{1,0:T(8,128)S(1)} %bitcast.221), channel_id=1, source_target_pairs={{0,1},{1,0},{2,3},{3,2},{4,5},{5,4},{6,7},{7,6},{8,9},{9,8},{10,11... | collective-permute-start | bytes 4718600 | tf_op jit(solution)/shard_map/ppermute | solution.py:126
  226.4 1.6 collective-permute-done.44
  228.0 2.2 collective-permute-done.45
  230.2 2.1 maximum_bitcast_fusion.1
  232.3 2.9 %maximum_select_fusion = f32[2,2,512,768]{3,2,1,0:T(8,128)} fusion(f32[2,1,512,768]{3,2,1,0:T(8,128)S(1)} %maximum_bitcast_fusion.1, f32[2,1,512,768]{3,2,1,0:T(8,128)S(1)} %maximum_bitcast_fusion, pred[]{:T(512)S(6)} %eq.45), kind=kLoop, calls=%fused_computation.6 | loop fusion | flops 4718592 | bytes 12582913 | tf_op jit(solution)/shard_map/jit(_where)/select_n | solution.py:128
  (129 shorter events, 19.7 us)
Async XLA Ops:
  0.0 13.6 %collective-permute-start = (f32[1024,96]{0,1:T(8,128)}, f32[1024,96]{0,1:T(8,128)}, u32[]{:S(2)}, u32[]{:S(2)}) collective-permute-start(f32[1024,96]{0,1:T(8,128)} %param.34), channel_id=1, source_target_pairs={{0,64},{64,0},{1,65},{65,1},{2,66},{66,2},{3,67},{67,3},{4,68},{68... | collective-permute-start | bytes 1179656 | tf_op jit(solution)/shard_map/ppermute | solution.py:87
  4.4 11.9 %collective-permute-start.1 = (f32[1024,96]{0,1:T(8,128)}, f32[1024,96]{0,1:T(8,128)S(1)}, u32[]{:S(2)}, u32[]{:S(2)}) collective-permute-start(f32[1024,96]{0,1:T(8,128)} %param.34), channel_id=1, source_target_pairs={{0,16},{16,32},{32,48},{48,0},{1,17},{17,33},{33,49},{49,1},{2,18}... | collective-permute-start | bytes 1179656 | tf_op jit(solution)/shard_map/ppermute | solution.py:92
  13.6 10.2 %collective-permute-start.2 = (f32[1024,96]{0,1:T(8,128)}, f32[1024,96]{0,1:T(8,128)}, u32[]{:S(2)}, u32[]{:S(2)}) collective-permute-start(f32[1024,96]{0,1:T(8,128)} %collective-permute-done), channel_id=1, source_target_pairs={{0,48},{16,0},{32,16},{48,32},{1,49},{17,1},{33,17},{49,33},{2,50}... | collective-permute-start | bytes 1179656 | tf_op jit(solution)/shard_map/ppermute | solution.py:93
  16.3 10.9 %collective-permute-start.3 = (f32[1024,96]{0,1:T(8,128)S(1)}, f32[1024,96]{0,1:T(8,128)}, u32[]{:S(2)}, u32[]{:S(2)}) collective-permute-start(f32[1024,96]{0,1:T(8,128)S(1)} %collective-permute-done.1), channel_id=1, source_target_pairs={{0,16},{16,32},{32,48},{48,0},{1,17},{17,33},{33,49},{49,1},{2,18}... | collective-permute-start | bytes 1179656 | tf_op jit(solution)/shard_map/ppermute | solution.py:92
  17.7 1.0 copy-start.2
  18.7 24.2 %copy-start.4 = (f32[2048,768]{1,0:T(8,128)S(1)}, f32[2048,768]{1,0:T(8,128)}, u32[]{:S(2)}) copy-start(f32[2048,768]{1,0:T(8,128)} %param.35) | copy-start | bytes 18874372
  23.8 10.0 %collective-permute-start.4 = (f32[1024,96]{0,1:T(8,128)}, f32[1024,96]{0,1:T(8,128)S(1)}, u32[]{:S(2)}, u32[]{:S(2)}) collective-permute-start(f32[1024,96]{0,1:T(8,128)} %collective-permute-done.2), channel_id=1, source_target_pairs={{0,48},{16,0},{32,16},{48,32},{1,49},{17,1},{33,17},{49,33},{2,50}... | collective-permute-start | bytes 1179656 | tf_op jit(solution)/shard_map/ppermute | solution.py:93
  27.2 10.4 %collective-permute-start.5 = (f32[1024,96]{0,1:T(8,128)}, f32[1024,96]{0,1:T(8,128)S(1)}, u32[]{:S(2)}, u32[]{:S(2)}) collective-permute-start(f32[1024,96]{0,1:T(8,128)} %collective-permute-done.3), channel_id=1, source_target_pairs={{0,16},{16,32},{32,48},{48,0},{1,17},{17,33},{33,49},{49,1},{2,18}... | collective-permute-start | bytes 1179656 | tf_op jit(solution)/shard_map/ppermute | solution.py:92
  33.8 9.1 %collective-permute-start.6 = (f32[1024,96]{0,1:T(8,128)S(1)}, f32[1024,96]{0,1:T(8,128)S(1)}, u32[]{:S(2)}, u32[]{:S(2)}) collective-permute-start(f32[1024,96]{0,1:T(8,128)S(1)} %collective-permute-done.4), channel_id=1, source_target_pairs={{0,48},{16,0},{32,16},{48,32},{1,49},{17,1},{33,17},{49,33},{2,50}... | collective-permute-start | bytes 1179656 | tf_op jit(solution)/shard_map/ppermute | solution.py:93
  42.9 34.6 %slice-start = ((s8[6291456]{0:T(1024)(128)(4,1)}), s8[4194304]{0:T(1024)(128)(4,1)S(1)}, s32[]{:S(2)}) async-start(s8[6291456]{0:T(1024)(128)(4,1)} %bitcast.256), calls=%async_computation | async-start | bytes 8388608
  42.9 34.6 %slice-start.1 = ((s8[6291456]{0:T(1024)(128)(4,1)}), s8[2097152]{0:T(1024)(128)(4,1)S(1)}, s32[]{:S(2)}) async-start(s8[6291456]{0:T(1024)(128)(4,1)} %bitcast.256), calls=%async_computation.1 | async-start | bytes 4194304
  66.9 4.1 %collective-permute-start.7 = (f32[2,1024]{1,0:T(2,128)S(1)}, f32[2,1024]{1,0:T(2,128)S(1)}, u32[]{:S(2)}, u32[]{:S(2)}) collective-permute-start(f32[2,1024]{1,0:T(2,128)S(1)} %pad_maximum_fusion.4), channel_id=1, source_target_pairs={{0,64},{64,0},{1,65},{65,1},{2,66},{66,2},{3,67},{67,3},{4,68},{68... | collective-permute-start | bytes 24584 | tf_op jit(solution)/shard_map/ppermute | solution.py:38
  71.0 2.6 %collective-permute-start.8 = (f32[2,1024]{1,0:T(2,128)S(1)}, f32[2,1024]{1,0:T(2,128)S(1)}, u32[]{:S(2)}, u32[]{:S(2)}) collective-permute-start(f32[2,1024]{1,0:T(2,128)S(1)} %pad_maximum_fusion.5), channel_id=1, source_target_pairs={{0,16},{16,0},{32,48},{48,32},{1,17},{17,1},{33,49},{49,33},{2,18}... | collective-permute-start | bytes 24584 | tf_op jit(solution)/shard_map/ppermute | solution.py:38
  73.6 26.1 %collective-permute-start.9 = (f32[2,1024]{1,0:T(2,128)S(1)}, f32[2,1024]{1,0:T(2,128)S(1)}, u32[]{:S(2)}, u32[]{:S(2)}) collective-permute-start(f32[2,1024]{1,0:T(2,128)S(1)} %pad_maximum_fusion.6), channel_id=1, source_target_pairs={{0,32},{16,48},{32,0},{48,16},{1,33},{17,49},{33,1},{49,17},{2,34}... | collective-permute-start | bytes 24584 | tf_op jit(solution)/shard_map/ppermute | solution.py:38
  104.6 6.9 %collective-permute-start.10 = (f32[2,2048]{1,0:T(2,128)S(1)}, f32[2,2048]{1,0:T(2,128)S(1)}, u32[]{:S(2)}, u32[]{:S(2)}) collective-permute-start(f32[2,2048]{1,0:T(2,128)S(1)} %pad_maximum_fusion), channel_id=1, source_target_pairs={{0,1},{1,0},{2,3},{3,2},{4,5},{5,4},{6,7},{7,6},{8,9},{9,8},{10,11... | collective-permute-start | bytes 49160 | tf_op jit(solution)/shard_map/ppermute | solution.py:38
  111.6 2.7 %collective-permute-start.11 = (f32[2,2048]{1,0:T(2,128)S(1)}, f32[2,2048]{1,0:T(2,128)S(1)}, u32[]{:S(2)}, u32[]{:S(2)}) collective-permute-start(f32[2,2048]{1,0:T(2,128)S(1)} %pad_maximum_fusion.1), channel_id=1, source_target_pairs={{0,2},{2,0},{1,3},{3,1},{4,6},{6,4},{5,7},{7,5},{8,10},{10,8},{9,1... | collective-permute-start | bytes 49160 | tf_op jit(solution)/shard_map/ppermute | solution.py:38
  114.3 13.8 %collective-permute-start.12 = (f32[2,2048]{1,0:T(2,128)S(1)}, f32[2,2048]{1,0:T(2,128)S(1)}, u32[]{:S(2)}, u32[]{:S(2)}) collective-permute-start(f32[2,2048]{1,0:T(2,128)S(1)} %pad_maximum_fusion.2), channel_id=1, source_target_pairs={{0,4},{4,0},{8,12},{12,8},{1,5},{5,1},{9,13},{13,9},{2,6},{6,2},{1... | collective-permute-start | bytes 49160 | tf_op jit(solution)/shard_map/ppermute | solution.py:38
  115.6 15.5 %copy-start.1 = (f32[2048,1024]{1,0:T(8,128)S(1)}, f32[2048,1024]{1,0:T(8,128)}, u32[]{:S(2)}) copy-start(f32[2048,1024]{1,0:T(8,128)} %get-tuple-element.198) | copy-start | bytes 25165828
  128.2 13.3 %collective-permute-start.13 = (f32[2,2048]{1,0:T(2,128)S(1)}, f32[2,2048]{1,0:T(2,128)S(1)}, u32[]{:S(2)}, u32[]{:S(2)}) collective-permute-start(f32[2,2048]{1,0:T(2,128)S(1)} %pad_maximum_fusion.3), channel_id=1, source_target_pairs={{0,8},{4,12},{8,0},{12,4},{1,9},{5,13},{9,1},{13,5},{2,10},{6,14},... | collective-permute-start | bytes 49160 | tf_op jit(solution)/shard_map/ppermute | solution.py:38
  142.1 4.8 %copy-start = (f32[1024,768]{1,0:T(8,128)}, f32[1024,768]{1,0:T(8,128)S(1)}, u32[]{:S(2)}) copy-start(f32[1024,768]{1,0:T(8,128)S(1)} %get-tuple-element.230) | copy-start | bytes 9437188
  142.1 5.1 %copy-start.3 = (s32[4]{0:T(128)S(1)}, s32[4]{0:T(128)}, u32[]{:S(2)}) copy-start(s32[4]{0:T(128)} %constant.569.clone.1) | copy-start | bytes 52
  143.5 6.1 %collective-permute-start.14 = (f32[512,768]{1,0:T(8,128)}, f32[512,768]{1,0:T(8,128)}, u32[]{:S(2)}, u32[]{:S(2)}) collective-permute-start(f32[512,768]{1,0:T(8,128)} %dynamic-slice_bitcast_fusion.1), channel_id=1, source_target_pairs={{0,1},{1,0},{2,3},{3,2},{4,5},{5,4},{6,7},{7,6},{8,9},{9,8},{10,11... | collective-permute-start | bytes 4718600 | tf_op jit(solution)/shard_map/ppermute | solution.py:61
  146.9 6.6 %collective-permute-start.29 = (f32[512,768]{1,0:T(8,128)}, f32[512,768]{1,0:T(8,128)}, u32[]{:S(2)}, u32[]{:S(2)}) collective-permute-start(f32[512,768]{1,0:T(8,128)} %dynamic-slice_bitcast_fusion), channel_id=1, source_target_pairs={{0,1},{1,0},{2,3},{3,2},{4,5},{5,4},{6,7},{7,6},{8,9},{9,8},{10,11... | collective-permute-start | bytes 4718600 | tf_op jit(solution)/shard_map/ppermute | solution.py:61
  151.8 6.2 %collective-permute-start.18 = (f32[64,768]{1,0:T(8,128)S(1)}, f32[64,768]{1,0:T(8,128)S(1)}, u32[]{:S(2)}, u32[]{:S(2)}) collective-permute-start(f32[64,768]{1,0:T(8,128)S(1)} %dynamic-slice_bitcast_fusion.4), channel_id=1, source_target_pairs={{0,12},{4,0},{8,4},{12,8},{1,13},{5,1},{9,5},{13,9},{2,14},{6,2},{... | collective-permute-start | bytes 589832 | tf_op jit(solution)/shard_map/ppermute | solution.py:66
  152.1 7.4 %collective-permute-start.15 = (f32[64,768]{1,0:T(8,128)S(1)}, f32[64,768]{1,0:T(8,128)S(1)}, u32[]{:S(2)}, u32[]{:S(2)}) collective-permute-start(f32[64,768]{1,0:T(8,128)S(1)} %dynamic-slice_bitcast_fusion.5), channel_id=1, source_target_pairs={{0,4},{4,8},{8,12},{12,0},{1,5},{5,9},{9,13},{13,1},{2,6},{6,10},{... | collective-permute-start | bytes 589832 | tf_op jit(solution)/shard_map/ppermute | solution.py:65
  155.2 7.1 %collective-permute-start.33 = (f32[64,768]{1,0:T(8,128)S(1)}, f32[64,768]{1,0:T(8,128)S(1)}, u32[]{:S(2)}, u32[]{:S(2)}) collective-permute-start(f32[64,768]{1,0:T(8,128)S(1)} %dynamic-slice_bitcast_fusion.2), channel_id=1, source_target_pairs={{0,12},{4,0},{8,4},{12,8},{1,13},{5,1},{9,5},{13,9},{2,14},{6,2},{... | collective-permute-start | bytes 589832 | tf_op jit(solution)/shard_map/ppermute | solution.py:66
  156.7 6.8 %collective-permute-start.30 = (f32[64,768]{1,0:T(8,128)S(1)}, f32[64,768]{1,0:T(8,128)S(1)}, u32[]{:S(2)}, u32[]{:S(2)}) collective-permute-start(f32[64,768]{1,0:T(8,128)S(1)} %dynamic-slice_bitcast_fusion.3), channel_id=1, source_target_pairs={{0,4},{4,8},{8,12},{12,0},{1,5},{5,9},{9,13},{13,1},{2,6},{6,10},{... | collective-permute-start | bytes 589832 | tf_op jit(solution)/shard_map/ppermute | solution.py:65
  158.1 8.4 %collective-permute-start.19 = (f32[64,768]{1,0:T(8,128)S(1)}, f32[64,768]{1,0:T(8,128)S(1)}, u32[]{:S(2)}, u32[]{:S(2)}) collective-permute-start(f32[64,768]{1,0:T(8,128)S(1)} %bitcast_add_fusion.10), channel_id=1, source_target_pairs={{0,12},{4,0},{8,4},{12,8},{1,13},{5,1},{9,5},{13,9},{2,14},{6,2},{... | collective-permute-start | bytes 589832 | tf_op jit(solution)/shard_map/ppermute | solution.py:66
  159.6 8.3 %collective-permute-start.16 = (f32[64,768]{1,0:T(8,128)S(1)}, f32[64,768]{1,0:T(8,128)S(1)}, u32[]{:S(2)}, u32[]{:S(2)}) collective-permute-start(f32[64,768]{1,0:T(8,128)S(1)} %bitcast_add_fusion.13), channel_id=1, source_target_pairs={{0,4},{4,8},{8,12},{12,0},{1,5},{5,9},{9,13},{13,1},{2,6},{6,10},{... | collective-permute-start | bytes 589832 | tf_op jit(solution)/shard_map/ppermute | solution.py:65
  162.3 8.4 %collective-permute-start.34 = (f32[64,768]{1,0:T(8,128)S(1)}, f32[64,768]{1,0:T(8,128)S(1)}, u32[]{:S(2)}, u32[]{:S(2)}) collective-permute-start(f32[64,768]{1,0:T(8,128)S(1)} %bitcast_add_fusion.4), channel_id=1, source_target_pairs={{0,12},{4,0},{8,4},{12,8},{1,13},{5,1},{9,5},{13,9},{2,14},{6,2},{... | collective-permute-start | bytes 589832 | tf_op jit(solution)/shard_map/ppermute | solution.py:66
  163.5 7.8 %collective-permute-start.31 = (f32[64,768]{1,0:T(8,128)S(1)}, f32[64,768]{1,0:T(8,128)S(1)}, u32[]{:S(2)}, u32[]{:S(2)}) collective-permute-start(f32[64,768]{1,0:T(8,128)S(1)} %bitcast_add_fusion.7), channel_id=1, source_target_pairs={{0,4},{4,8},{8,12},{12,0},{1,5},{5,9},{9,13},{13,1},{2,6},{6,10},{... | collective-permute-start | bytes 589832 | tf_op jit(solution)/shard_map/ppermute | solution.py:65
  166.5 8.4 %collective-permute-start.20 = (f32[64,768]{1,0:T(8,128)S(1)}, f32[64,768]{1,0:T(8,128)S(1)}, u32[]{:S(2)}, u32[]{:S(2)}) collective-permute-start(f32[64,768]{1,0:T(8,128)S(1)} %bitcast_add_fusion.9), channel_id=1, source_target_pairs={{0,12},{4,0},{8,4},{12,8},{1,13},{5,1},{9,5},{13,9},{2,14},{6,2},{... | collective-permute-start | bytes 589832 | tf_op jit(solution)/shard_map/ppermute | solution.py:66
  167.9 7.4 %collective-permute-start.17 = (f32[64,768]{1,0:T(8,128)S(1)}, f32[64,768]{1,0:T(8,128)S(1)}, u32[]{:S(2)}, u32[]{:S(2)}) collective-permute-start(f32[64,768]{1,0:T(8,128)S(1)} %bitcast_add_fusion.12), channel_id=1, source_target_pairs={{0,4},{4,8},{8,12},{12,0},{1,5},{5,9},{9,13},{13,1},{2,6},{6,10},{... | collective-permute-start | bytes 589832 | tf_op jit(solution)/shard_map/ppermute | solution.py:65
  170.7 8.4 %collective-permute-start.35 = (f32[64,768]{1,0:T(8,128)S(1)}, f32[64,768]{1,0:T(8,128)S(1)}, u32[]{:S(2)}, u32[]{:S(2)}) collective-permute-start(f32[64,768]{1,0:T(8,128)S(1)} %bitcast_add_fusion.3), channel_id=1, source_target_pairs={{0,12},{4,0},{8,4},{12,8},{1,13},{5,1},{9,5},{13,9},{2,14},{6,2},{... | collective-permute-start | bytes 589832 | tf_op jit(solution)/shard_map/ppermute | solution.py:66
  171.4 8.3 %collective-permute-start.32 = (f32[64,768]{1,0:T(8,128)S(1)}, f32[64,768]{1,0:T(8,128)S(1)}, u32[]{:S(2)}, u32[]{:S(2)}) collective-permute-start(f32[64,768]{1,0:T(8,128)S(1)} %bitcast_add_fusion.6), channel_id=1, source_target_pairs={{0,4},{4,8},{8,12},{12,0},{1,5},{5,9},{9,13},{13,1},{2,6},{6,10},{... | collective-permute-start | bytes 589832 | tf_op jit(solution)/shard_map/ppermute | solution.py:65
  175.3 4.9 %collective-permute-start.21 = (f32[64,768]{1,0:T(8,128)S(1)}, f32[64,768]{1,0:T(8,128)S(1)}, u32[]{:S(2)}, u32[]{:S(2)}) collective-permute-start(f32[64,768]{1,0:T(8,128)S(1)} %fusion.19), channel_id=1, source_target_pairs={{0,2},{2,0},{1,3},{3,1},{4,6},{6,4},{5,7},{7,5},{8,10},{10,8},{9,1... | collective-permute-start | bytes 589832 | tf_op jit(solution)/shard_map/ppermute | solution.py:68
  179.8 6.1 %collective-permute-start.36 = (f32[64,768]{1,0:T(8,128)S(1)}, f32[64,768]{1,0:T(8,128)S(1)}, u32[]{:S(2)}, u32[]{:S(2)}) collective-permute-start(f32[64,768]{1,0:T(8,128)S(1)} %fusion.13), channel_id=1, source_target_pairs={{0,2},{2,0},{1,3},{3,1},{4,6},{6,4},{5,7},{7,5},{8,10},{10,8},{9,1... | collective-permute-start | bytes 589832 | tf_op jit(solution)/shard_map/ppermute | solution.py:68
  180.3 9.7 %collective-permute-start.22 = (f32[64,768]{1,0:T(8,128)S(1)}, f32[64,768]{1,0:T(8,128)S(1)}, u32[]{:S(2)}, u32[]{:S(2)}) collective-permute-start(f32[64,768]{1,0:T(8,128)S(1)} %fusion.23), channel_id=1, source_target_pairs={{0,2},{2,0},{1,3},{3,1},{4,6},{6,4},{5,7},{7,5},{8,10},{10,8},{9,1... | collective-permute-start | bytes 589832 | tf_op jit(solution)/shard_map/ppermute | solution.py:71
  186.0 8.3 %collective-permute-start.37 = (f32[64,768]{1,0:T(8,128)S(1)}, f32[64,768]{1,0:T(8,128)S(1)}, u32[]{:S(2)}, u32[]{:S(2)}) collective-permute-start(f32[64,768]{1,0:T(8,128)S(1)} %fusion.17), channel_id=1, source_target_pairs={{0,2},{2,0},{1,3},{3,1},{4,6},{6,4},{5,7},{7,5},{8,10},{10,8},{9,1... | collective-permute-start | bytes 589832 | tf_op jit(solution)/shard_map/ppermute | solution.py:71
  190.1 8.4 %collective-permute-start.23 = (f32[64,768]{1,0:T(8,128)S(1)}, f32[64,768]{1,0:T(8,128)S(1)}, u32[]{:S(2)}, u32[]{:S(2)}) collective-permute-start(f32[64,768]{1,0:T(8,128)S(1)} %get-tuple-element.208), channel_id=1, source_target_pairs={{0,4},{4,8},{8,12},{12,0},{1,5},{5,9},{9,13},{13,1},{2,6},{6,10},{... | collective-permute-start | bytes 589832 | tf_op jit(solution)/shard_map/ppermute | solution.py:76
  191.6 7.2 %collective-permute-start.24 = (f32[64,768]{1,0:T(8,128)S(1)}, f32[64,768]{1,0:T(8,128)S(1)}, u32[]{:S(2)}, u32[]{:S(2)}) collective-permute-start(f32[64,768]{1,0:T(8,128)S(1)} %get-tuple-element.207), channel_id=1, source_target_pairs={{0,12},{4,0},{8,4},{12,8},{1,13},{5,1},{9,5},{13,9},{2,14},{6,2},{... | collective-permute-start | bytes 589832 | tf_op jit(solution)/shard_map/ppermute | solution.py:77
  194.4 7.0 %collective-permute-start.38 = (f32[64,768]{1,0:T(8,128)S(1)}, f32[64,768]{1,0:T(8,128)S(1)}, u32[]{:S(2)}, u32[]{:S(2)}) collective-permute-start(f32[64,768]{1,0:T(8,128)S(1)} %get-tuple-element.210), channel_id=1, source_target_pairs={{0,4},{4,8},{8,12},{12,0},{1,5},{5,9},{9,13},{13,1},{2,6},{6,10},{... | collective-permute-start | bytes 589832 | tf_op jit(solution)/shard_map/ppermute | solution.py:76
  195.8 8.2 %collective-permute-start.39 = (f32[64,768]{1,0:T(8,128)S(1)}, f32[64,768]{1,0:T(8,128)S(1)}, u32[]{:S(2)}, u32[]{:S(2)}) collective-permute-start(f32[64,768]{1,0:T(8,128)S(1)} %get-tuple-element.209), channel_id=1, source_target_pairs={{0,12},{4,0},{8,4},{12,8},{1,13},{5,1},{9,5},{13,9},{2,14},{6,2},{... | collective-permute-start | bytes 589832 | tf_op jit(solution)/shard_map/ppermute | solution.py:77
  198.6 8.2 %collective-permute-start.25 = (f32[64,768]{1,0:T(8,128)S(1)}, f32[64,768]{1,0:T(8,128)S(1)}, u32[]{:S(2)}, u32[]{:S(2)}) collective-permute-start(f32[64,768]{1,0:T(8,128)S(1)} %collective-permute-done.23), channel_id=1, source_target_pairs={{0,4},{4,8},{8,12},{12,0},{1,5},{5,9},{9,13},{13,1},{2,6},{6,10},{... | collective-permute-start | bytes 589832 | tf_op jit(solution)/shard_map/ppermute | solution.py:76
  198.8 8.1 %collective-permute-start.26 = (f32[64,768]{1,0:T(8,128)S(1)}, f32[64,768]{1,0:T(8,128)S(1)}, u32[]{:S(2)}, u32[]{:S(2)}) collective-permute-start(f32[64,768]{1,0:T(8,128)S(1)} %collective-permute-done.24), channel_id=1, source_target_pairs={{0,12},{4,0},{8,4},{12,8},{1,13},{5,1},{9,5},{13,9},{2,14},{6,2},{... | collective-permute-start | bytes 589832 | tf_op jit(solution)/shard_map/ppermute | solution.py:77
  201.3 8.2 %collective-permute-start.40 = (f32[64,768]{1,0:T(8,128)S(1)}, f32[64,768]{1,0:T(8,128)S(1)}, u32[]{:S(2)}, u32[]{:S(2)}) collective-permute-start(f32[64,768]{1,0:T(8,128)S(1)} %collective-permute-done.38), channel_id=1, source_target_pairs={{0,4},{4,8},{8,12},{12,0},{1,5},{5,9},{9,13},{13,1},{2,6},{6,10},{... | collective-permute-start | bytes 589832 | tf_op jit(solution)/shard_map/ppermute | solution.py:76
  204.0 8.3 %collective-permute-start.41 = (f32[64,768]{1,0:T(8,128)S(1)}, f32[64,768]{1,0:T(8,128)S(1)}, u32[]{:S(2)}, u32[]{:S(2)}) collective-permute-start(f32[64,768]{1,0:T(8,128)S(1)} %collective-permute-done.39), channel_id=1, source_target_pairs={{0,12},{4,0},{8,4},{12,8},{1,13},{5,1},{9,5},{13,9},{2,14},{6,2},{... | collective-permute-start | bytes 589832 | tf_op jit(solution)/shard_map/ppermute | solution.py:77
  206.8 8.3 %collective-permute-start.27 = (f32[64,768]{1,0:T(8,128)S(1)}, f32[64,768]{1,0:T(8,128)S(1)}, u32[]{:S(2)}, u32[]{:S(2)}) collective-permute-start(f32[64,768]{1,0:T(8,128)S(1)} %collective-permute-done.25), channel_id=1, source_target_pairs={{0,4},{4,8},{8,12},{12,0},{1,5},{5,9},{9,13},{13,1},{2,6},{6,10},{... | collective-permute-start | bytes 589832 | tf_op jit(solution)/shard_map/ppermute | solution.py:76
  206.9 8.8 %collective-permute-start.28 = (f32[64,768]{1,0:T(8,128)S(1)}, f32[64,768]{1,0:T(8,128)S(1)}, u32[]{:S(2)}, u32[]{:S(2)}) collective-permute-start(f32[64,768]{1,0:T(8,128)S(1)} %collective-permute-done.26), channel_id=1, source_target_pairs={{0,12},{4,0},{8,4},{12,8},{1,13},{5,1},{9,5},{13,9},{2,14},{6,2},{... | collective-permute-start | bytes 589832 | tf_op jit(solution)/shard_map/ppermute | solution.py:77
  209.5 15.3 %collective-permute-start.42 = (f32[64,768]{1,0:T(8,128)S(1)}, f32[64,768]{1,0:T(8,128)S(1)}, u32[]{:S(2)}, u32[]{:S(2)}) collective-permute-start(f32[64,768]{1,0:T(8,128)S(1)} %collective-permute-done.40), channel_id=1, source_target_pairs={{0,4},{4,8},{8,12},{12,0},{1,5},{5,9},{9,13},{13,1},{2,6},{6,10},{... | collective-permute-start | bytes 589832 | tf_op jit(solution)/shard_map/ppermute | solution.py:76
  212.3 13.2 %collective-permute-start.43 = (f32[64,768]{1,0:T(8,128)S(1)}, f32[64,768]{1,0:T(8,128)S(1)}, u32[]{:S(2)}, u32[]{:S(2)}) collective-permute-start(f32[64,768]{1,0:T(8,128)S(1)} %collective-permute-done.41), channel_id=1, source_target_pairs={{0,12},{4,0},{8,4},{12,8},{1,13},{5,1},{9,5},{13,9},{2,14},{6,2},{... | collective-permute-start | bytes 589832 | tf_op jit(solution)/shard_map/ppermute | solution.py:77
  216.3 11.7 %collective-permute-start.44 = (f32[512,768]{1,0:T(8,128)S(1)}, f32[512,768]{1,0:T(8,128)}, u32[]{:S(2)}, u32[]{:S(2)}) collective-permute-start(f32[512,768]{1,0:T(8,128)S(1)} %bitcast.221), channel_id=1, source_target_pairs={{0,1},{1,0},{2,3},{3,2},{4,5},{5,4},{6,7},{7,6},{8,9},{9,8},{10,11... | collective-permute-start | bytes 4718600 | tf_op jit(solution)/shard_map/ppermute | solution.py:126
  226.1 4.2 %collective-permute-start.45 = (f32[512,768]{1,0:T(8,128)S(1)}, f32[512,768]{1,0:T(8,128)}, u32[]{:S(2)}, u32[]{:S(2)}) collective-permute-start(f32[512,768]{1,0:T(8,128)S(1)} %bitcast.219), channel_id=1, source_target_pairs={{0,1},{1,0},{2,3},{3,2},{4,5},{5,4},{6,7},{7,6},{8,9},{9,8},{10,11... | collective-permute-start | bytes 4718600 | tf_op jit(solution)/shard_map/ppermute | solution.py:126

commit v12 on v11

--- a/solution.py
+++ b/solution.py
@@ -97,7 +97,7 @@
 
 
 def local(images, captions, bank, sizes):
-    img_rounds = [("zh", sizes["zh"], 1)] + [("y", sizes["y"], d) for d in (1, 2)]
+    img_rounds = [("y", sizes["y"], d) for d in (1, 2)] + [("zh", sizes["zh"], 1)]
     cap_rounds = [("core", sizes["core"], 1), ("zl", sizes["zl"], 1)] + [
         ("x", sizes["x"], d) for d in (1, 2)
     ]

time: 239 us -> 238 us (level)
  waiting for transfers between devices: 58.6 us -> 55.1 us
  starting transfers between devices: 70.4 us -> 73.1 us
  transfers between devices with their start and end apart: 46 -> 46, of which waited for: 22 -> 21; matrix products, arithmetic and copies ran while one was open for 29% -> 29% of each run, Pallas kernels for 0% -> 0%
where the time goes in v12:
time: 238 us; the launch traced here: 235 us
  starting transfers between devices  73.1 us (31%)
  matrix products  67.5 us (28%)
  waiting for transfers between devices  55.1 us (23%)
  other arithmetic  31.3 us (13%)
  local copies, waits for them, and re-layouts  6.62 us (3%)
    dot_general x2, matrix products, similar(): lax.dot_general(query_factor, target_factor, (((1,), (0,)), ((), ())), pr...  44.6 us
    dot_general x2, matrix products, rescaled_affinity(): lax.dot_general(weights, features, (((1,), (1,)), ((), ())), precision=la...  22.9 us
    ppermute x7, starting transfers between devices, merge_peaks(): other = lax.ppermute(pair, axis, [(j, j ^ dist) for j in range(size)])  17.3 us
    ppermute x6, waiting for transfers between devices, reduce_rows(): lax.ppermute(left, 'x', ring('x', x_size, -1))  14.4 us
    ppermute x3, waiting for transfers between devices, gather_features(): left = lax.ppermute(left, 'y', ring('y', y_size, -1))  12.7 us
    ppermute x6, starting transfers between devices, reduce_rows(): left = lax.ppermute(left, 'x', ring('x', x_size, -1))  10.9 us
    ppermute x3, starting transfers between devices, gather_features(): left = lax.ppermute(left, 'y', ring('y', y_size, -1))  9.89 us
    ppermute x2, starting transfers between devices, local(): lax.ppermute(part, 'core', [(0, 1), (1, 0)])  8.64 us
  transfers between devices with their start and end apart: 46, of which 21 were waited for; matrix products, arithmetic and copies ran while one was open for 29% of the time, Pallas kernels for 0%

profile of v12, /device:TPU:1, one launch (start us, length us, event | category | flops | bytes accessed | tf_op | source)
XLA Modules:
  0.0 234.6 jit_solution(17876754471086554499)
XLA Ops:
  0.0 4.4 %collective-permute-start = (f32[1024,96]{0,1:T(8,128)}, f32[1024,96]{0,1:T(8,128)}, u32[]{:S(2)}, u32[]{:S(2)}) collective-permute-start(f32[1024,96]{0,1:T(8,128)} %param.34), channel_id=1, source_target_pairs={{0,64},{64,0},{1,65},{65,1},{2,66},{66,2},{3,67},{67,3},{4,68},{68... | collective-permute-start | bytes 1179656 | tf_op jit(solution)/shard_map/ppermute | solution.py:87
  4.4 1.3 collective-permute-start.1
  5.7 7.9 %collective-permute-done = f32[1024,96]{0,1:T(8,128)} collective-permute-done((f32[1024,96]{0,1:T(8,128)}, f32[1024,96]{0,1:T(8,128)}, u32[]{:S(2)}, u32[]{:S(2)}) %collective-permute-start) | collective-permute-done | bytes 393248 | tf_op jit(solution)/shard_map/ppermute | solution.py:87
  13.6 2.7 %collective-permute-start.2 = (f32[1024,96]{0,1:T(8,128)}, f32[1024,96]{0,1:T(8,128)}, u32[]{:S(2)}, u32[]{:S(2)}) collective-permute-start(f32[1024,96]{0,1:T(8,128)} %collective-permute-done), channel_id=1, source_target_pairs={{0,48},{16,0},{32,16},{48,32},{1,49},{17,1},{33,17},{49,33},{2,50}... | collective-permute-start | bytes 1179656 | tf_op jit(solution)/shard_map/ppermute | solution.py:93
  16.3 1.4 and_reduce_fusion.7
  18.7 2.0 fusion.7
  20.8 3.0 %collective-permute-done.2 = f32[1024,96]{0,1:T(8,128)} collective-permute-done((f32[1024,96]{0,1:T(8,128)}, f32[1024,96]{0,1:T(8,128)}, u32[]{:S(2)}, u32[]{:S(2)}) %collective-permute-start.2) | collective-permute-done | bytes 393248 | tf_op jit(solution)/shard_map/ppermute | solution.py:93
  23.8 3.4 %collective-permute-start.4 = (f32[1024,96]{0,1:T(8,128)}, f32[1024,96]{0,1:T(8,128)S(1)}, u32[]{:S(2)}, u32[]{:S(2)}) collective-permute-start(f32[1024,96]{0,1:T(8,128)} %collective-permute-done.2), channel_id=1, source_target_pairs={{0,48},{16,0},{32,16},{48,32},{1,49},{17,1},{33,17},{49,33},{2,50}... | collective-permute-start | bytes 1179656 | tf_op jit(solution)/shard_map/ppermute | solution.py:93
  27.2 1.1 bitcast_dynamic-update-slice_fusion.2
  28.3 1.0 bitcast_dynamic-update-slice_fusion.1
  29.3 4.5 %collective-permute-done.4 = f32[1024,96]{0,1:T(8,128)S(1)} collective-permute-done((f32[1024,96]{0,1:T(8,128)}, f32[1024,96]{0,1:T(8,128)S(1)}, u32[]{:S(2)}, u32[]{:S(2)}) %collective-permute-start.4) | collective-permute-done | bytes 393248 | tf_op jit(solution)/shard_map/ppermute | solution.py:93
  33.8 3.7 %collective-permute-start.6 = (f32[1024,96]{0,1:T(8,128)S(1)}, f32[1024,96]{0,1:T(8,128)S(1)}, u32[]{:S(2)}, u32[]{:S(2)}) collective-permute-start(f32[1024,96]{0,1:T(8,128)S(1)} %collective-permute-done.4), channel_id=1, source_target_pairs={{0,48},{16,0},{32,16},{48,32},{1,49},{17,1},{33,17},{49,33},{2,50}... | collective-permute-start | bytes 1179656 | tf_op jit(solution)/shard_map/ppermute | solution.py:93
  37.6 5.2 %collective-permute-done.6 = f32[1024,96]{0,1:T(8,128)S(1)} collective-permute-done((f32[1024,96]{0,1:T(8,128)S(1)}, f32[1024,96]{0,1:T(8,128)S(1)}, u32[]{:S(2)}, u32[]{:S(2)}) %collective-permute-start.6) | collective-permute-done | bytes 393248 | tf_op jit(solution)/shard_map/ppermute | solution.py:93
  43.0 22.4 %fusion = (f32[1024]{0:T(1024)S(1)}, f32[1024,2048]{0,1:T(8,128)S(1)}) fusion(f32[768,1024]{1,0:T(8,128)S(1)} %bitcast.225, f32[2048,768]{1,0:T(8,128)S(1)} %copy-done.4), kind=kOutput, calls=%fused_computation.4 | convolution fusion | flops 19331547136 | bytes 17829888 | tf_op jit(solution)/shard_map/dot_general | solution.py:15
  65.4 1.4 exponential_reduce_fusion
  66.9 2.5 %collective-permute-done.7 = f32[2,1024]{1,0:T(2,128)S(1)} collective-permute-done((f32[2,1024]{1,0:T(2,128)S(1)}, f32[2,1024]{1,0:T(2,128)S(1)}, u32[]{:S(2)}, u32[]{:S(2)}) %collective-permute-start.7) | collective-permute-done | bytes 8224 | tf_op jit(solution)/shard_map/ppermute | solution.py:38
  69.5 3.2 %collective-permute-start.8 = (f32[2,1024]{1,0:T(2,128)S(1)}, f32[2,1024]{1,0:T(2,128)S(1)}, u32[]{:S(2)}, u32[]{:S(2)}) collective-permute-start(f32[2,1024]{1,0:T(2,128)S(1)} %pad_maximum_fusion.5), channel_id=1, source_target_pairs={{0,32},{16,48},{32,0},{48,16},{1,33},{17,49},{33,1},{49,17},{2,34}... | collective-permute-start | bytes 24584 | tf_op jit(solution)/shard_map/ppermute | solution.py:38
  72.7 1.0 collective-permute-done.8
  73.8 2.2 collective-permute-start.9
  76.0 22.2 %bitcast_multiply_fusion.1 = f32[2048,1024]{1,0:T(8,128)S(1)} fusion(f32[768,1024]{1,0:T(8,128)S(1)} %bitcast.226, f32[2048,768]{1,0:T(8,128)S(1)} %bitcast.257), kind=kOutput, calls=%fused_computation.1 | convolution fusion | flops 19329449984 | bytes 17825792 | tf_op jit(solution)/shard_map/dot_general | solution.py:15
  98.8 4.2 %fusion.48 = (f32[2048]{0:T(1024)S(1)}, f32[2048,1024]{1,0:T(8,128)}) fusion(f32[2048]{0:T(1024)S(1)} %subtract_reduce_fusion, f32[2048,1024]{1,0:T(8,128)S(1)} %bitcast_multiply_fusion.1, f32[1024]{0:T(1024)S(1)} %bitcast.247), kind=kLoop, calls=%fused_computation.168 | loop fusion | flops 6289408 | bytes 16797696 | tf_op jit(solution)/shard_map/reduce_sum | solution.py:114
  103.0 6.8 %collective-permute-start.10 = (f32[2,2048]{1,0:T(2,128)S(1)}, f32[2,2048]{1,0:T(2,128)S(1)}, u32[]{:S(2)}, u32[]{:S(2)}) collective-permute-start(f32[2,2048]{1,0:T(2,128)S(1)} %pad_maximum_fusion), channel_id=1, source_target_pairs={{0,1},{1,0},{2,3},{3,2},{4,5},{5,4},{6,7},{7,6},{8,9},{9,8},{10,11... | collective-permute-start | bytes 49160 | tf_op jit(solution)/shard_map/ppermute | solution.py:38
  109.8 0.8 collective-permute-done.10
  110.7 0.8 collective-permute-start.11
  111.6 1.9 collective-permute-done.11
  113.5 1.3 collective-permute-start.12
  114.8 12.5 %fusion.3 = f32[1024,768]{1,0:T(8,128)S(1)} fusion(f32[768,1024]{1,0:T(8,128)S(1)} %bitcast.227, f32[2048,1024]{1,0:T(8,128)} %get-tuple-element.198), kind=kOutput, calls=%fused_computation.9 | convolution fusion | flops 9663676416 | bytes 10485760 | tf_op jit(solution)/shard_map/dot_general | solution.py:26
  127.3 2.9 %collective-permute-start.13 = (f32[2,2048]{1,0:T(2,128)S(1)}, f32[2,2048]{1,0:T(2,128)S(1)}, u32[]{:S(2)}, u32[]{:S(2)}) collective-permute-start(f32[2,2048]{1,0:T(2,128)S(1)} %pad_maximum_fusion.3), channel_id=1, source_target_pairs={{0,8},{4,12},{8,0},{12,4},{1,9},{5,13},{9,1},{13,5},{2,10},{6,14},... | collective-permute-start | bytes 49160 | tf_op jit(solution)/shard_map/ppermute | solution.py:38
  130.3 10.4 %fusion.1 = f32[1024,768]{1,0:T(8,128)S(1)} fusion(f32[768,1024]{1,0:T(8,128)S(1)} %bitcast.228, f32[2048,1024]{1,0:T(8,128)S(1)} %copy-done.1), kind=kOutput, calls=%fused_computation.7 | convolution fusion | flops 9663676416 | bytes 10485760 | tf_op jit(solution)/shard_map/dot_general | solution.py:26
  141.3 1.4 dynamic-slice_bitcast_fusion.1
  142.7 2.1 collective-permute-start.14
  144.7 1.3 dynamic-slice_bitcast_fusion
  148.8 2.1 bitcast_add_fusion.1
  151.3 1.3 collective-permute-start.15
  152.6 1.6 bitcast_add_fusion
  154.4 1.5 collective-permute-start.33
  156.0 1.2 collective-permute-done.18
  157.3 1.5 collective-permute-start.19
  158.9 2.6 %collective-permute-done.33 = f32[64,768]{1,0:T(8,128)S(1)} collective-permute-done((f32[64,768]{1,0:T(8,128)S(1)}, f32[64,768]{1,0:T(8,128)S(1)}, u32[]{:S(2)}, u32[]{:S(2)}) %collective-permute-start.33) | collective-permute-done | bytes 196640 | tf_op jit(solution)/shard_map/ppermute | solution.py:66
  161.5 1.2 collective-permute-start.34
  163.1 2.6 %collective-permute-done.19 = f32[64,768]{1,0:T(8,128)S(1)} collective-permute-done((f32[64,768]{1,0:T(8,128)S(1)}, f32[64,768]{1,0:T(8,128)S(1)}, u32[]{:S(2)}, u32[]{:S(2)}) %collective-permute-start.19) | collective-permute-done | bytes 196640 | tf_op jit(solution)/shard_map/ppermute | solution.py:66
  165.7 1.3 collective-permute-start.20
  167.3 2.5 %collective-permute-done.34 = f32[64,768]{1,0:T(8,128)S(1)} collective-permute-done((f32[64,768]{1,0:T(8,128)S(1)}, f32[64,768]{1,0:T(8,128)S(1)}, u32[]{:S(2)}, u32[]{:S(2)}) %collective-permute-start.34) | collective-permute-done | bytes 196640 | tf_op jit(solution)/shard_map/ppermute | solution.py:66
  170.6 1.0 collective-permute-start.32
  171.5 2.6 %collective-permute-done.20 = f32[64,768]{1,0:T(8,128)S(1)} collective-permute-done((f32[64,768]{1,0:T(8,128)S(1)}, f32[64,768]{1,0:T(8,128)S(1)}, u32[]{:S(2)}, u32[]{:S(2)}) %collective-permute-start.20) | collective-permute-done | bytes 196640 | tf_op jit(solution)/shard_map/ppermute | solution.py:66
  175.3 3.0 %collective-permute-done.35 = f32[64,768]{1,0:T(8,128)S(1)} collective-permute-done((f32[64,768]{1,0:T(8,128)S(1)}, f32[64,768]{1,0:T(8,128)S(1)}, u32[]{:S(2)}, u32[]{:S(2)}) %collective-permute-start.35) | collective-permute-done | bytes 196640 | tf_op jit(solution)/shard_map/ppermute | solution.py:66
  180.7 4.4 %collective-permute-done.36 = f32[64,768]{1,0:T(8,128)S(1)} collective-permute-done((f32[64,768]{1,0:T(8,128)S(1)}, f32[64,768]{1,0:T(8,128)S(1)}, u32[]{:S(2)}, u32[]{:S(2)}) %collective-permute-start.36) | collective-permute-done | bytes 196640 | tf_op jit(solution)/shard_map/ppermute | solution.py:68
  185.9 3.3 %collective-permute-done.22 = f32[64,768]{1,0:T(8,128)S(1)} collective-permute-done((f32[64,768]{1,0:T(8,128)S(1)}, f32[64,768]{1,0:T(8,128)S(1)}, u32[]{:S(2)}, u32[]{:S(2)}) %collective-permute-start.22) | collective-permute-done | bytes 196640 | tf_op jit(solution)/shard_map/ppermute | solution.py:71
  189.3 1.4 collective-permute-start.23
  190.7 1.4 collective-permute-start.24
  192.1 1.4 collective-permute-done.37
  193.5 1.4 collective-permute-start.38
  194.9 1.4 collective-permute-start.39
  197.9 2.6 %collective-permute-start.26 = (f32[64,768]{1,0:T(8,128)S(1)}, f32[64,768]{1,0:T(8,128)S(1)}, u32[]{:S(2)}, u32[]{:S(2)}) collective-permute-start(f32[64,768]{1,0:T(8,128)S(1)} %collective-permute-done.24), channel_id=1, source_target_pairs={{0,12},{4,0},{8,4},{12,8},{1,13},{5,1},{9,5},{13,9},{2,14},{6,2},{... | collective-permute-start | bytes 589832 | tf_op jit(solution)/shard_map/ppermute | solution.py:77
  200.5 1.2 collective-permute-start.40
  203.1 1.6 collective-permute-start.41
  206.0 2.7 %collective-permute-start.28 = (f32[64,768]{1,0:T(8,128)S(1)}, f32[64,768]{1,0:T(8,128)S(1)}, u32[]{:S(2)}, u32[]{:S(2)}) collective-permute-start(f32[64,768]{1,0:T(8,128)S(1)} %collective-permute-done.26), channel_id=1, source_target_pairs={{0,12},{4,0},{8,4},{12,8},{1,13},{5,1},{9,5},{13,9},{2,14},{6,2},{... | collective-permute-start | bytes 589832 | tf_op jit(solution)/shard_map/ppermute | solution.py:77
  208.7 1.4 collective-permute-start.42
  211.4 1.4 collective-permute-start.43
  215.4 8.5 %collective-permute-start.44 = (f32[512,768]{1,0:T(8,128)S(1)}, f32[512,768]{1,0:T(8,128)}, u32[]{:S(2)}, u32[]{:S(2)}) collective-permute-start(f32[512,768]{1,0:T(8,128)S(1)} %bitcast.221), channel_id=1, source_target_pairs={{0,1},{1,0},{2,3},{3,2},{4,5},{5,4},{6,7},{7,6},{8,9},{9,8},{10,11... | collective-permute-start | bytes 4718600 | tf_op jit(solution)/shard_map/ppermute | solution.py:126
  225.6 1.6 collective-permute-done.44
  227.2 2.2 collective-permute-done.45
  229.4 2.1 maximum_bitcast_fusion.1
  231.5 2.9 %maximum_select_fusion = f32[2,2,512,768]{3,2,1,0:T(8,128)} fusion(f32[2,1,512,768]{3,2,1,0:T(8,128)S(1)} %maximum_bitcast_fusion.1, f32[2,1,512,768]{3,2,1,0:T(8,128)S(1)} %maximum_bitcast_fusion, pred[]{:T(512)S(6)} %eq.45), kind=kLoop, calls=%fused_computation.6 | loop fusion | flops 4718592 | bytes 12582913 | tf_op jit(solution)/shard_map/jit(_where)/select_n | solution.py:128
  (129 shorter events, 22.1 us)
Async XLA Ops:
  0.0 13.6 %collective-permute-start = (f32[1024,96]{0,1:T(8,128)}, f32[1024,96]{0,1:T(8,128)}, u32[]{:S(2)}, u32[]{:S(2)}) collective-permute-start(f32[1024,96]{0,1:T(8,128)} %param.34), channel_id=1, source_target_pairs={{0,64},{64,0},{1,65},{65,1},{2,66},{66,2},{3,67},{67,3},{4,68},{68... | collective-permute-start | bytes 1179656 | tf_op jit(solution)/shard_map/ppermute | solution.py:87
  4.4 11.9 %collective-permute-start.1 = (f32[1024,96]{0,1:T(8,128)}, f32[1024,96]{0,1:T(8,128)S(1)}, u32[]{:S(2)}, u32[]{:S(2)}) collective-permute-start(f32[1024,96]{0,1:T(8,128)} %param.34), channel_id=1, source_target_pairs={{0,16},{16,32},{32,48},{48,0},{1,17},{17,33},{33,49},{49,1},{2,18}... | collective-permute-start | bytes 1179656 | tf_op jit(solution)/shard_map/ppermute | solution.py:92
  13.6 10.2 %collective-permute-start.2 = (f32[1024,96]{0,1:T(8,128)}, f32[1024,96]{0,1:T(8,128)}, u32[]{:S(2)}, u32[]{:S(2)}) collective-permute-start(f32[1024,96]{0,1:T(8,128)} %collective-permute-done), channel_id=1, source_target_pairs={{0,48},{16,0},{32,16},{48,32},{1,49},{17,1},{33,17},{49,33},{2,50}... | collective-permute-start | bytes 1179656 | tf_op jit(solution)/shard_map/ppermute | solution.py:93
  16.3 10.9 %collective-permute-start.3 = (f32[1024,96]{0,1:T(8,128)S(1)}, f32[1024,96]{0,1:T(8,128)}, u32[]{:S(2)}, u32[]{:S(2)}) collective-permute-start(f32[1024,96]{0,1:T(8,128)S(1)} %collective-permute-done.1), channel_id=1, source_target_pairs={{0,16},{16,32},{32,48},{48,0},{1,17},{17,33},{33,49},{49,1},{2,18}... | collective-permute-start | bytes 1179656 | tf_op jit(solution)/shard_map/ppermute | solution.py:92
  17.7 1.0 copy-start.2
  18.7 24.2 %copy-start.4 = (f32[2048,768]{1,0:T(8,128)S(1)}, f32[2048,768]{1,0:T(8,128)}, u32[]{:S(2)}) copy-start(f32[2048,768]{1,0:T(8,128)} %param.35) | copy-start | bytes 18874372
  23.8 10.0 %collective-permute-start.4 = (f32[1024,96]{0,1:T(8,128)}, f32[1024,96]{0,1:T(8,128)S(1)}, u32[]{:S(2)}, u32[]{:S(2)}) collective-permute-start(f32[1024,96]{0,1:T(8,128)} %collective-permute-done.2), channel_id=1, source_target_pairs={{0,48},{16,0},{32,16},{48,32},{1,49},{17,1},{33,17},{49,33},{2,50}... | collective-permute-start | bytes 1179656 | tf_op jit(solution)/shard_map/ppermute | solution.py:93
  27.2 10.4 %collective-permute-start.5 = (f32[1024,96]{0,1:T(8,128)}, f32[1024,96]{0,1:T(8,128)S(1)}, u32[]{:S(2)}, u32[]{:S(2)}) collective-permute-start(f32[1024,96]{0,1:T(8,128)} %collective-permute-done.3), channel_id=1, source_target_pairs={{0,16},{16,32},{32,48},{48,0},{1,17},{17,33},{33,49},{49,1},{2,18}... | collective-permute-start | bytes 1179656 | tf_op jit(solution)/shard_map/ppermute | solution.py:92
  33.8 9.1 %collective-permute-start.6 = (f32[1024,96]{0,1:T(8,128)S(1)}, f32[1024,96]{0,1:T(8,128)S(1)}, u32[]{:S(2)}, u32[]{:S(2)}) collective-permute-start(f32[1024,96]{0,1:T(8,128)S(1)} %collective-permute-done.4), channel_id=1, source_target_pairs={{0,48},{16,0},{32,16},{48,32},{1,49},{17,1},{33,17},{49,33},{2,50}... | collective-permute-start | bytes 1179656 | tf_op jit(solution)/shard_map/ppermute | solution.py:93
  42.9 33.1 %slice-start = ((s8[6291456]{0:T(1024)(128)(4,1)}), s8[4194304]{0:T(1024)(128)(4,1)S(1)}, s32[]{:S(2)}) async-start(s8[6291456]{0:T(1024)(128)(4,1)} %bitcast.256), calls=%async_computation | async-start | bytes 8388608
  42.9 33.0 %slice-start.1 = ((s8[6291456]{0:T(1024)(128)(4,1)}), s8[2097152]{0:T(1024)(128)(4,1)S(1)}, s32[]{:S(2)}) async-start(s8[6291456]{0:T(1024)(128)(4,1)} %bitcast.256), calls=%async_computation.1 | async-start | bytes 4194304
  66.9 2.6 %collective-permute-start.7 = (f32[2,1024]{1,0:T(2,128)S(1)}, f32[2,1024]{1,0:T(2,128)S(1)}, u32[]{:S(2)}, u32[]{:S(2)}) collective-permute-start(f32[2,1024]{1,0:T(2,128)S(1)} %pad_maximum_fusion.4), channel_id=1, source_target_pairs={{0,16},{16,0},{32,48},{48,32},{1,17},{17,1},{33,49},{49,33},{2,18}... | collective-permute-start | bytes 24584 | tf_op jit(solution)/shard_map/ppermute | solution.py:38
  69.5 4.3 %collective-permute-start.8 = (f32[2,1024]{1,0:T(2,128)S(1)}, f32[2,1024]{1,0:T(2,128)S(1)}, u32[]{:S(2)}, u32[]{:S(2)}) collective-permute-start(f32[2,1024]{1,0:T(2,128)S(1)} %pad_maximum_fusion.5), channel_id=1, source_target_pairs={{0,32},{16,48},{32,0},{48,16},{1,33},{17,49},{33,1},{49,17},{2,34}... | collective-permute-start | bytes 24584 | tf_op jit(solution)/shard_map/ppermute | solution.py:38
  73.8 24.4 %collective-permute-start.9 = (f32[2,1024]{1,0:T(2,128)S(1)}, f32[2,1024]{1,0:T(2,128)S(1)}, u32[]{:S(2)}, u32[]{:S(2)}) collective-permute-start(f32[2,1024]{1,0:T(2,128)S(1)} %pad_maximum_fusion.6), channel_id=1, source_target_pairs={{0,64},{64,0},{1,65},{65,1},{2,66},{66,2},{3,67},{67,3},{4,68},{68... | collective-permute-start | bytes 24584 | tf_op jit(solution)/shard_map/ppermute | solution.py:38
  103.0 7.6 %collective-permute-start.10 = (f32[2,2048]{1,0:T(2,128)S(1)}, f32[2,2048]{1,0:T(2,128)S(1)}, u32[]{:S(2)}, u32[]{:S(2)}) collective-permute-start(f32[2,2048]{1,0:T(2,128)S(1)} %pad_maximum_fusion), channel_id=1, source_target_pairs={{0,1},{1,0},{2,3},{3,2},{4,5},{5,4},{6,7},{7,6},{8,9},{9,8},{10,11... | collective-permute-start | bytes 49160 | tf_op jit(solution)/shard_map/ppermute | solution.py:38
  110.7 2.7 %collective-permute-start.11 = (f32[2,2048]{1,0:T(2,128)S(1)}, f32[2,2048]{1,0:T(2,128)S(1)}, u32[]{:S(2)}, u32[]{:S(2)}) collective-permute-start(f32[2,2048]{1,0:T(2,128)S(1)} %pad_maximum_fusion.1), channel_id=1, source_target_pairs={{0,2},{2,0},{1,3},{3,1},{4,6},{6,4},{5,7},{7,5},{8,10},{10,8},{9,1... | collective-permute-start | bytes 49160 | tf_op jit(solution)/shard_map/ppermute | solution.py:38
  113.5 13.8 %collective-permute-start.12 = (f32[2,2048]{1,0:T(2,128)S(1)}, f32[2,2048]{1,0:T(2,128)S(1)}, u32[]{:S(2)}, u32[]{:S(2)}) collective-permute-start(f32[2,2048]{1,0:T(2,128)S(1)} %pad_maximum_fusion.2), channel_id=1, source_target_pairs={{0,4},{4,0},{8,12},{12,8},{1,5},{5,1},{9,13},{13,9},{2,6},{6,2},{1... | collective-permute-start | bytes 49160 | tf_op jit(solution)/shard_map/ppermute | solution.py:38
  114.8 15.5 %copy-start.1 = (f32[2048,1024]{1,0:T(8,128)S(1)}, f32[2048,1024]{1,0:T(8,128)}, u32[]{:S(2)}) copy-start(f32[2048,1024]{1,0:T(8,128)} %get-tuple-element.198) | copy-start | bytes 25165828
  127.3 13.4 %collective-permute-start.13 = (f32[2,2048]{1,0:T(2,128)S(1)}, f32[2,2048]{1,0:T(2,128)S(1)}, u32[]{:S(2)}, u32[]{:S(2)}) collective-permute-start(f32[2,2048]{1,0:T(2,128)S(1)} %pad_maximum_fusion.3), channel_id=1, source_target_pairs={{0,8},{4,12},{8,0},{12,4},{1,9},{5,13},{9,1},{13,5},{2,10},{6,14},... | collective-permute-start | bytes 49160 | tf_op jit(solution)/shard_map/ppermute | solution.py:38
  141.3 4.8 %copy-start = (f32[1024,768]{1,0:T(8,128)}, f32[1024,768]{1,0:T(8,128)S(1)}, u32[]{:S(2)}) copy-start(f32[1024,768]{1,0:T(8,128)S(1)} %get-tuple-element.230) | copy-start | bytes 9437188
  141.3 5.1 %copy-start.3 = (s32[4]{0:T(128)S(1)}, s32[4]{0:T(128)}, u32[]{:S(2)}) copy-start(s32[4]{0:T(128)} %constant.569.clone.1) | copy-start | bytes 52
  142.7 6.1 %collective-permute-start.14 = (f32[512,768]{1,0:T(8,128)}, f32[512,768]{1,0:T(8,128)}, u32[]{:S(2)}, u32[]{:S(2)}) collective-permute-start(f32[512,768]{1,0:T(8,128)} %dynamic-slice_bitcast_fusion.1), channel_id=1, source_target_pairs={{0,1},{1,0},{2,3},{3,2},{4,5},{5,4},{6,7},{7,6},{8,9},{9,8},{10,11... | collective-permute-start | bytes 4718600 | tf_op jit(solution)/shard_map/ppermute | solution.py:61
  146.0 6.6 %collective-permute-start.29 = (f32[512,768]{1,0:T(8,128)}, f32[512,768]{1,0:T(8,128)}, u32[]{:S(2)}, u32[]{:S(2)}) collective-permute-start(f32[512,768]{1,0:T(8,128)} %dynamic-slice_bitcast_fusion), channel_id=1, source_target_pairs={{0,1},{1,0},{2,3},{3,2},{4,5},{5,4},{6,7},{7,6},{8,9},{9,8},{10,11... | collective-permute-start | bytes 4718600 | tf_op jit(solution)/shard_map/ppermute | solution.py:61
  151.0 6.2 %collective-permute-start.18 = (f32[64,768]{1,0:T(8,128)S(1)}, f32[64,768]{1,0:T(8,128)S(1)}, u32[]{:S(2)}, u32[]{:S(2)}) collective-permute-start(f32[64,768]{1,0:T(8,128)S(1)} %dynamic-slice_bitcast_fusion.4), channel_id=1, source_target_pairs={{0,12},{4,0},{8,4},{12,8},{1,13},{5,1},{9,5},{13,9},{2,14},{6,2},{... | collective-permute-start | bytes 589832 | tf_op jit(solution)/shard_map/ppermute | solution.py:66
  151.3 7.4 %collective-permute-start.15 = (f32[64,768]{1,0:T(8,128)S(1)}, f32[64,768]{1,0:T(8,128)S(1)}, u32[]{:S(2)}, u32[]{:S(2)}) collective-permute-start(f32[64,768]{1,0:T(8,128)S(1)} %dynamic-slice_bitcast_fusion.5), channel_id=1, source_target_pairs={{0,4},{4,8},{8,12},{12,0},{1,5},{5,9},{9,13},{13,1},{2,6},{6,10},{... | collective-permute-start | bytes 589832 | tf_op jit(solution)/shard_map/ppermute | solution.py:65
  154.4 7.1 %collective-permute-start.33 = (f32[64,768]{1,0:T(8,128)S(1)}, f32[64,768]{1,0:T(8,128)S(1)}, u32[]{:S(2)}, u32[]{:S(2)}) collective-permute-start(f32[64,768]{1,0:T(8,128)S(1)} %dynamic-slice_bitcast_fusion.2), channel_id=1, source_target_pairs={{0,12},{4,0},{8,4},{12,8},{1,13},{5,1},{9,5},{13,9},{2,14},{6,2},{... | collective-permute-start | bytes 589832 | tf_op jit(solution)/shard_map/ppermute | solution.py:66
  155.9 6.8 %collective-permute-start.30 = (f32[64,768]{1,0:T(8,128)S(1)}, f32[64,768]{1,0:T(8,128)S(1)}, u32[]{:S(2)}, u32[]{:S(2)}) collective-permute-start(f32[64,768]{1,0:T(8,128)S(1)} %dynamic-slice_bitcast_fusion.3), channel_id=1, source_target_pairs={{0,4},{4,8},{8,12},{12,0},{1,5},{5,9},{9,13},{13,1},{2,6},{6,10},{... | collective-permute-start | bytes 589832 | tf_op jit(solution)/shard_map/ppermute | solution.py:65
  157.3 8.4 %collective-permute-start.19 = (f32[64,768]{1,0:T(8,128)S(1)}, f32[64,768]{1,0:T(8,128)S(1)}, u32[]{:S(2)}, u32[]{:S(2)}) collective-permute-start(f32[64,768]{1,0:T(8,128)S(1)} %bitcast_add_fusion.10), channel_id=1, source_target_pairs={{0,12},{4,0},{8,4},{12,8},{1,13},{5,1},{9,5},{13,9},{2,14},{6,2},{... | collective-permute-start | bytes 589832 | tf_op jit(solution)/shard_map/ppermute | solution.py:66
  158.8 8.3 %collective-permute-start.16 = (f32[64,768]{1,0:T(8,128)S(1)}, f32[64,768]{1,0:T(8,128)S(1)}, u32[]{:S(2)}, u32[]{:S(2)}) collective-permute-start(f32[64,768]{1,0:T(8,128)S(1)} %bitcast_add_fusion.13), channel_id=1, source_target_pairs={{0,4},{4,8},{8,12},{12,0},{1,5},{5,9},{9,13},{13,1},{2,6},{6,10},{... | collective-permute-start | bytes 589832 | tf_op jit(solution)/shard_map/ppermute | solution.py:65
  161.5 8.4 %collective-permute-start.34 = (f32[64,768]{1,0:T(8,128)S(1)}, f32[64,768]{1,0:T(8,128)S(1)}, u32[]{:S(2)}, u32[]{:S(2)}) collective-permute-start(f32[64,768]{1,0:T(8,128)S(1)} %bitcast_add_fusion.4), channel_id=1, source_target_pairs={{0,12},{4,0},{8,4},{12,8},{1,13},{5,1},{9,5},{13,9},{2,14},{6,2},{... | collective-permute-start | bytes 589832 | tf_op jit(solution)/shard_map/ppermute | solution.py:66
  162.7 7.8 %collective-permute-start.31 = (f32[64,768]{1,0:T(8,128)S(1)}, f32[64,768]{1,0:T(8,128)S(1)}, u32[]{:S(2)}, u32[]{:S(2)}) collective-permute-start(f32[64,768]{1,0:T(8,128)S(1)} %bitcast_add_fusion.7), channel_id=1, source_target_pairs={{0,4},{4,8},{8,12},{12,0},{1,5},{5,9},{9,13},{13,1},{2,6},{6,10},{... | collective-permute-start | bytes 589832 | tf_op jit(solution)/shard_map/ppermute | solution.py:65
  165.7 8.4 %collective-permute-start.20 = (f32[64,768]{1,0:T(8,128)S(1)}, f32[64,768]{1,0:T(8,128)S(1)}, u32[]{:S(2)}, u32[]{:S(2)}) collective-permute-start(f32[64,768]{1,0:T(8,128)S(1)} %bitcast_add_fusion.9), channel_id=1, source_target_pairs={{0,12},{4,0},{8,4},{12,8},{1,13},{5,1},{9,5},{13,9},{2,14},{6,2},{... | collective-permute-start | bytes 589832 | tf_op jit(solution)/shard_map/ppermute | solution.py:66
  167.1 7.4 %collective-permute-start.17 = (f32[64,768]{1,0:T(8,128)S(1)}, f32[64,768]{1,0:T(8,128)S(1)}, u32[]{:S(2)}, u32[]{:S(2)}) collective-permute-start(f32[64,768]{1,0:T(8,128)S(1)} %bitcast_add_fusion.12), channel_id=1, source_target_pairs={{0,4},{4,8},{8,12},{12,0},{1,5},{5,9},{9,13},{13,1},{2,6},{6,10},{... | collective-permute-start | bytes 589832 | tf_op jit(solution)/shard_map/ppermute | solution.py:65
  169.9 8.4 %collective-permute-start.35 = (f32[64,768]{1,0:T(8,128)S(1)}, f32[64,768]{1,0:T(8,128)S(1)}, u32[]{:S(2)}, u32[]{:S(2)}) collective-permute-start(f32[64,768]{1,0:T(8,128)S(1)} %bitcast_add_fusion.3), channel_id=1, source_target_pairs={{0,12},{4,0},{8,4},{12,8},{1,13},{5,1},{9,5},{13,9},{2,14},{6,2},{... | collective-permute-start | bytes 589832 | tf_op jit(solution)/shard_map/ppermute | solution.py:66
  170.6 8.3 %collective-permute-start.32 = (f32[64,768]{1,0:T(8,128)S(1)}, f32[64,768]{1,0:T(8,128)S(1)}, u32[]{:S(2)}, u32[]{:S(2)}) collective-permute-start(f32[64,768]{1,0:T(8,128)S(1)} %bitcast_add_fusion.6), channel_id=1, source_target_pairs={{0,4},{4,8},{8,12},{12,0},{1,5},{5,9},{9,13},{13,1},{2,6},{6,10},{... | collective-permute-start | bytes 589832 | tf_op jit(solution)/shard_map/ppermute | solution.py:65
  174.5 5.3 %collective-permute-start.21 = (f32[64,768]{1,0:T(8,128)S(1)}, f32[64,768]{1,0:T(8,128)S(1)}, u32[]{:S(2)}, u32[]{:S(2)}) collective-permute-start(f32[64,768]{1,0:T(8,128)S(1)} %fusion.19), channel_id=1, source_target_pairs={{0,2},{2,0},{1,3},{3,1},{4,6},{6,4},{5,7},{7,5},{8,10},{10,8},{9,1... | collective-permute-start | bytes 589832 | tf_op jit(solution)/shard_map/ppermute | solution.py:68
  178.9 6.1 %collective-permute-start.36 = (f32[64,768]{1,0:T(8,128)S(1)}, f32[64,768]{1,0:T(8,128)S(1)}, u32[]{:S(2)}, u32[]{:S(2)}) collective-permute-start(f32[64,768]{1,0:T(8,128)S(1)} %fusion.13), channel_id=1, source_target_pairs={{0,2},{2,0},{1,3},{3,1},{4,6},{6,4},{5,7},{7,5},{8,10},{10,8},{9,1... | collective-permute-start | bytes 589832 | tf_op jit(solution)/shard_map/ppermute | solution.py:68
  179.9 9.4 %collective-permute-start.22 = (f32[64,768]{1,0:T(8,128)S(1)}, f32[64,768]{1,0:T(8,128)S(1)}, u32[]{:S(2)}, u32[]{:S(2)}) collective-permute-start(f32[64,768]{1,0:T(8,128)S(1)} %fusion.23), channel_id=1, source_target_pairs={{0,2},{2,0},{1,3},{3,1},{4,6},{6,4},{5,7},{7,5},{8,10},{10,8},{9,1... | collective-permute-start | bytes 589832 | tf_op jit(solution)/shard_map/ppermute | solution.py:71
  185.1 8.3 %collective-permute-start.37 = (f32[64,768]{1,0:T(8,128)S(1)}, f32[64,768]{1,0:T(8,128)S(1)}, u32[]{:S(2)}, u32[]{:S(2)}) collective-permute-start(f32[64,768]{1,0:T(8,128)S(1)} %fusion.17), channel_id=1, source_target_pairs={{0,2},{2,0},{1,3},{3,1},{4,6},{6,4},{5,7},{7,5},{8,10},{10,8},{9,1... | collective-permute-start | bytes 589832 | tf_op jit(solution)/shard_map/ppermute | solution.py:71
  189.3 8.4 %collective-permute-start.23 = (f32[64,768]{1,0:T(8,128)S(1)}, f32[64,768]{1,0:T(8,128)S(1)}, u32[]{:S(2)}, u32[]{:S(2)}) collective-permute-start(f32[64,768]{1,0:T(8,128)S(1)} %get-tuple-element.208), channel_id=1, source_target_pairs={{0,4},{4,8},{8,12},{12,0},{1,5},{5,9},{9,13},{13,1},{2,6},{6,10},{... | collective-permute-start | bytes 589832 | tf_op jit(solution)/shard_map/ppermute | solution.py:76
  190.7 7.2 %collective-permute-start.24 = (f32[64,768]{1,0:T(8,128)S(1)}, f32[64,768]{1,0:T(8,128)S(1)}, u32[]{:S(2)}, u32[]{:S(2)}) collective-permute-start(f32[64,768]{1,0:T(8,128)S(1)} %get-tuple-element.207), channel_id=1, source_target_pairs={{0,12},{4,0},{8,4},{12,8},{1,13},{5,1},{9,5},{13,9},{2,14},{6,2},{... | collective-permute-start | bytes 589832 | tf_op jit(solution)/shard_map/ppermute | solution.py:77
  193.5 7.0 %collective-permute-start.38 = (f32[64,768]{1,0:T(8,128)S(1)}, f32[64,768]{1,0:T(8,128)S(1)}, u32[]{:S(2)}, u32[]{:S(2)}) collective-permute-start(f32[64,768]{1,0:T(8,128)S(1)} %get-tuple-element.210), channel_id=1, source_target_pairs={{0,4},{4,8},{8,12},{12,0},{1,5},{5,9},{9,13},{13,1},{2,6},{6,10},{... | collective-permute-start | bytes 589832 | tf_op jit(solution)/shard_map/ppermute | solution.py:76
  194.9 8.2 %collective-permute-start.39 = (f32[64,768]{1,0:T(8,128)S(1)}, f32[64,768]{1,0:T(8,128)S(1)}, u32[]{:S(2)}, u32[]{:S(2)}) collective-permute-start(f32[64,768]{1,0:T(8,128)S(1)} %get-tuple-element.209), channel_id=1, source_target_pairs={{0,12},{4,0},{8,4},{12,8},{1,13},{5,1},{9,5},{13,9},{2,14},{6,2},{... | collective-permute-start | bytes 589832 | tf_op jit(solution)/shard_map/ppermute | solution.py:77
  197.7 8.2 %collective-permute-start.25 = (f32[64,768]{1,0:T(8,128)S(1)}, f32[64,768]{1,0:T(8,128)S(1)}, u32[]{:S(2)}, u32[]{:S(2)}) collective-permute-start(f32[64,768]{1,0:T(8,128)S(1)} %collective-permute-done.23), channel_id=1, source_target_pairs={{0,4},{4,8},{8,12},{12,0},{1,5},{5,9},{9,13},{13,1},{2,6},{6,10},{... | collective-permute-start | bytes 589832 | tf_op jit(solution)/shard_map/ppermute | solution.py:76
  197.9 8.1 %collective-permute-start.26 = (f32[64,768]{1,0:T(8,128)S(1)}, f32[64,768]{1,0:T(8,128)S(1)}, u32[]{:S(2)}, u32[]{:S(2)}) collective-permute-start(f32[64,768]{1,0:T(8,128)S(1)} %collective-permute-done.24), channel_id=1, source_target_pairs={{0,12},{4,0},{8,4},{12,8},{1,13},{5,1},{9,5},{13,9},{2,14},{6,2},{... | collective-permute-start | bytes 589832 | tf_op jit(solution)/shard_map/ppermute | solution.py:77
  200.5 8.2 %collective-permute-start.40 = (f32[64,768]{1,0:T(8,128)S(1)}, f32[64,768]{1,0:T(8,128)S(1)}, u32[]{:S(2)}, u32[]{:S(2)}) collective-permute-start(f32[64,768]{1,0:T(8,128)S(1)} %collective-permute-done.38), channel_id=1, source_target_pairs={{0,4},{4,8},{8,12},{12,0},{1,5},{5,9},{9,13},{13,1},{2,6},{6,10},{... | collective-permute-start | bytes 589832 | tf_op jit(solution)/shard_map/ppermute | solution.py:76
  203.1 8.3 %collective-permute-start.41 = (f32[64,768]{1,0:T(8,128)S(1)}, f32[64,768]{1,0:T(8,128)S(1)}, u32[]{:S(2)}, u32[]{:S(2)}) collective-permute-start(f32[64,768]{1,0:T(8,128)S(1)} %collective-permute-done.39), channel_id=1, source_target_pairs={{0,12},{4,0},{8,4},{12,8},{1,13},{5,1},{9,5},{13,9},{2,14},{6,2},{... | collective-permute-start | bytes 589832 | tf_op jit(solution)/shard_map/ppermute | solution.py:77
  205.9 8.3 %collective-permute-start.27 = (f32[64,768]{1,0:T(8,128)S(1)}, f32[64,768]{1,0:T(8,128)S(1)}, u32[]{:S(2)}, u32[]{:S(2)}) collective-permute-start(f32[64,768]{1,0:T(8,128)S(1)} %collective-permute-done.25), channel_id=1, source_target_pairs={{0,4},{4,8},{8,12},{12,0},{1,5},{5,9},{9,13},{13,1},{2,6},{6,10},{... | collective-permute-start | bytes 589832 | tf_op jit(solution)/shard_map/ppermute | solution.py:76
  206.0 8.8 %collective-permute-start.28 = (f32[64,768]{1,0:T(8,128)S(1)}, f32[64,768]{1,0:T(8,128)S(1)}, u32[]{:S(2)}, u32[]{:S(2)}) collective-permute-start(f32[64,768]{1,0:T(8,128)S(1)} %collective-permute-done.26), channel_id=1, source_target_pairs={{0,12},{4,0},{8,4},{12,8},{1,13},{5,1},{9,5},{13,9},{2,14},{6,2},{... | collective-permute-start | bytes 589832 | tf_op jit(solution)/shard_map/ppermute | solution.py:77
  208.7 15.3 %collective-permute-start.42 = (f32[64,768]{1,0:T(8,128)S(1)}, f32[64,768]{1,0:T(8,128)S(1)}, u32[]{:S(2)}, u32[]{:S(2)}) collective-permute-start(f32[64,768]{1,0:T(8,128)S(1)} %collective-permute-done.40), channel_id=1, source_target_pairs={{0,4},{4,8},{8,12},{12,0},{1,5},{5,9},{9,13},{13,1},{2,6},{6,10},{... | collective-permute-start | bytes 589832 | tf_op jit(solution)/shard_map/ppermute | solution.py:76
  211.4 13.3 %collective-permute-start.43 = (f32[64,768]{1,0:T(8,128)S(1)}, f32[64,768]{1,0:T(8,128)S(1)}, u32[]{:S(2)}, u32[]{:S(2)}) collective-permute-start(f32[64,768]{1,0:T(8,128)S(1)} %collective-permute-done.41), channel_id=1, source_target_pairs={{0,12},{4,0},{8,4},{12,8},{1,13},{5,1},{9,5},{13,9},{2,14},{6,2},{... | collective-permute-start | bytes 589832 | tf_op jit(solution)/shard_map/ppermute | solution.py:77
  215.4 11.7 %collective-permute-start.44 = (f32[512,768]{1,0:T(8,128)S(1)}, f32[512,768]{1,0:T(8,128)}, u32[]{:S(2)}, u32[]{:S(2)}) collective-permute-start(f32[512,768]{1,0:T(8,128)S(1)} %bitcast.221), channel_id=1, source_target_pairs={{0,1},{1,0},{2,3},{3,2},{4,5},{5,4},{6,7},{7,6},{8,9},{9,8},{10,11... | collective-permute-start | bytes 4718600 | tf_op jit(solution)/shard_map/ppermute | solution.py:126
  225.2 4.2 %collective-permute-start.45 = (f32[512,768]{1,0:T(8,128)S(1)}, f32[512,768]{1,0:T(8,128)}, u32[]{:S(2)}, u32[]{:S(2)}) collective-permute-start(f32[512,768]{1,0:T(8,128)S(1)} %bitcast.219), channel_id=1, source_target_pairs={{0,1},{1,0},{2,3},{3,2},{4,5},{5,4},{6,7},{7,6},{8,9},{9,8},{10,11... | collective-permute-start | bytes 4718600 | tf_op jit(solution)/shard_map/ppermute | solution.py:126
